TPU v7x, 256 devices: a whole 4x4x8 slice. The times are simulated.
256 devices in a mesh: grid: 16 (over y_hi, z), states: 16 (over y_lo, x, core).
Axes of the slice: x: 4, y: 4 (y_hi: 2, y_lo: 2; y = y_hi * 2 + y_lo), z: 8, core: 2. Of those that a mesh axis runs over, the one named last changes fastest.
Arguments:
- states_in: float32 [16, 256, 32, 128], P('states', 'grid'), may hold values from -10 to 10
- potential: float32 [256, 32, 128], P('grid'), may hold values from -2 to 0.5
- projectors: bfloat16 [16, 32, 8, 4096], P('grid', 'states'), may hold values from -0.0625 to 0.0625
- proj_gains: bfloat16 [16, 32, 8], P('grid', 'states'), may hold values from 1 to 6
- atom_owner: int32 [160], P('grid'), may hold values from 0 to 15, as said below
- atom_rows: int32 [160, 32], P('grid'), may hold values from -1 to 8191, as said below
- wrap_rows: int32 [32], replicated, may hold values from 0 to 31, as said below
Outputs:
- filtered: float32 [16, 256, 32, 128], P('states', 'grid')
Inputs may be any that keep to these rules, and one draw needn't show every extreme that they name: `atom_owner`: atom a belongs to tile a // 10. At most 2 atoms of one tile share an owner, and one owner takes exactly 2 atoms of every tile. `atom_rows`: A row r is the line of cells at x = r // 32, y = r % 32. Each list holds distinct rows whose x lies in the atom's own tile of 16 planes, followed by -1 entries; each list has 16 rows or more, and the first atom of every tile fills all 32. wrap_rows[y] = (y + t) mod 32 for one t of 1 to 31.
All inputs are finite; a program needn't handle non-finite values.
Results may differ from a plain program's by a relative error of at most 0.00082.
Values may be sent and summed in bfloat16 or wider, within the bound.
No kernel may reach another device: no remote copies, remote signals or barrier semaphores. Data moves between devices by JAX's collectives and lax.ppermute only.
A program may use at most 64 MiB of HBM per device.

v0:
```python
import math

import jax
import jax.numpy as jnp
from jax import lax
from jax.sharding import PartitionSpec as P

RADIUS = 6
PAIR_CAP = 2


MIXED_WEIGHT = 0.7
CENTER = 12.0
HALF_WIDTH = 8.0


def padded_2(shard, sides, width):
    for axis, dim in sides:
        count, length = (lax.axis_size(axis), shard.shape[dim])
        up = [(i, (i + 1) % count) for i in range(count)]
        down = [(j, i) for i, j in up]
        last = lax.slice_in_dim(shard, length - width, length, axis=dim)
        initial = lax.slice_in_dim(shard, 0, width, axis=dim)
        before = lax.ppermute(last, axis, up)
        after = lax.ppermute(initial, axis, down)
        shard = jnp.concatenate([before, shard, after], axis=dim)
    return shard


def second_table(radius):
    weights = [-2.0 * sum((1.0 / (k * k) for k in range(1, radius + 1)))]
    for k in range(1, radius + 1):
        weights.append(
            2.0
            * (-1) ** (k + 1)
            * math.factorial(radius) ** 2
            / (k * k * math.factorial(radius - k) * math.factorial(radius + k))
        )
    return weights


def first_table(radius):
    weights = [0.0]
    for k in range(1, radius + 1):
        weights.append(
            (-1) ** (k + 1)
            * math.factorial(radius) ** 2
            / (k * math.factorial(radius - k) * math.factorial(radius + k))
        )
    return weights


def laplacian(padded, plane_count):
    second_weights = second_table(RADIUS)
    first_weights = first_table(RADIUS)
    interior = padded[:, RADIUS : RADIUS + plane_count]
    line_depth = interior.shape[3]
    z_padded = jnp.pad(interior, ((0, 0), (0, 0), (0, 0), (RADIUS, RADIUS)))
    summed = 3.0 * second_weights[0] * interior
    y_slope = jnp.zeros_like(padded)
    for k in range(1, RADIUS + 1):
        summed = summed + second_weights[k] * (
            padded[:, RADIUS + k : RADIUS + k + plane_count]
            + padded[:, RADIUS - k : RADIUS - k + plane_count]
        )
        summed = summed + second_weights[k] * (jnp.roll(interior, -k, 2) + jnp.roll(interior, k, 2))
        summed = summed + second_weights[k] * (
            z_padded[:, :, :, RADIUS + k : RADIUS + k + line_depth]
            + z_padded[:, :, :, RADIUS - k : RADIUS - k + line_depth]
        )
        y_slope = y_slope + first_weights[k] * (jnp.roll(padded, -k, 2) - jnp.roll(padded, k, 2))
    cross_term = jnp.zeros_like(interior)
    for k in range(1, RADIUS + 1):
        cross_term = cross_term + first_weights[k] * (
            y_slope[:, RADIUS + k : RADIUS + k + plane_count]
            - y_slope[:, RADIUS - k : RADIUS - k + plane_count]
        )
    return summed + MIXED_WEIGHT * cross_term


def shards(states_in, potential, projectors, proj_gains, atom_owner, atom_rows, wrap_rows):
    state_count, tile_width, breadth, line_depth = states_in.shape
    n_grid = lax.axis_size("grid")
    n_states = lax.axis_size("states")
    tile_index = lax.axis_index("grid")
    tile_lines = tile_width * breadth
    block_rows = atom_rows.shape[1]
    line_span = block_rows * line_depth
    proj_count = projectors.shape[2]
    home_count = atom_owner.shape[0]
    slot_pairs = projectors.shape[1]
    row_order = jnp.arange(breadth, dtype=jnp.int32)
    unwrap_rows = jnp.sum(
        row_order[None, :] * (wrap_rows[None, :] == row_order[:, None]).astype(jnp.int32), axis=1
    )
    atom_order = jnp.arange(home_count, dtype=jnp.int32)
    same_owner = (atom_owner[:, None] == atom_owner[None, :]) & (
        atom_order[None, :] < atom_order[:, None]
    )
    owner_rank = jnp.sum(same_owner.astype(jnp.int32), axis=1)
    atom_slot = atom_owner * PAIR_CAP + owner_rank
    local_rows = jnp.where(atom_rows >= 0, atom_rows - tile_index * tile_lines, tile_lines)

    gain_lanes = jnp.zeros((1, slot_pairs, proj_count, 128), jnp.bfloat16)
    gain_lanes = gain_lanes.at[..., 0].set(proj_gains)
    packed = jnp.concatenate([projectors, gain_lanes], axis=3)
    pairs = [(o * n_states + t, t * n_states + o) for o in range(n_grid) for t in range(n_states)]
    packed = lax.ppermute(packed, ("grid", "states"), pairs)
    gathered = lax.all_gather(packed[0], "states", axis=0, tiled=True)
    gathered = gathered.reshape(n_states * slot_pairs, proj_count, line_span + 128)
    atom_pack = jnp.take(gathered, atom_slot, axis=0)
    proj_rows = atom_pack[:, :, :line_span].reshape(home_count * proj_count, line_span)
    atom_gain = atom_pack[:, :, line_span].astype(jnp.float32)
    selector = (
        local_rows.reshape(-1)[:, None] == jnp.arange(tile_lines, dtype=jnp.int32)[None, :]
    ).astype(jnp.bfloat16)
    atom_eye = jnp.eye(home_count, dtype=jnp.float32)

    def extended(grid_field):
        padded = padded_2(grid_field, (("grid", 1),), RADIUS)
        low_rim = padded[:, :RADIUS]
        high_rim = padded[:, RADIUS + tile_width :]
        low_rim = jnp.where(tile_index == 0, jnp.take(low_rim, wrap_rows, axis=2), low_rim)
        high_rim = jnp.where(
            tile_index == n_grid - 1, jnp.take(high_rim, unwrap_rows, axis=2), high_rim
        )
        return jnp.concatenate([low_rim, padded[:, RADIUS : RADIUS + tile_width], high_rim], axis=1)

    def nonlocal_part(grid_field):
        lines_here = grid_field.reshape(tile_lines, line_depth).astype(jnp.bfloat16)
        picked = jnp.dot(selector, lines_here, preferred_element_type=jnp.float32)
        picked = picked.astype(jnp.bfloat16).reshape(home_count, line_span)
        every_pair = lax.dot_general(
            proj_rows, picked, (((1,), (1,)), ((), ())), preferred_element_type=jnp.float32
        ).reshape(home_count, proj_count, home_count)
        coefficients = jnp.sum(every_pair * atom_eye[:, None, :], axis=2)
        scaled = (coefficients * atom_gain).astype(jnp.bfloat16)
        block_scaled = (atom_eye.astype(jnp.bfloat16)[:, :, None] * scaled[None, :, :]).reshape(
            home_count, home_count * proj_count
        )
        projected = jnp.dot(block_scaled, proj_rows, preferred_element_type=jnp.float32)
        projected = projected.astype(jnp.bfloat16).reshape(home_count * block_rows, line_depth)
        summed = lax.dot_general(
            selector, projected, (((0,), (0,)), ((), ())), preferred_element_type=jnp.float32
        )
        return summed.reshape(state_count, tile_width, breadth, line_depth)

    def operate(grid_field):
        padded = extended(grid_field)
        return (
            -0.5 * laplacian(padded, tile_width)
            + potential[None] * grid_field
            + nonlocal_part(grid_field)
        )

    def shifted(grid_field):
        return (operate(grid_field) - CENTER * grid_field) / HALF_WIDTH

    first_term = shifted(states_in)
    second_term = 2.0 * shifted(first_term) - states_in
    return 2.0 * shifted(second_term) - first_term


def solution(mesh):
    in_specs = (
        P("states", "grid", None, None),
        P("grid", None, None),
        P("grid", "states", None, None),
        P("grid", "states", None),
        P("grid"),
        P("grid", None),
        P(),
    )
    out_specs = P("states", "grid", None, None)
    return jax.shard_map(shards, mesh=mesh, in_specs=in_specs, out_specs=out_specs, check_vma=False)
```

profile of v0, /device:TPU:6, one launch (start us, length us, event | category | flops | bytes accessed | tf_op | source)
XLA Modules:
  0.0 135.0 jit_solution(8653599819950323269)
XLA Ops:
  7.3 0.9 fusion.328
  8.3 8.1 %collective-permute-start.2 = (bf16[1,2,8,4224]{3,2,0,1:T(8,128)(2,1)S(1)}, bf16[1,2,8,4224]{3,2,0,1:T(8,128)(2,1)S(1)}, u32[]{:S(2)}, u32[]{:S(2)}) collective-permute-start(bf16[1,2,8,4224]{3,2,0,1:T(8,128)(2,1)S(1)} %fusion.328), channel_id=1, source_target_pairs={{0,0},{1,16},{2,32},{3,48},{4,64},{5,80},{6,96},{7,112},{8,128},{9... | collective-permute-start | bytes 405512 | tf_op jit(solution)/shard_map/ppermute | solution.py:108
  16.4 1.0 fusion.419
  17.4 2.7 %collective-permute-start = (f32[1,6,32,128]{3,2,1,0:T(8,128)S(1)}, f32[1,6,32,128]{3,2,1,0:T(8,128)S(1)}, u32[]{:S(2)}, u32[]{:S(2)}) collective-permute-start(f32[1,6,32,128]{3,2,1,0:T(8,128)S(1)} %get-tuple-element.164), channel_id=1, source_target_pairs={{16,0},{32,16},{48,32},{64,48},{80,64},{96,80},{112,96},{128,112},... | collective-permute-start | bytes 294920 | tf_op jit(solution)/shard_map/ppermute | solution.py:25
  20.0 1.0 convert_element_type.119
  23.2 0.8 fusion.412
  26.2 0.9 fusion.416
  36.2 30.0 %all-gather.3.cloned.1.call-done = bf16[1,32,8,4224]{3,2,0,1:T(8,128)(2,1)} async-done(((bf16[1,2,8,4224]{3,2,0,1:T(8,128)(2,1)}), bf16[1,32,8,4224]{3,2,0,1:T(8,128)(2,1)}) %all-gather.3.cloned.1.call-update) | async-done | bytes 2162704 | tf_op jit(solution)/shard_map/all_gather | solution.py:109
  66.2 2.2 %gather_fusion = bf16[10,8,4224]{2,1,0:T(8,128)(2,1)S(1)} fusion(bf16[32,8,4224]{2,1,0:T(8,128)(2,1)} %bitcast.111, s32[1024]{0:T(1024)S(1)} %pad_clamp_fusion), kind=kCustom, calls=%fused_computation.6 | custom fusion | bytes 1351720 | tf_op jit(solution)/shard_map/jit(_take)/gather | solution.py:111
  68.4 0.9 copy_select_fusion
  69.5 1.3 fusion.48
  71.8 4.3 %broadcast_multiply_fusion = (f32[1,16,32,128]{3,2,1,0:T(8,128)S(1)}, bf16[1,16,32,128]{3,2,1,0:T(8,128)(2,1)S(1)}, f32[1,16,32,128]{3,2,1,0:T(8,128)}) fusion(f32[1,16,32,128]{3,2,1,0:T(8,128)S(1)} %copy-done, bf16[320,128,1]{1,0,2:T(8,128)(2,1)S(1)} %reshape.2362, s32[16,32]{1,0:T(8,128)S(1)} %multiply_add_fusion, s32[320]{0:T(512)} %copy-done.55, ...), kind=kOutput, calls=%fused_computation.493 | convolution fusion | flops 49053696 | bytes 7752960 | tf_op jit(solution)/shard_map/dot_general | solution.py:143
  79.0 0.8 fusion.401
  80.4 0.8 fusion.403
  82.5 1.3 fusion.49
  84.3 5.5 %collective-permute-start.3 = (f32[1,6,32,128]{3,2,1,0:T(8,128)S(1)}, f32[1,6,32,128]{3,2,1,0:T(8,128)S(1)}, u32[]{:S(2)}, u32[]{:S(2)}) collective-permute-start(f32[1,6,32,128]{3,2,1,0:T(8,128)S(1)} %get-tuple-element.136), channel_id=1, source_target_pairs={{16,0},{32,16},{48,32},{64,48},{80,64},{96,80},{112,96},{128,112},... | collective-permute-start | bytes 294920 | tf_op jit(solution)/shard_map/ppermute | solution.py:25
  91.2 1.1 collective-permute-done.3
  93.0 5.2 %collective-permute-done.4 = f32[1,6,32,128]{3,2,1,0:T(8,128)S(1)} collective-permute-done((f32[1,6,32,128]{3,2,1,0:T(8,128)S(1)}, f32[1,6,32,128]{3,2,1,0:T(8,128)S(1)}, u32[]{:S(2)}, u32[]{:S(2)}) %collective-permute-start.4) | collective-permute-done | bytes 98336 | tf_op jit(solution)/shard_map/ppermute | solution.py:24
  102.8 1.4 %fusion.420 = (bf16[1,16,32,128]{3,2,1,0:T(8,128)(2,1)S(1)}, f32[1,16,32,128]{3,2,1,0:T(8,128)S(1)}) fusion(f32[1,16,32,128]{3,2,1,0:T(8,128)S(1)} %copy-done, f32[1,16,32,128]{3,2,1,0:T(8,128)S(1)} %copy-done.63, bf16[320,128,1]{1,0,2:T(8,128)(2,1)S(1)} %copy-done.18, s32[16,32]{1,0:T(8,128)S(1)} %multiply_add_fusion, s32[320]{0:T(512)S(1)} %copy-done.57, ...), kind=kOutput, calls=%fused_computation.611 | convolution fusion | flops 49119232 | bytes 8015104 | tf_op jit(solution)/shard_map/dot_general | solution.py:143
  108.5 0.8 fusion.384
  111.3 1.3 fusion.50
  113.1 5.6 %collective-permute-start.5 = (f32[1,6,32,128]{3,2,1,0:T(8,128)S(1)}, f32[1,6,32,128]{3,2,1,0:T(8,128)S(1)}, u32[]{:S(2)}, u32[]{:S(2)}) collective-permute-start(f32[1,6,32,128]{3,2,1,0:T(8,128)S(1)} %get-tuple-element.110), channel_id=1, source_target_pairs={{16,0},{32,16},{48,32},{64,48},{80,64},{96,80},{112,96},{128,112},... | collective-permute-start | bytes 294920 | tf_op jit(solution)/shard_map/ppermute | solution.py:25
  119.4 1.9 %collective-permute-done.6 = f32[1,6,32,128]{3,2,1,0:T(8,128)S(1)} collective-permute-done((f32[1,6,32,128]{3,2,1,0:T(8,128)S(1)}, f32[1,6,32,128]{3,2,1,0:T(8,128)S(1)}, u32[]{:S(2)}, u32[]{:S(2)}) %collective-permute-start.6) | collective-permute-done | bytes 98336 | tf_op jit(solution)/shard_map/ppermute | solution.py:24
  125.5 2.7 %fusion.27 = f32[1,16,32,128]{3,2,1,0:T(8,128)} fusion(bf16[320,128,1]{1,0,2:T(8,128)(2,1)S(1)} %reshape.2368, s32[16,32]{1,0:T(8,128)S(1)} %multiply_add_fusion, s32[320]{0:T(512)S(1)} %copy-done.58, f32[1,16,32,128]{3,2,1,0:T(8,128)S(1)} %get-tuple-element.168, f32[1,6,32,128]{3,2,1,0:T(8,128)S(1)} %fusion.329, f32[1,6,32,128]{3,2,1,0:T(8,128)S(1)} %fusion.330, ...), kind=kOutput, calls=%fused_computation.61 | convolution fusion | flops 49119232 | bytes 7621888 | tf_op jit(solution)/shard_map/dot_general | solution.py:143
  (262 shorter events, 37.4 us)
Async XLA Ops:
  6.5 15.3 %copy-start = (f32[1,16,32,128]{3,2,1,0:T(8,128)S(1)}, f32[1,16,32,128]{3,2,1,0:T(8,128)}, u32[]{:S(2)}) copy-start(f32[1,16,32,128]{3,2,1,0:T(8,128)} %param.11) | copy-start | bytes 786436
  6.5 15.1 %copy-start.62 = (s32[32]{0:T(128)S(1)}, s32[32]{0:T(128)}, u32[]{:S(2)}) copy-start(s32[32]{0:T(128)} %param.17) | copy-start | bytes 388
  6.5 59.6 %all-gather.3.cloned.1.call-start = ((), (), s32[]{:S(2)}) async-start(), calls=%async_computation | async-start | bytes 2297856 | tf_op jit(solution)/shard_map/all_gather | solution.py:109
  8.3 21.2 %collective-permute-start.2 = (bf16[1,2,8,4224]{3,2,0,1:T(8,128)(2,1)S(1)}, bf16[1,2,8,4224]{3,2,0,1:T(8,128)(2,1)S(1)}, u32[]{:S(2)}, u32[]{:S(2)}) collective-permute-start(bf16[1,2,8,4224]{3,2,0,1:T(8,128)(2,1)S(1)} %fusion.328), channel_id=1, source_target_pairs={{0,0},{1,16},{2,32},{3,48},{4,64},{5,80},{6,96},{7,112},{8,128},{9... | collective-permute-start | bytes 405512 | tf_op jit(solution)/shard_map/ppermute | solution.py:108
  17.4 15.7 %collective-permute-start = (f32[1,6,32,128]{3,2,1,0:T(8,128)S(1)}, f32[1,6,32,128]{3,2,1,0:T(8,128)S(1)}, u32[]{:S(2)}, u32[]{:S(2)}) collective-permute-start(f32[1,6,32,128]{3,2,1,0:T(8,128)S(1)} %get-tuple-element.164), channel_id=1, source_target_pairs={{16,0},{32,16},{48,32},{64,48},{80,64},{96,80},{112,96},{128,112},... | collective-permute-start | bytes 294920 | tf_op jit(solution)/shard_map/ppermute | solution.py:25
  20.0 13.1 %collective-permute-start.1 = (f32[1,6,32,128]{3,2,1,0:T(8,128)S(1)}, f32[1,6,32,128]{3,2,1,0:T(8,128)S(1)}, u32[]{:S(2)}, u32[]{:S(2)}) collective-permute-start(f32[1,6,32,128]{3,2,1,0:T(8,128)S(1)} %get-tuple-element.165), channel_id=1, source_target_pairs={{0,16},{16,32},{32,48},{48,64},{64,80},{80,96},{96,112},{112,128},... | collective-permute-start | bytes 294920 | tf_op jit(solution)/shard_map/ppermute | solution.py:24
  21.8 12.7 %copy-start.48 = (pred[32]{0:T(512)(128)(4,1)}, pred[32]{0:T(512)(128)(4,1)S(1)}, u32[]{:S(2)}) copy-start(pred[32]{0:T(512)(128)(4,1)S(1)} %compare_and_fusion.1) | copy-start | bytes 100
  21.8 12.7 %copy-start.50 = (pred[32]{0:T(512)(128)(4,1)}, pred[32]{0:T(512)(128)(4,1)S(1)}, u32[]{:S(2)}) copy-start(pred[32]{0:T(512)(128)(4,1)S(1)} %compare_and_fusion) | copy-start | bytes 100
  24.7 3.5 %copy-start.59 = (s32[10]{0:T(128)S(1)}, s32[10]{0:T(128)}, u32[]{:S(2)}) copy-start(s32[10]{0:T(128)} %param.15) | copy-start | bytes 124
  24.7 4.3 %copy-start.38 = (s32[10,32]{1,0:T(8,128)S(1)}, s32[10,32]{1,0:T(8,128)}, u32[]{:S(2)}) copy-start(s32[10,32]{1,0:T(8,128)} %param.16) | copy-start | bytes 3844
  29.2 4.0 %copy-start.55 = (s32[320]{0:T(512)}, s32[320]{0:T(512)S(1)}, u32[]{:S(2)}) copy-start(s32[320]{0:T(512)S(1)} %eq.101) | copy-start | bytes 3844
  33.1 1.5 %copy-start.47 = (s32[1024]{0:T(1024)}, s32[1024]{0:T(1024)S(1)}, u32[]{:S(2)}) copy-start(s32[1024]{0:T(1024)S(1)} %pad_clamp_fusion.1) | copy-start | bytes 12292
  69.4 1.5 %copy-start.52 = (bf16[10,10]{1,0:T(8,128)(2,1)S(1)}, bf16[10,10]{1,0:T(8,128)(2,1)}, u32[]{:S(2)}) copy-start(bf16[10,10]{1,0:T(8,128)(2,1)} %copy.43) | copy-start | bytes 604
  80.4 1.7 %copy-start.56 = (s32[320]{0:T(512)S(1)}, s32[320]{0:T(512)}, u32[]{:S(2)}) copy-start(s32[320]{0:T(512)} %copy-done.55) | copy-start | bytes 3844
  84.3 8.0 %collective-permute-start.3 = (f32[1,6,32,128]{3,2,1,0:T(8,128)S(1)}, f32[1,6,32,128]{3,2,1,0:T(8,128)S(1)}, u32[]{:S(2)}, u32[]{:S(2)}) collective-permute-start(f32[1,6,32,128]{3,2,1,0:T(8,128)S(1)} %get-tuple-element.136), channel_id=1, source_target_pairs={{16,0},{32,16},{48,32},{64,48},{80,64},{96,80},{112,96},{128,112},... | collective-permute-start | bytes 294920 | tf_op jit(solution)/shard_map/ppermute | solution.py:25
  89.8 8.3 %collective-permute-start.4 = (f32[1,6,32,128]{3,2,1,0:T(8,128)S(1)}, f32[1,6,32,128]{3,2,1,0:T(8,128)S(1)}, u32[]{:S(2)}, u32[]{:S(2)}) collective-permute-start(f32[1,6,32,128]{3,2,1,0:T(8,128)S(1)} %get-tuple-element.137), channel_id=1, source_target_pairs={{0,16},{16,32},{32,48},{48,64},{64,80},{80,96},{96,112},{112,128},... | collective-permute-start | bytes 294920 | tf_op jit(solution)/shard_map/ppermute | solution.py:24
  101.3 1.5 %copy-start.60 = (f32[16,32,128]{2,1,0:T(8,128)S(1)}, f32[16,32,128]{2,1,0:T(8,128)}, u32[]{:S(2)}) copy-start(f32[16,32,128]{2,1,0:T(8,128)} %param.12) | copy-start | bytes 786436
  101.3 1.6 %copy-start.63 = (f32[1,16,32,128]{3,2,1,0:T(8,128)S(1)}, f32[1,16,32,128]{3,2,1,0:T(8,128)}, u32[]{:S(2)}) copy-start(f32[1,16,32,128]{3,2,1,0:T(8,128)} %get-tuple-element.166) | copy-start | bytes 786436
  109.4 1.9 %copy-start.41 = (f32[10,10]{0,1:T(8,128)S(1)}, f32[10,10]{0,1:T(8,128)}, u32[]{:S(2)}) copy-start(f32[10,10]{0,1:T(8,128)} %fusion.344) | copy-start | bytes 1204
  112.6 10.2 %copy-start.51 = (pred[32]{0:T(512)(128)(4,1)S(1)}, pred[32]{0:T(512)(128)(4,1)}, u32[]{:S(2)}) copy-start(pred[32]{0:T(512)(128)(4,1)} %copy-done.50) | copy-start | bytes 100
  113.1 9.8 %copy-start.49 = (pred[32]{0:T(512)(128)(4,1)S(1)}, pred[32]{0:T(512)(128)(4,1)}, u32[]{:S(2)}) copy-start(pred[32]{0:T(512)(128)(4,1)} %copy-done.48) | copy-start | bytes 100
  113.1 8.3 %collective-permute-start.6 = (f32[1,6,32,128]{3,2,1,0:T(8,128)S(1)}, f32[1,6,32,128]{3,2,1,0:T(8,128)S(1)}, u32[]{:S(2)}, u32[]{:S(2)}) collective-permute-start(f32[1,6,32,128]{3,2,1,0:T(8,128)S(1)} %get-tuple-element.111), channel_id=1, source_target_pairs={{0,16},{16,32},{32,48},{48,64},{64,80},{80,96},{96,112},{112,128},... | collective-permute-start | bytes 294920 | tf_op jit(solution)/shard_map/ppermute | solution.py:24
  113.1 9.0 %collective-permute-start.5 = (f32[1,6,32,128]{3,2,1,0:T(8,128)S(1)}, f32[1,6,32,128]{3,2,1,0:T(8,128)S(1)}, u32[]{:S(2)}, u32[]{:S(2)}) collective-permute-start(f32[1,6,32,128]{3,2,1,0:T(8,128)S(1)} %get-tuple-element.110), channel_id=1, source_target_pairs={{16,0},{32,16},{48,32},{64,48},{80,64},{96,80},{112,96},{128,112},... | collective-permute-start | bytes 294920 | tf_op jit(solution)/shard_map/ppermute | solution.py:25
  123.9 1.6 %copy-start.64 = (f32[1,16,32,128]{3,2,1,0:T(8,128)S(1)}, f32[1,16,32,128]{3,2,1,0:T(8,128)}, u32[]{:S(2)}) copy-start(f32[1,16,32,128]{3,2,1,0:T(8,128)} %get-tuple-element.166) | copy-start | bytes 786436
  (49 other events, 60.9 us)
Sparse Core Ops, SparseCore 0:
  30.3 35.8 all-gather.2
where the time goes:
time: 136 us; the launch traced here: 135 us
  waiting for transfers between devices  38.2 us (28%)
  local copies, waits for them, and re-layouts  36.5 us (27%)
  starting transfers between devices  22 us (16%)
  matrix products  14.8 us (11%)
  between operations  14.7 us (11%)
  other arithmetic  8.83 us (6%)
    all_gather x1, waiting for transfers between devices, shards(): gathered = lax.all_gather(packed[0], 'states', axis=0, tiled=True)  30 us
    slice x36, local copies, waits for them, and re-layouts, laplacian(): jnp.roll(interior, k, 2)  21.6 us
    ppermute x3, starting transfers between devices, padded_2(): after = lax.ppermute(initial, axis, down)  13.8 us
    dot_general x3, matrix products, nonlocal_part(): lax.dot_general(selector, projected, (((0,), (0,)), ((), ())), preferred_...  8.52 us
    ppermute x1, starting transfers between devices, shards(): packed = lax.ppermute(packed, ('grid', 'states'), pairs)  8.12 us
    ppermute x3, waiting for transfers between devices, padded_2(): before = lax.ppermute(last, axis, up)  7.08 us
    dot_general x3, matrix products, nonlocal_part(): lax.dot_general(proj_rows, picked, (((1,), (1,)), ((), ())), preferred_el...  4.03 us
    unnamed x131, local copies, waits for them, and re-layouts  3.32 us
  transfers between devices with their start and end apart: 8, of which 4 were waited for; matrix products, arithmetic and copies ran while one was open for 14% of the time, Pallas kernels for 0%

commit v1 on v0

--- a/solution.py
+++ b/solution.py
@@ -106,9 +106,11 @@
     packed = jnp.concatenate([projectors, gain_lanes], axis=3)
     pairs = [(o * n_states + t, t * n_states + o) for o in range(n_grid) for t in range(n_states)]
     packed = lax.ppermute(packed, ("grid", "states"), pairs)
-    gathered = lax.all_gather(packed[0], "states", axis=0, tiled=True)
-    gathered = gathered.reshape(n_states * slot_pairs, proj_count, line_span + 128)
-    atom_pack = jnp.take(gathered, atom_slot, axis=0)
+    mine = atom_owner == lax.axis_index("states")
+    atom_pack = jnp.where(
+        mine[:, None, None], jnp.take(packed[0], owner_rank, axis=0), jnp.zeros((), jnp.bfloat16)
+    )
+    atom_pack = lax.psum(atom_pack, "states")
     proj_rows = atom_pack[:, :, :line_span].reshape(home_count * proj_count, line_span)
     atom_gain = atom_pack[:, :, line_span].astype(jnp.float32)
     selector = (

time: 136 us -> 237 us (1.74)
  waiting for transfers between devices: 38.2 us -> 127 us
  other arithmetic: 8.83 us -> 13.1 us
  matrix products: 14.8 us -> 18.6 us
    psum x0 -> x1, waiting for transfers between devices: none -> 119 us  [shards(): atom_pack = lax.psum(atom_pack, 'states')]
    all_gather x1 -> x0, waiting for transfers between devices: 30 us -> none  [shards(): gathered = lax.all_gather(packed[0], 'states', axis=0, tiled=True)]
    slice x33, local copies, waits for them, and re-layouts: 1.77 us -> 6.87 us  [laplacian(): jnp.roll(padded, k, 2)]
    dot_general x3, matrix products: 4.03 us -> 7.92 us  [nonlocal_part(): lax.dot_general(proj_rows, picked, (((1,), (1,)), ((), ())), preferred_el...]
    slice x36, local copies, waits for them, and re-layouts: 21.6 us -> 18.8 us  [laplacian(): jnp.roll(interior, k, 2)]
  transfers between devices with their start and end apart: 8 -> 8, of which waited for: 4 -> 4; matrix products, arithmetic and copies ran while one was open for 14% -> 12% of each run, Pallas kernels for 0% -> 0%
where the time goes in v1:
time: 237 us; the launch traced here: 234 us
  waiting for transfers between devices  127 us (54%)
  local copies, waits for them, and re-layouts  37.9 us (16%)
  starting transfers between devices  22.4 us (9%)
  matrix products  18.6 us (8%)
  between operations  14.9 us (6%)
  other arithmetic  13.1 us (6%)
    psum x1, waiting for transfers between devices, shards(): atom_pack = lax.psum(atom_pack, 'states')  119 us
    slice x36, local copies, waits for them, and re-layouts, laplacian(): jnp.roll(interior, k, 2)  18.8 us
    ppermute x3, starting transfers between devices, padded_2(): after = lax.ppermute(initial, axis, down)  14.1 us
    dot_general x3, matrix products, nonlocal_part(): lax.dot_general(selector, projected, (((0,), (0,)), ((), ())), preferred_...  8.39 us
    ppermute x1, starting transfers between devices, shards(): packed = lax.ppermute(packed, ('grid', 'states'), pairs)  8.12 us
    dot_general x3, matrix products, nonlocal_part(): lax.dot_general(proj_rows, picked, (((1,), (1,)), ((), ())), preferred_el...  7.92 us
    slice x33, local copies, waits for them, and re-layouts, laplacian(): jnp.roll(padded, k, 2)  6.87 us
    ppermute x3, waiting for transfers between devices, padded_2(): before = lax.ppermute(last, axis, up)  6.79 us
  transfers between devices with their start and end apart: 8, of which 4 were waited for; matrix products, arithmetic and copies ran while one was open for 12% of the time, Pallas kernels for 0%

profile of v1, /device:TPU:6, one launch (start us, length us, event | category | flops | bytes accessed | tf_op | source)
XLA Modules:
  0.0 233.8 jit_solution(16048125886329095664)
XLA Ops:
  7.3 0.9 fusion.329
  8.3 8.1 %collective-permute-start.2 = (bf16[1,2,8,4224]{3,2,1,0:T(8,128)(2,1)S(1)}, bf16[1,2,8,4224]{3,2,1,0:T(8,128)(2,1)S(1)}, u32[]{:S(2)}, u32[]{:S(2)}) collective-permute-start(bf16[1,2,8,4224]{3,2,1,0:T(8,128)(2,1)S(1)} %fusion.329), channel_id=1, source_target_pairs={{0,0},{1,16},{2,32},{3,48},{4,64},{5,80},{6,96},{7,112},{8,128},{9... | collective-permute-start | bytes 405512 | tf_op jit(solution)/shard_map/ppermute | solution.py:108
  16.4 1.0 fusion.421
  17.4 2.7 %collective-permute-start = (f32[1,6,32,128]{3,2,1,0:T(8,128)S(1)}, f32[1,6,32,128]{3,2,1,0:T(8,128)S(1)}, u32[]{:S(2)}, u32[]{:S(2)}) collective-permute-start(f32[1,6,32,128]{3,2,1,0:T(8,128)S(1)} %get-tuple-element.162), channel_id=1, source_target_pairs={{16,0},{32,16},{48,32},{64,48},{80,64},{96,80},{112,96},{128,112},... | collective-permute-start | bytes 294920 | tf_op jit(solution)/shard_map/ppermute | solution.py:25
  20.0 1.0 convert_element_type.119
  25.4 0.9 fusion.414
  26.9 0.8 fusion.416
  29.8 0.9 fusion.420
  37.4 1.0 fusion.379
  39.1 1.0 fusion.377
  42.9 1.9 fusion.51
  47.5 119.2 %all-reduce.6.cloned.1.call-done = bf16[10,8,4224]{2,0,1:T(8,128)(2,1)} async-done(((bf16[10,8,4224]{2,0,1:T(8,128)(2,1)}), bf16[10,8,4224]{2,0,1:T(8,128)(2,1)}) %all-reduce.6.cloned.1.call-update) | async-done | bytes 675856 | tf_op jit(solution)/shard_map/psum | solution.py:113
  166.7 0.9 convert_reduce_fusion
  167.7 2.6 %fusion.48 = f32[10,8]{0,1:T(8,128)S(1)} fusion(bf16[10,4096,1]{1,0,2:T(8,128)(2,1)} %reshape.2372, bf16[10,8,4224]{2,0,1:T(8,128)(2,1)} %all-reduce.6.cloned.1.call-done, f32[10,10]{0,1:T(8,128)S(1)} %copy-done.53), kind=kOutput, calls=%fused_computation.74 | convolution fusion | flops 6555120 | bytes 1180368 | tf_op jit(solution)/shard_map/dot_general | solution.py:135
  171.7 4.2 %broadcast_multiply_fusion = (f32[1,16,32,128]{3,2,1,0:T(8,128)S(1)}, bf16[1,16,32,128]{3,2,1,0:T(8,128)(2,1)S(1)}, f32[1,16,32,128]{3,2,1,0:T(8,128)}) fusion(f32[1,16,32,128]{3,2,1,0:T(8,128)S(1)} %copy-done, bf16[320,128,1]{1,0,2:T(8,128)(2,1)S(1)} %reshape.2374, s32[16,32]{1,0:T(8,128)S(1)} %copy-done.51, s32[320]{0:T(512)} %copy-done.69, ...), kind=kOutput, calls=%fused_computation.494 | convolution fusion | flops 49053696 | bytes 7752960 | tf_op jit(solution)/shard_map/dot_general | solution.py:145
  180.7 2.7 %fusion.49 = f32[10,8]{0,1:T(8,128)S(1)} fusion(bf16[10,4096,1]{1,0,2:T(8,128)(2,1)S(1)} %reshape.2375, bf16[10,8,4224]{2,0,1:T(8,128)(2,1)} %all-reduce.6.cloned.1.call-done, f32[10,10]{0,1:T(8,128)S(1)} %copy-done.54), kind=kOutput, calls=%fused_computation.75 | convolution fusion | flops 6555120 | bytes 1131216 | tf_op jit(solution)/shard_map/dot_general | solution.py:135
  183.4 5.8 %collective-permute-start.3 = (f32[1,6,32,128]{3,2,1,0:T(8,128)S(1)}, f32[1,6,32,128]{3,2,1,0:T(8,128)S(1)}, u32[]{:S(2)}, u32[]{:S(2)}) collective-permute-start(f32[1,6,32,128]{3,2,1,0:T(8,128)S(1)} %get-tuple-element.134), channel_id=1, source_target_pairs={{16,0},{32,16},{48,32},{64,48},{80,64},{96,80},{112,96},{128,112},... | collective-permute-start | bytes 294920 | tf_op jit(solution)/shard_map/ppermute | solution.py:25
  190.4 1.0 collective-permute-done.3
  192.1 5.3 %collective-permute-done.4 = f32[1,6,32,128]{3,2,1,0:T(8,128)S(1)} collective-permute-done((f32[1,6,32,128]{3,2,1,0:T(8,128)S(1)}, f32[1,6,32,128]{3,2,1,0:T(8,128)S(1)}, u32[]{:S(2)}, u32[]{:S(2)}) %collective-permute-start.4) | collective-permute-done | bytes 98336 | tf_op jit(solution)/shard_map/ppermute | solution.py:24
  201.9 1.4 fusion.422
  208.1 2.7 %fusion.50 = f32[10,8]{0,1:T(8,128)S(1)} fusion(bf16[10,4096,1]{1,0,2:T(8,128)(2,1)S(1)} %reshape.2378, bf16[10,8,4224]{2,0,1:T(8,128)(2,1)} %all-reduce.6.cloned.1.call-done, f32[10,10]{0,1:T(8,128)S(1)} %copy-done.55), kind=kOutput, calls=%fused_computation.76 | convolution fusion | flops 6555120 | bytes 1131216 | tf_op jit(solution)/shard_map/dot_general | solution.py:135
  210.8 5.6 %collective-permute-start.5 = (f32[1,6,32,128]{3,2,1,0:T(8,128)S(1)}, f32[1,6,32,128]{3,2,1,0:T(8,128)S(1)}, u32[]{:S(2)}, u32[]{:S(2)}) collective-permute-start(f32[1,6,32,128]{3,2,1,0:T(8,128)S(1)} %get-tuple-element.108), channel_id=1, source_target_pairs={{16,0},{32,16},{48,32},{64,48},{80,64},{96,80},{112,96},{128,112},... | collective-permute-start | bytes 294920 | tf_op jit(solution)/shard_map/ppermute | solution.py:25
  217.6 1.4 collective-permute-done.6
  224.2 2.8 %fusion.27 = f32[1,16,32,128]{3,2,1,0:T(8,128)} fusion(bf16[320,128,1]{1,0,2:T(8,128)(2,1)S(1)} %reshape.2380, s32[16,32]{1,0:T(8,128)S(1)} %copy-done.52, s32[320]{0:T(512)S(1)} %copy-done.72, f32[1,16,32,128]{3,2,1,0:T(8,128)S(1)} %get-tuple-element.166, f32[1,6,32,128]{3,2,1,0:T(8,128)S(1)} %fusion.330, f32[1,6,32,128]{3,2,1,0:T(8,128)S(1)} %fusion.331, ...), kind=kOutput, calls=%fused_computation.61 | convolution fusion | flops 49119232 | bytes 7621888 | tf_op jit(solution)/shard_map/dot_general | solution.py:145
  (297 shorter events, 43.0 us)
Async XLA Ops:
  6.5 15.9 %copy-start = (f32[1,16,32,128]{3,2,1,0:T(8,128)S(1)}, f32[1,16,32,128]{3,2,1,0:T(8,128)}, u32[]{:S(2)}) copy-start(f32[1,16,32,128]{3,2,1,0:T(8,128)} %param.11) | copy-start | bytes 786436
  6.5 15.7 %copy-start.79 = (s32[32]{0:T(128)S(1)}, s32[32]{0:T(128)}, u32[]{:S(2)}) copy-start(s32[32]{0:T(128)} %param.17) | copy-start | bytes 388
  6.5 160.2 %all-reduce.6.cloned.1.call-start = ((), (), s32[]{:S(2)}) async-start(), calls=%async_computation | async-start | bytes 2162688 | tf_op jit(solution)/shard_map/psum | solution.py:113
  8.3 33.9 %collective-permute-start.2 = (bf16[1,2,8,4224]{3,2,1,0:T(8,128)(2,1)S(1)}, bf16[1,2,8,4224]{3,2,1,0:T(8,128)(2,1)S(1)}, u32[]{:S(2)}, u32[]{:S(2)}) collective-permute-start(bf16[1,2,8,4224]{3,2,1,0:T(8,128)(2,1)S(1)} %fusion.329), channel_id=1, source_target_pairs={{0,0},{1,16},{2,32},{3,48},{4,64},{5,80},{6,96},{7,112},{8,128},{9... | collective-permute-start | bytes 405512 | tf_op jit(solution)/shard_map/ppermute | solution.py:108
  17.4 17.2 %collective-permute-start = (f32[1,6,32,128]{3,2,1,0:T(8,128)S(1)}, f32[1,6,32,128]{3,2,1,0:T(8,128)S(1)}, u32[]{:S(2)}, u32[]{:S(2)}) collective-permute-start(f32[1,6,32,128]{3,2,1,0:T(8,128)S(1)} %get-tuple-element.162), channel_id=1, source_target_pairs={{16,0},{32,16},{48,32},{64,48},{80,64},{96,80},{112,96},{128,112},... | collective-permute-start | bytes 294920 | tf_op jit(solution)/shard_map/ppermute | solution.py:25
  20.0 14.6 %collective-permute-start.1 = (f32[1,6,32,128]{3,2,1,0:T(8,128)S(1)}, f32[1,6,32,128]{3,2,1,0:T(8,128)S(1)}, u32[]{:S(2)}, u32[]{:S(2)}) collective-permute-start(f32[1,6,32,128]{3,2,1,0:T(8,128)S(1)} %get-tuple-element.163), channel_id=1, source_target_pairs={{0,16},{16,32},{32,48},{48,64},{64,80},{80,96},{96,112},{112,128},... | collective-permute-start | bytes 294920 | tf_op jit(solution)/shard_map/ppermute | solution.py:24
  22.4 13.5 %copy-start.64 = (pred[32]{0:T(512)(128)(4,1)}, pred[32]{0:T(512)(128)(4,1)S(1)}, u32[]{:S(2)}) copy-start(pred[32]{0:T(512)(128)(4,1)S(1)} %compare_and_fusion.1) | copy-start | bytes 100
  22.4 13.5 %copy-start.65 = (pred[32]{0:T(512)(128)(4,1)}, pred[32]{0:T(512)(128)(4,1)S(1)}, u32[]{:S(2)}) copy-start(pred[32]{0:T(512)(128)(4,1)S(1)} %compare_and_fusion) | copy-start | bytes 100
  28.4 4.3 %copy-start.50 = (s32[10,32]{1,0:T(8,128)S(1)}, s32[10,32]{1,0:T(8,128)}, u32[]{:S(2)}) copy-start(s32[10,32]{1,0:T(8,128)} %param.16) | copy-start | bytes 3844
  34.5 157.1 %copy-start.62 = (s32[1024]{0:T(1024)}, s32[1024]{0:T(1024)S(1)}, u32[]{:S(2)}) copy-start(s32[1024]{0:T(1024)S(1)} %pad_clamp_fusion.2) | copy-start | bytes 12292
  46.7 120.9 %copy-start.53 = (f32[10,10]{0,1:T(8,128)S(1)}, f32[10,10]{0,1:T(8,128)}, u32[]{:S(2)}) copy-start(f32[10,10]{0,1:T(8,128)} %fusion.345) | copy-start | bytes 1204
  47.5 122.9 %copy-start.66 = (bf16[10,10]{1,0:T(8,128)(2,1)S(1)}, bf16[10,10]{1,0:T(8,128)(2,1)}, u32[]{:S(2)}) copy-start(bf16[10,10]{1,0:T(8,128)(2,1)} %copy.51) | copy-start | bytes 604
  166.7 3.8 %copy-start.73 = (bf16[10,8,4224]{2,0,1:T(8,128)(2,1)S(1)}, bf16[10,8,4224]{2,0,1:T(8,128)(2,1)}, u32[]{:S(2)}) copy-start(bf16[10,8,4224]{2,0,1:T(8,128)(2,1)} %all-reduce.6.cloned.1.call-done) | copy-start | bytes 2027524
  167.7 3.3 %copy-start.17 = (f32[1,16,29,128]{3,2,1,0:T(8,128)S(1)}, f32[1,16,29,128]{3,2,1,0:T(8,128)}, u32[]{:S(2)}) copy-start(f32[1,16,29,128]{3,2,1,0:T(8,128)} %get-tuple-element.152) | copy-start | bytes 712708
  167.7 3.3 %copy-start.30 = (f32[1,16,5,128]{3,2,1,0:T(8,128)S(1)}, f32[1,16,5,128]{3,2,1,0:T(8,128)}, u32[]{:S(2)}) copy-start(f32[1,16,5,128]{3,2,1,0:T(8,128)} %get-tuple-element.142) | copy-start | bytes 122884
  167.7 3.3 %copy-start.31 = (f32[1,16,5,128]{3,2,1,0:T(8,128)S(1)}, f32[1,16,5,128]{3,2,1,0:T(8,128)}, u32[]{:S(2)}) copy-start(f32[1,16,5,128]{3,2,1,0:T(8,128)} %get-tuple-element.143) | copy-start | bytes 122884
  180.6 8.6 %copy-start.67 = (bf16[10,10]{1,0:T(8,128)(2,1)S(1)}, bf16[10,10]{1,0:T(8,128)(2,1)}, u32[]{:S(2)}) copy-start(bf16[10,10]{1,0:T(8,128)(2,1)} %copy.51) | copy-start | bytes 604
  180.7 8.5 %copy-start.74 = (bf16[10,8,4224]{2,0,1:T(8,128)(2,1)S(1)}, bf16[10,8,4224]{2,0,1:T(8,128)(2,1)}, u32[]{:S(2)}) copy-start(bf16[10,8,4224]{2,0,1:T(8,128)(2,1)} %all-reduce.6.cloned.1.call-done) | copy-start | bytes 2027524
  183.4 8.1 %collective-permute-start.3 = (f32[1,6,32,128]{3,2,1,0:T(8,128)S(1)}, f32[1,6,32,128]{3,2,1,0:T(8,128)S(1)}, u32[]{:S(2)}, u32[]{:S(2)}) collective-permute-start(f32[1,6,32,128]{3,2,1,0:T(8,128)S(1)} %get-tuple-element.134), channel_id=1, source_target_pairs={{16,0},{32,16},{48,32},{64,48},{80,64},{96,80},{112,96},{128,112},... | collective-permute-start | bytes 294920 | tf_op jit(solution)/shard_map/ppermute | solution.py:25
  189.3 8.2 %collective-permute-start.4 = (f32[1,6,32,128]{3,2,1,0:T(8,128)S(1)}, f32[1,6,32,128]{3,2,1,0:T(8,128)S(1)}, u32[]{:S(2)}, u32[]{:S(2)}) collective-permute-start(f32[1,6,32,128]{3,2,1,0:T(8,128)S(1)} %get-tuple-element.135), channel_id=1, source_target_pairs={{0,16},{16,32},{32,48},{48,64},{64,80},{80,96},{96,112},{112,128},... | collective-permute-start | bytes 294920 | tf_op jit(solution)/shard_map/ppermute | solution.py:24
  208.0 8.5 %copy-start.68 = (bf16[10,10]{1,0:T(8,128)(2,1)S(1)}, bf16[10,10]{1,0:T(8,128)(2,1)}, u32[]{:S(2)}) copy-start(bf16[10,10]{1,0:T(8,128)(2,1)} %copy.51) | copy-start | bytes 604
  208.1 8.4 %copy-start.75 = (bf16[10,8,4224]{2,0,1:T(8,128)(2,1)S(1)}, bf16[10,8,4224]{2,0,1:T(8,128)(2,1)}, u32[]{:S(2)}) copy-start(bf16[10,8,4224]{2,0,1:T(8,128)(2,1)} %all-reduce.6.cloned.1.call-done) | copy-start | bytes 2027524
  210.7 8.3 %collective-permute-start.6 = (f32[1,6,32,128]{3,2,1,0:T(8,128)S(1)}, f32[1,6,32,128]{3,2,1,0:T(8,128)S(1)}, u32[]{:S(2)}, u32[]{:S(2)}) collective-permute-start(f32[1,6,32,128]{3,2,1,0:T(8,128)S(1)} %get-tuple-element.109), channel_id=1, source_target_pairs={{0,16},{16,32},{32,48},{48,64},{64,80},{80,96},{96,112},{112,128},... | collective-permute-start | bytes 294920 | tf_op jit(solution)/shard_map/ppermute | solution.py:24
  210.8 9.0 %collective-permute-start.5 = (f32[1,6,32,128]{3,2,1,0:T(8,128)S(1)}, f32[1,6,32,128]{3,2,1,0:T(8,128)S(1)}, u32[]{:S(2)}, u32[]{:S(2)}) collective-permute-start(f32[1,6,32,128]{3,2,1,0:T(8,128)S(1)} %get-tuple-element.108), channel_id=1, source_target_pairs={{16,0},{32,16},{48,32},{64,48},{80,64},{96,80},{112,96},{128,112},... | collective-permute-start | bytes 294920 | tf_op jit(solution)/shard_map/ppermute | solution.py:25
  (66 other events, 83.1 us)
Sparse Core Ops, SparseCore 0:
  45.0 121.6 all-reduce.5

commit v2 on v0

--- a/solution.py
+++ b/solution.py
@@ -106,6 +106,7 @@
     packed = jnp.concatenate([projectors, gain_lanes], axis=3)
     pairs = [(o * n_states + t, t * n_states + o) for o in range(n_grid) for t in range(n_states)]
     packed = lax.ppermute(packed, ("grid", "states"), pairs)
+    packed, states_held = lax.optimization_barrier((packed, states_in))
     gathered = lax.all_gather(packed[0], "states", axis=0, tiled=True)
     gathered = gathered.reshape(n_states * slot_pairs, proj_count, line_span + 128)
     atom_pack = jnp.take(gathered, atom_slot, axis=0)
@@ -145,18 +146,22 @@
         )
         return summed.reshape(state_count, tile_width, breadth, line_depth)
 
-    def operate(grid_field):
+    def operate(grid_field, interior):
         padded = extended(grid_field)
+        padded = jnp.concatenate(
+            [padded[:, :RADIUS], interior, padded[:, RADIUS + tile_width :]], axis=1
+        )
         return (
             -0.5 * laplacian(padded, tile_width)
-            + potential[None] * grid_field
-            + nonlocal_part(grid_field)
+            + potential[None] * interior
+            + nonlocal_part(interior)
         )
 
-    def shifted(grid_field):
-        return (operate(grid_field) - CENTER * grid_field) / HALF_WIDTH
+    def shifted(grid_field, interior=None):
+        interior = grid_field if interior is None else interior
+        return (operate(grid_field, interior) - CENTER * interior) / HALF_WIDTH
 
-    first_term = shifted(states_in)
+    first_term = shifted(states_in, states_held)
     second_term = 2.0 * shifted(first_term) - states_in
     return 2.0 * shifted(second_term) - first_term
 

time: 136 us -> 137 us (level)
  waiting for transfers between devices: 38.2 us -> 30.9 us
  local copies, waits for them, and re-layouts: 36.5 us -> 40.4 us
  other arithmetic: 8.83 us -> 11.8 us
    slice x0 -> x13, local copies, waits for them, and re-layouts: none -> 8.96 us  [the longest x12 8 us: laplacian(): jnp.roll(interior, -k, 2) + jnp.roll(interior, k, 2)]
    all_gather x1, waiting for transfers between devices: 30 us -> 22.8 us  [shards(): gathered = lax.all_gather(packed[0], 'states', axis=0, tiled=True)]
    slice x36 -> x24, local copies, waits for them, and re-layouts: 21.6 us -> 15 us  [laplacian(): jnp.roll(interior, k, 2)]
    dot_general x3, matrix products: 0.89 us -> 2.42 us  [nonlocal_part(): picked = jnp.dot(selector, lines_here, preferred_element_type=jnp.float32)]
  transfers between devices with their start and end apart: 8 -> 8, of which waited for: 4 -> 5; matrix products, arithmetic and copies ran while one was open for 14% -> 20% of each run, Pallas kernels for 0% -> 0%
where the time goes in v2:
time: 137 us; the launch traced here: 136 us
  local copies, waits for them, and re-layouts  40.4 us (29%)
  waiting for transfers between devices  30.9 us (23%)
  starting transfers between devices  22 us (16%)
  matrix products  15.7 us (11%)
  between operations  14.7 us (11%)
  other arithmetic  11.8 us (9%)
    all_gather x1, waiting for transfers between devices, shards(): gathered = lax.all_gather(packed[0], 'states', axis=0, tiled=True)  22.8 us
    slice x24, local copies, waits for them, and re-layouts, laplacian(): jnp.roll(interior, k, 2)  15 us
    ppermute x3, starting transfers between devices, padded_2(): after = lax.ppermute(initial, axis, down)  13.8 us
    ppermute x1, starting transfers between devices, shards(): packed = lax.ppermute(packed, ('grid', 'states'), pairs)  8.12 us
    slice x12, local copies, waits for them, and re-layouts, laplacian(): jnp.roll(interior, -k, 2) + jnp.roll(interior, k, 2)  8 us
    dot_general x3, matrix products, nonlocal_part(): lax.dot_general(selector, projected, (((0,), (0,)), ((), ())), preferred_...  7.88 us
    ppermute x3, waiting for transfers between devices, padded_2(): before = lax.ppermute(last, axis, up)  6.91 us
    dot_general x3, matrix products, nonlocal_part(): lax.dot_general(proj_rows, picked, (((1,), (1,)), ((), ())), preferred_el...  4.03 us
  transfers between devices with their start and end apart: 8, of which 5 were waited for; matrix products, arithmetic and copies ran while one was open for 20% of the time, Pallas kernels for 0%

profile of v2, /device:TPU:6, one launch (start us, length us, event | category | flops | bytes accessed | tf_op | source)
XLA Modules:
  0.0 135.5 jit_solution(10909846731734862149)
XLA Ops:
  7.3 1.0 fusion.324
  8.3 8.1 %collective-permute-start = (bf16[1,2,8,4224]{3,2,0,1:T(8,128)(2,1)S(1)}, bf16[1,2,8,4224]{3,2,0,1:T(8,128)(2,1)S(1)}, u32[]{:S(2)}, u32[]{:S(2)}) collective-permute-start(bf16[1,2,8,4224]{3,2,0,1:T(8,128)(2,1)S(1)} %fusion.324), channel_id=1, source_target_pairs={{0,0},{1,16},{2,32},{3,48},{4,64},{5,80},{6,96},{7,112},{8,128},{9... | collective-permute-start | bytes 405512 | tf_op jit(solution)/shard_map/ppermute | solution.py:108
  16.4 1.0 fusion.416
  17.3 2.7 %collective-permute-start.1 = (f32[1,6,32,128]{3,2,1,0:T(8,128)S(1)}, f32[1,6,32,128]{3,2,1,0:T(8,128)S(1)}, u32[]{:S(2)}, u32[]{:S(2)}) collective-permute-start(f32[1,6,32,128]{3,2,1,0:T(8,128)S(1)} %get-tuple-element.169), channel_id=1, source_target_pairs={{16,0},{32,16},{48,32},{64,48},{80,64},{96,80},{112,96},{128,112},... | collective-permute-start | bytes 294920 | tf_op jit(solution)/shard_map/ppermute | solution.py:25
  23.4 0.9 convert_reduce_fusion.1
  24.3 1.2 compare_and_fusion.2
  31.4 1.8 %convolution_convert_fusion.2 = bf16[320,128]{1,0:T(8,128)(2,1)} fusion(bf16[512,128]{1,0:T(8,128)(2,1)} %bitcast.109, s32[320]{0:T(512)S(1)} %eq.101), kind=kOutput, calls=%fused_computation.68 | convolution fusion | flops 42147840 | bytes 214272 | tf_op jit(solution)/shard_map/dot_general | solution.py:132
  33.2 1.6 %reshape.2360 = bf16[10,4096,1]{1,0,2:T(8,128)(2,1)} reshape(bf16[320,128]{1,0:T(8,128)(2,1)} %convolution_convert_fusion.2) | data formatting | bytes 163840 | tf_op jit(solution)/shard_map/reshape | solution.py:133
  40.6 0.8 fusion.410
  41.5 0.9 fusion.408
  42.3 0.9 fusion.406
  44.0 22.8 %all-gather.3.cloned.1.call-done = bf16[1,32,8,4224]{3,2,0,1:T(8,128)(2,1)} async-done(((bf16[1,2,8,4224]{3,2,0,1:T(8,128)(2,1)}), bf16[1,32,8,4224]{3,2,0,1:T(8,128)(2,1)}) %all-gather.3.cloned.1.call-update) | async-done | bytes 2162704 | tf_op jit(solution)/shard_map/all_gather | solution.py:110
  66.8 2.4 %gather_fusion = bf16[10,8,4224]{2,1,0:T(8,128)(2,1)S(1)} fusion(bf16[32,8,4224]{2,1,0:T(8,128)(2,1)} %bitcast.108, s32[1024]{0:T(1024)} %pad_clamp_fusion), kind=kCustom, calls=%fused_computation.6 | custom fusion | bytes 1351720 | tf_op jit(solution)/shard_map/jit(_take)/gather | solution.py:112
  70.1 1.3 fusion.42
  72.7 3.7 %broadcast_multiply_fusion = (f32[1,16,32,128]{3,2,1,0:T(8,128)S(1)}, f32[1,16,32,128]{3,2,1,0:T(8,128)S(1)}) fusion(f32[1,16,32,128]{3,2,1,0:T(8,128)S(1)} %copy-done, f32[16,32,128]{2,1,0:T(8,128)} %param.12, f32[1,28,32,128]{3,2,1,0:T(8,128)S(1)} %fusion.70, f32[1,16,26,128]{3,2,1,0:T(8,128)S(1)} %get-tuple-element.165, ...), kind=kOutput, calls=%fused_computation.493 | convolution fusion | flops 48988160 | bytes 7621888 | tf_op jit(solution)/shard_map/dot_general | solution.py:144
  84.2 1.3 fusion.43
  86.0 5.5 %collective-permute-start.3 = (f32[1,6,32,128]{3,2,1,0:T(8,128)S(1)}, f32[1,6,32,128]{3,2,1,0:T(8,128)S(1)}, u32[]{:S(2)}, u32[]{:S(2)}) collective-permute-start(f32[1,6,32,128]{3,2,1,0:T(8,128)S(1)} %get-tuple-element.142), channel_id=1, source_target_pairs={{16,0},{32,16},{48,32},{64,48},{80,64},{96,80},{112,96},{128,112},... | collective-permute-start | bytes 294920 | tf_op jit(solution)/shard_map/ppermute | solution.py:25
  92.8 1.2 collective-permute-done.3
  94.7 5.0 %collective-permute-done.4 = f32[1,6,32,128]{3,2,1,0:T(8,128)S(1)} collective-permute-done((f32[1,6,32,128]{3,2,1,0:T(8,128)S(1)}, f32[1,6,32,128]{3,2,1,0:T(8,128)S(1)}, u32[]{:S(2)}, u32[]{:S(2)}) %collective-permute-start.4) | collective-permute-done | bytes 98336 | tf_op jit(solution)/shard_map/ppermute | solution.py:24
  103.3 1.4 %fusion.417 = (bf16[1,16,32,128]{3,2,1,0:T(8,128)(2,1)S(1)}, f32[1,16,32,128]{3,2,1,0:T(8,128)S(1)}) fusion(f32[1,16,32,128]{3,2,1,0:T(8,128)S(1)} %copy-done, f32[1,16,32,128]{3,2,1,0:T(8,128)S(1)} %get-tuple-element.23, bf16[320,128,1]{1,0,2:T(8,128)(2,1)S(1)} %copy-done.21, s32[16,32]{1,0:T(8,128)S(1)} %copy-done.42, s32[320]{0:T(512)S(1)} %copy-done.61, ...), kind=kOutput, calls=%fused_computation.611 | convolution fusion | flops 49119232 | bytes 8015104 | tf_op jit(solution)/shard_map/dot_general | solution.py:144
  111.6 1.3 fusion.44
  113.5 5.6 %collective-permute-start.5 = (f32[1,6,32,128]{3,2,1,0:T(8,128)S(1)}, f32[1,6,32,128]{3,2,1,0:T(8,128)S(1)}, u32[]{:S(2)}, u32[]{:S(2)}) collective-permute-start(f32[1,6,32,128]{3,2,1,0:T(8,128)S(1)} %get-tuple-element.116), channel_id=1, source_target_pairs={{16,0},{32,16},{48,32},{64,48},{80,64},{96,80},{112,96},{128,112},... | collective-permute-start | bytes 294920 | tf_op jit(solution)/shard_map/ppermute | solution.py:25
  120.4 1.3 collective-permute-done.6
  125.9 2.8 %fusion.27 = f32[1,16,32,128]{3,2,1,0:T(8,128)} fusion(bf16[320,128,1]{1,0,2:T(8,128)(2,1)S(1)} %copy-done.20, s32[16,32]{1,0:T(8,128)S(1)} %copy-done.42, s32[320]{0:T(512)S(1)} %copy-done.62, f32[1,16,32,128]{3,2,1,0:T(8,128)S(1)} %get-tuple-element.171, f32[1,6,32,128]{3,2,1,0:T(8,128)S(1)} %fusion.325, f32[1,6,32,128]{3,2,1,0:T(8,128)S(1)} %fusion.326, ...), kind=kOutput, calls=%fused_computation.61 | convolution fusion | flops 49119232 | bytes 7621888 | tf_op jit(solution)/shard_map/dot_general | solution.py:144
  (263 shorter events, 44.3 us)
Async XLA Ops:
  6.5 60.3 %all-gather.3.cloned.1.call-start = ((), (), s32[]{:S(2)}) async-start(), calls=%async_computation | async-start | bytes 2297856 | tf_op jit(solution)/shard_map/all_gather | solution.py:110
  7.3 23.1 %copy-start = (f32[1,16,32,128]{3,2,1,0:T(8,128)S(1)}, f32[1,16,32,128]{3,2,1,0:T(8,128)}, u32[]{:S(2)}) copy-start(f32[1,16,32,128]{3,2,1,0:T(8,128)} %param.11) | copy-start | bytes 786436
  8.3 21.4 %collective-permute-start = (bf16[1,2,8,4224]{3,2,0,1:T(8,128)(2,1)S(1)}, bf16[1,2,8,4224]{3,2,0,1:T(8,128)(2,1)S(1)}, u32[]{:S(2)}, u32[]{:S(2)}) collective-permute-start(bf16[1,2,8,4224]{3,2,0,1:T(8,128)(2,1)S(1)} %fusion.324), channel_id=1, source_target_pairs={{0,0},{1,16},{2,32},{3,48},{4,64},{5,80},{6,96},{7,112},{8,128},{9... | collective-permute-start | bytes 405512 | tf_op jit(solution)/shard_map/ppermute | solution.py:108
  17.3 10.3 %collective-permute-start.1 = (f32[1,6,32,128]{3,2,1,0:T(8,128)S(1)}, f32[1,6,32,128]{3,2,1,0:T(8,128)S(1)}, u32[]{:S(2)}, u32[]{:S(2)}) collective-permute-start(f32[1,6,32,128]{3,2,1,0:T(8,128)S(1)} %get-tuple-element.169), channel_id=1, source_target_pairs={{16,0},{32,16},{48,32},{64,48},{80,64},{96,80},{112,96},{128,112},... | collective-permute-start | bytes 294920 | tf_op jit(solution)/shard_map/ppermute | solution.py:25
  20.0 8.2 %collective-permute-start.2 = (f32[1,6,32,128]{3,2,1,0:T(8,128)S(1)}, f32[1,6,32,128]{3,2,1,0:T(8,128)S(1)}, u32[]{:S(2)}, u32[]{:S(2)}) collective-permute-start(f32[1,6,32,128]{3,2,1,0:T(8,128)S(1)} %get-tuple-element.168), channel_id=1, source_target_pairs={{0,16},{16,32},{32,48},{48,64},{64,80},{80,96},{96,112},{112,128},... | collective-permute-start | bytes 294920 | tf_op jit(solution)/shard_map/ppermute | solution.py:24
  20.8 8.9 %copy-start.50 = (pred[32]{0:T(512)(128)(4,1)}, pred[32]{0:T(512)(128)(4,1)S(1)}, u32[]{:S(2)}) copy-start(pred[32]{0:T(512)(128)(4,1)S(1)} %compare_and_fusion.1) | copy-start | bytes 100
  22.2 7.5 %copy-start.52 = (pred[32]{0:T(512)(128)(4,1)}, pred[32]{0:T(512)(128)(4,1)S(1)}, u32[]{:S(2)}) copy-start(pred[32]{0:T(512)(128)(4,1)S(1)} %compare_and_fusion) | copy-start | bytes 100
  26.1 3.6 %copy-start.48 = (s32[1024]{0:T(1024)}, s32[1024]{0:T(1024)S(1)}, u32[]{:S(2)}) copy-start(s32[1024]{0:T(1024)S(1)} %pad_clamp_fusion.2) | copy-start | bytes 12292
  26.9 4.5 %copy-start.59 = (s32[320]{0:T(512)}, s32[320]{0:T(512)S(1)}, u32[]{:S(2)}) copy-start(s32[320]{0:T(512)S(1)} %eq.101) | copy-start | bytes 3844
  27.6 2.1 %copy-start.49 = (s32[1024]{0:T(1024)}, s32[1024]{0:T(1024)S(1)}, u32[]{:S(2)}) copy-start(s32[1024]{0:T(1024)S(1)} %pad_clamp_fusion.1) | copy-start | bytes 12292
  43.2 26.0 %copy-start.58 = (pred[10]{0:T(512)(128)(4,1)S(1)}, pred[10]{0:T(512)(128)(4,1)}, u32[]{:S(2)}) copy-start(pred[10]{0:T(512)(128)(4,1)} %get-tuple-element.24) | copy-start | bytes 34
  69.5 2.0 %copy-start.55 = (bf16[10,10]{1,0:T(8,128)(2,1)S(1)}, bf16[10,10]{1,0:T(8,128)(2,1)}, u32[]{:S(2)}) copy-start(bf16[10,10]{1,0:T(8,128)(2,1)} %copy.45) | copy-start | bytes 604
  81.5 2.3 %copy-start.60 = (s32[320]{0:T(512)S(1)}, s32[320]{0:T(512)}, u32[]{:S(2)}) copy-start(s32[320]{0:T(512)} %copy-done.59) | copy-start | bytes 3844
  82.3 1.9 %copy-start.44 = (f32[10,10]{0,1:T(8,128)S(1)}, f32[10,10]{0,1:T(8,128)}, u32[]{:S(2)}) copy-start(f32[10,10]{0,1:T(8,128)} %fusion.340) | copy-start | bytes 1204
  85.5 15.0 %copy-start.51 = (pred[32]{0:T(512)(128)(4,1)S(1)}, pred[32]{0:T(512)(128)(4,1)}, u32[]{:S(2)}) copy-start(pred[32]{0:T(512)(128)(4,1)} %copy-done.50) | copy-start | bytes 100
  86.0 14.7 %copy-start.53 = (pred[32]{0:T(512)(128)(4,1)S(1)}, pred[32]{0:T(512)(128)(4,1)}, u32[]{:S(2)}) copy-start(pred[32]{0:T(512)(128)(4,1)} %copy-done.52) | copy-start | bytes 100
  86.0 8.0 %collective-permute-start.3 = (f32[1,6,32,128]{3,2,1,0:T(8,128)S(1)}, f32[1,6,32,128]{3,2,1,0:T(8,128)S(1)}, u32[]{:S(2)}, u32[]{:S(2)}) collective-permute-start(f32[1,6,32,128]{3,2,1,0:T(8,128)S(1)} %get-tuple-element.142), channel_id=1, source_target_pairs={{16,0},{32,16},{48,32},{64,48},{80,64},{96,80},{112,96},{128,112},... | collective-permute-start | bytes 294920 | tf_op jit(solution)/shard_map/ppermute | solution.py:25
  91.5 8.3 %collective-permute-start.4 = (f32[1,6,32,128]{3,2,1,0:T(8,128)S(1)}, f32[1,6,32,128]{3,2,1,0:T(8,128)S(1)}, u32[]{:S(2)}, u32[]{:S(2)}) collective-permute-start(f32[1,6,32,128]{3,2,1,0:T(8,128)S(1)} %get-tuple-element.143), channel_id=1, source_target_pairs={{0,16},{16,32},{32,48},{48,64},{64,80},{80,96},{96,112},{112,128},... | collective-permute-start | bytes 294920 | tf_op jit(solution)/shard_map/ppermute | solution.py:24
  101.5 1.5 %copy-start.21 = (bf16[320,128,1]{1,0,2:T(8,128)(2,1)S(1)}, bf16[320,128,1]{1,0,2:T(8,128)(2,1)}, u32[]{:S(2)}) copy-start(bf16[320,128,1]{1,0,2:T(8,128)(2,1)} %reshape.2365) | copy-start | bytes 245764
  101.7 1.6 %copy-start.63 = (f32[16,32,128]{2,1,0:T(8,128)S(1)}, f32[16,32,128]{2,1,0:T(8,128)}, u32[]{:S(2)}) copy-start(f32[16,32,128]{2,1,0:T(8,128)} %param.12) | copy-start | bytes 786436
  109.8 1.9 %copy-start.45 = (f32[10,10]{0,1:T(8,128)S(1)}, f32[10,10]{0,1:T(8,128)}, u32[]{:S(2)}) copy-start(f32[10,10]{0,1:T(8,128)} %fusion.340) | copy-start | bytes 1204
  113.0 10.3 %copy-start.54 = (pred[32]{0:T(512)(128)(4,1)S(1)}, pred[32]{0:T(512)(128)(4,1)}, u32[]{:S(2)}) copy-start(pred[32]{0:T(512)(128)(4,1)} %copy-done.52) | copy-start | bytes 100
  113.5 8.2 %collective-permute-start.6 = (f32[1,6,32,128]{3,2,1,0:T(8,128)S(1)}, f32[1,6,32,128]{3,2,1,0:T(8,128)S(1)}, u32[]{:S(2)}, u32[]{:S(2)}) collective-permute-start(f32[1,6,32,128]{3,2,1,0:T(8,128)S(1)} %get-tuple-element.117), channel_id=1, source_target_pairs={{0,16},{16,32},{32,48},{48,64},{64,80},{80,96},{96,112},{112,128},... | collective-permute-start | bytes 294920 | tf_op jit(solution)/shard_map/ppermute | solution.py:24
  113.5 9.0 %collective-permute-start.5 = (f32[1,6,32,128]{3,2,1,0:T(8,128)S(1)}, f32[1,6,32,128]{3,2,1,0:T(8,128)S(1)}, u32[]{:S(2)}, u32[]{:S(2)}) collective-permute-start(f32[1,6,32,128]{3,2,1,0:T(8,128)S(1)} %get-tuple-element.116), channel_id=1, source_target_pairs={{16,0},{32,16},{48,32},{64,48},{80,64},{96,80},{112,96},{128,112},... | collective-permute-start | bytes 294920 | tf_op jit(solution)/shard_map/ppermute | solution.py:25
  (49 other events, 64.4 us)
Sparse Core Ops, SparseCore 0:
  31.5 35.2 all-gather.2

commit v3 on v0

--- a/solution.py
+++ b/solution.py
@@ -3,6 +3,8 @@
 import jax
 import jax.numpy as jnp
 from jax import lax
+from jax.experimental import pallas as pl
+from jax.experimental.pallas import tpu as pltpu
 from jax.sharding import PartitionSpec as P
 
 RADIUS = 6
@@ -77,6 +79,51 @@
         )
     return summed + MIXED_WEIGHT * cross_term
 
+
+def make_kernel(scale, with_prev):
+    sw = second_table(RADIUS); fw = first_table(RADIUS)
+    def kernel(lo_ref, v_ref, hi_ref, pot_ref, nl_ref, *rest):
+        if with_prev:
+            prev_ref, out_ref, pad_ref = rest
+        else:
+            out_ref, pad_ref = rest
+        planes, breadth, depth = v_ref.shape
+        v = v_ref[...]
+        pad_ref[0:RADIUS] = lo_ref[...]
+        pad_ref[RADIUS:RADIUS + planes] = v
+        pad_ref[RADIUS + planes:] = hi_ref[...]
+        lane = jax.lax.broadcasted_iota(jnp.int32, v.shape, 2)
+        summed = (3.0 * sw[0]) * v
+        for k in range(1, RADIUS + 1):
+            xs = pad_ref[RADIUS + k:RADIUS + k + planes] + pad_ref[RADIUS - k:RADIUS - k + planes]
+            ys = pltpu.roll(v, breadth - k, 1) + pltpu.roll(v, k, 1)
+            zs = (jnp.where(lane < depth - k, pltpu.roll(v, depth - k, 2), 0.0)
+                  + jnp.where(lane >= k, pltpu.roll(v, k, 2), 0.0))
+            summed = summed + sw[k] * xs + sw[k] * ys + sw[k] * zs
+        padded = pad_ref[...]
+        slope = fw[1] * (pltpu.roll(padded, breadth - 1, 1) - pltpu.roll(padded, 1, 1))
+        for k in range(2, RADIUS + 1):
+            slope = slope + fw[k] * (pltpu.roll(padded, breadth - k, 1) - pltpu.roll(padded, k, 1))
+        cross = fw[1] * (slope[RADIUS + 1:RADIUS + 1 + planes] - slope[RADIUS - 1:RADIUS - 1 + planes])
+        for k in range(2, RADIUS + 1):
+            cross = cross + fw[k] * (slope[RADIUS + k:RADIUS + k + planes] - slope[RADIUS - k:RADIUS - k + planes])
+        lap = summed + 0.7 * cross
+        hv = -0.5 * lap + pot_ref[...] * v + nl_ref[...]
+        kv = (hv - 12.0 * v) / 8.0
+        if with_prev:
+            out_ref[...] = scale * kv - prev_ref[...]
+        else:
+            out_ref[...] = kv
+    return kernel
+
+def apply_op(lo, v, hi, pot, nl, prev=None, scale=1.0):
+    planes, breadth, depth = v.shape
+    args = [lo, v, hi, pot, nl] + ([prev] if prev is not None else [])
+    return pl.pallas_call(
+        make_kernel(scale, prev is not None),
+        out_shape=jax.ShapeDtypeStruct(v.shape, jnp.float32),
+        scratch_shapes=[pltpu.VMEM((planes + 2 * RADIUS, breadth, depth), jnp.float32)],
+    )(*args)
 
 def shards(states_in, potential, projectors, proj_gains, atom_owner, atom_rows, wrap_rows):
     state_count, tile_width, breadth, line_depth = states_in.shape
@@ -116,7 +163,7 @@
     ).astype(jnp.bfloat16)
     atom_eye = jnp.eye(home_count, dtype=jnp.float32)
 
-    def extended(grid_field):
+    def rims(grid_field):
         padded = padded_2(grid_field, (("grid", 1),), RADIUS)
         low_rim = padded[:, :RADIUS]
         high_rim = padded[:, RADIUS + tile_width :]
@@ -124,7 +171,7 @@
         high_rim = jnp.where(
             tile_index == n_grid - 1, jnp.take(high_rim, unwrap_rows, axis=2), high_rim
         )
-        return jnp.concatenate([low_rim, padded[:, RADIUS : RADIUS + tile_width], high_rim], axis=1)
+        return low_rim[0], high_rim[0]
 
     def nonlocal_part(grid_field):
         lines_here = grid_field.reshape(tile_lines, line_depth).astype(jnp.bfloat16)
@@ -145,20 +192,17 @@
         )
         return summed.reshape(state_count, tile_width, breadth, line_depth)
 
-    def operate(grid_field):
-        padded = extended(grid_field)
-        return (
-            -0.5 * laplacian(padded, tile_width)
-            + potential[None] * grid_field
-            + nonlocal_part(grid_field)
-        )
-
-    def shifted(grid_field):
-        return (operate(grid_field) - CENTER * grid_field) / HALF_WIDTH
-
-    first_term = shifted(states_in)
-    second_term = 2.0 * shifted(first_term) - states_in
-    return 2.0 * shifted(second_term) - first_term
+    def step(grid_field, prev=None, scale=1.0):
+        low_rim, high_rim = rims(grid_field)
+        nonlocal_lines = nonlocal_part(grid_field)[0]
+        out = apply_op(
+            low_rim, grid_field[0], high_rim, potential, nonlocal_lines, prev, scale
+        )
+        return out[None]
+
+    first_term = step(states_in)
+    second_term = step(first_term, states_in[0], 2.0)
+    return step(second_term, first_term[0], 2.0)
 
 
 def solution(mesh):

time: 136 us -> 120 us (0.88)
  local copies, waits for them, and re-layouts: 36.5 us -> 10.5 us
  waiting for transfers between devices: 38.2 us -> 48.8 us
  Pallas kernels: 0 us -> 10.1 us
  matrix products: 14.8 us -> 9.32 us
  starting transfers between devices: 22 us -> 17.7 us
    slice x69 -> x0, local copies, waits for them, and re-layouts: 23.4 us -> none  [the longest x36 21.6 us: laplacian(): jnp.roll(interior, k, 2)]
    pallas_call x0 -> x3, Pallas kernels: none -> 10.1 us  [apply_op(): pl.pallas_call(make_kernel(scale, prev is not None), out_shape=jax.ShapeD...]
    ppermute x1, waiting for transfers between devices: 0.01 us -> 8.73 us  [shards(): packed = lax.ppermute(packed, ('grid', 'states'), pairs)]
    ppermute x3, starting transfers between devices: 13.8 us -> 6.83 us  [padded_2(): after = lax.ppermute(initial, axis, down)]
    dot_general x3, matrix products: 8.52 us -> 3.04 us  [nonlocal_part(): lax.dot_general(selector, projected, (((0,), (0,)), ((), ())), preferred_...]
    ppermute x3, waiting for transfers between devices: 7.08 us -> 12.2 us  [padded_2(): before = lax.ppermute(last, axis, up)]
    all_gather x1, waiting for transfers between devices: 30 us -> 24.9 us  [shards(): gathered = lax.all_gather(packed[0], 'states', axis=0, tiled=True)]
    squeeze x0 -> x6, other arithmetic: none -> 4.3 us  [rims(): return (low_rim[0], high_rim[0])]
  transfers between devices with their start and end apart: 8 -> 8, of which waited for: 4 -> 7; matrix products, arithmetic and copies ran while one was open for 14% -> 9% of each run, Pallas kernels for 0% -> 0%
where the time goes in v3:
time: 120 us; the launch traced here: 119 us
  waiting for transfers between devices  48.8 us (41%)
  starting transfers between devices  17.7 us (15%)
  between operations  13.7 us (11%)
  local copies, waits for them, and re-layouts  10.5 us (9%)
  Pallas kernels  10.1 us (8%)
  matrix products  9.32 us (8%)
  other arithmetic  8.84 us (7%)
    all_gather x1, waiting for transfers between devices, shards(): gathered = lax.all_gather(packed[0], 'states', axis=0, tiled=True)  24.9 us
    ppermute x3, waiting for transfers between devices, padded_2(): before = lax.ppermute(last, axis, up)  12.2 us
    pallas_call x3, Pallas kernels, apply_op(): pl.pallas_call(make_kernel(scale, prev is not None), out_shape=jax.ShapeD...  10.1 us
    ppermute x1, waiting for transfers between devices, shards(): packed = lax.ppermute(packed, ('grid', 'states'), pairs)  8.73 us
    ppermute x1, starting transfers between devices, shards(): packed = lax.ppermute(packed, ('grid', 'states'), pairs)  8.12 us
    ppermute x3, starting transfers between devices, padded_2(): after = lax.ppermute(initial, axis, down)  6.83 us
    squeeze x6, other arithmetic, rims(): return (low_rim[0], high_rim[0])  4.3 us
    dot_general x3, matrix products, nonlocal_part(): lax.dot_general(proj_rows, picked, (((1,), (1,)), ((), ())), preferred_el...  4.03 us
  transfers between devices with their start and end apart: 8, of which 7 were waited for; matrix products, arithmetic and copies ran while one was open for 9% of the time, Pallas kernels for 0%

profile of v3, /device:TPU:6, one launch (start us, length us, event | category | flops | bytes accessed | tf_op | source)
XLA Modules:
  0.0 118.9 jit_solution(16525281014486648740)
XLA Ops:
  8.2 8.1 %collective-permute-start.2 = (bf16[1,2,8,4224]{3,2,0,1:T(8,128)(2,1)S(1)}, bf16[1,2,8,4224]{3,2,0,1:T(8,128)(2,1)S(1)}, u32[]{:S(2)}, u32[]{:S(2)}) collective-permute-start(bf16[1,2,8,4224]{3,2,0,1:T(8,128)(2,1)S(1)} %fusion.28), channel_id=1, source_target_pairs={{0,0},{1,16},{2,32},{3,48},{4,64},{5,80},{6,96},{7,112},{8,128},{9... | collective-permute-start | bytes 405512 | tf_op jit(solution)/shard_map/ppermute | solution.py:155
  16.4 8.7 %collective-permute-done.2 = bf16[1,2,8,4224]{3,2,0,1:T(8,128)(2,1)S(1)} collective-permute-done((bf16[1,2,8,4224]{3,2,0,1:T(8,128)(2,1)S(1)}, bf16[1,2,8,4224]{3,2,0,1:T(8,128)(2,1)S(1)}, u32[]{:S(2)}, u32[]{:S(2)}) %collective-permute-start.2) | collective-permute-done | bytes 135200 | tf_op jit(solution)/shard_map/ppermute | solution.py:155
  26.8 2.0 %collective-permute-start = (f32[1,6,32,128]{3,2,1,0:T(8,128)S(1)}, f32[1,6,32,128]{3,2,1,0:T(8,128)S(1)}, u32[]{:S(2)}, u32[]{:S(2)}) collective-permute-start(f32[1,6,32,128]{3,2,1,0:T(8,128)S(1)} %get-tuple-element.25), channel_id=1, source_target_pairs={{0,16},{16,32},{32,48},{48,64},{64,80},{80,96},{96,112},{112,128},... | collective-permute-start | bytes 294920 | tf_op jit(solution)/shard_map/ppermute | solution.py:26
  28.9 1.0 convert_element_type.115
  30.9 1.3 %collective-permute-done.1 = f32[1,6,32,128]{3,2,1,0:T(8,128)S(1)} collective-permute-done((f32[1,6,32,128]{3,2,1,0:T(8,128)S(1)}, f32[1,6,32,128]{3,2,1,0:T(8,128)S(1)}, u32[]{:S(2)}, u32[]{:S(2)}) %collective-permute-start.1) | collective-permute-done | bytes 98336 | tf_op jit(solution)/shard_map/ppermute | solution.py:27
  32.2 3.6 %collective-permute-done = f32[1,6,32,128]{3,2,1,0:T(8,128)S(1)} collective-permute-done((f32[1,6,32,128]{3,2,1,0:T(8,128)S(1)}, f32[1,6,32,128]{3,2,1,0:T(8,128)S(1)}, u32[]{:S(2)}, u32[]{:S(2)}) %collective-permute-start) | collective-permute-done | bytes 98336 | tf_op jit(solution)/shard_map/ppermute | solution.py:26
  38.6 24.9 %all-gather.3.cloned.1.call-done = bf16[1,32,8,4224]{3,2,0,1:T(8,128)(2,1)} async-done(((bf16[1,2,8,4224]{3,2,0,1:T(8,128)(2,1)}), bf16[1,32,8,4224]{3,2,0,1:T(8,128)(2,1)}) %all-gather.3.cloned.1.call-update) | async-done | bytes 2162704 | tf_op jit(solution)/shard_map/all_gather | solution.py:156
  63.4 2.2 %gather_fusion = bf16[10,8,4224]{2,1,0:T(8,128)(2,1)S(1)} fusion(bf16[32,8,4224]{2,1,0:T(8,128)(2,1)} %bitcast.107, s32[1024]{0:T(1024)S(1)} %pad_clamp_fusion), kind=kCustom, calls=%fused_computation.6 | custom fusion | bytes 1351720 | tf_op jit(solution)/shard_map/jit(_take)/gather | solution.py:158
  66.0 1.3 %fusion.9 = f32[10,8]{0,1:T(8,128)S(1)} fusion(bf16[10,4096,1]{1,0,2:T(8,128)(2,1)S(1)} %reshape.270, bf16[10,8,4224]{2,0,1:T(8,128)(2,1)S(1)} %copy_select_fusion, f32[10,10]{0,1:T(8,128)S(1)} %fusion.50), kind=kOutput, calls=%fused_computation.25 | convolution fusion | flops 6555120 | bytes 1188160 | tf_op jit(solution)/shard_map/dot_general | solution.py:180
  67.9 1.0 fusion.7.nl_ref
  68.9 3.3 %shard_map.73.v_ref.rest_0_ = f32[16,32,128]{2,1,0:T(8,128)} custom-call(f32[6,32,128]{2,1,0:T(8,128)} %fusion.40.lo_ref, f32[16,32,128]{2,1,0:T(8,128)} %bitcast.98, f32[6,32,128]{2,1,0:T(8,128)} %fusion.38.hi_ref, f32[16,32,128]{2,1,0:T(8,128)} %pot_ref.5, f32[16,32,128]{2,1,0:T(8,128)} %fusion.7.nl_ref), custom_call_target="tpu_custom_call" | custom-call | tf_op jit(solution)/shard_map/pallas_call | solution.py:122
  72.2 1.0 convert_element_type.122
  74.2 5.3 %collective-permute-start.4 = (f32[1,6,32,128]{3,2,1,0:T(8,128)S(1)}, f32[1,6,32,128]{3,2,1,0:T(8,128)S(1)}, u32[]{:S(2)}, u32[]{:S(2)}) collective-permute-start(f32[1,6,32,128]{3,2,1,0:T(8,128)S(1)} %get-tuple-element.22), channel_id=1, source_target_pairs={{16,0},{32,16},{48,32},{64,48},{80,64},{96,80},{112,96},{128,112},... | collective-permute-start | bytes 294920 | tf_op jit(solution)/shard_map/ppermute | solution.py:27
  79.9 1.3 %fusion.10 = f32[10,8]{0,1:T(8,128)S(1)} fusion(bf16[10,4096,1]{1,0,2:T(8,128)(2,1)S(1)} %reshape.273, bf16[10,8,4224]{2,0,1:T(8,128)(2,1)S(1)} %copy_select_fusion, f32[10,10]{0,1:T(8,128)S(1)} %fusion.50), kind=kOutput, calls=%fused_computation.26 | convolution fusion | flops 6555120 | bytes 1188160 | tf_op jit(solution)/shard_map/dot_general | solution.py:180
  81.8 1.0 fusion.5.nl_ref
  83.4 4.3 %collective-permute-done.3 = f32[1,6,32,128]{3,2,1,0:T(8,128)S(1)} collective-permute-done((f32[1,6,32,128]{3,2,1,0:T(8,128)S(1)}, f32[1,6,32,128]{3,2,1,0:T(8,128)S(1)}, u32[]{:S(2)}, u32[]{:S(2)}) %collective-permute-start.3) | collective-permute-done | bytes 98336 | tf_op jit(solution)/shard_map/ppermute | solution.py:26
  89.8 3.4 %shard_map.74.v_ref = f32[16,32,128]{2,1,0:T(8,128)} custom-call(f32[6,32,128]{2,1,0:T(8,128)} %fusion.36.lo_ref, f32[16,32,128]{2,1,0:T(8,128)} %shard_map.73.v_ref.rest_0_, f32[6,32,128]{2,1,0:T(8,128)} %fusion.34.hi_ref, f32[16,32,128]{2,1,0:T(8,128)} %pot_ref.5, f32[16,32,128]{2,1,0:T(8,128)} %fusion.5.nl_ref, f32[16,32,128]{2,1,0:T(8,128)} %bitcast.99), custom_call_target="tpu_custom_call" | custom-call | tf_op jit(solution)/shard_map/pallas_call | solution.py:122
  93.2 1.0 convert_element_type.127
  94.6 1.3 %fusion.11 = f32[10,8]{0,1:T(8,128)S(1)} fusion(bf16[10,4096,1]{1,0,2:T(8,128)(2,1)S(1)} %reshape.276, bf16[10,8,4224]{2,0,1:T(8,128)(2,1)S(1)} %copy_select_fusion, f32[10,10]{0,1:T(8,128)S(1)} %fusion.50), kind=kOutput, calls=%fused_computation.27 | convolution fusion | flops 6555120 | bytes 1188160 | tf_op jit(solution)/shard_map/dot_general | solution.py:180
  96.9 1.4 %collective-permute-start.6 = (f32[1,6,32,128]{3,2,1,0:T(8,128)S(1)}, f32[1,6,32,128]{3,2,1,0:T(8,128)S(1)}, u32[]{:S(2)}, u32[]{:S(2)}) collective-permute-start(f32[1,6,32,128]{3,2,1,0:T(8,128)S(1)} %get-tuple-element.20), channel_id=1, source_target_pairs={{16,0},{32,16},{48,32},{64,48},{80,64},{96,80},{112,96},{128,112},... | collective-permute-start | bytes 294920 | tf_op jit(solution)/shard_map/ppermute | solution.py:27
  99.0 1.0 fusion.3.nl_ref
  100.0 1.6 %collective-permute-done.6 = f32[1,6,32,128]{3,2,1,0:T(8,128)S(1)} collective-permute-done((f32[1,6,32,128]{3,2,1,0:T(8,128)S(1)}, f32[1,6,32,128]{3,2,1,0:T(8,128)S(1)}, u32[]{:S(2)}, u32[]{:S(2)}) %collective-permute-start.6) | collective-permute-done | bytes 98336 | tf_op jit(solution)/shard_map/ppermute | solution.py:27
  102.2 4.3 %collective-permute-done.5 = f32[1,6,32,128]{3,2,1,0:T(8,128)S(1)} collective-permute-done((f32[1,6,32,128]{3,2,1,0:T(8,128)S(1)}, f32[1,6,32,128]{3,2,1,0:T(8,128)S(1)}, u32[]{:S(2)}, u32[]{:S(2)}) %collective-permute-start.5) | collective-permute-done | bytes 98336 | tf_op jit(solution)/shard_map/ppermute | solution.py:26
  108.6 3.4 %shard_map.75 = f32[16,32,128]{2,1,0:T(8,128)} custom-call(f32[6,32,128]{2,1,0:T(8,128)} %fusion.32.lo_ref, f32[16,32,128]{2,1,0:T(8,128)} %shard_map.74.v_ref, f32[6,32,128]{2,1,0:T(8,128)} %fusion.30.hi_ref, f32[16,32,128]{2,1,0:T(8,128)} %pot_ref.5, f32[16,32,128]{2,1,0:T(8,128)} %fusion.3.nl_ref, f32[16,32,128]{2,1,0:T(8,128)} %shard_map.73.v_ref.rest_0_), custom_call_target="tpu_custom_call" | custom-call | tf_op jit(solution)/shard_map/pallas_call | solution.py:122
  (72 shorter events, 17.2 us)
Async XLA Ops:
  6.5 23.3 %copy-start.2 = (s32[10,32]{1,0:T(8,128)S(1)}, s32[10,32]{1,0:T(8,128)}, u32[]{:S(2)}) copy-start(s32[10,32]{1,0:T(8,128)} %param.16) | copy-start | bytes 3844
  6.5 23.9 %copy-start.3 = (s32[10]{0:T(128)S(1)}, s32[10]{0:T(128)}, u32[]{:S(2)}) copy-start(s32[10]{0:T(128)} %param.15) | copy-start | bytes 124
  6.5 24.1 %copy-start.4 = (s32[32]{0:T(128)S(1)}, s32[32]{0:T(128)}, u32[]{:S(2)}) copy-start(s32[32]{0:T(128)} %param.17) | copy-start | bytes 388
  6.5 56.9 %all-gather.3.cloned.1.call-start = ((), (), s32[]{:S(2)}) async-start(), calls=%async_computation | async-start | bytes 2297856 | tf_op jit(solution)/shard_map/all_gather | solution.py:156
  8.2 16.9 %collective-permute-start.2 = (bf16[1,2,8,4224]{3,2,0,1:T(8,128)(2,1)S(1)}, bf16[1,2,8,4224]{3,2,0,1:T(8,128)(2,1)S(1)}, u32[]{:S(2)}, u32[]{:S(2)}) collective-permute-start(bf16[1,2,8,4224]{3,2,0,1:T(8,128)(2,1)S(1)} %fusion.28), channel_id=1, source_target_pairs={{0,0},{1,16},{2,32},{3,48},{4,64},{5,80},{6,96},{7,112},{8,128},{9... | collective-permute-start | bytes 405512 | tf_op jit(solution)/shard_map/ppermute | solution.py:155
  25.1 0.7 copy-start.1
  26.8 5.4 %collective-permute-start.1 = (f32[1,6,32,128]{3,2,1,0:T(8,128)S(1)}, f32[1,6,32,128]{3,2,1,0:T(8,128)S(1)}, u32[]{:S(2)}, u32[]{:S(2)}) collective-permute-start(f32[1,6,32,128]{3,2,1,0:T(8,128)S(1)} %get-tuple-element.24), channel_id=1, source_target_pairs={{16,0},{32,16},{48,32},{64,48},{80,64},{96,80},{112,96},{128,112},... | collective-permute-start | bytes 294920 | tf_op jit(solution)/shard_map/ppermute | solution.py:27
  26.8 9.0 %collective-permute-start = (f32[1,6,32,128]{3,2,1,0:T(8,128)S(1)}, f32[1,6,32,128]{3,2,1,0:T(8,128)S(1)}, u32[]{:S(2)}, u32[]{:S(2)}) collective-permute-start(f32[1,6,32,128]{3,2,1,0:T(8,128)S(1)} %get-tuple-element.25), channel_id=1, source_target_pairs={{0,16},{16,32},{32,48},{48,64},{64,80},{80,96},{96,112},{112,128},... | collective-permute-start | bytes 294920 | tf_op jit(solution)/shard_map/ppermute | solution.py:26
  74.2 8.6 %collective-permute-start.4 = (f32[1,6,32,128]{3,2,1,0:T(8,128)S(1)}, f32[1,6,32,128]{3,2,1,0:T(8,128)S(1)}, u32[]{:S(2)}, u32[]{:S(2)}) collective-permute-start(f32[1,6,32,128]{3,2,1,0:T(8,128)S(1)} %get-tuple-element.22), channel_id=1, source_target_pairs={{16,0},{32,16},{48,32},{64,48},{80,64},{96,80},{112,96},{128,112},... | collective-permute-start | bytes 294920 | tf_op jit(solution)/shard_map/ppermute | solution.py:27
  79.5 8.3 %collective-permute-start.3 = (f32[1,6,32,128]{3,2,1,0:T(8,128)S(1)}, f32[1,6,32,128]{3,2,1,0:T(8,128)S(1)}, u32[]{:S(2)}, u32[]{:S(2)}) collective-permute-start(f32[1,6,32,128]{3,2,1,0:T(8,128)S(1)} %get-tuple-element.23), channel_id=1, source_target_pairs={{0,16},{16,32},{32,48},{48,64},{64,80},{80,96},{96,112},{112,128},... | collective-permute-start | bytes 294920 | tf_op jit(solution)/shard_map/ppermute | solution.py:26
  95.9 1.0 copy-start
  96.9 4.7 %collective-permute-start.6 = (f32[1,6,32,128]{3,2,1,0:T(8,128)S(1)}, f32[1,6,32,128]{3,2,1,0:T(8,128)S(1)}, u32[]{:S(2)}, u32[]{:S(2)}) collective-permute-start(f32[1,6,32,128]{3,2,1,0:T(8,128)S(1)} %get-tuple-element.20), channel_id=1, source_target_pairs={{16,0},{32,16},{48,32},{64,48},{80,64},{96,80},{112,96},{128,112},... | collective-permute-start | bytes 294920 | tf_op jit(solution)/shard_map/ppermute | solution.py:27
  98.3 8.2 %collective-permute-start.5 = (f32[1,6,32,128]{3,2,1,0:T(8,128)S(1)}, f32[1,6,32,128]{3,2,1,0:T(8,128)S(1)}, u32[]{:S(2)}, u32[]{:S(2)}) collective-permute-start(f32[1,6,32,128]{3,2,1,0:T(8,128)S(1)} %get-tuple-element.21), channel_id=1, source_target_pairs={{0,16},{16,32},{32,48},{48,64},{64,80},{80,96},{96,112},{112,128},... | collective-permute-start | bytes 294920 | tf_op jit(solution)/shard_map/ppermute | solution.py:26
Sparse Core Ops, SparseCore 0:
  25.9 37.4 all-gather.2

commit v4 on v3

--- a/solution.py
+++ b/solution.py
@@ -153,8 +153,36 @@
     packed = jnp.concatenate([projectors, gain_lanes], axis=3)
     pairs = [(o * n_states + t, t * n_states + o) for o in range(n_grid) for t in range(n_states)]
     packed = lax.ppermute(packed, ("grid", "states"), pairs)
-    gathered = lax.all_gather(packed[0], "states", axis=0, tiled=True)
+    def flip_y(s):
+        return s ^ 8
+
+    def flip_x(s):
+        return s ^ 2
+
+    def mirror_x(s):
+        x = (s // 2) % 4
+        return s + (3 - x - x) * 2
+
+    def flip_core(s):
+        return s ^ 1
+
+    exchanges = (flip_y, flip_x, mirror_x, flip_core)
+
+    def origins(me, done):
+        if not done:
+            return [me]
+        return origins(me, done[:-1]) + origins(done[-1](me), done[:-1])
+
+    gathered = packed[0]
+    for exchange in exchanges:
+        partner = lax.ppermute(
+            gathered, "states", [(s, exchange(s)) for s in range(n_states)]
+        )
+        gathered = jnp.concatenate([gathered, partner], axis=0)
+    block_owner = jnp.stack(origins(lax.axis_index("states"), exchanges))
+    owner_block = jnp.argmax(block_owner[None, :] == atom_owner[:, None], axis=1)
     gathered = gathered.reshape(n_states * slot_pairs, proj_count, line_span + 128)
+    atom_slot = owner_block * PAIR_CAP + owner_rank
     atom_pack = jnp.take(gathered, atom_slot, axis=0)
     proj_rows = atom_pack[:, :, :line_span].reshape(home_count * proj_count, line_span)
     atom_gain = atom_pack[:, :, line_span].astype(jnp.float32)

time: 120 us -> 95.4 us (0.80)
  waiting for transfers between devices: 48.8 us -> 27.4 us
  between operations: 13.7 us -> 0.53 us
  starting transfers between devices: 17.7 us -> 26.8 us
  other arithmetic: 8.84 us -> 11.7 us
  local copies, waits for them, and re-layouts: 10.5 us -> 9.06 us
    all_gather x1 -> x0, waiting for transfers between devices: 24.9 us -> none  [shards(): gathered = lax.all_gather(packed[0], 'states', axis=0, tiled=True)]
    ppermute x0 -> x4, waiting for transfers between devices: none -> 21.7 us  [shards(): lax.ppermute(gathered, 'states', [(s, exchange(s)) for s in range(n_state...]
    ppermute x3, starting transfers between devices: 6.83 us -> 20.3 us  [padded_2(): after = lax.ppermute(initial, axis, down)]
    ppermute x3, waiting for transfers between devices: 12.2 us -> 0.01 us  [padded_2(): before = lax.ppermute(last, axis, up)]
    ppermute x1, starting transfers between devices: 8.12 us -> 1.92 us  [shards(): packed = lax.ppermute(packed, ('grid', 'states'), pairs)]
    ppermute x1, waiting for transfers between devices: 8.73 us -> 5.62 us  [shards(): packed = lax.ppermute(packed, ('grid', 'states'), pairs)]
    ppermute x3, waiting for transfers between devices: 2.9 us -> 0.01 us  [padded_2(): after = lax.ppermute(initial, axis, down)]
    ppermute x0 -> x4, starting transfers between devices: none -> 2.42 us  [shards(): lax.ppermute(gathered, 'states', [(s, exchange(s)) for s in range(n_state...]
  transfers between devices with their start and end apart: 8 -> 11, of which waited for: 7 -> 5; matrix products, arithmetic and copies ran while one was open for 9% -> 18% of each run, Pallas kernels for 0% -> 0%
where the time goes in v4:
time: 95.4 us; the launch traced here: 94.9 us
  waiting for transfers between devices  27.4 us (29%)
  starting transfers between devices  26.8 us (28%)
  other arithmetic  11.7 us (12%)
  Pallas kernels  10.1 us (11%)
  matrix products  9.33 us (10%)
  local copies, waits for them, and re-layouts  9.06 us (9%)
    ppermute x4, waiting for transfers between devices, shards(): lax.ppermute(gathered, 'states', [(s, exchange(s)) for s in range(n_state...  21.7 us
    ppermute x3, starting transfers between devices, padded_2(): after = lax.ppermute(initial, axis, down)  20.3 us
    pallas_call x3, Pallas kernels, apply_op(): pl.pallas_call(make_kernel(scale, prev is not None), out_shape=jax.ShapeD...  10.1 us
    ppermute x1, waiting for transfers between devices, shards(): packed = lax.ppermute(packed, ('grid', 'states'), pairs)  5.62 us
    squeeze x6, other arithmetic, rims(): return (low_rim[0], high_rim[0])  4.29 us
    dot_general x3, matrix products, nonlocal_part(): lax.dot_general(proj_rows, picked, (((1,), (1,)), ((), ())), preferred_el...  4.03 us
    dot_general x3, matrix products, nonlocal_part(): lax.dot_general(selector, projected, (((0,), (0,)), ((), ())), preferred_...  3.05 us
    convert_element_type x3, other arithmetic, nonlocal_part(): lines_here = grid_field.reshape(tile_lines, line_depth).astype(jnp.bfloat16)  2.91 us
  transfers between devices with their start and end apart: 11, of which 5 were waited for; matrix products, arithmetic and copies ran while one was open for 18% of the time, Pallas kernels for 0%

profile of v4, /device:TPU:6, one launch (start us, length us, event | category | flops | bytes accessed | tf_op | source)
XLA Modules:
  0.0 94.9 jit_solution(17019583506167285436)
XLA Ops:
  0.0 1.0 %fusion.55 = (f32[1,6,32,128]{3,2,1,0:T(8,128)S(1)}, f32[1,6,32,128]{3,2,1,0:T(8,128)S(1)}) fusion(f32[1,16,32,128]{3,2,1,0:T(8,128)} %param.11), kind=kLoop, calls=%fused_computation.109 | loop fusion | bytes 393216 | tf_op jit(solution)/shard_map/slice | solution.py:25
  1.0 2.0 %collective-permute-start = (f32[1,6,32,128]{3,2,1,0:T(8,128)S(1)}, f32[1,6,32,128]{3,2,1,0:T(8,128)S(1)}, u32[]{:S(2)}, u32[]{:S(2)}) collective-permute-start(f32[1,6,32,128]{3,2,1,0:T(8,128)S(1)} %get-tuple-element.27), channel_id=1, source_target_pairs={{0,16},{16,32},{32,48},{48,64},{64,80},{80,96},{96,112},{112,128},... | collective-permute-start | bytes 294920 | tf_op jit(solution)/shard_map/ppermute | solution.py:26
  3.0 6.7 %collective-permute-start.1 = (f32[1,6,32,128]{3,2,1,0:T(8,128)S(1)}, f32[1,6,32,128]{3,2,1,0:T(8,128)S(1)}, u32[]{:S(2)}, u32[]{:S(2)}) collective-permute-start(f32[1,6,32,128]{3,2,1,0:T(8,128)S(1)} %get-tuple-element.26), channel_id=1, source_target_pairs={{16,0},{32,16},{48,32},{64,48},{80,64},{96,80},{112,96},{128,112},... | collective-permute-start | bytes 294920 | tf_op jit(solution)/shard_map/ppermute | solution.py:27
  11.3 1.9 %collective-permute-start.2 = (bf16[1,2,8,4224]{3,2,1,0:T(8,128)(2,1)S(1)}, bf16[1,2,8,4224]{3,2,1,0:T(8,128)(2,1)S(1)}, u32[]{:S(2)}, u32[]{:S(2)}) collective-permute-start(bf16[1,2,8,4224]{3,2,1,0:T(8,128)(2,1)S(1)} %fusion.28), channel_id=1, source_target_pairs={{0,0},{1,16},{2,32},{3,48},{4,64},{5,80},{6,96},{7,112},{8,128},{9... | collective-permute-start | bytes 405512 | tf_op jit(solution)/shard_map/ppermute | solution.py:155
  15.4 1.0 %convert_element_type.115 = bf16[1,16,32,128]{3,2,1,0:T(8,128)(2,1)S(1)} convert(f32[1,16,32,128]{3,2,1,0:T(8,128)} %param.11) | non-fusion elementwise | flops 65536 | bytes 393216 | tf_op jit(solution)/shard_map/convert_element_type | solution.py:205
  20.1 5.6 %collective-permute-done.2 = bf16[1,2,8,4224]{3,2,1,0:T(8,128)(2,1)S(1)} collective-permute-done((bf16[1,2,8,4224]{3,2,1,0:T(8,128)(2,1)S(1)}, bf16[1,2,8,4224]{3,2,1,0:T(8,128)(2,1)S(1)}, u32[]{:S(2)}, u32[]{:S(2)}) %collective-permute-start.2) | collective-permute-done | bytes 135200 | tf_op jit(solution)/shard_map/ppermute | solution.py:155
  25.8 1.6 %collective-permute-start.3 = (bf16[2,8,4224]{2,1,0:T(8,128)(2,1)S(1)}, bf16[2,8,4224]{2,1,0:T(8,128)(2,1)S(1)}, u32[]{:S(2)}, u32[]{:S(2)}) collective-permute-start(bf16[2,8,4224]{2,1,0:T(8,128)(2,1)S(1)} %bitcast.117), channel_id=1, source_target_pairs={{0,8},{1,9},{2,10},{3,11},{4,12},{5,13},{6,14},{7,15},{8,0},{9,1},... | collective-permute-start | bytes 405512 | tf_op jit(solution)/shard_map/ppermute | solution.py:178
  28.1 2.7 %collective-permute-done.3 = bf16[2,8,4224]{2,1,0:T(8,128)(2,1)S(1)} collective-permute-done((bf16[2,8,4224]{2,1,0:T(8,128)(2,1)S(1)}, bf16[2,8,4224]{2,1,0:T(8,128)(2,1)S(1)}, u32[]{:S(2)}, u32[]{:S(2)}) %collective-permute-start.3) | collective-permute-done | bytes 135200 | tf_op jit(solution)/shard_map/ppermute | solution.py:178
  31.5 5.9 %collective-permute-done.4 = bf16[4,8,4224]{2,1,0:T(8,128)(2,1)S(1)} collective-permute-done((bf16[4,8,4224]{2,1,0:T(8,128)(2,1)S(1)}, bf16[4,8,4224]{2,1,0:T(8,128)(2,1)S(1)}, u32[]{:S(2)}, u32[]{:S(2)}) %collective-permute-start.4) | collective-permute-done | bytes 270368 | tf_op jit(solution)/shard_map/ppermute | solution.py:178
  37.5 10.5 %collective-permute-done.5 = bf16[8,8,4224]{2,1,0:T(8,128)(2,1)S(1)} collective-permute-done((bf16[8,8,4224]{2,1,0:T(8,128)(2,1)S(1)}, bf16[8,8,4224]{2,1,0:T(8,128)(2,1)S(1)}, u32[]{:S(2)}, u32[]{:S(2)}) %collective-permute-start.5) | collective-permute-done | bytes 540704 | tf_op jit(solution)/shard_map/ppermute | solution.py:178
  48.4 2.6 %collective-permute-done.6 = bf16[16,8,4224]{2,1,0:T(8,128)(2,1)S(1)} collective-permute-done((bf16[16,8,4224]{2,1,0:T(8,128)(2,1)S(1)}, bf16[16,8,4224]{2,1,0:T(8,128)(2,1)S(1)}, u32[]{:S(2)}, u32[]{:S(2)}) %collective-permute-start.6) | collective-permute-done | bytes 1081376 | tf_op jit(solution)/shard_map/ppermute | solution.py:178
  52.1 1.3 %fusion.9 = f32[10,8]{0,1:T(8,128)S(1)} fusion(bf16[10,4096,1]{1,0,2:T(8,128)(2,1)S(1)} %reshape.270, bf16[10,8,4224]{2,0,1:T(8,128)(2,1)S(1)} %copy_select_fusion, f32[10,10]{0,1:T(8,128)S(1)} %fusion.50), kind=kOutput, calls=%fused_computation.25 | convolution fusion | flops 6555120 | bytes 1188160 | tf_op jit(solution)/shard_map/dot_general | solution.py:208
  54.0 1.0 %fusion.7.nl_ref = f32[16,32,128]{2,1,0:T(8,128)} fusion(bf16[320,128,1]{1,0,2:T(8,128)(2,1)S(1)} %reshape.272, s32[16,32]{1,0:T(8,128)S(1)} %multiply_add_fusion, s32[320]{0:T(512)S(1)} %eq.119), kind=kOutput, calls=%fused_computation.17 | convolution fusion | flops 42106880 | bytes 347392 | tf_op jit(solution)/shard_map/dot_general | solution.py:218
  55.0 3.3 %shard_map.73.v_ref.rest_0_ = f32[16,32,128]{2,1,0:T(8,128)} custom-call(f32[6,32,128]{2,1,0:T(8,128)} %fusion.40.lo_ref, f32[16,32,128]{2,1,0:T(8,128)} %bitcast.114, f32[6,32,128]{2,1,0:T(8,128)} %fusion.38.hi_ref, f32[16,32,128]{2,1,0:T(8,128)} %pot_ref.5, f32[16,32,128]{2,1,0:T(8,128)} %fusion.7.nl_ref), custom_call_target="tpu_custom_call" | custom-call | tf_op jit(solution)/shard_map/pallas_call | solution.py:122
  58.3 1.0 %convert_element_type.122 = bf16[16,32,128]{2,1,0:T(8,128)(2,1)S(1)} convert(f32[16,32,128]{2,1,0:T(8,128)} %shard_map.73.v_ref.rest_0_) | non-fusion elementwise | flops 65536 | bytes 393216 | tf_op jit(solution)/shard_map/convert_element_type | solution.py:205
  60.3 8.0 %collective-permute-start.8 = (f32[1,6,32,128]{3,2,1,0:T(8,128)S(1)}, f32[1,6,32,128]{3,2,1,0:T(8,128)S(1)}, u32[]{:S(2)}, u32[]{:S(2)}) collective-permute-start(f32[1,6,32,128]{3,2,1,0:T(8,128)S(1)} %get-tuple-element.24), channel_id=1, source_target_pairs={{16,0},{32,16},{48,32},{64,48},{80,64},{96,80},{112,96},{128,112},... | collective-permute-start | bytes 294920 | tf_op jit(solution)/shard_map/ppermute | solution.py:27
  68.7 1.3 %fusion.10 = f32[10,8]{0,1:T(8,128)S(1)} fusion(bf16[10,4096,1]{1,0,2:T(8,128)(2,1)S(1)} %reshape.273, bf16[10,8,4224]{2,0,1:T(8,128)(2,1)S(1)} %copy_select_fusion, f32[10,10]{0,1:T(8,128)S(1)} %fusion.50), kind=kOutput, calls=%fused_computation.26 | convolution fusion | flops 6555120 | bytes 1188160 | tf_op jit(solution)/shard_map/dot_general | solution.py:208
  70.6 1.0 %fusion.5.nl_ref = f32[16,32,128]{2,1,0:T(8,128)} fusion(bf16[320,128,1]{1,0,2:T(8,128)(2,1)S(1)} %reshape.275, s32[16,32]{1,0:T(8,128)S(1)} %multiply_add_fusion, s32[320]{0:T(512)S(1)} %eq.119), kind=kOutput, calls=%fused_computation.15 | convolution fusion | flops 42106880 | bytes 347392 | tf_op jit(solution)/shard_map/dot_general | solution.py:218
  74.4 3.4 %shard_map.74.v_ref = f32[16,32,128]{2,1,0:T(8,128)} custom-call(f32[6,32,128]{2,1,0:T(8,128)} %fusion.36.lo_ref, f32[16,32,128]{2,1,0:T(8,128)} %shard_map.73.v_ref.rest_0_, f32[6,32,128]{2,1,0:T(8,128)} %fusion.34.hi_ref, f32[16,32,128]{2,1,0:T(8,128)} %pot_ref.5, f32[16,32,128]{2,1,0:T(8,128)} %fusion.5.nl_ref, f32[16,32,128]{2,1,0:T(8,128)} %bitcast.115), custom_call_target="tpu_custom_call" | custom-call | tf_op jit(solution)/shard_map/pallas_call | solution.py:122
  77.8 1.0 %convert_element_type.127 = bf16[16,32,128]{2,1,0:T(8,128)(2,1)S(1)} convert(f32[16,32,128]{2,1,0:T(8,128)} %shard_map.74.v_ref) | non-fusion elementwise | flops 65536 | bytes 393216 | tf_op jit(solution)/shard_map/convert_element_type | solution.py:205
  79.8 5.6 %collective-permute-start.10 = (f32[1,6,32,128]{3,2,1,0:T(8,128)S(1)}, f32[1,6,32,128]{3,2,1,0:T(8,128)S(1)}, u32[]{:S(2)}, u32[]{:S(2)}) collective-permute-start(f32[1,6,32,128]{3,2,1,0:T(8,128)S(1)} %get-tuple-element.22), channel_id=1, source_target_pairs={{16,0},{32,16},{48,32},{64,48},{80,64},{96,80},{112,96},{128,112},... | collective-permute-start | bytes 294920 | tf_op jit(solution)/shard_map/ppermute | solution.py:27
  85.8 1.3 %fusion.11 = f32[10,8]{0,1:T(8,128)S(1)} fusion(bf16[10,4096,1]{1,0,2:T(8,128)(2,1)S(1)} %reshape.276, bf16[10,8,4224]{2,0,1:T(8,128)(2,1)S(1)} %copy_select_fusion, f32[10,10]{0,1:T(8,128)S(1)} %fusion.50), kind=kOutput, calls=%fused_computation.27 | convolution fusion | flops 6555120 | bytes 1188160 | tf_op jit(solution)/shard_map/dot_general | solution.py:208
  87.7 1.0 %fusion.3.nl_ref = f32[16,32,128]{2,1,0:T(8,128)} fusion(bf16[320,128,1]{1,0,2:T(8,128)(2,1)S(1)} %reshape.278, s32[16,32]{1,0:T(8,128)S(1)} %multiply_add_fusion, s32[320]{0:T(512)S(1)} %eq.119), kind=kOutput, calls=%fused_computation.13 | convolution fusion | flops 42106880 | bytes 347392 | tf_op jit(solution)/shard_map/dot_general | solution.py:218
  91.5 3.4 %shard_map.75 = f32[16,32,128]{2,1,0:T(8,128)} custom-call(f32[6,32,128]{2,1,0:T(8,128)} %fusion.32.lo_ref, f32[16,32,128]{2,1,0:T(8,128)} %shard_map.74.v_ref, f32[6,32,128]{2,1,0:T(8,128)} %fusion.30.hi_ref, f32[16,32,128]{2,1,0:T(8,128)} %pot_ref.5, f32[16,32,128]{2,1,0:T(8,128)} %fusion.3.nl_ref, f32[16,32,128]{2,1,0:T(8,128)} %shard_map.73.v_ref.rest_0_), custom_call_target="tpu_custom_call" | custom-call | tf_op jit(solution)/shard_map/pallas_call | solution.py:122
  (81 shorter events, 20.2 us)
Async XLA Ops:
  0.0 16.5 %copy-start.1 = (s32[10]{0:T(128)S(1)}, s32[10]{0:T(128)}, u32[]{:S(2)}) copy-start(s32[10]{0:T(128)} %param.15) | copy-start | bytes 124
  0.0 17.5 %copy-start = (s32[10,32]{1,0:T(8,128)S(1)}, s32[10,32]{1,0:T(8,128)}, u32[]{:S(2)}) copy-start(s32[10,32]{1,0:T(8,128)} %param.16) | copy-start | bytes 3844
  1.0 17.1 %collective-permute-start = (f32[1,6,32,128]{3,2,1,0:T(8,128)S(1)}, f32[1,6,32,128]{3,2,1,0:T(8,128)S(1)}, u32[]{:S(2)}, u32[]{:S(2)}) collective-permute-start(f32[1,6,32,128]{3,2,1,0:T(8,128)S(1)} %get-tuple-element.27), channel_id=1, source_target_pairs={{0,16},{16,32},{32,48},{48,64},{64,80},{80,96},{96,112},{112,128},... | collective-permute-start | bytes 294920 | tf_op jit(solution)/shard_map/ppermute | solution.py:26
  3.0 15.2 %collective-permute-start.1 = (f32[1,6,32,128]{3,2,1,0:T(8,128)S(1)}, f32[1,6,32,128]{3,2,1,0:T(8,128)S(1)}, u32[]{:S(2)}, u32[]{:S(2)}) collective-permute-start(f32[1,6,32,128]{3,2,1,0:T(8,128)S(1)} %get-tuple-element.26), channel_id=1, source_target_pairs={{16,0},{32,16},{48,32},{64,48},{80,64},{96,80},{112,96},{128,112},... | collective-permute-start | bytes 294920 | tf_op jit(solution)/shard_map/ppermute | solution.py:27
  11.3 14.4 %collective-permute-start.2 = (bf16[1,2,8,4224]{3,2,1,0:T(8,128)(2,1)S(1)}, bf16[1,2,8,4224]{3,2,1,0:T(8,128)(2,1)S(1)}, u32[]{:S(2)}, u32[]{:S(2)}) collective-permute-start(bf16[1,2,8,4224]{3,2,1,0:T(8,128)(2,1)S(1)} %fusion.28), channel_id=1, source_target_pairs={{0,0},{1,16},{2,32},{3,48},{4,64},{5,80},{6,96},{7,112},{8,128},{9... | collective-permute-start | bytes 405512 | tf_op jit(solution)/shard_map/ppermute | solution.py:155
  25.8 5.0 %collective-permute-start.3 = (bf16[2,8,4224]{2,1,0:T(8,128)(2,1)S(1)}, bf16[2,8,4224]{2,1,0:T(8,128)(2,1)S(1)}, u32[]{:S(2)}, u32[]{:S(2)}) collective-permute-start(bf16[2,8,4224]{2,1,0:T(8,128)(2,1)S(1)} %bitcast.117), channel_id=1, source_target_pairs={{0,8},{1,9},{2,10},{3,11},{4,12},{5,13},{6,14},{7,15},{8,0},{9,1},... | collective-permute-start | bytes 405512 | tf_op jit(solution)/shard_map/ppermute | solution.py:178
  30.8 6.5 %collective-permute-start.4 = (bf16[4,8,4224]{2,1,0:T(8,128)(2,1)S(1)}, bf16[4,8,4224]{2,1,0:T(8,128)(2,1)S(1)}, u32[]{:S(2)}, u32[]{:S(2)}) collective-permute-start(bf16[4,8,4224]{2,1,0:T(8,128)(2,1)S(1)} %pad_maximum_fusion.2), channel_id=1, source_target_pairs={{0,2},{1,3},{2,0},{3,1},{4,6},{5,7},{6,4},{7,5},{8,10},{9,11},{10,... | collective-permute-start | bytes 811016 | tf_op jit(solution)/shard_map/ppermute | solution.py:178
  37.4 10.7 %collective-permute-start.5 = (bf16[8,8,4224]{2,1,0:T(8,128)(2,1)S(1)}, bf16[8,8,4224]{2,1,0:T(8,128)(2,1)S(1)}, u32[]{:S(2)}, u32[]{:S(2)}) collective-permute-start(bf16[8,8,4224]{2,1,0:T(8,128)(2,1)S(1)} %pad_maximum_fusion.1), channel_id=1, source_target_pairs={{0,6},{1,7},{2,4},{3,5},{4,2},{5,3},{6,0},{7,1},{8,14},{9,15},{10,... | collective-permute-start | bytes 1622024 | tf_op jit(solution)/shard_map/ppermute | solution.py:178
  48.2 2.8 %collective-permute-start.6 = (bf16[16,8,4224]{2,1,0:T(8,128)(2,1)S(1)}, bf16[16,8,4224]{2,1,0:T(8,128)(2,1)S(1)}, u32[]{:S(2)}, u32[]{:S(2)}) collective-permute-start(bf16[16,8,4224]{2,1,0:T(8,128)(2,1)S(1)} %pad_maximum_fusion), channel_id=1, source_target_pairs={{0,1},{1,0},{2,3},{3,2},{4,5},{5,4},{6,7},{7,6},{8,9},{9,8},{10,11... | collective-permute-start | bytes 3244040 | tf_op jit(solution)/shard_map/ppermute | solution.py:178
  60.3 11.4 %collective-permute-start.7 = (f32[1,6,32,128]{3,2,1,0:T(8,128)S(1)}, f32[1,6,32,128]{3,2,1,0:T(8,128)S(1)}, u32[]{:S(2)}, u32[]{:S(2)}) collective-permute-start(f32[1,6,32,128]{3,2,1,0:T(8,128)S(1)} %get-tuple-element.25), channel_id=1, source_target_pairs={{0,16},{16,32},{32,48},{48,64},{64,80},{80,96},{96,112},{112,128},... | collective-permute-start | bytes 294920 | tf_op jit(solution)/shard_map/ppermute | solution.py:26
  60.3 12.0 %collective-permute-start.8 = (f32[1,6,32,128]{3,2,1,0:T(8,128)S(1)}, f32[1,6,32,128]{3,2,1,0:T(8,128)S(1)}, u32[]{:S(2)}, u32[]{:S(2)}) collective-permute-start(f32[1,6,32,128]{3,2,1,0:T(8,128)S(1)} %get-tuple-element.24), channel_id=1, source_target_pairs={{16,0},{32,16},{48,32},{64,48},{80,64},{96,80},{112,96},{128,112},... | collective-permute-start | bytes 294920 | tf_op jit(solution)/shard_map/ppermute | solution.py:27
  79.7 9.0 %collective-permute-start.9 = (f32[1,6,32,128]{3,2,1,0:T(8,128)S(1)}, f32[1,6,32,128]{3,2,1,0:T(8,128)S(1)}, u32[]{:S(2)}, u32[]{:S(2)}) collective-permute-start(f32[1,6,32,128]{3,2,1,0:T(8,128)S(1)} %get-tuple-element.23), channel_id=1, source_target_pairs={{0,16},{16,32},{32,48},{48,64},{64,80},{80,96},{96,112},{112,128},... | collective-permute-start | bytes 294920 | tf_op jit(solution)/shard_map/ppermute | solution.py:26
  79.8 9.6 %collective-permute-start.10 = (f32[1,6,32,128]{3,2,1,0:T(8,128)S(1)}, f32[1,6,32,128]{3,2,1,0:T(8,128)S(1)}, u32[]{:S(2)}, u32[]{:S(2)}) collective-permute-start(f32[1,6,32,128]{3,2,1,0:T(8,128)S(1)} %get-tuple-element.22), channel_id=1, source_target_pairs={{16,0},{32,16},{48,32},{64,48},{80,64},{96,80},{112,96},{128,112},... | collective-permute-start | bytes 294920 | tf_op jit(solution)/shard_map/ppermute | solution.py:27

commit v5 on v4

--- a/solution.py
+++ b/solution.py
@@ -153,6 +153,7 @@
     packed = jnp.concatenate([projectors, gain_lanes], axis=3)
     pairs = [(o * n_states + t, t * n_states + o) for o in range(n_grid) for t in range(n_states)]
     packed = lax.ppermute(packed, ("grid", "states"), pairs)
+    packed, states_in = lax.optimization_barrier((packed, states_in))
     def flip_y(s):
         return s ^ 8
 

time: 95.4 us -> 99.7 us (1.045)
  starting transfers between devices: 26.8 us -> 30.2 us
  other arithmetic: 11.7 us -> 12.9 us
    ppermute x1, starting transfers between devices: 1.92 us -> 8.12 us  [shards(): packed = lax.ppermute(packed, ('grid', 'states'), pairs)]
    ppermute x3, starting transfers between devices: 20.3 us -> 16.4 us  [padded_2(): after = lax.ppermute(initial, axis, down)]
    ppermute x4, starting transfers between devices: 2.42 us -> 4.95 us  [shards(): lax.ppermute(gathered, 'states', [(s, exchange(s)) for s in range(n_state...]
    ppermute x1, waiting for transfers between devices: 5.62 us -> 3.22 us  [shards(): packed = lax.ppermute(packed, ('grid', 'states'), pairs)]
    ppermute x3, starting transfers between devices: 2.16 us -> 0.72 us  [padded_2(): before = lax.ppermute(last, axis, up)]
    ppermute x4, waiting for transfers between devices: 21.7 us -> 23.1 us  [shards(): lax.ppermute(gathered, 'states', [(s, exchange(s)) for s in range(n_state...]
  transfers between devices with their start and end apart: 11 -> 11, of which waited for: 5 -> 6; matrix products, arithmetic and copies ran while one was open for 18% -> 17% of each run, Pallas kernels for 0% -> 0%
where the time goes in v5:
time: 99.7 us; the launch traced here: 99.2 us
  starting transfers between devices  30.2 us (30%)
  waiting for transfers between devices  26.6 us (27%)
  other arithmetic  12.9 us (13%)
  Pallas kernels  10.1 us (10%)
  local copies, waits for them, and re-layouts  9.71 us (10%)
  matrix products  9.32 us (9%)
    ppermute x4, waiting for transfers between devices, shards(): lax.ppermute(gathered, 'states', [(s, exchange(s)) for s in range(n_state...  23.1 us
    ppermute x3, starting transfers between devices, padded_2(): after = lax.ppermute(initial, axis, down)  16.4 us
    pallas_call x3, Pallas kernels, apply_op(): pl.pallas_call(make_kernel(scale, prev is not None), out_shape=jax.ShapeD...  10.1 us
    ppermute x1, starting transfers between devices, shards(): packed = lax.ppermute(packed, ('grid', 'states'), pairs)  8.12 us
    ppermute x4, starting transfers between devices, shards(): lax.ppermute(gathered, 'states', [(s, exchange(s)) for s in range(n_state...  4.95 us
    squeeze x6, other arithmetic, rims(): return (low_rim[0], high_rim[0])  4.29 us
    dot_general x3, matrix products, nonlocal_part(): lax.dot_general(proj_rows, picked, (((1,), (1,)), ((), ())), preferred_el...  4.03 us
    slice x3, local copies, waits for them, and re-layouts, padded_2(): initial = lax.slice_in_dim(shard, 0, width, axis=dim)  3.5 us
  transfers between devices with their start and end apart: 11, of which 6 were waited for; matrix products, arithmetic and copies ran while one was open for 17% of the time, Pallas kernels for 0%

profile of v5, /device:TPU:6, one launch (start us, length us, event | category | flops | bytes accessed | tf_op | source)
XLA Modules:
  0.0 99.2 jit_solution(7278248123172217696)
XLA Ops:
  1.7 8.1 %collective-permute-start = (bf16[1,2,8,4224]{3,2,1,0:T(8,128)(2,1)S(1)}, bf16[1,2,8,4224]{3,2,1,0:T(8,128)(2,1)S(1)}, u32[]{:S(2)}, u32[]{:S(2)}) collective-permute-start(bf16[1,2,8,4224]{3,2,1,0:T(8,128)(2,1)S(1)} %fusion.28), channel_id=1, source_target_pairs={{0,0},{1,16},{2,32},{3,48},{4,64},{5,80},{6,96},{7,112},{8,128},{9... | collective-permute-start | bytes 405512 | tf_op jit(solution)/shard_map/ppermute | solution.py:155
  13.1 1.4 %iota_reduce_fusion = (pred[10]{0:T(512)(128)(4,1)}, s32[10]{0:T(128)S(1)}) fusion(s32[16]{0:T(128)S(1)} %stack.67, s32[10]{0:T(128)} %param.15), kind=kLoop, calls=%fused_computation.88 | loop fusion | flops 1210 | bytes 154 | tf_op jit(solution)/shard_map/shards/reduce | solution.py:184
  15.4 3.2 %collective-permute-done = bf16[1,2,8,4224]{3,2,1,0:T(8,128)(2,1)S(1)} collective-permute-done((bf16[1,2,8,4224]{3,2,1,0:T(8,128)(2,1)S(1)}, bf16[1,2,8,4224]{3,2,1,0:T(8,128)(2,1)S(1)}, u32[]{:S(2)}, u32[]{:S(2)}) %collective-permute-start) | collective-permute-done | bytes 135200 | tf_op jit(solution)/shard_map/ppermute | solution.py:155
  18.6 1.6 %fusion.55 = (f32[1,6,32,128]{3,2,1,0:T(8,128)}, f32[1,6,32,128]{3,2,1,0:T(8,128)S(1)}) fusion(f32[1,16,32,128]{3,2,1,0:T(8,128)} %param.11), kind=kLoop, calls=%fused_computation.109 | loop fusion | bytes 393216 | tf_op jit(solution)/shard_map/slice | solution.py:25
  20.8 5.2 %collective-permute-start.2 = (f32[1,6,32,128]{3,2,1,0:T(8,128)}, f32[1,6,32,128]{3,2,1,0:T(8,128)S(1)}, u32[]{:S(2)}, u32[]{:S(2)}) collective-permute-start(f32[1,6,32,128]{3,2,1,0:T(8,128)} %get-tuple-element.30), channel_id=1, source_target_pairs={{16,0},{32,16},{48,32},{64,48},{80,64},{96,80},{112,96},{128,112},... | collective-permute-start | bytes 294920 | tf_op jit(solution)/shard_map/ppermute | solution.py:27
  25.9 2.7 %collective-permute-start.3 = (bf16[2,8,4224]{2,1,0:T(8,128)(2,1)S(1)}, bf16[2,8,4224]{2,1,0:T(8,128)(2,1)S(1)}, u32[]{:S(2)}, u32[]{:S(2)}) collective-permute-start(bf16[2,8,4224]{2,1,0:T(8,128)(2,1)S(1)} %bitcast.117), channel_id=1, source_target_pairs={{0,8},{1,9},{2,10},{3,11},{4,12},{5,13},{6,14},{7,15},{8,0},{9,1},... | collective-permute-start | bytes 405512 | tf_op jit(solution)/shard_map/ppermute | solution.py:179
  29.9 2.6 %collective-permute-done.3 = bf16[2,8,4224]{2,1,0:T(8,128)(2,1)S(1)} collective-permute-done((bf16[2,8,4224]{2,1,0:T(8,128)(2,1)S(1)}, bf16[2,8,4224]{2,1,0:T(8,128)(2,1)S(1)}, u32[]{:S(2)}, u32[]{:S(2)}) %collective-permute-start.3) | collective-permute-done | bytes 135200 | tf_op jit(solution)/shard_map/ppermute | solution.py:179
  32.5 1.2 %collective-permute-start.4 = (bf16[4,8,4224]{2,1,0:T(8,128)(2,1)S(1)}, bf16[4,8,4224]{2,1,0:T(8,128)(2,1)S(1)}, u32[]{:S(2)}, u32[]{:S(2)}) collective-permute-start(bf16[4,8,4224]{2,1,0:T(8,128)(2,1)S(1)} %pad_maximum_fusion.2), channel_id=1, source_target_pairs={{0,2},{1,3},{2,0},{3,1},{4,6},{5,7},{6,4},{7,5},{8,10},{9,11},{10,... | collective-permute-start | bytes 811016 | tf_op jit(solution)/shard_map/ppermute | solution.py:179
  35.8 4.8 %collective-permute-done.4 = bf16[4,8,4224]{2,1,0:T(8,128)(2,1)S(1)} collective-permute-done((bf16[4,8,4224]{2,1,0:T(8,128)(2,1)S(1)}, bf16[4,8,4224]{2,1,0:T(8,128)(2,1)S(1)}, u32[]{:S(2)}, u32[]{:S(2)}) %collective-permute-start.4) | collective-permute-done | bytes 270368 | tf_op jit(solution)/shard_map/ppermute | solution.py:179
  40.6 1.0 %collective-permute-start.5 = (bf16[8,8,4224]{2,1,0:T(8,128)(2,1)S(1)}, bf16[8,8,4224]{2,1,0:T(8,128)(2,1)S(1)}, u32[]{:S(2)}, u32[]{:S(2)}) collective-permute-start(bf16[8,8,4224]{2,1,0:T(8,128)(2,1)S(1)} %pad_maximum_fusion.1), channel_id=1, source_target_pairs={{0,6},{1,7},{2,4},{3,5},{4,2},{5,3},{6,0},{7,1},{8,14},{9,15},{10,... | collective-permute-start | bytes 1622024 | tf_op jit(solution)/shard_map/ppermute | solution.py:179
  41.7 13.1 %collective-permute-done.5 = bf16[8,8,4224]{2,1,0:T(8,128)(2,1)S(1)} collective-permute-done((bf16[8,8,4224]{2,1,0:T(8,128)(2,1)S(1)}, bf16[8,8,4224]{2,1,0:T(8,128)(2,1)S(1)}, u32[]{:S(2)}, u32[]{:S(2)}) %collective-permute-start.5) | collective-permute-done | bytes 540704 | tf_op jit(solution)/shard_map/ppermute | solution.py:179
  55.1 2.6 %collective-permute-done.6 = bf16[16,8,4224]{2,1,0:T(8,128)(2,1)S(1)} collective-permute-done((bf16[16,8,4224]{2,1,0:T(8,128)(2,1)S(1)}, bf16[16,8,4224]{2,1,0:T(8,128)(2,1)S(1)}, u32[]{:S(2)}, u32[]{:S(2)}) %collective-permute-start.6) | collective-permute-done | bytes 1081376 | tf_op jit(solution)/shard_map/ppermute | solution.py:179
  58.8 1.3 %fusion.9 = f32[10,8]{0,1:T(8,128)S(1)} fusion(bf16[10,4096,1]{1,0,2:T(8,128)(2,1)S(1)} %reshape.270, bf16[10,8,4224]{2,0,1:T(8,128)(2,1)S(1)} %copy_select_fusion, f32[10,10]{0,1:T(8,128)S(1)} %fusion.50), kind=kOutput, calls=%fused_computation.25 | convolution fusion | flops 6555120 | bytes 1188160 | tf_op jit(solution)/shard_map/dot_general | solution.py:209
  60.7 1.0 %fusion.7.nl_ref = f32[16,32,128]{2,1,0:T(8,128)} fusion(bf16[320,128,1]{1,0,2:T(8,128)(2,1)S(1)} %reshape.272, s32[16,32]{1,0:T(8,128)S(1)} %multiply_add_fusion, s32[320]{0:T(512)S(1)} %eq.119), kind=kOutput, calls=%fused_computation.17 | convolution fusion | flops 42106880 | bytes 347392 | tf_op jit(solution)/shard_map/dot_general | solution.py:219
  61.8 3.3 %shard_map.73.v_ref.rest_0_ = f32[16,32,128]{2,1,0:T(8,128)} custom-call(f32[6,32,128]{2,1,0:T(8,128)} %fusion.40.lo_ref, f32[16,32,128]{2,1,0:T(8,128)} %bitcast.114, f32[6,32,128]{2,1,0:T(8,128)} %fusion.38.hi_ref, f32[16,32,128]{2,1,0:T(8,128)} %pot_ref.5, f32[16,32,128]{2,1,0:T(8,128)} %fusion.7.nl_ref), custom_call_target="tpu_custom_call" | custom-call | tf_op jit(solution)/shard_map/pallas_call | solution.py:122
  65.0 1.0 convert_element_type.122
  67.1 5.6 %collective-permute-start.8 = (f32[1,6,32,128]{3,2,1,0:T(8,128)S(1)}, f32[1,6,32,128]{3,2,1,0:T(8,128)S(1)}, u32[]{:S(2)}, u32[]{:S(2)}) collective-permute-start(f32[1,6,32,128]{3,2,1,0:T(8,128)S(1)} %get-tuple-element.28), channel_id=1, source_target_pairs={{16,0},{32,16},{48,32},{64,48},{80,64},{96,80},{112,96},{128,112},... | collective-permute-start | bytes 294920 | tf_op jit(solution)/shard_map/ppermute | solution.py:27
  73.1 1.3 %fusion.10 = f32[10,8]{0,1:T(8,128)S(1)} fusion(bf16[10,4096,1]{1,0,2:T(8,128)(2,1)S(1)} %reshape.273, bf16[10,8,4224]{2,0,1:T(8,128)(2,1)S(1)} %copy_select_fusion, f32[10,10]{0,1:T(8,128)S(1)} %fusion.50), kind=kOutput, calls=%fused_computation.26 | convolution fusion | flops 6555120 | bytes 1188160 | tf_op jit(solution)/shard_map/dot_general | solution.py:209
  75.0 1.0 %fusion.5.nl_ref = f32[16,32,128]{2,1,0:T(8,128)} fusion(bf16[320,128,1]{1,0,2:T(8,128)(2,1)S(1)} %reshape.275, s32[16,32]{1,0:T(8,128)S(1)} %multiply_add_fusion, s32[320]{0:T(512)S(1)} %eq.119), kind=kOutput, calls=%fused_computation.15 | convolution fusion | flops 42106880 | bytes 347392 | tf_op jit(solution)/shard_map/dot_general | solution.py:219
  78.7 3.4 %shard_map.74.v_ref = f32[16,32,128]{2,1,0:T(8,128)} custom-call(f32[6,32,128]{2,1,0:T(8,128)} %fusion.36.lo_ref, f32[16,32,128]{2,1,0:T(8,128)} %shard_map.73.v_ref.rest_0_, f32[6,32,128]{2,1,0:T(8,128)} %fusion.34.hi_ref, f32[16,32,128]{2,1,0:T(8,128)} %pot_ref.5, f32[16,32,128]{2,1,0:T(8,128)} %fusion.5.nl_ref, f32[16,32,128]{2,1,0:T(8,128)} %bitcast.115), custom_call_target="tpu_custom_call" | custom-call | tf_op jit(solution)/shard_map/pallas_call | solution.py:122
  84.2 5.6 %collective-permute-start.10 = (f32[1,6,32,128]{3,2,1,0:T(8,128)S(1)}, f32[1,6,32,128]{3,2,1,0:T(8,128)S(1)}, u32[]{:S(2)}, u32[]{:S(2)}) collective-permute-start(f32[1,6,32,128]{3,2,1,0:T(8,128)S(1)} %get-tuple-element.26), channel_id=1, source_target_pairs={{16,0},{32,16},{48,32},{64,48},{80,64},{96,80},{112,96},{128,112},... | collective-permute-start | bytes 294920 | tf_op jit(solution)/shard_map/ppermute | solution.py:27
  90.1 1.3 %fusion.11 = f32[10,8]{0,1:T(8,128)S(1)} fusion(bf16[10,4096,1]{1,0,2:T(8,128)(2,1)S(1)} %reshape.276, bf16[10,8,4224]{2,0,1:T(8,128)(2,1)S(1)} %copy_select_fusion, f32[10,10]{0,1:T(8,128)S(1)} %fusion.50), kind=kOutput, calls=%fused_computation.27 | convolution fusion | flops 6555120 | bytes 1188160 | tf_op jit(solution)/shard_map/dot_general | solution.py:209
  92.0 1.0 %fusion.3.nl_ref = f32[16,32,128]{2,1,0:T(8,128)} fusion(bf16[320,128,1]{1,0,2:T(8,128)(2,1)S(1)} %reshape.278, s32[16,32]{1,0:T(8,128)S(1)} %multiply_add_fusion, s32[320]{0:T(512)S(1)} %eq.119), kind=kOutput, calls=%fused_computation.13 | convolution fusion | flops 42106880 | bytes 347392 | tf_op jit(solution)/shard_map/dot_general | solution.py:219
  95.8 3.4 %shard_map.75 = f32[16,32,128]{2,1,0:T(8,128)} custom-call(f32[6,32,128]{2,1,0:T(8,128)} %fusion.32.lo_ref, f32[16,32,128]{2,1,0:T(8,128)} %shard_map.74.v_ref, f32[6,32,128]{2,1,0:T(8,128)} %fusion.30.hi_ref, f32[16,32,128]{2,1,0:T(8,128)} %pot_ref.5, f32[16,32,128]{2,1,0:T(8,128)} %fusion.3.nl_ref, f32[16,32,128]{2,1,0:T(8,128)} %shard_map.73.v_ref.rest_0_), custom_call_target="tpu_custom_call" | custom-call | tf_op jit(solution)/shard_map/pallas_call | solution.py:122
  (79 shorter events, 22.0 us)
Async XLA Ops:
  0.0 20.2 %copy-start = (f32[1,16,32,128]{3,2,1,0:T(8,128)S(1)}, f32[1,16,32,128]{3,2,1,0:T(8,128)}, u32[]{:S(2)}) copy-start(f32[1,16,32,128]{3,2,1,0:T(8,128)} %param.11) | copy-start | bytes 786436
  1.7 16.9 %collective-permute-start = (bf16[1,2,8,4224]{3,2,1,0:T(8,128)(2,1)S(1)}, bf16[1,2,8,4224]{3,2,1,0:T(8,128)(2,1)S(1)}, u32[]{:S(2)}, u32[]{:S(2)}) collective-permute-start(bf16[1,2,8,4224]{3,2,1,0:T(8,128)(2,1)S(1)} %fusion.28), channel_id=1, source_target_pairs={{0,0},{1,16},{2,32},{3,48},{4,64},{5,80},{6,96},{7,112},{8,128},{9... | collective-permute-start | bytes 405512 | tf_op jit(solution)/shard_map/ppermute | solution.py:155
  20.2 9.0 %collective-permute-start.1 = (f32[1,6,32,128]{3,2,1,0:T(8,128)S(1)}, f32[1,6,32,128]{3,2,1,0:T(8,128)S(1)}, u32[]{:S(2)}, u32[]{:S(2)}) collective-permute-start(f32[1,6,32,128]{3,2,1,0:T(8,128)S(1)} %get-tuple-element.31), channel_id=1, source_target_pairs={{0,16},{16,32},{32,48},{48,64},{64,80},{80,96},{96,112},{112,128},... | collective-permute-start | bytes 294920 | tf_op jit(solution)/shard_map/ppermute | solution.py:26
  20.8 13.6 %collective-permute-start.2 = (f32[1,6,32,128]{3,2,1,0:T(8,128)}, f32[1,6,32,128]{3,2,1,0:T(8,128)S(1)}, u32[]{:S(2)}, u32[]{:S(2)}) collective-permute-start(f32[1,6,32,128]{3,2,1,0:T(8,128)} %get-tuple-element.30), channel_id=1, source_target_pairs={{16,0},{32,16},{48,32},{64,48},{80,64},{96,80},{112,96},{128,112},... | collective-permute-start | bytes 294920 | tf_op jit(solution)/shard_map/ppermute | solution.py:27
  25.9 6.5 %collective-permute-start.3 = (bf16[2,8,4224]{2,1,0:T(8,128)(2,1)S(1)}, bf16[2,8,4224]{2,1,0:T(8,128)(2,1)S(1)}, u32[]{:S(2)}, u32[]{:S(2)}) collective-permute-start(bf16[2,8,4224]{2,1,0:T(8,128)(2,1)S(1)} %bitcast.117), channel_id=1, source_target_pairs={{0,8},{1,9},{2,10},{3,11},{4,12},{5,13},{6,14},{7,15},{8,0},{9,1},... | collective-permute-start | bytes 405512 | tf_op jit(solution)/shard_map/ppermute | solution.py:179
  32.5 8.1 %collective-permute-start.4 = (bf16[4,8,4224]{2,1,0:T(8,128)(2,1)S(1)}, bf16[4,8,4224]{2,1,0:T(8,128)(2,1)S(1)}, u32[]{:S(2)}, u32[]{:S(2)}) collective-permute-start(bf16[4,8,4224]{2,1,0:T(8,128)(2,1)S(1)} %pad_maximum_fusion.2), channel_id=1, source_target_pairs={{0,2},{1,3},{2,0},{3,1},{4,6},{5,7},{6,4},{7,5},{8,10},{9,11},{10,... | collective-permute-start | bytes 811016 | tf_op jit(solution)/shard_map/ppermute | solution.py:179
  40.6 14.2 %collective-permute-start.5 = (bf16[8,8,4224]{2,1,0:T(8,128)(2,1)S(1)}, bf16[8,8,4224]{2,1,0:T(8,128)(2,1)S(1)}, u32[]{:S(2)}, u32[]{:S(2)}) collective-permute-start(bf16[8,8,4224]{2,1,0:T(8,128)(2,1)S(1)} %pad_maximum_fusion.1), channel_id=1, source_target_pairs={{0,6},{1,7},{2,4},{3,5},{4,2},{5,3},{6,0},{7,1},{8,14},{9,15},{10,... | collective-permute-start | bytes 1622024 | tf_op jit(solution)/shard_map/ppermute | solution.py:179
  54.9 2.8 %collective-permute-start.6 = (bf16[16,8,4224]{2,1,0:T(8,128)(2,1)S(1)}, bf16[16,8,4224]{2,1,0:T(8,128)(2,1)S(1)}, u32[]{:S(2)}, u32[]{:S(2)}) collective-permute-start(bf16[16,8,4224]{2,1,0:T(8,128)(2,1)S(1)} %pad_maximum_fusion), channel_id=1, source_target_pairs={{0,1},{1,0},{2,3},{3,2},{4,5},{5,4},{6,7},{7,6},{8,9},{9,8},{10,11... | collective-permute-start | bytes 3244040 | tf_op jit(solution)/shard_map/ppermute | solution.py:179
  67.0 9.0 %collective-permute-start.7 = (f32[1,6,32,128]{3,2,1,0:T(8,128)S(1)}, f32[1,6,32,128]{3,2,1,0:T(8,128)S(1)}, u32[]{:S(2)}, u32[]{:S(2)}) collective-permute-start(f32[1,6,32,128]{3,2,1,0:T(8,128)S(1)} %get-tuple-element.29), channel_id=1, source_target_pairs={{0,16},{16,32},{32,48},{48,64},{64,80},{80,96},{96,112},{112,128},... | collective-permute-start | bytes 294920 | tf_op jit(solution)/shard_map/ppermute | solution.py:26
  67.1 9.6 %collective-permute-start.8 = (f32[1,6,32,128]{3,2,1,0:T(8,128)S(1)}, f32[1,6,32,128]{3,2,1,0:T(8,128)S(1)}, u32[]{:S(2)}, u32[]{:S(2)}) collective-permute-start(f32[1,6,32,128]{3,2,1,0:T(8,128)S(1)} %get-tuple-element.28), channel_id=1, source_target_pairs={{16,0},{32,16},{48,32},{64,48},{80,64},{96,80},{112,96},{128,112},... | collective-permute-start | bytes 294920 | tf_op jit(solution)/shard_map/ppermute | solution.py:27
  84.1 9.0 %collective-permute-start.9 = (f32[1,6,32,128]{3,2,1,0:T(8,128)S(1)}, f32[1,6,32,128]{3,2,1,0:T(8,128)S(1)}, u32[]{:S(2)}, u32[]{:S(2)}) collective-permute-start(f32[1,6,32,128]{3,2,1,0:T(8,128)S(1)} %get-tuple-element.27), channel_id=1, source_target_pairs={{0,16},{16,32},{32,48},{48,64},{64,80},{80,96},{96,112},{112,128},... | collective-permute-start | bytes 294920 | tf_op jit(solution)/shard_map/ppermute | solution.py:26
  84.2 9.6 %collective-permute-start.10 = (f32[1,6,32,128]{3,2,1,0:T(8,128)S(1)}, f32[1,6,32,128]{3,2,1,0:T(8,128)S(1)}, u32[]{:S(2)}, u32[]{:S(2)}) collective-permute-start(f32[1,6,32,128]{3,2,1,0:T(8,128)S(1)} %get-tuple-element.26), channel_id=1, source_target_pairs={{16,0},{32,16},{48,32},{64,48},{80,64},{96,80},{112,96},{128,112},... | collective-permute-start | bytes 294920 | tf_op jit(solution)/shard_map/ppermute | solution.py:27

commit v6 on v4

--- a/solution.py
+++ b/solution.py
@@ -80,19 +80,47 @@
     return summed + MIXED_WEIGHT * cross_term
 
 
-def make_kernel(scale, with_prev):
-    sw = second_table(RADIUS); fw = first_table(RADIUS)
-    def kernel(lo_ref, v_ref, hi_ref, pot_ref, nl_ref, *rest):
+def make_kernel(scale, with_prev, home_count, proj_count, block_rows):
+    sw = second_table(RADIUS)
+    fw = first_table(RADIUS)
+
+    def kernel(shift_ref, lo_ref, v_ref, hi_ref, pot_ref, pick_ref, place_ref, proj_ref, gain_ref, *rest):
         if with_prev:
-            prev_ref, out_ref, pad_ref = rest
+            prev_ref, out_ref, pad_ref, rows_ref = rest
         else:
-            out_ref, pad_ref = rest
+            out_ref, pad_ref, rows_ref = rest
         planes, breadth, depth = v_ref.shape
         v = v_ref[...]
-        pad_ref[0:RADIUS] = lo_ref[...]
+        pad_ref[0:RADIUS] = pltpu.roll(lo_ref[...], shift_ref[0], 1)
         pad_ref[RADIUS:RADIUS + planes] = v
-        pad_ref[RADIUS + planes:] = hi_ref[...]
-        lane = jax.lax.broadcasted_iota(jnp.int32, v.shape, 2)
+        pad_ref[RADIUS + planes:] = pltpu.roll(hi_ref[...], shift_ref[1], 1)
+
+        lines = v.reshape(planes * breadth, depth).astype(jnp.bfloat16)
+        picked = jnp.dot(pick_ref[...], lines, preferred_element_type=jnp.float32)
+
+        def one_atom(a, carry):
+            base = pl.multiple_of(a * block_rows, block_rows)
+            here = picked_ref_load(base)
+            acc = jnp.zeros((block_rows, depth), jnp.float32)
+            for j in range(proj_count):
+                proj = proj_ref[a * proj_count + j].astype(jnp.float32)
+                coef = jnp.sum(jnp.sum(proj * here, axis=0, keepdims=True), axis=1, keepdims=True)
+                gain = gain_ref[a * proj_count + j]
+                scaled = (coef * gain).astype(jnp.bfloat16).astype(jnp.float32)
+                acc = acc + proj * scaled
+            rows_ref[pl.ds(base, block_rows), :] = acc.astype(jnp.bfloat16)
+            return carry
+
+        rows_ref[...] = picked.astype(jnp.bfloat16)
+
+        def picked_ref_load(base):
+            return rows_ref[pl.ds(base, block_rows), :].astype(jnp.float32)
+
+        lax.fori_loop(0, home_count, one_atom, 0)
+        nonlocal_lines = jnp.dot(place_ref[...], rows_ref[...], preferred_element_type=jnp.float32)
+        nonlocal_lines = nonlocal_lines.reshape(planes, breadth, depth)
+
+        lane = lax.broadcasted_iota(jnp.int32, v.shape, 2)
         summed = (3.0 * sw[0]) * v
         for k in range(1, RADIUS + 1):
             xs = pad_ref[RADIUS + k:RADIUS + k + planes] + pad_ref[RADIUS - k:RADIUS - k + planes]
@@ -108,22 +136,35 @@
         for k in range(2, RADIUS + 1):
             cross = cross + fw[k] * (slope[RADIUS + k:RADIUS + k + planes] - slope[RADIUS - k:RADIUS - k + planes])
         lap = summed + 0.7 * cross
-        hv = -0.5 * lap + pot_ref[...] * v + nl_ref[...]
+        hv = -0.5 * lap + pot_ref[...] * v + nonlocal_lines
         kv = (hv - 12.0 * v) / 8.0
         if with_prev:
             out_ref[...] = scale * kv - prev_ref[...]
         else:
             out_ref[...] = kv
+
     return kernel
 
-def apply_op(lo, v, hi, pot, nl, prev=None, scale=1.0):
+
+def apply_op(shifts, lo, v, hi, pot, pick, place, proj, gain, prev=None, scale=1.0):
     planes, breadth, depth = v.shape
-    args = [lo, v, hi, pot, nl] + ([prev] if prev is not None else [])
+    picked_rows = pick.shape[0]
+    home_count = proj.shape[0] // 8
+    block_rows = picked_rows // home_count
+    args = [shifts, lo, v, hi, pot, pick, place, proj, gain] + ([prev] if prev is not None else [])
+    vspec = pl.BlockSpec(memory_space=pltpu.VMEM)
+    in_specs = [pl.BlockSpec(memory_space=pltpu.SMEM)] + [vspec] * (len(args) - 1)
     return pl.pallas_call(
-        make_kernel(scale, prev is not None),
+        make_kernel(scale, prev is not None, home_count, proj.shape[0] // home_count, block_rows),
         out_shape=jax.ShapeDtypeStruct(v.shape, jnp.float32),
-        scratch_shapes=[pltpu.VMEM((planes + 2 * RADIUS, breadth, depth), jnp.float32)],
+        in_specs=in_specs,
+        out_specs=vspec,
+        scratch_shapes=[
+            pltpu.VMEM((planes + 2 * RADIUS, breadth, depth), jnp.float32),
+            pltpu.VMEM((picked_rows, depth), jnp.bfloat16),
+        ],
     )(*args)
+
 
 def shards(states_in, potential, projectors, proj_gains, atom_owner, atom_rows, wrap_rows):
     state_count, tile_width, breadth, line_depth = states_in.shape
@@ -186,45 +227,32 @@
     atom_pack = jnp.take(gathered, atom_slot, axis=0)
     proj_rows = atom_pack[:, :, :line_span].reshape(home_count * proj_count, line_span)
     atom_gain = atom_pack[:, :, line_span].astype(jnp.float32)
-    selector = (
+    pick = (
         local_rows.reshape(-1)[:, None] == jnp.arange(tile_lines, dtype=jnp.int32)[None, :]
     ).astype(jnp.bfloat16)
-    atom_eye = jnp.eye(home_count, dtype=jnp.float32)
-
-    def rims(grid_field):
-        padded = padded_2(grid_field, (("grid", 1),), RADIUS)
-        low_rim = padded[:, :RADIUS]
-        high_rim = padded[:, RADIUS + tile_width :]
-        low_rim = jnp.where(tile_index == 0, jnp.take(low_rim, wrap_rows, axis=2), low_rim)
-        high_rim = jnp.where(
-            tile_index == n_grid - 1, jnp.take(high_rim, unwrap_rows, axis=2), high_rim
-        )
-        return low_rim[0], high_rim[0]
-
-    def nonlocal_part(grid_field):
-        lines_here = grid_field.reshape(tile_lines, line_depth).astype(jnp.bfloat16)
-        picked = jnp.dot(selector, lines_here, preferred_element_type=jnp.float32)
-        picked = picked.astype(jnp.bfloat16).reshape(home_count, line_span)
-        every_pair = lax.dot_general(
-            proj_rows, picked, (((1,), (1,)), ((), ())), preferred_element_type=jnp.float32
-        ).reshape(home_count, proj_count, home_count)
-        coefficients = jnp.sum(every_pair * atom_eye[:, None, :], axis=2)
-        scaled = (coefficients * atom_gain).astype(jnp.bfloat16)
-        block_scaled = (atom_eye.astype(jnp.bfloat16)[:, :, None] * scaled[None, :, :]).reshape(
-            home_count, home_count * proj_count
-        )
-        projected = jnp.dot(block_scaled, proj_rows, preferred_element_type=jnp.float32)
-        projected = projected.astype(jnp.bfloat16).reshape(home_count * block_rows, line_depth)
-        summed = lax.dot_general(
-            selector, projected, (((0,), (0,)), ((), ())), preferred_element_type=jnp.float32
-        )
-        return summed.reshape(state_count, tile_width, breadth, line_depth)
+    place = pick.T
+    proj_in = proj_rows.reshape(home_count * proj_count, breadth, line_depth)
+    gain_in = jnp.broadcast_to(
+        atom_gain.reshape(home_count * proj_count, 1, 1), (home_count * proj_count, 1, line_depth)
+    )
+    skew = wrap_rows[0]
+    shifts = jnp.stack(
+        [
+            jnp.where(tile_index == 0, (breadth - skew) % breadth, 0),
+            jnp.where(tile_index == n_grid - 1, skew, 0),
+            jnp.zeros((), jnp.int32),
+            jnp.zeros((), jnp.int32),
+        ]
+    ).astype(jnp.int32)
+    up = [(i, (i + 1) % n_grid) for i in range(n_grid)]
+    down = [(j, i) for i, j in up]
 
     def step(grid_field, prev=None, scale=1.0):
-        low_rim, high_rim = rims(grid_field)
-        nonlocal_lines = nonlocal_part(grid_field)[0]
+        field = grid_field[0]
+        low_rim = lax.ppermute(field[tile_width - RADIUS :], "grid", up)
+        high_rim = lax.ppermute(field[:RADIUS], "grid", down)
         out = apply_op(
-            low_rim, grid_field[0], high_rim, potential, nonlocal_lines, prev, scale
+            shifts, low_rim, field, high_rim, potential, pick, place, proj_in, gain_in, prev, scale
         )
         return out[None]
 

time: 95.4 us -> 94.6 us (level)
  matrix products: 9.33 us -> 0 us
  Pallas kernels: 10.1 us -> 16.6 us
  waiting for transfers between devices: 27.4 us -> 33.7 us
  other arithmetic: 11.7 us -> 6.73 us
  between operations: 0.53 us -> 1.49 us
    dot_general x12 -> x0, matrix products: 9.33 us -> none  [the longest x3 4.03 us: nonlocal_part(): lax.dot_general(proj_rows, picked, (((1,), (1,)), ((), ())), preferred_el...]
    pallas_call x3, Pallas kernels: 10.1 us -> 16.6 us  [apply_op(): pl.pallas_call(make_kernel(scale, prev is not None, home_count, proj.shap...]
    ppermute x6, waiting for transfers between devices: 0.02 us -> 5.61 us  [the longest x3 5.6 us: step(): low_rim = lax.ppermute(field[tile_width - RADIUS:], 'grid', up)]
    unnamed x8 -> x19, local copies, waits for them, and re-layouts: 0.11 us -> 4.47 us
    squeeze x6 -> x0, other arithmetic: 4.29 us -> none  [rims(): return (low_rim[0], high_rim[0])]
    gather x6 -> x0, local copies, waits for them, and re-layouts: 3.51 us -> none  [the longest x3 1.76 us: rims(): jnp.take(high_rim, unwrap_rows, axis=2)]
    convert_element_type x8 -> x2, other arithmetic: 2.94 us -> 1.71 us  [shards(): pick = (local_rows.reshape(-1)[:, None] == jnp.arange(tile_lines, dtype=j...]
    another operation x7 -> x1, local copies, waits for them, and re-layouts: 1.13 us -> 0.01 us
  transfers between devices with their start and end apart: 11 -> 11, of which waited for: 5 -> 7; matrix products, arithmetic and copies ran while one was open for 18% -> 10% of each run, Pallas kernels for 0% -> 0%
where the time goes in v6:
time: 94.6 us; the launch traced here: 94.2 us
  waiting for transfers between devices  33.7 us (36%)
  starting transfers between devices  26.6 us (28%)
  Pallas kernels  16.6 us (18%)
  local copies, waits for them, and re-layouts  9.11 us (10%)
  other arithmetic  6.73 us (7%)
  between operations  1.49 us (2%)
    ppermute x4, waiting for transfers between devices, shards(): lax.ppermute(gathered, 'states', [(s, exchange(s)) for s in range(n_state...  21.8 us
    ppermute x3, starting transfers between devices, step(): high_rim = lax.ppermute(field[:RADIUS], 'grid', down)  20.1 us
    pallas_call x3, Pallas kernels, apply_op(): pl.pallas_call(make_kernel(scale, prev is not None, home_count, proj.shap...  16.6 us
    ppermute x1, waiting for transfers between devices, shards(): packed = lax.ppermute(packed, ('grid', 'states'), pairs)  6.31 us
    ppermute x3, waiting for transfers between devices, step(): low_rim = lax.ppermute(field[tile_width - RADIUS:], 'grid', up)  5.6 us
    unnamed x19, local copies, waits for them, and re-layouts  4.47 us
    slice x3, local copies, waits for them, and re-layouts, step(): high_rim = lax.ppermute(field[:RADIUS], 'grid', down)  2.86 us
    ppermute x4, starting transfers between devices, shards(): lax.ppermute(gathered, 'states', [(s, exchange(s)) for s in range(n_state...  2.42 us
  transfers between devices with their start and end apart: 11, of which 7 were waited for; matrix products, arithmetic and copies ran while one was open for 10% of the time, Pallas kernels for 0%

profile of v6, /device:TPU:6, one launch (start us, length us, event | category | flops | bytes accessed | tf_op | source)
XLA Modules:
  0.0 94.2 jit_solution(11611401076442176315)
XLA Ops:
  0.0 1.0 %slice_bitcast_fusion.1 = (f32[6,32,128]{2,1,0:T(8,128)S(1)}, f32[6,32,128]{2,1,0:T(8,128)S(1)}) fusion(f32[1,16,32,128]{3,2,1,0:T(8,128)} %param.9), kind=kLoop, calls=%fused_computation.13 | loop fusion | bytes 393216 | tf_op jit(solution)/shard_map/slice | solution.py:253
  1.0 2.0 %collective-permute-start = (f32[6,32,128]{2,1,0:T(8,128)S(1)}, f32[6,32,128]{2,1,0:T(8,128)S(1)}, u32[]{:S(2)}, u32[]{:S(2)}) collective-permute-start(f32[6,32,128]{2,1,0:T(8,128)S(1)} %get-tuple-element.26), channel_id=1, source_target_pairs={{0,16},{16,32},{32,48},{48,64},{64,80},{80,96},{96,112},{112,128},... | collective-permute-start | bytes 294920 | tf_op jit(solution)/shard_map/ppermute | solution.py:252
  3.0 6.7 %collective-permute-start.1 = (f32[6,32,128]{2,1,0:T(8,128)S(1)}, f32[6,32,128]{2,1,0:T(8,128)S(1)}, u32[]{:S(2)}, u32[]{:S(2)}) collective-permute-start(f32[6,32,128]{2,1,0:T(8,128)S(1)} %get-tuple-element.25), channel_id=1, source_target_pairs={{16,0},{32,16},{48,32},{64,48},{80,64},{96,80},{112,96},{128,112},... | collective-permute-start | bytes 294920 | tf_op jit(solution)/shard_map/ppermute | solution.py:253
  10.4 0.9 fusion.3
  11.3 1.9 %collective-permute-start.2 = (bf16[1,2,8,4224]{3,2,1,0:T(8,128)(2,1)S(1)}, bf16[1,2,8,4224]{3,2,1,0:T(8,128)(2,1)S(1)}, u32[]{:S(2)}, u32[]{:S(2)}) collective-permute-start(bf16[1,2,8,4224]{3,2,1,0:T(8,128)(2,1)S(1)} %fusion.3), channel_id=1, source_target_pairs={{0,0},{1,16},{2,32},{3,48},{4,64},{5,80},{6,96},{7,112},{8,128},{9... | collective-permute-start | bytes 405512 | tf_op jit(solution)/shard_map/ppermute | solution.py:196
  14.7 0.9 fusion.1.pick_ref
  17.0 0.9 convert_reduce_fusion.1
  18.0 1.4 %iota_reduce_fusion = (pred[10]{0:T(512)(128)(4,1)}, s32[10]{0:T(128)S(1)}) fusion(s32[16]{0:T(128)S(1)} %stack.79, s32[10]{0:T(128)} %param.13), kind=kLoop, calls=%fused_computation.23 | loop fusion | flops 1210 | bytes 154 | tf_op jit(solution)/shard_map/shards/reduce | solution.py:224
  19.4 6.3 %collective-permute-done.2 = bf16[1,2,8,4224]{3,2,1,0:T(8,128)(2,1)S(1)} collective-permute-done((bf16[1,2,8,4224]{3,2,1,0:T(8,128)(2,1)S(1)}, bf16[1,2,8,4224]{3,2,1,0:T(8,128)(2,1)S(1)}, u32[]{:S(2)}, u32[]{:S(2)}) %collective-permute-start.2) | collective-permute-done | bytes 135200 | tf_op jit(solution)/shard_map/ppermute | solution.py:196
  25.7 1.6 %collective-permute-start.3 = (bf16[2,8,4224]{2,1,0:T(8,128)(2,1)S(1)}, bf16[2,8,4224]{2,1,0:T(8,128)(2,1)S(1)}, u32[]{:S(2)}, u32[]{:S(2)}) collective-permute-start(bf16[2,8,4224]{2,1,0:T(8,128)(2,1)S(1)} %bitcast.36), channel_id=1, source_target_pairs={{0,8},{1,9},{2,10},{3,11},{4,12},{5,13},{6,14},{7,15},{8,0},{9,1},... | collective-permute-start | bytes 405512 | tf_op jit(solution)/shard_map/ppermute | solution.py:219
  28.0 2.8 %collective-permute-done.3 = bf16[2,8,4224]{2,1,0:T(8,128)(2,1)S(1)} collective-permute-done((bf16[2,8,4224]{2,1,0:T(8,128)(2,1)S(1)}, bf16[2,8,4224]{2,1,0:T(8,128)(2,1)S(1)}, u32[]{:S(2)}, u32[]{:S(2)}) %collective-permute-start.3) | collective-permute-done | bytes 135200 | tf_op jit(solution)/shard_map/ppermute | solution.py:219
  31.4 5.9 %collective-permute-done.4 = bf16[4,8,4224]{2,1,0:T(8,128)(2,1)S(1)} collective-permute-done((bf16[4,8,4224]{2,1,0:T(8,128)(2,1)S(1)}, bf16[4,8,4224]{2,1,0:T(8,128)(2,1)S(1)}, u32[]{:S(2)}, u32[]{:S(2)}) %collective-permute-start.4) | collective-permute-done | bytes 270368 | tf_op jit(solution)/shard_map/ppermute | solution.py:219
  37.5 10.5 %collective-permute-done.5 = bf16[8,8,4224]{2,1,0:T(8,128)(2,1)S(1)} collective-permute-done((bf16[8,8,4224]{2,1,0:T(8,128)(2,1)S(1)}, bf16[8,8,4224]{2,1,0:T(8,128)(2,1)S(1)}, u32[]{:S(2)}, u32[]{:S(2)}) %collective-permute-start.5) | collective-permute-done | bytes 540704 | tf_op jit(solution)/shard_map/ppermute | solution.py:219
  48.4 2.6 %collective-permute-done.6 = bf16[16,8,4224]{2,1,0:T(8,128)(2,1)S(1)} collective-permute-done((bf16[16,8,4224]{2,1,0:T(8,128)(2,1)S(1)}, bf16[16,8,4224]{2,1,0:T(8,128)(2,1)S(1)}, u32[]{:S(2)}, u32[]{:S(2)}) %collective-permute-start.6) | collective-permute-done | bytes 1081376 | tf_op jit(solution)/shard_map/ppermute | solution.py:219
  51.9 1.0 %copy.12 = bf16[10,8,32,128]{3,2,1,0:T(8,128)(2,1)} copy(bf16[10,8,32,128]{3,1,2,0:T(8,128)(2,1)S(1)} %slice_bitcast_fusion) | data formatting | bytes 1310720
  53.9 5.5 %shard_map.73.v_ref.rest_0_ = f32[16,32,128]{2,1,0:T(8,128)} custom-call(s32[4]{0:T(128)} %pad_add_fusion.shift_ref, f32[6,32,128]{2,1,0:T(8,128)} %copy-done.4, f32[16,32,128]{2,1,0:T(8,128)} %bitcast.40, f32[6,32,128]{2,1,0:T(8,128)} %copy-done.5, f32[16,32,128]{2,1,0:T(8,128)} %pot_ref.5, bf16[320,512]{1,0:T(8,128)(2,1)} %fusion.1.pick_ref, ...), custom_call_target="tpu_custom_call" | custom-call | tf_op jit(solution)/shard_map/pallas_call | solution.py:157
  59.4 1.0 %fusion.6 = (f32[6,32,128]{2,1,0:T(8,128)S(1)}, f32[6,32,128]{2,1,0:T(8,128)S(1)}) fusion(f32[16,32,128]{2,1,0:T(8,128)} %shard_map.73.v_ref.rest_0_), kind=kLoop, calls=%fused_computation.31 | loop fusion | bytes 393216 | tf_op jit(solution)/shard_map/slice | solution.py:253
  60.4 7.8 %collective-permute-start.8 = (f32[6,32,128]{2,1,0:T(8,128)S(1)}, f32[6,32,128]{2,1,0:T(8,128)S(1)}, u32[]{:S(2)}, u32[]{:S(2)}) collective-permute-start(f32[6,32,128]{2,1,0:T(8,128)S(1)} %get-tuple-element.23), channel_id=1, source_target_pairs={{16,0},{32,16},{48,32},{64,48},{80,64},{96,80},{112,96},{128,112},... | collective-permute-start | bytes 294920 | tf_op jit(solution)/shard_map/ppermute | solution.py:253
  68.2 3.0 %collective-permute-done.7.lo_ref = f32[6,32,128]{2,1,0:T(8,128)S(1)} collective-permute-done((f32[6,32,128]{2,1,0:T(8,128)S(1)}, f32[6,32,128]{2,1,0:T(8,128)S(1)}, u32[]{:S(2)}, u32[]{:S(2)}) %collective-permute-start.7) | collective-permute-done | bytes 98336 | tf_op jit(solution)/shard_map/ppermute | solution.py:252
  72.5 5.6 %shard_map.74.v_ref = f32[16,32,128]{2,1,0:T(8,128)} custom-call(s32[4]{0:T(128)} %pad_add_fusion.shift_ref, f32[6,32,128]{2,1,0:T(8,128)} %copy-done.2, f32[16,32,128]{2,1,0:T(8,128)} %shard_map.73.v_ref.rest_0_, f32[6,32,128]{2,1,0:T(8,128)} %copy-done.3, f32[16,32,128]{2,1,0:T(8,128)} %pot_ref.5, bf16[320,512]{1,0:T(8,128)(2,1)} %fusion.1.pick_ref, ...), custom_call_target="tpu_custom_call" | custom-call | tf_op jit(solution)/shard_map/pallas_call | solution.py:157
  78.1 1.0 %fusion.5 = (f32[6,32,128]{2,1,0:T(8,128)S(1)}, f32[6,32,128]{2,1,0:T(8,128)S(1)}) fusion(f32[16,32,128]{2,1,0:T(8,128)} %shard_map.74.v_ref), kind=kLoop, calls=%fused_computation.30 | loop fusion | bytes 393216 | tf_op jit(solution)/shard_map/slice | solution.py:253
  79.2 5.6 %collective-permute-start.10 = (f32[6,32,128]{2,1,0:T(8,128)S(1)}, f32[6,32,128]{2,1,0:T(8,128)S(1)}, u32[]{:S(2)}, u32[]{:S(2)}) collective-permute-start(f32[6,32,128]{2,1,0:T(8,128)S(1)} %get-tuple-element.21), channel_id=1, source_target_pairs={{16,0},{32,16},{48,32},{64,48},{80,64},{96,80},{112,96},{128,112},... | collective-permute-start | bytes 294920 | tf_op jit(solution)/shard_map/ppermute | solution.py:253
  84.8 2.6 %collective-permute-done.9.lo_ref = f32[6,32,128]{2,1,0:T(8,128)S(1)} collective-permute-done((f32[6,32,128]{2,1,0:T(8,128)S(1)}, f32[6,32,128]{2,1,0:T(8,128)S(1)}, u32[]{:S(2)}, u32[]{:S(2)}) %collective-permute-start.9) | collective-permute-done | bytes 98336 | tf_op jit(solution)/shard_map/ppermute | solution.py:252
  88.7 5.6 %shard_map.75 = f32[16,32,128]{2,1,0:T(8,128)} custom-call(s32[4]{0:T(128)} %pad_add_fusion.shift_ref, f32[6,32,128]{2,1,0:T(8,128)} %copy-done, f32[16,32,128]{2,1,0:T(8,128)} %shard_map.74.v_ref, f32[6,32,128]{2,1,0:T(8,128)} %copy-done.1, f32[16,32,128]{2,1,0:T(8,128)} %pot_ref.5, bf16[320,512]{1,0:T(8,128)(2,1)} %fusion.1.pick_ref, ...), custom_call_target="tpu_custom_call" | custom-call | tf_op jit(solution)/shard_map/pallas_call | solution.py:157
  (44 shorter events, 9.0 us)
Async XLA Ops:
  1.0 52.1 %collective-permute-start = (f32[6,32,128]{2,1,0:T(8,128)S(1)}, f32[6,32,128]{2,1,0:T(8,128)S(1)}, u32[]{:S(2)}, u32[]{:S(2)}) collective-permute-start(f32[6,32,128]{2,1,0:T(8,128)S(1)} %get-tuple-element.26), channel_id=1, source_target_pairs={{0,16},{16,32},{32,48},{48,64},{64,80},{80,96},{96,112},{112,128},... | collective-permute-start | bytes 294920 | tf_op jit(solution)/shard_map/ppermute | solution.py:252
  3.0 50.2 %collective-permute-start.1 = (f32[6,32,128]{2,1,0:T(8,128)S(1)}, f32[6,32,128]{2,1,0:T(8,128)S(1)}, u32[]{:S(2)}, u32[]{:S(2)}) collective-permute-start(f32[6,32,128]{2,1,0:T(8,128)S(1)} %get-tuple-element.25), channel_id=1, source_target_pairs={{16,0},{32,16},{48,32},{64,48},{80,64},{96,80},{112,96},{128,112},... | collective-permute-start | bytes 294920 | tf_op jit(solution)/shard_map/ppermute | solution.py:253
  11.3 14.4 %collective-permute-start.2 = (bf16[1,2,8,4224]{3,2,1,0:T(8,128)(2,1)S(1)}, bf16[1,2,8,4224]{3,2,1,0:T(8,128)(2,1)S(1)}, u32[]{:S(2)}, u32[]{:S(2)}) collective-permute-start(bf16[1,2,8,4224]{3,2,1,0:T(8,128)(2,1)S(1)} %fusion.3), channel_id=1, source_target_pairs={{0,0},{1,16},{2,32},{3,48},{4,64},{5,80},{6,96},{7,112},{8,128},{9... | collective-permute-start | bytes 405512 | tf_op jit(solution)/shard_map/ppermute | solution.py:196
  25.7 5.0 %collective-permute-start.3 = (bf16[2,8,4224]{2,1,0:T(8,128)(2,1)S(1)}, bf16[2,8,4224]{2,1,0:T(8,128)(2,1)S(1)}, u32[]{:S(2)}, u32[]{:S(2)}) collective-permute-start(bf16[2,8,4224]{2,1,0:T(8,128)(2,1)S(1)} %bitcast.36), channel_id=1, source_target_pairs={{0,8},{1,9},{2,10},{3,11},{4,12},{5,13},{6,14},{7,15},{8,0},{9,1},... | collective-permute-start | bytes 405512 | tf_op jit(solution)/shard_map/ppermute | solution.py:219
  30.8 6.5 %collective-permute-start.4 = (bf16[4,8,4224]{2,1,0:T(8,128)(2,1)S(1)}, bf16[4,8,4224]{2,1,0:T(8,128)(2,1)S(1)}, u32[]{:S(2)}, u32[]{:S(2)}) collective-permute-start(bf16[4,8,4224]{2,1,0:T(8,128)(2,1)S(1)} %pad_maximum_fusion.2), channel_id=1, source_target_pairs={{0,2},{1,3},{2,0},{3,1},{4,6},{5,7},{6,4},{7,5},{8,10},{9,11},{10,... | collective-permute-start | bytes 811016 | tf_op jit(solution)/shard_map/ppermute | solution.py:219
  37.4 10.7 %collective-permute-start.5 = (bf16[8,8,4224]{2,1,0:T(8,128)(2,1)S(1)}, bf16[8,8,4224]{2,1,0:T(8,128)(2,1)S(1)}, u32[]{:S(2)}, u32[]{:S(2)}) collective-permute-start(bf16[8,8,4224]{2,1,0:T(8,128)(2,1)S(1)} %pad_maximum_fusion.1), channel_id=1, source_target_pairs={{0,6},{1,7},{2,4},{3,5},{4,2},{5,3},{6,0},{7,1},{8,14},{9,15},{10,... | collective-permute-start | bytes 1622024 | tf_op jit(solution)/shard_map/ppermute | solution.py:219
  48.2 2.8 %collective-permute-start.6 = (bf16[16,8,4224]{2,1,0:T(8,128)(2,1)S(1)}, bf16[16,8,4224]{2,1,0:T(8,128)(2,1)S(1)}, u32[]{:S(2)}, u32[]{:S(2)}) collective-permute-start(bf16[16,8,4224]{2,1,0:T(8,128)(2,1)S(1)} %pad_maximum_fusion), channel_id=1, source_target_pairs={{0,1},{1,0},{2,3},{3,2},{4,5},{5,4},{6,7},{7,6},{8,9},{9,8},{10,11... | collective-permute-start | bytes 3244040 | tf_op jit(solution)/shard_map/ppermute | solution.py:219
  53.1 0.8 copy-start.4
  53.1 0.8 copy-start.5
  60.3 10.9 %collective-permute-start.7 = (f32[6,32,128]{2,1,0:T(8,128)S(1)}, f32[6,32,128]{2,1,0:T(8,128)S(1)}, u32[]{:S(2)}, u32[]{:S(2)}) collective-permute-start(f32[6,32,128]{2,1,0:T(8,128)S(1)} %get-tuple-element.24), channel_id=1, source_target_pairs={{0,16},{16,32},{32,48},{48,64},{64,80},{80,96},{96,112},{112,128},... | collective-permute-start | bytes 294920 | tf_op jit(solution)/shard_map/ppermute | solution.py:252
  60.4 10.8 %collective-permute-start.8 = (f32[6,32,128]{2,1,0:T(8,128)S(1)}, f32[6,32,128]{2,1,0:T(8,128)S(1)}, u32[]{:S(2)}, u32[]{:S(2)}) collective-permute-start(f32[6,32,128]{2,1,0:T(8,128)S(1)} %get-tuple-element.23), channel_id=1, source_target_pairs={{16,0},{32,16},{48,32},{64,48},{80,64},{96,80},{112,96},{128,112},... | collective-permute-start | bytes 294920 | tf_op jit(solution)/shard_map/ppermute | solution.py:253
  71.3 0.6 copy-start.2
  71.9 0.7 copy-start.3
  79.1 8.3 %collective-permute-start.9 = (f32[6,32,128]{2,1,0:T(8,128)S(1)}, f32[6,32,128]{2,1,0:T(8,128)S(1)}, u32[]{:S(2)}, u32[]{:S(2)}) collective-permute-start(f32[6,32,128]{2,1,0:T(8,128)S(1)} %get-tuple-element.22), channel_id=1, source_target_pairs={{0,16},{16,32},{32,48},{48,64},{64,80},{80,96},{96,112},{112,128},... | collective-permute-start | bytes 294920 | tf_op jit(solution)/shard_map/ppermute | solution.py:252
  79.2 8.2 %collective-permute-start.10 = (f32[6,32,128]{2,1,0:T(8,128)S(1)}, f32[6,32,128]{2,1,0:T(8,128)S(1)}, u32[]{:S(2)}, u32[]{:S(2)}) collective-permute-start(f32[6,32,128]{2,1,0:T(8,128)S(1)} %get-tuple-element.21), channel_id=1, source_target_pairs={{16,0},{32,16},{48,32},{64,48},{80,64},{96,80},{112,96},{128,112},... | collective-permute-start | bytes 294920 | tf_op jit(solution)/shard_map/ppermute | solution.py:253
  87.4 0.7 copy-start
  88.0 0.7 copy-start.1

commit v7 on v6

--- a/solution.py
+++ b/solution.py
@@ -194,36 +194,13 @@
     packed = jnp.concatenate([projectors, gain_lanes], axis=3)
     pairs = [(o * n_states + t, t * n_states + o) for o in range(n_grid) for t in range(n_states)]
     packed = lax.ppermute(packed, ("grid", "states"), pairs)
-    def flip_y(s):
-        return s ^ 8
-
-    def flip_x(s):
-        return s ^ 2
-
-    def mirror_x(s):
-        x = (s // 2) % 4
-        return s + (3 - x - x) * 2
-
-    def flip_core(s):
-        return s ^ 1
-
-    exchanges = (flip_y, flip_x, mirror_x, flip_core)
-
-    def origins(me, done):
-        if not done:
-            return [me]
-        return origins(me, done[:-1]) + origins(done[-1](me), done[:-1])
-
-    gathered = packed[0]
-    for exchange in exchanges:
-        partner = lax.ppermute(
-            gathered, "states", [(s, exchange(s)) for s in range(n_states)]
-        )
-        gathered = jnp.concatenate([gathered, partner], axis=0)
-    block_owner = jnp.stack(origins(lax.axis_index("states"), exchanges))
-    owner_block = jnp.argmax(block_owner[None, :] == atom_owner[:, None], axis=1)
+    me = lax.axis_index("states")
+    blocks = [packed[0]]
+    for d in range(1, n_states):
+        blocks.append(lax.ppermute(packed[0], "states", [(s, s ^ d) for s in range(n_states)]))
+    gathered = jnp.concatenate(blocks, axis=0)
     gathered = gathered.reshape(n_states * slot_pairs, proj_count, line_span + 128)
-    atom_slot = owner_block * PAIR_CAP + owner_rank
+    atom_slot = (atom_owner ^ me) * PAIR_CAP + owner_rank
     atom_pack = jnp.take(gathered, atom_slot, axis=0)
     proj_rows = atom_pack[:, :, :line_span].reshape(home_count * proj_count, line_span)
     atom_gain = atom_pack[:, :, line_span].astype(jnp.float32)

time: 94.6 us -> 109 us (1.15); the launches traced: 94.2 us -> 107 us
  starting transfers between devices: 26.6 us -> 51 us
  waiting for transfers between devices: 33.7 us -> 23.6 us
    ppermute x4 -> x15, starting transfers between devices: 2.42 us -> 25.7 us  [shards(): lax.ppermute(packed[0], 'states', [(s, s ^ d) for s in range(n_states)])]
    ppermute x1, waiting for transfers between devices: 6.31 us -> 0.01 us  [shards(): packed = lax.ppermute(packed, ('grid', 'states'), pairs)]
    ppermute x1, starting transfers between devices: 1.92 us -> 8.12 us  [shards(): packed = lax.ppermute(packed, ('grid', 'states'), pairs)]
    ppermute x3, starting transfers between devices: 20.1 us -> 15.8 us  [step(): high_rim = lax.ppermute(field[:RADIUS], 'grid', down)]
    ppermute x4 -> x15, waiting for transfers between devices: 21.8 us -> 18.2 us  [shards(): lax.ppermute(packed[0], 'states', [(s, s ^ d) for s in range(n_states)])]
    another operation x1 -> x0, other arithmetic: 1.37 us -> none  [shards(): jnp.argmax(block_owner[None, :] == atom_owner[:, None], axis=1)]
    unnamed x19 -> x30, local copies, waits for them, and re-layouts: 4.47 us -> 4.55 us
  transfers between devices with their start and end apart: 11 -> 22, of which waited for: 7 -> 12; matrix products, arithmetic and copies ran while one was open for 10% -> 7% of each run, Pallas kernels for 0% -> 0%
where the time goes in v7:
time: 109 us; the launch traced here: 107 us
  starting transfers between devices  51 us (47%)
  waiting for transfers between devices  23.6 us (22%)
  Pallas kernels  16.6 us (15%)
  local copies, waits for them, and re-layouts  8.98 us (8%)
  other arithmetic  5.74 us (5%)
  between operations  1.51 us (1%)
    ppermute x15, starting transfers between devices, shards(): lax.ppermute(packed[0], 'states', [(s, s ^ d) for s in range(n_states)])  25.7 us
    ppermute x15, waiting for transfers between devices, shards(): lax.ppermute(packed[0], 'states', [(s, s ^ d) for s in range(n_states)])  18.2 us
    pallas_call x3, Pallas kernels, apply_op(): pl.pallas_call(make_kernel(scale, prev is not None, home_count, proj.shap...  16.6 us
    ppermute x3, starting transfers between devices, step(): high_rim = lax.ppermute(field[:RADIUS], 'grid', down)  15.8 us
    ppermute x1, starting transfers between devices, shards(): packed = lax.ppermute(packed, ('grid', 'states'), pairs)  8.12 us
    ppermute x3, waiting for transfers between devices, step(): low_rim = lax.ppermute(field[tile_width - RADIUS:], 'grid', up)  5.38 us
    unnamed x30, local copies, waits for them, and re-layouts  4.55 us
    slice x3, local copies, waits for them, and re-layouts, step(): high_rim = lax.ppermute(field[:RADIUS], 'grid', down)  2.86 us
  transfers between devices with their start and end apart: 22, of which 12 were waited for; matrix products, arithmetic and copies ran while one was open for 7% of the time, Pallas kernels for 0%

profile of v7, /device:TPU:6, one launch (start us, length us, event | category | flops | bytes accessed | tf_op | source)
XLA Modules:
  0.0 107.5 jit_solution(2342001291359670922)
XLA Ops:
  1.7 8.1 %collective-permute-start.2 = (bf16[1,2,8,4224]{3,2,1,0:T(8,128)(2,1)S(1)}, bf16[1,2,8,4224]{3,2,1,0:T(8,128)(2,1)S(1)}, u32[]{:S(2)}, u32[]{:S(2)}) collective-permute-start(bf16[1,2,8,4224]{3,2,1,0:T(8,128)(2,1)S(1)} %fusion.3), channel_id=1, source_target_pairs={{0,0},{1,16},{2,32},{3,48},{4,64},{5,80},{6,96},{7,112},{8,128},{9... | collective-permute-start | bytes 405512 | tf_op jit(solution)/shard_map/ppermute | solution.py:196
  11.7 4.7 %collective-permute-start.1 = (f32[6,32,128]{2,1,0:T(8,128)S(1)}, f32[6,32,128]{2,1,0:T(8,128)S(1)}, u32[]{:S(2)}, u32[]{:S(2)}) collective-permute-start(f32[6,32,128]{2,1,0:T(8,128)S(1)} %get-tuple-element.23), channel_id=1, source_target_pairs={{16,0},{32,16},{48,32},{64,48},{80,64},{96,80},{112,96},{128,112},... | collective-permute-start | bytes 294920 | tf_op jit(solution)/shard_map/ppermute | solution.py:230
  22.6 1.8 %collective-permute-start.4 = (bf16[2,8,4224]{2,1,0:T(8,128)(2,1)S(1)}, bf16[2,8,4224]{2,1,0:T(8,128)(2,1)S(1)}, u32[]{:S(2)}, u32[]{:S(2)}) collective-permute-start(bf16[2,8,4224]{2,1,0:T(8,128)(2,1)S(1)} %bitcast.23), channel_id=1, source_target_pairs={{0,2},{1,3},{2,0},{3,1},{4,6},{5,7},{6,4},{7,5},{8,10},{9,11},{10,... | collective-permute-start | bytes 405512 | tf_op jit(solution)/shard_map/ppermute | solution.py:200
  24.6 4.4 %collective-permute-done.4 = bf16[2,8,4224]{2,1,0:T(8,128)(2,1)S(1)} collective-permute-done((bf16[2,8,4224]{2,1,0:T(8,128)(2,1)S(1)}, bf16[2,8,4224]{2,1,0:T(8,128)(2,1)S(1)}, u32[]{:S(2)}, u32[]{:S(2)}) %collective-permute-start.4) | collective-permute-done | bytes 135200 | tf_op jit(solution)/shard_map/ppermute | solution.py:200
  29.1 2.1 %collective-permute-done.5 = bf16[2,8,4224]{2,1,0:T(8,128)(2,1)S(1)} collective-permute-done((bf16[2,8,4224]{2,1,0:T(8,128)(2,1)S(1)}, bf16[2,8,4224]{2,1,0:T(8,128)(2,1)S(1)}, u32[]{:S(2)}, u32[]{:S(2)}) %collective-permute-start.5) | collective-permute-done | bytes 135200 | tf_op jit(solution)/shard_map/ppermute | solution.py:200
  32.4 1.8 %collective-permute-done.6 = bf16[2,8,4224]{2,1,0:T(8,128)(2,1)S(1)} collective-permute-done((bf16[2,8,4224]{2,1,0:T(8,128)(2,1)S(1)}, bf16[2,8,4224]{2,1,0:T(8,128)(2,1)S(1)}, u32[]{:S(2)}, u32[]{:S(2)}) %collective-permute-start.6) | collective-permute-done | bytes 135200 | tf_op jit(solution)/shard_map/ppermute | solution.py:200
  34.2 2.1 %collective-permute-start.9 = (bf16[2,8,4224]{2,1,0:T(8,128)(2,1)S(1)}, bf16[2,8,4224]{2,1,0:T(8,128)(2,1)S(1)}, u32[]{:S(2)}, u32[]{:S(2)}) collective-permute-start(bf16[2,8,4224]{2,1,0:T(8,128)(2,1)S(1)} %bitcast.28), channel_id=1, source_target_pairs={{0,7},{1,6},{2,5},{3,4},{4,3},{5,2},{6,1},{7,0},{8,15},{9,14},{10,... | collective-permute-start | bytes 405512 | tf_op jit(solution)/shard_map/ppermute | solution.py:200
  36.6 2.6 %collective-permute-start.10 = (bf16[2,8,4224]{2,1,0:T(8,128)(2,1)S(1)}, bf16[2,8,4224]{2,1,0:T(8,128)(2,1)S(1)}, u32[]{:S(2)}, u32[]{:S(2)}) collective-permute-start(bf16[2,8,4224]{2,1,0:T(8,128)(2,1)S(1)} %bitcast.29), channel_id=1, source_target_pairs={{0,8},{1,9},{2,10},{3,11},{4,12},{5,13},{6,14},{7,15},{8,0},{9,1},... | collective-permute-start | bytes 405512 | tf_op jit(solution)/shard_map/ppermute | solution.py:200
  39.2 2.3 %collective-permute-start.11 = (bf16[2,8,4224]{2,1,0:T(8,128)(2,1)S(1)}, bf16[2,8,4224]{2,1,0:T(8,128)(2,1)S(1)}, u32[]{:S(2)}, u32[]{:S(2)}) collective-permute-start(bf16[2,8,4224]{2,1,0:T(8,128)(2,1)S(1)} %bitcast.30), channel_id=1, source_target_pairs={{0,9},{1,8},{2,11},{3,10},{4,13},{5,12},{6,15},{7,14},{8,1},{9,0},... | collective-permute-start | bytes 405512 | tf_op jit(solution)/shard_map/ppermute | solution.py:200
  42.0 3.8 %collective-permute-start.12 = (bf16[2,8,4224]{2,1,0:T(8,128)(2,1)S(1)}, bf16[2,8,4224]{2,1,0:T(8,128)(2,1)S(1)}, u32[]{:S(2)}, u32[]{:S(2)}) collective-permute-start(bf16[2,8,4224]{2,1,0:T(8,128)(2,1)S(1)} %bitcast.31), channel_id=1, source_target_pairs={{0,10},{1,11},{2,8},{3,9},{4,14},{5,15},{6,12},{7,13},{8,2},{9,3},... | collective-permute-start | bytes 405512 | tf_op jit(solution)/shard_map/ppermute | solution.py:200
  46.5 4.5 %collective-permute-start.14 = (bf16[2,8,4224]{2,1,0:T(8,128)(2,1)S(1)}, bf16[2,8,4224]{2,1,0:T(8,128)(2,1)S(1)}, u32[]{:S(2)}, u32[]{:S(2)}) collective-permute-start(bf16[2,8,4224]{2,1,0:T(8,128)(2,1)S(1)} %bitcast.33), channel_id=1, source_target_pairs={{0,12},{1,13},{2,14},{3,15},{4,8},{5,9},{6,10},{7,11},{8,4},{9,5},... | collective-permute-start | bytes 405512 | tf_op jit(solution)/shard_map/ppermute | solution.py:200
  51.1 2.6 %collective-permute-start.15 = (bf16[2,8,4224]{2,1,0:T(8,128)(2,1)S(1)}, bf16[2,8,4224]{2,1,0:T(8,128)(2,1)S(1)}, u32[]{:S(2)}, u32[]{:S(2)}) collective-permute-start(bf16[2,8,4224]{2,1,0:T(8,128)(2,1)S(1)} %bitcast.34), channel_id=1, source_target_pairs={{0,13},{1,12},{2,15},{3,14},{4,9},{5,8},{6,11},{7,10},{8,5},{9,4},... | collective-permute-start | bytes 405512 | tf_op jit(solution)/shard_map/ppermute | solution.py:200
  53.7 2.9 %collective-permute-start.16 = (bf16[2,8,4224]{2,1,0:T(8,128)(2,1)S(1)}, bf16[2,8,4224]{2,1,0:T(8,128)(2,1)S(1)}, u32[]{:S(2)}, u32[]{:S(2)}) collective-permute-start(bf16[2,8,4224]{2,1,0:T(8,128)(2,1)S(1)} %bitcast.35), channel_id=1, source_target_pairs={{0,14},{1,15},{2,12},{3,13},{4,10},{5,11},{6,8},{7,9},{8,6},{9,7},... | collective-permute-start | bytes 405512 | tf_op jit(solution)/shard_map/ppermute | solution.py:200
  56.6 1.5 %collective-permute-done.14 = bf16[2,8,4224]{2,1,0:T(8,128)(2,1)S(1)} collective-permute-done((bf16[2,8,4224]{2,1,0:T(8,128)(2,1)S(1)}, bf16[2,8,4224]{2,1,0:T(8,128)(2,1)S(1)}, u32[]{:S(2)}, u32[]{:S(2)}) %collective-permute-start.14) | collective-permute-done | bytes 135200 | tf_op jit(solution)/shard_map/ppermute | solution.py:200
  58.1 1.6 %collective-permute-start.17 = (bf16[2,8,4224]{2,1,0:T(8,128)(2,1)S(1)}, bf16[2,8,4224]{2,1,0:T(8,128)(2,1)S(1)}, u32[]{:S(2)}, u32[]{:S(2)}) collective-permute-start(bf16[2,8,4224]{2,1,0:T(8,128)(2,1)S(1)} %bitcast.36), channel_id=1, source_target_pairs={{0,15},{1,14},{2,13},{3,12},{4,11},{5,10},{6,9},{7,8},{8,7},{9,6},... | collective-permute-start | bytes 405512 | tf_op jit(solution)/shard_map/ppermute | solution.py:200
  61.2 2.7 %collective-permute-done.16 = bf16[2,8,4224]{2,1,0:T(8,128)(2,1)S(1)} collective-permute-done((bf16[2,8,4224]{2,1,0:T(8,128)(2,1)S(1)}, bf16[2,8,4224]{2,1,0:T(8,128)(2,1)S(1)}, u32[]{:S(2)}, u32[]{:S(2)}) %collective-permute-start.16) | collective-permute-done | bytes 135200 | tf_op jit(solution)/shard_map/ppermute | solution.py:200
  63.9 2.9 %collective-permute-done.17 = bf16[2,8,4224]{2,1,0:T(8,128)(2,1)S(1)} collective-permute-done((bf16[2,8,4224]{2,1,0:T(8,128)(2,1)S(1)}, bf16[2,8,4224]{2,1,0:T(8,128)(2,1)S(1)}, u32[]{:S(2)}, u32[]{:S(2)}) %collective-permute-start.17) | collective-permute-done | bytes 135200 | tf_op jit(solution)/shard_map/ppermute | solution.py:200
  69.6 5.5 %shard_map.73.v_ref.rest_0_ = f32[16,32,128]{2,1,0:T(8,128)} custom-call(s32[4]{0:T(128)} %pad_add_fusion.shift_ref, f32[6,32,128]{2,1,0:T(8,128)} %copy-done.4, f32[16,32,128]{2,1,0:T(8,128)} %bitcast.20, f32[6,32,128]{2,1,0:T(8,128)} %copy-done.5, f32[16,32,128]{2,1,0:T(8,128)} %pot_ref.5, bf16[320,512]{1,0:T(8,128)(2,1)} %fusion.1.pick_ref, ...), custom_call_target="tpu_custom_call" | custom-call | tf_op jit(solution)/shard_map/pallas_call | solution.py:157
  76.3 5.4 %collective-permute-start.19 = (f32[6,32,128]{2,1,0:T(8,128)S(1)}, f32[6,32,128]{2,1,0:T(8,128)S(1)}, u32[]{:S(2)}, u32[]{:S(2)}) collective-permute-start(f32[6,32,128]{2,1,0:T(8,128)S(1)} %get-tuple-element.21), channel_id=1, source_target_pairs={{16,0},{32,16},{48,32},{64,48},{80,64},{96,80},{112,96},{128,112},... | collective-permute-start | bytes 294920 | tf_op jit(solution)/shard_map/ppermute | solution.py:230
  81.7 2.8 %collective-permute-done.18.lo_ref = f32[6,32,128]{2,1,0:T(8,128)S(1)} collective-permute-done((f32[6,32,128]{2,1,0:T(8,128)S(1)}, f32[6,32,128]{2,1,0:T(8,128)S(1)}, u32[]{:S(2)}, u32[]{:S(2)}) %collective-permute-start.18) | collective-permute-done | bytes 98336 | tf_op jit(solution)/shard_map/ppermute | solution.py:229
  85.8 5.6 %shard_map.74.v_ref = f32[16,32,128]{2,1,0:T(8,128)} custom-call(s32[4]{0:T(128)} %pad_add_fusion.shift_ref, f32[6,32,128]{2,1,0:T(8,128)} %copy-done.2, f32[16,32,128]{2,1,0:T(8,128)} %shard_map.73.v_ref.rest_0_, f32[6,32,128]{2,1,0:T(8,128)} %copy-done.3, f32[16,32,128]{2,1,0:T(8,128)} %pot_ref.5, bf16[320,512]{1,0:T(8,128)(2,1)} %fusion.1.pick_ref, ...), custom_call_target="tpu_custom_call" | custom-call | tf_op jit(solution)/shard_map/pallas_call | solution.py:157
  92.4 5.6 %collective-permute-start.21 = (f32[6,32,128]{2,1,0:T(8,128)S(1)}, f32[6,32,128]{2,1,0:T(8,128)S(1)}, u32[]{:S(2)}, u32[]{:S(2)}) collective-permute-start(f32[6,32,128]{2,1,0:T(8,128)S(1)} %get-tuple-element.19), channel_id=1, source_target_pairs={{16,0},{32,16},{48,32},{64,48},{80,64},{96,80},{112,96},{128,112},... | collective-permute-start | bytes 294920 | tf_op jit(solution)/shard_map/ppermute | solution.py:230
  98.1 2.6 %collective-permute-done.20.lo_ref = f32[6,32,128]{2,1,0:T(8,128)S(1)} collective-permute-done((f32[6,32,128]{2,1,0:T(8,128)S(1)}, f32[6,32,128]{2,1,0:T(8,128)S(1)}, u32[]{:S(2)}, u32[]{:S(2)}) %collective-permute-start.20) | collective-permute-done | bytes 98336 | tf_op jit(solution)/shard_map/ppermute | solution.py:229
  101.9 5.6 %shard_map.75 = f32[16,32,128]{2,1,0:T(8,128)} custom-call(s32[4]{0:T(128)} %pad_add_fusion.shift_ref, f32[6,32,128]{2,1,0:T(8,128)} %copy-done, f32[16,32,128]{2,1,0:T(8,128)} %shard_map.74.v_ref, f32[6,32,128]{2,1,0:T(8,128)} %copy-done.1, f32[16,32,128]{2,1,0:T(8,128)} %pot_ref.5, bf16[320,512]{1,0:T(8,128)(2,1)} %fusion.1.pick_ref, ...), custom_call_target="tpu_custom_call" | custom-call | tf_op jit(solution)/shard_map/pallas_call | solution.py:157
  (72 shorter events, 20.4 us)
Async XLA Ops:
  1.7 20.8 %collective-permute-start.2 = (bf16[1,2,8,4224]{3,2,1,0:T(8,128)(2,1)S(1)}, bf16[1,2,8,4224]{3,2,1,0:T(8,128)(2,1)S(1)}, u32[]{:S(2)}, u32[]{:S(2)}) collective-permute-start(bf16[1,2,8,4224]{3,2,1,0:T(8,128)(2,1)S(1)} %fusion.3), channel_id=1, source_target_pairs={{0,0},{1,16},{2,32},{3,48},{4,64},{5,80},{6,96},{7,112},{8,128},{9... | collective-permute-start | bytes 405512 | tf_op jit(solution)/shard_map/ppermute | solution.py:196
  10.8 58.0 %collective-permute-start = (f32[6,32,128]{2,1,0:T(8,128)S(1)}, f32[6,32,128]{2,1,0:T(8,128)S(1)}, u32[]{:S(2)}, u32[]{:S(2)}) collective-permute-start(f32[6,32,128]{2,1,0:T(8,128)S(1)} %get-tuple-element.24), channel_id=1, source_target_pairs={{0,16},{16,32},{32,48},{48,64},{64,80},{80,96},{96,112},{112,128},... | collective-permute-start | bytes 294920 | tf_op jit(solution)/shard_map/ppermute | solution.py:229
  11.7 57.0 %collective-permute-start.1 = (f32[6,32,128]{2,1,0:T(8,128)S(1)}, f32[6,32,128]{2,1,0:T(8,128)S(1)}, u32[]{:S(2)}, u32[]{:S(2)}) collective-permute-start(f32[6,32,128]{2,1,0:T(8,128)S(1)} %get-tuple-element.23), channel_id=1, source_target_pairs={{16,0},{32,16},{48,32},{64,48},{80,64},{96,80},{112,96},{128,112},... | collective-permute-start | bytes 294920 | tf_op jit(solution)/shard_map/ppermute | solution.py:230
  22.5 2.0 %collective-permute-start.3 = (bf16[2,8,4224]{2,1,0:T(8,128)(2,1)S(1)}, bf16[2,8,4224]{2,1,0:T(8,128)(2,1)S(1)}, u32[]{:S(2)}, u32[]{:S(2)}) collective-permute-start(bf16[2,8,4224]{2,1,0:T(8,128)(2,1)S(1)} %bitcast.22), channel_id=1, source_target_pairs={{0,1},{1,0},{2,3},{3,2},{4,5},{5,4},{6,7},{7,6},{8,9},{9,8},{10,11... | collective-permute-start | bytes 405512 | tf_op jit(solution)/shard_map/ppermute | solution.py:200
  22.6 6.5 %collective-permute-start.4 = (bf16[2,8,4224]{2,1,0:T(8,128)(2,1)S(1)}, bf16[2,8,4224]{2,1,0:T(8,128)(2,1)S(1)}, u32[]{:S(2)}, u32[]{:S(2)}) collective-permute-start(bf16[2,8,4224]{2,1,0:T(8,128)(2,1)S(1)} %bitcast.23), channel_id=1, source_target_pairs={{0,2},{1,3},{2,0},{3,1},{4,6},{5,7},{6,4},{7,5},{8,10},{9,11},{10,... | collective-permute-start | bytes 405512 | tf_op jit(solution)/shard_map/ppermute | solution.py:200
  24.4 6.8 %collective-permute-start.5 = (bf16[2,8,4224]{2,1,0:T(8,128)(2,1)S(1)}, bf16[2,8,4224]{2,1,0:T(8,128)(2,1)S(1)}, u32[]{:S(2)}, u32[]{:S(2)}) collective-permute-start(bf16[2,8,4224]{2,1,0:T(8,128)(2,1)S(1)} %bitcast.24), channel_id=1, source_target_pairs={{0,3},{1,2},{2,1},{3,0},{4,7},{5,6},{6,5},{7,4},{8,11},{9,10},{10,... | collective-permute-start | bytes 405512 | tf_op jit(solution)/shard_map/ppermute | solution.py:200
  24.5 9.7 %collective-permute-start.6 = (bf16[2,8,4224]{2,1,0:T(8,128)(2,1)S(1)}, bf16[2,8,4224]{2,1,0:T(8,128)(2,1)S(1)}, u32[]{:S(2)}, u32[]{:S(2)}) collective-permute-start(bf16[2,8,4224]{2,1,0:T(8,128)(2,1)S(1)} %bitcast.25), channel_id=1, source_target_pairs={{0,4},{1,5},{2,6},{3,7},{4,0},{5,1},{6,2},{7,3},{8,12},{9,13},{10,... | collective-permute-start | bytes 405512 | tf_op jit(solution)/shard_map/ppermute | solution.py:200
  29.1 7.5 %collective-permute-start.7 = (bf16[2,8,4224]{2,1,0:T(8,128)(2,1)S(1)}, bf16[2,8,4224]{2,1,0:T(8,128)(2,1)S(1)}, u32[]{:S(2)}, u32[]{:S(2)}) collective-permute-start(bf16[2,8,4224]{2,1,0:T(8,128)(2,1)S(1)} %bitcast.26), channel_id=1, source_target_pairs={{0,5},{1,4},{2,7},{3,6},{4,1},{5,0},{6,3},{7,2},{8,13},{9,12},{10,... | collective-permute-start | bytes 405512 | tf_op jit(solution)/shard_map/ppermute | solution.py:200
  31.2 8.0 %collective-permute-start.8 = (bf16[2,8,4224]{2,1,0:T(8,128)(2,1)S(1)}, bf16[2,8,4224]{2,1,0:T(8,128)(2,1)S(1)}, u32[]{:S(2)}, u32[]{:S(2)}) collective-permute-start(bf16[2,8,4224]{2,1,0:T(8,128)(2,1)S(1)} %bitcast.27), channel_id=1, source_target_pairs={{0,6},{1,7},{2,4},{3,5},{4,2},{5,3},{6,0},{7,1},{8,14},{9,15},{10,... | collective-permute-start | bytes 405512 | tf_op jit(solution)/shard_map/ppermute | solution.py:200
  34.2 7.9 %collective-permute-start.9 = (bf16[2,8,4224]{2,1,0:T(8,128)(2,1)S(1)}, bf16[2,8,4224]{2,1,0:T(8,128)(2,1)S(1)}, u32[]{:S(2)}, u32[]{:S(2)}) collective-permute-start(bf16[2,8,4224]{2,1,0:T(8,128)(2,1)S(1)} %bitcast.28), channel_id=1, source_target_pairs={{0,7},{1,6},{2,5},{3,4},{4,3},{5,2},{6,1},{7,0},{8,15},{9,14},{10,... | collective-permute-start | bytes 405512 | tf_op jit(solution)/shard_map/ppermute | solution.py:200
  36.6 9.2 %collective-permute-start.10 = (bf16[2,8,4224]{2,1,0:T(8,128)(2,1)S(1)}, bf16[2,8,4224]{2,1,0:T(8,128)(2,1)S(1)}, u32[]{:S(2)}, u32[]{:S(2)}) collective-permute-start(bf16[2,8,4224]{2,1,0:T(8,128)(2,1)S(1)} %bitcast.29), channel_id=1, source_target_pairs={{0,8},{1,9},{2,10},{3,11},{4,12},{5,13},{6,14},{7,15},{8,0},{9,1},... | collective-permute-start | bytes 405512 | tf_op jit(solution)/shard_map/ppermute | solution.py:200
  39.2 7.3 %collective-permute-start.11 = (bf16[2,8,4224]{2,1,0:T(8,128)(2,1)S(1)}, bf16[2,8,4224]{2,1,0:T(8,128)(2,1)S(1)}, u32[]{:S(2)}, u32[]{:S(2)}) collective-permute-start(bf16[2,8,4224]{2,1,0:T(8,128)(2,1)S(1)} %bitcast.30), channel_id=1, source_target_pairs={{0,9},{1,8},{2,11},{3,10},{4,13},{5,12},{6,15},{7,14},{8,1},{9,0},... | collective-permute-start | bytes 405512 | tf_op jit(solution)/shard_map/ppermute | solution.py:200
  42.0 9.0 %collective-permute-start.12 = (bf16[2,8,4224]{2,1,0:T(8,128)(2,1)S(1)}, bf16[2,8,4224]{2,1,0:T(8,128)(2,1)S(1)}, u32[]{:S(2)}, u32[]{:S(2)}) collective-permute-start(bf16[2,8,4224]{2,1,0:T(8,128)(2,1)S(1)} %bitcast.31), channel_id=1, source_target_pairs={{0,10},{1,11},{2,8},{3,9},{4,14},{5,15},{6,12},{7,13},{8,2},{9,3},... | collective-permute-start | bytes 405512 | tf_op jit(solution)/shard_map/ppermute | solution.py:200
  45.8 7.9 %collective-permute-start.13 = (bf16[2,8,4224]{2,1,0:T(8,128)(2,1)S(1)}, bf16[2,8,4224]{2,1,0:T(8,128)(2,1)S(1)}, u32[]{:S(2)}, u32[]{:S(2)}) collective-permute-start(bf16[2,8,4224]{2,1,0:T(8,128)(2,1)S(1)} %bitcast.32), channel_id=1, source_target_pairs={{0,11},{1,10},{2,9},{3,8},{4,15},{5,14},{6,13},{7,12},{8,3},{9,2},... | collective-permute-start | bytes 405512 | tf_op jit(solution)/shard_map/ppermute | solution.py:200
  46.5 11.6 %collective-permute-start.14 = (bf16[2,8,4224]{2,1,0:T(8,128)(2,1)S(1)}, bf16[2,8,4224]{2,1,0:T(8,128)(2,1)S(1)}, u32[]{:S(2)}, u32[]{:S(2)}) collective-permute-start(bf16[2,8,4224]{2,1,0:T(8,128)(2,1)S(1)} %bitcast.33), channel_id=1, source_target_pairs={{0,12},{1,13},{2,14},{3,15},{4,8},{5,9},{6,10},{7,11},{8,4},{9,5},... | collective-permute-start | bytes 405512 | tf_op jit(solution)/shard_map/ppermute | solution.py:200
  51.1 10.1 %collective-permute-start.15 = (bf16[2,8,4224]{2,1,0:T(8,128)(2,1)S(1)}, bf16[2,8,4224]{2,1,0:T(8,128)(2,1)S(1)}, u32[]{:S(2)}, u32[]{:S(2)}) collective-permute-start(bf16[2,8,4224]{2,1,0:T(8,128)(2,1)S(1)} %bitcast.34), channel_id=1, source_target_pairs={{0,13},{1,12},{2,15},{3,14},{4,9},{5,8},{6,11},{7,10},{8,5},{9,4},... | collective-permute-start | bytes 405512 | tf_op jit(solution)/shard_map/ppermute | solution.py:200
  53.7 10.1 %collective-permute-start.16 = (bf16[2,8,4224]{2,1,0:T(8,128)(2,1)S(1)}, bf16[2,8,4224]{2,1,0:T(8,128)(2,1)S(1)}, u32[]{:S(2)}, u32[]{:S(2)}) collective-permute-start(bf16[2,8,4224]{2,1,0:T(8,128)(2,1)S(1)} %bitcast.35), channel_id=1, source_target_pairs={{0,14},{1,15},{2,12},{3,13},{4,10},{5,11},{6,8},{7,9},{8,6},{9,7},... | collective-permute-start | bytes 405512 | tf_op jit(solution)/shard_map/ppermute | solution.py:200
  58.1 8.6 %collective-permute-start.17 = (bf16[2,8,4224]{2,1,0:T(8,128)(2,1)S(1)}, bf16[2,8,4224]{2,1,0:T(8,128)(2,1)S(1)}, u32[]{:S(2)}, u32[]{:S(2)}) collective-permute-start(bf16[2,8,4224]{2,1,0:T(8,128)(2,1)S(1)} %bitcast.36), channel_id=1, source_target_pairs={{0,15},{1,14},{2,13},{3,12},{4,11},{5,10},{6,9},{7,8},{8,7},{9,6},... | collective-permute-start | bytes 405512 | tf_op jit(solution)/shard_map/ppermute | solution.py:200
  68.8 0.8 copy-start.4
  68.8 0.8 copy-start.5
  76.0 8.5 %collective-permute-start.18 = (f32[6,32,128]{2,1,0:T(8,128)S(1)}, f32[6,32,128]{2,1,0:T(8,128)S(1)}, u32[]{:S(2)}, u32[]{:S(2)}) collective-permute-start(f32[6,32,128]{2,1,0:T(8,128)S(1)} %get-tuple-element.22), channel_id=1, source_target_pairs={{0,16},{16,32},{32,48},{48,64},{64,80},{80,96},{96,112},{112,128},... | collective-permute-start | bytes 294920 | tf_op jit(solution)/shard_map/ppermute | solution.py:229
  76.3 8.2 %collective-permute-start.19 = (f32[6,32,128]{2,1,0:T(8,128)S(1)}, f32[6,32,128]{2,1,0:T(8,128)S(1)}, u32[]{:S(2)}, u32[]{:S(2)}) collective-permute-start(f32[6,32,128]{2,1,0:T(8,128)S(1)} %get-tuple-element.21), channel_id=1, source_target_pairs={{16,0},{32,16},{48,32},{64,48},{80,64},{96,80},{112,96},{128,112},... | collective-permute-start | bytes 294920 | tf_op jit(solution)/shard_map/ppermute | solution.py:230
  92.3 8.3 %collective-permute-start.20 = (f32[6,32,128]{2,1,0:T(8,128)S(1)}, f32[6,32,128]{2,1,0:T(8,128)S(1)}, u32[]{:S(2)}, u32[]{:S(2)}) collective-permute-start(f32[6,32,128]{2,1,0:T(8,128)S(1)} %get-tuple-element.20), channel_id=1, source_target_pairs={{0,16},{16,32},{32,48},{48,64},{64,80},{80,96},{96,112},{112,128},... | collective-permute-start | bytes 294920 | tf_op jit(solution)/shard_map/ppermute | solution.py:229
  92.4 8.2 %collective-permute-start.21 = (f32[6,32,128]{2,1,0:T(8,128)S(1)}, f32[6,32,128]{2,1,0:T(8,128)S(1)}, u32[]{:S(2)}, u32[]{:S(2)}) collective-permute-start(f32[6,32,128]{2,1,0:T(8,128)S(1)} %get-tuple-element.19), channel_id=1, source_target_pairs={{16,0},{32,16},{48,32},{64,48},{80,64},{96,80},{112,96},{128,112},... | collective-permute-start | bytes 294920 | tf_op jit(solution)/shard_map/ppermute | solution.py:230
  (4 other events, 2.5 us)

commit v8 on v6

--- a/solution.py
+++ b/solution.py
@@ -193,6 +193,10 @@
     gain_lanes = gain_lanes.at[..., 0].set(proj_gains)
     packed = jnp.concatenate([projectors, gain_lanes], axis=3)
     pairs = [(o * n_states + t, t * n_states + o) for o in range(n_grid) for t in range(n_states)]
+    pairs_far = [
+        (o * n_states + t, t * n_states + (o ^ 8)) for o in range(n_grid) for t in range(n_states)
+    ]
+    packed_far = lax.ppermute(packed, ("grid", "states"), pairs_far)
     packed = lax.ppermute(packed, ("grid", "states"), pairs)
     def flip_y(s):
         return s ^ 8
@@ -207,14 +211,14 @@
     def flip_core(s):
         return s ^ 1
 
-    exchanges = (flip_y, flip_x, mirror_x, flip_core)
+    exchanges = (flip_x, mirror_x, flip_core)
 
     def origins(me, done):
         if not done:
-            return [me]
+            return [me, flip_y(me)]
         return origins(me, done[:-1]) + origins(done[-1](me), done[:-1])
 
-    gathered = packed[0]
+    gathered = jnp.concatenate([packed[0], packed_far[0]], axis=0)
     for exchange in exchanges:
         partner = lax.ppermute(
             gathered, "states", [(s, exchange(s)) for s in range(n_states)]

time: 94.6 us -> 96.8 us (1.023); the launches traced: 94.2 us -> 95.2 us
  starting transfers between devices: 26.6 us -> 30.5 us
  waiting for transfers between devices: 33.7 us -> 30.8 us
    ppermute x1, waiting for transfers between devices: 6.31 us -> 0.01 us  [shards(): packed = lax.ppermute(packed, ('grid', 'states'), pairs)]
    ppermute x1, starting transfers between devices: 1.92 us -> 8.12 us  [shards(): packed = lax.ppermute(packed, ('grid', 'states'), pairs)]
    ppermute x3, starting transfers between devices: 20.1 us -> 14.4 us  [step(): high_rim = lax.ppermute(field[:RADIUS], 'grid', down)]
    ppermute x0 -> x1, waiting for transfers between devices: none -> 2.16 us  [shards(): packed_far = lax.ppermute(packed, ('grid', 'states'), pairs_far)]
    ppermute x0 -> x1, starting transfers between devices: none -> 2.13 us  [shards(): packed_far = lax.ppermute(packed, ('grid', 'states'), pairs_far)]
    ppermute x4 -> x3, waiting for transfers between devices: 21.8 us -> 23 us  [shards(): lax.ppermute(gathered, 'states', [(s, exchange(s)) for s in range(n_state...]
    ppermute x4 -> x3, starting transfers between devices: 2.42 us -> 2.9 us  [shards(): lax.ppermute(gathered, 'states', [(s, exchange(s)) for s in range(n_state...]
  transfers between devices with their start and end apart: 11 -> 11, of which waited for: 7 -> 6; matrix products, arithmetic and copies ran while one was open for 10% -> 9% of each run, Pallas kernels for 0% -> 0%
where the time goes in v8:
time: 96.8 us; the launch traced here: 95.2 us
  waiting for transfers between devices  30.8 us (32%)
  starting transfers between devices  30.5 us (32%)
  Pallas kernels  16.6 us (17%)
  local copies, waits for them, and re-layouts  9.11 us (9%)
  other arithmetic  6.73 us (7%)
  between operations  1.47 us (2%)
    ppermute x3, waiting for transfers between devices, shards(): lax.ppermute(gathered, 'states', [(s, exchange(s)) for s in range(n_state...  23 us
    pallas_call x3, Pallas kernels, apply_op(): pl.pallas_call(make_kernel(scale, prev is not None, home_count, proj.shap...  16.6 us
    ppermute x3, starting transfers between devices, step(): high_rim = lax.ppermute(field[:RADIUS], 'grid', down)  14.4 us
    ppermute x1, starting transfers between devices, shards(): packed = lax.ppermute(packed, ('grid', 'states'), pairs)  8.12 us
    ppermute x3, waiting for transfers between devices, step(): low_rim = lax.ppermute(field[tile_width - RADIUS:], 'grid', up)  5.62 us
    unnamed x19, local copies, waits for them, and re-layouts  4.47 us
    ppermute x3, starting transfers between devices, step(): low_rim = lax.ppermute(field[tile_width - RADIUS:], 'grid', up)  2.96 us
    ppermute x3, starting transfers between devices, shards(): lax.ppermute(gathered, 'states', [(s, exchange(s)) for s in range(n_state...  2.9 us
  transfers between devices with their start and end apart: 11, of which 6 were waited for; matrix products, arithmetic and copies ran while one was open for 9% of the time, Pallas kernels for 0%

profile of v8, /device:TPU:6, one launch (start us, length us, event | category | flops | bytes accessed | tf_op | source)
XLA Modules:
  0.0 95.2 jit_solution(1881505815640270628)
XLA Ops:
  0.8 0.9 fusion.3
  1.7 8.1 %collective-permute-start.2 = (bf16[1,2,8,4224]{3,2,1,0:T(8,128)(2,1)S(1)}, bf16[1,2,8,4224]{3,2,1,0:T(8,128)(2,1)S(1)}, u32[]{:S(2)}, u32[]{:S(2)}) collective-permute-start(bf16[1,2,8,4224]{3,2,1,0:T(8,128)(2,1)S(1)} %fusion.3), channel_id=1, source_target_pairs={{0,0},{1,16},{2,32},{3,48},{4,64},{5,80},{6,96},{7,112},{8,128},{9... | collective-permute-start | bytes 405512 | tf_op jit(solution)/shard_map/ppermute | solution.py:200
  9.8 2.1 %collective-permute-start.3 = (bf16[1,2,8,4224]{3,2,1,0:T(8,128)(2,1)S(1)}, bf16[1,2,8,4224]{3,2,1,0:T(8,128)(2,1)S(1)}, u32[]{:S(2)}, u32[]{:S(2)}) collective-permute-start(bf16[1,2,8,4224]{3,2,1,0:T(8,128)(2,1)S(1)} %fusion.3), channel_id=1, source_target_pairs={{0,8},{1,24},{2,40},{3,56},{4,72},{5,88},{6,104},{7,120},{8,136},{... | collective-permute-start | bytes 405512 | tf_op jit(solution)/shard_map/ppermute | solution.py:199
  11.9 1.0 %slice_bitcast_fusion.1 = (f32[6,32,128]{2,1,0:T(8,128)S(1)}, f32[6,32,128]{2,1,0:T(8,128)S(1)}) fusion(f32[1,16,32,128]{3,2,1,0:T(8,128)} %param.9), kind=kLoop, calls=%fused_computation.13 | loop fusion | bytes 393216 | tf_op jit(solution)/shard_map/slice | solution.py:257
  12.9 2.6 %collective-permute-start = (f32[6,32,128]{2,1,0:T(8,128)S(1)}, f32[6,32,128]{2,1,0:T(8,128)S(1)}, u32[]{:S(2)}, u32[]{:S(2)}) collective-permute-start(f32[6,32,128]{2,1,0:T(8,128)S(1)} %get-tuple-element.26), channel_id=1, source_target_pairs={{0,16},{16,32},{32,48},{48,64},{64,80},{80,96},{96,112},{112,128},... | collective-permute-start | bytes 294920 | tf_op jit(solution)/shard_map/ppermute | solution.py:256
  15.5 3.1 %collective-permute-start.1 = (f32[6,32,128]{2,1,0:T(8,128)S(1)}, f32[6,32,128]{2,1,0:T(8,128)S(1)}, u32[]{:S(2)}, u32[]{:S(2)}) collective-permute-start(f32[6,32,128]{2,1,0:T(8,128)S(1)} %get-tuple-element.25), channel_id=1, source_target_pairs={{16,0},{32,16},{48,32},{64,48},{80,64},{96,80},{112,96},{128,112},... | collective-permute-start | bytes 294920 | tf_op jit(solution)/shard_map/ppermute | solution.py:257
  22.4 0.9 convert_reduce_fusion.1
  23.4 1.4 %iota_reduce_fusion = (pred[10]{0:T(512)(128)(4,1)}, s32[10]{0:T(128)S(1)}) fusion(s32[16]{0:T(128)S(1)} %stack.79, s32[10]{0:T(128)} %param.13), kind=kLoop, calls=%fused_computation.23 | loop fusion | flops 1210 | bytes 154 | tf_op jit(solution)/shard_map/shards/reduce | solution.py:228
  25.5 2.2 %collective-permute-done.3 = bf16[1,2,8,4224]{3,2,1,0:T(8,128)(2,1)S(1)} collective-permute-done((bf16[1,2,8,4224]{3,2,1,0:T(8,128)(2,1)S(1)}, bf16[1,2,8,4224]{3,2,1,0:T(8,128)(2,1)S(1)}, u32[]{:S(2)}, u32[]{:S(2)}) %collective-permute-start.3) | collective-permute-done | bytes 135200 | tf_op jit(solution)/shard_map/ppermute | solution.py:199
  28.6 6.4 %collective-permute-done.4 = bf16[4,8,4224]{2,1,0:T(8,128)(2,1)S(1)} collective-permute-done((bf16[4,8,4224]{2,1,0:T(8,128)(2,1)S(1)}, bf16[4,8,4224]{2,1,0:T(8,128)(2,1)S(1)}, u32[]{:S(2)}, u32[]{:S(2)}) %collective-permute-start.4) | collective-permute-done | bytes 270368 | tf_op jit(solution)/shard_map/ppermute | solution.py:223
  35.0 1.1 %collective-permute-start.5 = (bf16[8,8,4224]{2,1,0:T(8,128)(2,1)S(1)}, bf16[8,8,4224]{2,1,0:T(8,128)(2,1)S(1)}, u32[]{:S(2)}, u32[]{:S(2)}) collective-permute-start(bf16[8,8,4224]{2,1,0:T(8,128)(2,1)S(1)} %pad_maximum_fusion.1), channel_id=1, source_target_pairs={{0,6},{1,7},{2,4},{3,5},{4,2},{5,3},{6,0},{7,1},{8,14},{9,15},{10,... | collective-permute-start | bytes 1622024 | tf_op jit(solution)/shard_map/ppermute | solution.py:223
  36.2 14.3 %collective-permute-done.5 = bf16[8,8,4224]{2,1,0:T(8,128)(2,1)S(1)} collective-permute-done((bf16[8,8,4224]{2,1,0:T(8,128)(2,1)S(1)}, bf16[8,8,4224]{2,1,0:T(8,128)(2,1)S(1)}, u32[]{:S(2)}, u32[]{:S(2)}) %collective-permute-start.5) | collective-permute-done | bytes 540704 | tf_op jit(solution)/shard_map/ppermute | solution.py:223
  50.6 0.9 collective-permute-start.6
  51.6 2.3 %collective-permute-done.6 = bf16[16,8,4224]{2,1,0:T(8,128)(2,1)S(1)} collective-permute-done((bf16[16,8,4224]{2,1,0:T(8,128)(2,1)S(1)}, bf16[16,8,4224]{2,1,0:T(8,128)(2,1)S(1)}, u32[]{:S(2)}, u32[]{:S(2)}) %collective-permute-start.6) | collective-permute-done | bytes 1081376 | tf_op jit(solution)/shard_map/ppermute | solution.py:223
  54.8 1.0 %copy.12 = bf16[10,8,32,128]{3,2,1,0:T(8,128)(2,1)} copy(bf16[10,8,32,128]{3,1,2,0:T(8,128)(2,1)S(1)} %slice_bitcast_fusion) | data formatting | bytes 1310720
  56.8 5.5 %shard_map.73.v_ref.rest_0_ = f32[16,32,128]{2,1,0:T(8,128)} custom-call(s32[4]{0:T(128)} %pad_add_fusion.shift_ref, f32[6,32,128]{2,1,0:T(8,128)} %copy-done.4, f32[16,32,128]{2,1,0:T(8,128)} %bitcast.44, f32[6,32,128]{2,1,0:T(8,128)} %copy-done.5, f32[16,32,128]{2,1,0:T(8,128)} %pot_ref.5, bf16[320,512]{1,0:T(8,128)(2,1)} %fusion.1.pick_ref, ...), custom_call_target="tpu_custom_call" | custom-call | tf_op jit(solution)/shard_map/pallas_call | solution.py:157
  62.3 1.0 %fusion.6 = (f32[6,32,128]{2,1,0:T(8,128)S(1)}, f32[6,32,128]{2,1,0:T(8,128)S(1)}) fusion(f32[16,32,128]{2,1,0:T(8,128)} %shard_map.73.v_ref.rest_0_), kind=kLoop, calls=%fused_computation.31 | loop fusion | bytes 393216 | tf_op jit(solution)/shard_map/slice | solution.py:257
  63.3 5.6 %collective-permute-start.8 = (f32[6,32,128]{2,1,0:T(8,128)S(1)}, f32[6,32,128]{2,1,0:T(8,128)S(1)}, u32[]{:S(2)}, u32[]{:S(2)}) collective-permute-start(f32[6,32,128]{2,1,0:T(8,128)S(1)} %get-tuple-element.23), channel_id=1, source_target_pairs={{16,0},{32,16},{48,32},{64,48},{80,64},{96,80},{112,96},{128,112},... | collective-permute-start | bytes 294920 | tf_op jit(solution)/shard_map/ppermute | solution.py:257
  69.0 3.0 %collective-permute-done.7.lo_ref = f32[6,32,128]{2,1,0:T(8,128)S(1)} collective-permute-done((f32[6,32,128]{2,1,0:T(8,128)S(1)}, f32[6,32,128]{2,1,0:T(8,128)S(1)}, u32[]{:S(2)}, u32[]{:S(2)}) %collective-permute-start.7) | collective-permute-done | bytes 98336 | tf_op jit(solution)/shard_map/ppermute | solution.py:256
  73.3 5.6 %shard_map.74.v_ref = f32[16,32,128]{2,1,0:T(8,128)} custom-call(s32[4]{0:T(128)} %pad_add_fusion.shift_ref, f32[6,32,128]{2,1,0:T(8,128)} %copy-done.2, f32[16,32,128]{2,1,0:T(8,128)} %shard_map.73.v_ref.rest_0_, f32[6,32,128]{2,1,0:T(8,128)} %copy-done.3, f32[16,32,128]{2,1,0:T(8,128)} %pot_ref.5, bf16[320,512]{1,0:T(8,128)(2,1)} %fusion.1.pick_ref, ...), custom_call_target="tpu_custom_call" | custom-call | tf_op jit(solution)/shard_map/pallas_call | solution.py:157
  78.8 1.0 %fusion.5 = (f32[6,32,128]{2,1,0:T(8,128)S(1)}, f32[6,32,128]{2,1,0:T(8,128)S(1)}) fusion(f32[16,32,128]{2,1,0:T(8,128)} %shard_map.74.v_ref), kind=kLoop, calls=%fused_computation.30 | loop fusion | bytes 393216 | tf_op jit(solution)/shard_map/slice | solution.py:257
  80.1 5.6 %collective-permute-start.10 = (f32[6,32,128]{2,1,0:T(8,128)S(1)}, f32[6,32,128]{2,1,0:T(8,128)S(1)}, u32[]{:S(2)}, u32[]{:S(2)}) collective-permute-start(f32[6,32,128]{2,1,0:T(8,128)S(1)} %get-tuple-element.21), channel_id=1, source_target_pairs={{16,0},{32,16},{48,32},{64,48},{80,64},{96,80},{112,96},{128,112},... | collective-permute-start | bytes 294920 | tf_op jit(solution)/shard_map/ppermute | solution.py:257
  85.7 2.6 %collective-permute-done.9.lo_ref = f32[6,32,128]{2,1,0:T(8,128)S(1)} collective-permute-done((f32[6,32,128]{2,1,0:T(8,128)S(1)}, f32[6,32,128]{2,1,0:T(8,128)S(1)}, u32[]{:S(2)}, u32[]{:S(2)}) %collective-permute-start.9) | collective-permute-done | bytes 98336 | tf_op jit(solution)/shard_map/ppermute | solution.py:256
  89.6 5.6 %shard_map.75 = f32[16,32,128]{2,1,0:T(8,128)} custom-call(s32[4]{0:T(128)} %pad_add_fusion.shift_ref, f32[6,32,128]{2,1,0:T(8,128)} %copy-done, f32[16,32,128]{2,1,0:T(8,128)} %shard_map.74.v_ref, f32[6,32,128]{2,1,0:T(8,128)} %copy-done.1, f32[16,32,128]{2,1,0:T(8,128)} %pot_ref.5, bf16[320,512]{1,0:T(8,128)(2,1)} %fusion.1.pick_ref, ...), custom_call_target="tpu_custom_call" | custom-call | tf_op jit(solution)/shard_map/pallas_call | solution.py:157
  (44 shorter events, 10.0 us)
Async XLA Ops:
  1.7 23.8 %collective-permute-start.2 = (bf16[1,2,8,4224]{3,2,1,0:T(8,128)(2,1)S(1)}, bf16[1,2,8,4224]{3,2,1,0:T(8,128)(2,1)S(1)}, u32[]{:S(2)}, u32[]{:S(2)}) collective-permute-start(bf16[1,2,8,4224]{3,2,1,0:T(8,128)(2,1)S(1)} %fusion.3), channel_id=1, source_target_pairs={{0,0},{1,16},{2,32},{3,48},{4,64},{5,80},{6,96},{7,112},{8,128},{9... | collective-permute-start | bytes 405512 | tf_op jit(solution)/shard_map/ppermute | solution.py:200
  9.8 17.9 %collective-permute-start.3 = (bf16[1,2,8,4224]{3,2,1,0:T(8,128)(2,1)S(1)}, bf16[1,2,8,4224]{3,2,1,0:T(8,128)(2,1)S(1)}, u32[]{:S(2)}, u32[]{:S(2)}) collective-permute-start(bf16[1,2,8,4224]{3,2,1,0:T(8,128)(2,1)S(1)} %fusion.3), channel_id=1, source_target_pairs={{0,8},{1,24},{2,40},{3,56},{4,72},{5,88},{6,104},{7,120},{8,136},{... | collective-permute-start | bytes 405512 | tf_op jit(solution)/shard_map/ppermute | solution.py:199
  12.9 43.1 %collective-permute-start = (f32[6,32,128]{2,1,0:T(8,128)S(1)}, f32[6,32,128]{2,1,0:T(8,128)S(1)}, u32[]{:S(2)}, u32[]{:S(2)}) collective-permute-start(f32[6,32,128]{2,1,0:T(8,128)S(1)} %get-tuple-element.26), channel_id=1, source_target_pairs={{0,16},{16,32},{32,48},{48,64},{64,80},{80,96},{96,112},{112,128},... | collective-permute-start | bytes 294920 | tf_op jit(solution)/shard_map/ppermute | solution.py:256
  15.5 40.5 %collective-permute-start.1 = (f32[6,32,128]{2,1,0:T(8,128)S(1)}, f32[6,32,128]{2,1,0:T(8,128)S(1)}, u32[]{:S(2)}, u32[]{:S(2)}) collective-permute-start(f32[6,32,128]{2,1,0:T(8,128)S(1)} %get-tuple-element.25), channel_id=1, source_target_pairs={{16,0},{32,16},{48,32},{64,48},{80,64},{96,80},{112,96},{128,112},... | collective-permute-start | bytes 294920 | tf_op jit(solution)/shard_map/ppermute | solution.py:257
  27.7 7.3 %collective-permute-start.4 = (bf16[4,8,4224]{2,1,0:T(8,128)(2,1)S(1)}, bf16[4,8,4224]{2,1,0:T(8,128)(2,1)S(1)}, u32[]{:S(2)}, u32[]{:S(2)}) collective-permute-start(bf16[4,8,4224]{2,1,0:T(8,128)(2,1)S(1)} %pad_maximum_fusion.2), channel_id=1, source_target_pairs={{0,2},{1,3},{2,0},{3,1},{4,6},{5,7},{6,4},{7,5},{8,10},{9,11},{10,... | collective-permute-start | bytes 811016 | tf_op jit(solution)/shard_map/ppermute | solution.py:223
  35.0 15.4 %collective-permute-start.5 = (bf16[8,8,4224]{2,1,0:T(8,128)(2,1)S(1)}, bf16[8,8,4224]{2,1,0:T(8,128)(2,1)S(1)}, u32[]{:S(2)}, u32[]{:S(2)}) collective-permute-start(bf16[8,8,4224]{2,1,0:T(8,128)(2,1)S(1)} %pad_maximum_fusion.1), channel_id=1, source_target_pairs={{0,6},{1,7},{2,4},{3,5},{4,2},{5,3},{6,0},{7,1},{8,14},{9,15},{10,... | collective-permute-start | bytes 1622024 | tf_op jit(solution)/shard_map/ppermute | solution.py:223
  50.6 3.3 %collective-permute-start.6 = (bf16[16,8,4224]{2,1,0:T(8,128)(2,1)S(1)}, bf16[16,8,4224]{2,1,0:T(8,128)(2,1)S(1)}, u32[]{:S(2)}, u32[]{:S(2)}) collective-permute-start(bf16[16,8,4224]{2,1,0:T(8,128)(2,1)S(1)} %pad_maximum_fusion), channel_id=1, source_target_pairs={{0,1},{1,0},{2,3},{3,2},{4,5},{5,4},{6,7},{7,6},{8,9},{9,8},{10,11... | collective-permute-start | bytes 3244040 | tf_op jit(solution)/shard_map/ppermute | solution.py:223
  56.0 0.8 copy-start.4
  56.0 0.8 copy-start.5
  63.2 8.8 %collective-permute-start.7 = (f32[6,32,128]{2,1,0:T(8,128)S(1)}, f32[6,32,128]{2,1,0:T(8,128)S(1)}, u32[]{:S(2)}, u32[]{:S(2)}) collective-permute-start(f32[6,32,128]{2,1,0:T(8,128)S(1)} %get-tuple-element.24), channel_id=1, source_target_pairs={{0,16},{16,32},{32,48},{48,64},{64,80},{80,96},{96,112},{112,128},... | collective-permute-start | bytes 294920 | tf_op jit(solution)/shard_map/ppermute | solution.py:256
  63.3 8.7 %collective-permute-start.8 = (f32[6,32,128]{2,1,0:T(8,128)S(1)}, f32[6,32,128]{2,1,0:T(8,128)S(1)}, u32[]{:S(2)}, u32[]{:S(2)}) collective-permute-start(f32[6,32,128]{2,1,0:T(8,128)S(1)} %get-tuple-element.23), channel_id=1, source_target_pairs={{16,0},{32,16},{48,32},{64,48},{80,64},{96,80},{112,96},{128,112},... | collective-permute-start | bytes 294920 | tf_op jit(solution)/shard_map/ppermute | solution.py:257
  72.0 0.6 copy-start.2
  72.6 0.7 copy-start.3
  79.8 8.5 %collective-permute-start.9 = (f32[6,32,128]{2,1,0:T(8,128)S(1)}, f32[6,32,128]{2,1,0:T(8,128)S(1)}, u32[]{:S(2)}, u32[]{:S(2)}) collective-permute-start(f32[6,32,128]{2,1,0:T(8,128)S(1)} %get-tuple-element.22), channel_id=1, source_target_pairs={{0,16},{16,32},{32,48},{48,64},{64,80},{80,96},{96,112},{112,128},... | collective-permute-start | bytes 294920 | tf_op jit(solution)/shard_map/ppermute | solution.py:256
  80.1 8.2 %collective-permute-start.10 = (f32[6,32,128]{2,1,0:T(8,128)S(1)}, f32[6,32,128]{2,1,0:T(8,128)S(1)}, u32[]{:S(2)}, u32[]{:S(2)}) collective-permute-start(f32[6,32,128]{2,1,0:T(8,128)S(1)} %get-tuple-element.21), channel_id=1, source_target_pairs={{16,0},{32,16},{48,32},{64,48},{80,64},{96,80},{112,96},{128,112},... | collective-permute-start | bytes 294920 | tf_op jit(solution)/shard_map/ppermute | solution.py:257
  88.3 0.7 copy-start
  88.9 0.7 copy-start.1

commit v9 on v6

--- a/solution.py
+++ b/solution.py
@@ -86,9 +86,9 @@
 
     def kernel(shift_ref, lo_ref, v_ref, hi_ref, pot_ref, pick_ref, place_ref, proj_ref, gain_ref, *rest):
         if with_prev:
-            prev_ref, out_ref, pad_ref, rows_ref = rest
+            prev_ref, out_ref, up_ref, down_ref, pad_ref, rows_ref = rest
         else:
-            out_ref, pad_ref, rows_ref = rest
+            out_ref, up_ref, down_ref, pad_ref, rows_ref = rest
         planes, breadth, depth = v_ref.shape
         v = v_ref[...]
         pad_ref[0:RADIUS] = pltpu.roll(lo_ref[...], shift_ref[0], 1)
@@ -139,9 +139,12 @@
         hv = -0.5 * lap + pot_ref[...] * v + nonlocal_lines
         kv = (hv - 12.0 * v) / 8.0
         if with_prev:
-            out_ref[...] = scale * kv - prev_ref[...]
+            result = scale * kv - prev_ref[...]
         else:
-            out_ref[...] = kv
+            result = kv
+        out_ref[...] = result
+        up_ref[...] = result[planes - RADIUS:]
+        down_ref[...] = result[:RADIUS]
 
     return kernel
 
@@ -154,11 +157,12 @@
     args = [shifts, lo, v, hi, pot, pick, place, proj, gain] + ([prev] if prev is not None else [])
     vspec = pl.BlockSpec(memory_space=pltpu.VMEM)
     in_specs = [pl.BlockSpec(memory_space=pltpu.SMEM)] + [vspec] * (len(args) - 1)
+    rim_shape = jax.ShapeDtypeStruct((RADIUS, breadth, depth), jnp.float32)
     return pl.pallas_call(
         make_kernel(scale, prev is not None, home_count, proj.shape[0] // home_count, block_rows),
-        out_shape=jax.ShapeDtypeStruct(v.shape, jnp.float32),
+        out_shape=(jax.ShapeDtypeStruct(v.shape, jnp.float32), rim_shape, rim_shape),
         in_specs=in_specs,
-        out_specs=vspec,
+        out_specs=(vspec, vspec, vspec),
         scratch_shapes=[
             pltpu.VMEM((planes + 2 * RADIUS, breadth, depth), jnp.float32),
             pltpu.VMEM((picked_rows, depth), jnp.bfloat16),
@@ -247,18 +251,18 @@
     up = [(i, (i + 1) % n_grid) for i in range(n_grid)]
     down = [(j, i) for i, j in up]
 
-    def step(grid_field, prev=None, scale=1.0):
-        field = grid_field[0]
-        low_rim = lax.ppermute(field[tile_width - RADIUS :], "grid", up)
-        high_rim = lax.ppermute(field[:RADIUS], "grid", down)
-        out = apply_op(
+    def step(field, send_up, send_down, prev=None, scale=1.0):
+        low_rim = lax.ppermute(send_up, "grid", up)
+        high_rim = lax.ppermute(send_down, "grid", down)
+        return apply_op(
             shifts, low_rim, field, high_rim, potential, pick, place, proj_in, gain_in, prev, scale
         )
-        return out[None]
-
-    first_term = step(states_in)
-    second_term = step(first_term, states_in[0], 2.0)
-    return step(second_term, first_term[0], 2.0)
+
+    field = states_in[0]
+    first_term = step(field, field[tile_width - RADIUS :], field[:RADIUS])
+    second_term = step(*first_term, field, 2.0)
+    filtered = step(*second_term, first_term[0], 2.0)
+    return filtered[0][None]
 
 
 def solution(mesh):

time: 94.6 us -> 91.8 us (0.970)
  local copies, waits for them, and re-layouts: 9.11 us -> 5.94 us
    slice x3 -> x1, local copies, waits for them, and re-layouts: 2.86 us -> 0.95 us  [shards(): first_term = step(field, field[tile_width - RADIUS:], field[:RADIUS])]
    unnamed x19, local copies, waits for them, and re-layouts: 4.47 us -> 3.21 us
where the time goes in v9:
time: 91.8 us; the launch traced here: 91.5 us
  waiting for transfers between devices  34.2 us (37%)
  starting transfers between devices  26.5 us (29%)
  Pallas kernels  16.7 us (18%)
  other arithmetic  6.63 us (7%)
  local copies, waits for them, and re-layouts  5.94 us (6%)
  between operations  1.47 us (2%)
    ppermute x4, waiting for transfers between devices, shards(): lax.ppermute(gathered, 'states', [(s, exchange(s)) for s in range(n_state...  21.9 us
    ppermute x3, starting transfers between devices, step(): high_rim = lax.ppermute(send_down, 'grid', down)  20.1 us
    pallas_call x3, Pallas kernels, apply_op(): pl.pallas_call(make_kernel(scale, prev is not None, home_count, proj.shap...  16.7 us
    ppermute x1, waiting for transfers between devices, shards(): packed = lax.ppermute(packed, ('grid', 'states'), pairs)  6.33 us
    ppermute x3, waiting for transfers between devices, step(): low_rim = lax.ppermute(send_up, 'grid', up)  6.02 us
    unnamed x19, local copies, waits for them, and re-layouts  3.21 us
    ppermute x4, starting transfers between devices, shards(): lax.ppermute(gathered, 'states', [(s, exchange(s)) for s in range(n_state...  2.42 us
    ppermute x3, starting transfers between devices, step(): low_rim = lax.ppermute(send_up, 'grid', up)  2 us
  transfers between devices with their start and end apart: 11, of which 7 were waited for; matrix products, arithmetic and copies ran while one was open for 10% of the time, Pallas kernels for 0%

profile of v9, /device:TPU:6, one launch (start us, length us, event | category | flops | bytes accessed | tf_op | source)
XLA Modules:
  0.0 91.5 jit_solution(1808344910955669091)
XLA Ops:
  0.0 1.0 %slice_bitcast_fusion.1 = (f32[6,32,128]{2,1,0:T(8,128)S(1)}, f32[6,32,128]{2,1,0:T(8,128)S(1)}) fusion(f32[1,16,32,128]{3,2,1,0:T(8,128)} %param.9), kind=kLoop, calls=%fused_computation.13 | loop fusion | bytes 393216 | tf_op jit(solution)/shard_map/slice | solution.py:262
  1.0 2.0 %collective-permute-start = (f32[6,32,128]{2,1,0:T(8,128)S(1)}, f32[6,32,128]{2,1,0:T(8,128)S(1)}, u32[]{:S(2)}, u32[]{:S(2)}) collective-permute-start(f32[6,32,128]{2,1,0:T(8,128)S(1)} %get-tuple-element.36), channel_id=1, source_target_pairs={{0,16},{16,32},{32,48},{48,64},{64,80},{80,96},{96,112},{112,128},... | collective-permute-start | bytes 294920 | tf_op jit(solution)/shard_map/ppermute | solution.py:255
  3.0 6.7 %collective-permute-start.1 = (f32[6,32,128]{2,1,0:T(8,128)S(1)}, f32[6,32,128]{2,1,0:T(8,128)S(1)}, u32[]{:S(2)}, u32[]{:S(2)}) collective-permute-start(f32[6,32,128]{2,1,0:T(8,128)S(1)} %get-tuple-element.35), channel_id=1, source_target_pairs={{16,0},{32,16},{48,32},{64,48},{80,64},{96,80},{112,96},{128,112},... | collective-permute-start | bytes 294920 | tf_op jit(solution)/shard_map/ppermute | solution.py:256
  10.4 0.9 fusion.3
  11.3 1.9 %collective-permute-start.2 = (bf16[1,2,8,4224]{3,2,1,0:T(8,128)(2,1)S(1)}, bf16[1,2,8,4224]{3,2,1,0:T(8,128)(2,1)S(1)}, u32[]{:S(2)}, u32[]{:S(2)}) collective-permute-start(bf16[1,2,8,4224]{3,2,1,0:T(8,128)(2,1)S(1)} %fusion.3), channel_id=1, source_target_pairs={{0,0},{1,16},{2,32},{3,48},{4,64},{5,80},{6,96},{7,112},{8,128},{9... | collective-permute-start | bytes 405512 | tf_op jit(solution)/shard_map/ppermute | solution.py:200
  14.7 0.9 fusion.1.pick_ref
  15.5 0.8 fusion.place_ref
  17.0 0.9 convert_reduce_fusion.1
  18.0 1.3 %iota_reduce_fusion = (pred[10]{0:T(512)(128)(4,1)}, s32[10]{0:T(128)S(1)}) fusion(s32[16]{0:T(128)S(1)} %stack.79, s32[10]{0:T(128)} %param.13), kind=kLoop, calls=%fused_computation.23 | loop fusion | flops 1210 | bytes 154 | tf_op jit(solution)/shard_map/shards/reduce | solution.py:228
  19.4 6.3 %collective-permute-done.2 = bf16[1,2,8,4224]{3,2,1,0:T(8,128)(2,1)S(1)} collective-permute-done((bf16[1,2,8,4224]{3,2,1,0:T(8,128)(2,1)S(1)}, bf16[1,2,8,4224]{3,2,1,0:T(8,128)(2,1)S(1)}, u32[]{:S(2)}, u32[]{:S(2)}) %collective-permute-start.2) | collective-permute-done | bytes 135200 | tf_op jit(solution)/shard_map/ppermute | solution.py:200
  25.7 1.6 %collective-permute-start.3 = (bf16[2,8,4224]{2,1,0:T(8,128)(2,1)S(1)}, bf16[2,8,4224]{2,1,0:T(8,128)(2,1)S(1)}, u32[]{:S(2)}, u32[]{:S(2)}) collective-permute-start(bf16[2,8,4224]{2,1,0:T(8,128)(2,1)S(1)} %bitcast.36), channel_id=1, source_target_pairs={{0,8},{1,9},{2,10},{3,11},{4,12},{5,13},{6,14},{7,15},{8,0},{9,1},... | collective-permute-start | bytes 405512 | tf_op jit(solution)/shard_map/ppermute | solution.py:223
  27.9 2.8 %collective-permute-done.3 = bf16[2,8,4224]{2,1,0:T(8,128)(2,1)S(1)} collective-permute-done((bf16[2,8,4224]{2,1,0:T(8,128)(2,1)S(1)}, bf16[2,8,4224]{2,1,0:T(8,128)(2,1)S(1)}, u32[]{:S(2)}, u32[]{:S(2)}) %collective-permute-start.3) | collective-permute-done | bytes 135200 | tf_op jit(solution)/shard_map/ppermute | solution.py:223
  31.4 5.9 %collective-permute-done.4 = bf16[4,8,4224]{2,1,0:T(8,128)(2,1)S(1)} collective-permute-done((bf16[4,8,4224]{2,1,0:T(8,128)(2,1)S(1)}, bf16[4,8,4224]{2,1,0:T(8,128)(2,1)S(1)}, u32[]{:S(2)}, u32[]{:S(2)}) %collective-permute-start.4) | collective-permute-done | bytes 270368 | tf_op jit(solution)/shard_map/ppermute | solution.py:223
  37.5 10.5 %collective-permute-done.5 = bf16[8,8,4224]{2,1,0:T(8,128)(2,1)S(1)} collective-permute-done((bf16[8,8,4224]{2,1,0:T(8,128)(2,1)S(1)}, bf16[8,8,4224]{2,1,0:T(8,128)(2,1)S(1)}, u32[]{:S(2)}, u32[]{:S(2)}) %collective-permute-start.5) | collective-permute-done | bytes 540704 | tf_op jit(solution)/shard_map/ppermute | solution.py:223
  48.4 2.6 %collective-permute-done.6 = bf16[16,8,4224]{2,1,0:T(8,128)(2,1)S(1)} collective-permute-done((bf16[16,8,4224]{2,1,0:T(8,128)(2,1)S(1)}, bf16[16,8,4224]{2,1,0:T(8,128)(2,1)S(1)}, u32[]{:S(2)}, u32[]{:S(2)}) %collective-permute-start.6) | collective-permute-done | bytes 1081376 | tf_op jit(solution)/shard_map/ppermute | solution.py:223
  51.9 1.0 %copy.12 = bf16[10,8,32,128]{3,2,1,0:T(8,128)(2,1)} copy(bf16[10,8,32,128]{3,1,2,0:T(8,128)(2,1)S(1)} %slice_bitcast_fusion) | data formatting | bytes 1310720
  53.1 0.8 broadcast_in_dim.36.gain_ref
  53.9 5.5 %shard_map.73 = (f32[16,32,128]{2,1,0:T(8,128)}, f32[6,32,128]{2,1,0:T(8,128)}, f32[6,32,128]{2,1,0:T(8,128)}) custom-call(s32[4]{0:T(128)} %pad_add_fusion.shift_ref, f32[6,32,128]{2,1,0:T(8,128)} %copy-done, f32[16,32,128]{2,1,0:T(8,128)} %bitcast.40, f32[6,32,128]{2,1,0:T(8,128)} %copy-done.1, f32[16,32,128]{2,1,0:T(8,128)} %pot_ref.5, ...), custom_call_target="tpu_custom_call" | custom-call | tf_op jit(solution)/shard_map/pallas_call | solution.py:161
  59.4 7.8 %collective-permute-start.8 = (f32[6,32,128]{2,1,0:T(8,128)}, f32[6,32,128]{2,1,0:T(8,128)S(1)}, u32[]{:S(2)}, u32[]{:S(2)}) collective-permute-start(f32[6,32,128]{2,1,0:T(8,128)} %get-tuple-element.28), channel_id=1, source_target_pairs={{16,0},{32,16},{48,32},{64,48},{80,64},{96,80},{112,96},{128,112},... | collective-permute-start | bytes 294920 | tf_op jit(solution)/shard_map/ppermute | solution.py:256
  67.2 3.2 %collective-permute-done.7.lo_ref = f32[6,32,128]{2,1,0:T(8,128)S(1)} collective-permute-done((f32[6,32,128]{2,1,0:T(8,128)}, f32[6,32,128]{2,1,0:T(8,128)S(1)}, u32[]{:S(2)}, u32[]{:S(2)}) %collective-permute-start.7) | collective-permute-done | bytes 98336 | tf_op jit(solution)/shard_map/ppermute | solution.py:255
  71.1 5.6 %shard_map.74 = (f32[16,32,128]{2,1,0:T(8,128)}, f32[6,32,128]{2,1,0:T(8,128)}, f32[6,32,128]{2,1,0:T(8,128)}) custom-call(s32[4]{0:T(128)} %pad_add_fusion.shift_ref, f32[6,32,128]{2,1,0:T(8,128)} %copy-done.4, f32[16,32,128]{2,1,0:T(8,128)} %get-tuple-element.27.v_ref.rest_0_, f32[6,32,128]{2,1,0:T(8,128)} %copy-done.5, f32[16,32,128]{2,1,0:T(8,128)} %pot_ref.5, ...), custom_call_target="tpu_custom_call" | custom-call | tf_op jit(solution)/shard_map/pallas_call | solution.py:161
  76.7 5.7 %collective-permute-start.10 = (f32[6,32,128]{2,1,0:T(8,128)}, f32[6,32,128]{2,1,0:T(8,128)S(1)}, u32[]{:S(2)}, u32[]{:S(2)}) collective-permute-start(f32[6,32,128]{2,1,0:T(8,128)} %get-tuple-element.31), channel_id=1, source_target_pairs={{16,0},{32,16},{48,32},{64,48},{80,64},{96,80},{112,96},{128,112},... | collective-permute-start | bytes 294920 | tf_op jit(solution)/shard_map/ppermute | solution.py:256
  82.4 2.8 %collective-permute-done.9.lo_ref = f32[6,32,128]{2,1,0:T(8,128)S(1)} collective-permute-done((f32[6,32,128]{2,1,0:T(8,128)}, f32[6,32,128]{2,1,0:T(8,128)S(1)}, u32[]{:S(2)}, u32[]{:S(2)}) %collective-permute-start.9) | collective-permute-done | bytes 98336 | tf_op jit(solution)/shard_map/ppermute | solution.py:255
  85.9 5.6 %shard_map.75 = (f32[16,32,128]{2,1,0:T(8,128)}, f32[6,32,128]{2,1,0:T(8,128)}, f32[6,32,128]{2,1,0:T(8,128)}) custom-call(s32[4]{0:T(128)} %pad_add_fusion.shift_ref, f32[6,32,128]{2,1,0:T(8,128)} %copy-done.2, f32[16,32,128]{2,1,0:T(8,128)} %get-tuple-element.30.v_ref, f32[6,32,128]{2,1,0:T(8,128)} %copy-done.3, f32[16,32,128]{2,1,0:T(8,128)} %pot_ref.5, ...), custom_call_target="tpu_custom_call" | custom-call | tf_op jit(solution)/shard_map/pallas_call | solution.py:161
  (42 shorter events, 5.9 us)
Async XLA Ops:
  1.0 52.1 %collective-permute-start = (f32[6,32,128]{2,1,0:T(8,128)S(1)}, f32[6,32,128]{2,1,0:T(8,128)S(1)}, u32[]{:S(2)}, u32[]{:S(2)}) collective-permute-start(f32[6,32,128]{2,1,0:T(8,128)S(1)} %get-tuple-element.36), channel_id=1, source_target_pairs={{0,16},{16,32},{32,48},{48,64},{64,80},{80,96},{96,112},{112,128},... | collective-permute-start | bytes 294920 | tf_op jit(solution)/shard_map/ppermute | solution.py:255
  3.0 50.2 %collective-permute-start.1 = (f32[6,32,128]{2,1,0:T(8,128)S(1)}, f32[6,32,128]{2,1,0:T(8,128)S(1)}, u32[]{:S(2)}, u32[]{:S(2)}) collective-permute-start(f32[6,32,128]{2,1,0:T(8,128)S(1)} %get-tuple-element.35), channel_id=1, source_target_pairs={{16,0},{32,16},{48,32},{64,48},{80,64},{96,80},{112,96},{128,112},... | collective-permute-start | bytes 294920 | tf_op jit(solution)/shard_map/ppermute | solution.py:256
  11.3 14.4 %collective-permute-start.2 = (bf16[1,2,8,4224]{3,2,1,0:T(8,128)(2,1)S(1)}, bf16[1,2,8,4224]{3,2,1,0:T(8,128)(2,1)S(1)}, u32[]{:S(2)}, u32[]{:S(2)}) collective-permute-start(bf16[1,2,8,4224]{3,2,1,0:T(8,128)(2,1)S(1)} %fusion.3), channel_id=1, source_target_pairs={{0,0},{1,16},{2,32},{3,48},{4,64},{5,80},{6,96},{7,112},{8,128},{9... | collective-permute-start | bytes 405512 | tf_op jit(solution)/shard_map/ppermute | solution.py:200
  25.7 5.0 %collective-permute-start.3 = (bf16[2,8,4224]{2,1,0:T(8,128)(2,1)S(1)}, bf16[2,8,4224]{2,1,0:T(8,128)(2,1)S(1)}, u32[]{:S(2)}, u32[]{:S(2)}) collective-permute-start(bf16[2,8,4224]{2,1,0:T(8,128)(2,1)S(1)} %bitcast.36), channel_id=1, source_target_pairs={{0,8},{1,9},{2,10},{3,11},{4,12},{5,13},{6,14},{7,15},{8,0},{9,1},... | collective-permute-start | bytes 405512 | tf_op jit(solution)/shard_map/ppermute | solution.py:223
  30.8 6.5 %collective-permute-start.4 = (bf16[4,8,4224]{2,1,0:T(8,128)(2,1)S(1)}, bf16[4,8,4224]{2,1,0:T(8,128)(2,1)S(1)}, u32[]{:S(2)}, u32[]{:S(2)}) collective-permute-start(bf16[4,8,4224]{2,1,0:T(8,128)(2,1)S(1)} %pad_maximum_fusion.2), channel_id=1, source_target_pairs={{0,2},{1,3},{2,0},{3,1},{4,6},{5,7},{6,4},{7,5},{8,10},{9,11},{10,... | collective-permute-start | bytes 811016 | tf_op jit(solution)/shard_map/ppermute | solution.py:223
  37.4 10.7 %collective-permute-start.5 = (bf16[8,8,4224]{2,1,0:T(8,128)(2,1)S(1)}, bf16[8,8,4224]{2,1,0:T(8,128)(2,1)S(1)}, u32[]{:S(2)}, u32[]{:S(2)}) collective-permute-start(bf16[8,8,4224]{2,1,0:T(8,128)(2,1)S(1)} %pad_maximum_fusion.1), channel_id=1, source_target_pairs={{0,6},{1,7},{2,4},{3,5},{4,2},{5,3},{6,0},{7,1},{8,14},{9,15},{10,... | collective-permute-start | bytes 1622024 | tf_op jit(solution)/shard_map/ppermute | solution.py:223
  48.2 2.8 %collective-permute-start.6 = (bf16[16,8,4224]{2,1,0:T(8,128)(2,1)S(1)}, bf16[16,8,4224]{2,1,0:T(8,128)(2,1)S(1)}, u32[]{:S(2)}, u32[]{:S(2)}) collective-permute-start(bf16[16,8,4224]{2,1,0:T(8,128)(2,1)S(1)} %pad_maximum_fusion), channel_id=1, source_target_pairs={{0,1},{1,0},{2,3},{3,2},{4,5},{5,4},{6,7},{7,6},{8,9},{9,8},{10,11... | collective-permute-start | bytes 3244040 | tf_op jit(solution)/shard_map/ppermute | solution.py:223
  53.1 0.8 copy-start
  53.1 0.8 copy-start.1
  59.4 11.1 %collective-permute-start.7 = (f32[6,32,128]{2,1,0:T(8,128)}, f32[6,32,128]{2,1,0:T(8,128)S(1)}, u32[]{:S(2)}, u32[]{:S(2)}) collective-permute-start(f32[6,32,128]{2,1,0:T(8,128)} %get-tuple-element.26), channel_id=1, source_target_pairs={{0,16},{16,32},{32,48},{48,64},{64,80},{80,96},{96,112},{112,128},... | collective-permute-start | bytes 294920 | tf_op jit(solution)/shard_map/ppermute | solution.py:255
  59.4 11.1 %collective-permute-start.8 = (f32[6,32,128]{2,1,0:T(8,128)}, f32[6,32,128]{2,1,0:T(8,128)S(1)}, u32[]{:S(2)}, u32[]{:S(2)}) collective-permute-start(f32[6,32,128]{2,1,0:T(8,128)} %get-tuple-element.28), channel_id=1, source_target_pairs={{16,0},{32,16},{48,32},{64,48},{80,64},{96,80},{112,96},{128,112},... | collective-permute-start | bytes 294920 | tf_op jit(solution)/shard_map/ppermute | solution.py:256
  70.5 0.6 copy-start.4
  70.5 0.7 copy-start.5
  76.7 8.4 %collective-permute-start.9 = (f32[6,32,128]{2,1,0:T(8,128)}, f32[6,32,128]{2,1,0:T(8,128)S(1)}, u32[]{:S(2)}, u32[]{:S(2)}) collective-permute-start(f32[6,32,128]{2,1,0:T(8,128)} %get-tuple-element.29), channel_id=1, source_target_pairs={{0,16},{16,32},{32,48},{48,64},{64,80},{80,96},{96,112},{112,128},... | collective-permute-start | bytes 294920 | tf_op jit(solution)/shard_map/ppermute | solution.py:255
  76.7 8.4 %collective-permute-start.10 = (f32[6,32,128]{2,1,0:T(8,128)}, f32[6,32,128]{2,1,0:T(8,128)S(1)}, u32[]{:S(2)}, u32[]{:S(2)}) collective-permute-start(f32[6,32,128]{2,1,0:T(8,128)} %get-tuple-element.31), channel_id=1, source_target_pairs={{16,0},{32,16},{48,32},{64,48},{80,64},{96,80},{112,96},{128,112},... | collective-permute-start | bytes 294920 | tf_op jit(solution)/shard_map/ppermute | solution.py:256
  85.2 0.6 copy-start.2
  85.2 0.7 copy-start.3

commit v10 on v9

--- a/solution.py
+++ b/solution.py
@@ -84,7 +84,7 @@
     sw = second_table(RADIUS)
     fw = first_table(RADIUS)
 
-    def kernel(shift_ref, lo_ref, v_ref, hi_ref, pot_ref, pick_ref, place_ref, proj_ref, gain_ref, *rest):
+    def kernel(shift_ref, lo_ref, v_ref, hi_ref, pot_ref, pick_ref, place_ref, proj_ref, *rest):
         if with_prev:
             prev_ref, out_ref, up_ref, down_ref, pad_ref, rows_ref = rest
         else:
@@ -103,9 +103,10 @@
             here = picked_ref_load(base)
             acc = jnp.zeros((block_rows, depth), jnp.float32)
             for j in range(proj_count):
-                proj = proj_ref[a * proj_count + j].astype(jnp.float32)
+                block = proj_ref[a * proj_count + j].astype(jnp.float32)
+                proj = block[:block_rows]
                 coef = jnp.sum(jnp.sum(proj * here, axis=0, keepdims=True), axis=1, keepdims=True)
-                gain = gain_ref[a * proj_count + j]
+                gain = block[block_rows:]
                 scaled = (coef * gain).astype(jnp.bfloat16).astype(jnp.float32)
                 acc = acc + proj * scaled
             rows_ref[pl.ds(base, block_rows), :] = acc.astype(jnp.bfloat16)
@@ -149,12 +150,12 @@
     return kernel
 
 
-def apply_op(shifts, lo, v, hi, pot, pick, place, proj, gain, prev=None, scale=1.0):
+def apply_op(shifts, lo, v, hi, pot, pick, place, proj, prev=None, scale=1.0):
     planes, breadth, depth = v.shape
     picked_rows = pick.shape[0]
     home_count = proj.shape[0] // 8
     block_rows = picked_rows // home_count
-    args = [shifts, lo, v, hi, pot, pick, place, proj, gain] + ([prev] if prev is not None else [])
+    args = [shifts, lo, v, hi, pot, pick, place, proj] + ([prev] if prev is not None else [])
     vspec = pl.BlockSpec(memory_space=pltpu.VMEM)
     in_specs = [pl.BlockSpec(memory_space=pltpu.SMEM)] + [vspec] * (len(args) - 1)
     rim_shape = jax.ShapeDtypeStruct((RADIUS, breadth, depth), jnp.float32)
@@ -193,9 +194,11 @@
     atom_slot = atom_owner * PAIR_CAP + owner_rank
     local_rows = jnp.where(atom_rows >= 0, atom_rows - tile_index * tile_lines, tile_lines)
 
-    gain_lanes = jnp.zeros((1, slot_pairs, proj_count, 128), jnp.bfloat16)
-    gain_lanes = gain_lanes.at[..., 0].set(proj_gains)
-    packed = jnp.concatenate([projectors, gain_lanes], axis=3)
+    gain_row = jnp.broadcast_to(
+        proj_gains[..., None, None], (1, slot_pairs, proj_count, 1, line_depth)
+    )
+    proj_block = projectors.reshape(1, slot_pairs, proj_count, block_rows, line_depth)
+    packed = jnp.concatenate([proj_block, gain_row], axis=3)
     pairs = [(o * n_states + t, t * n_states + o) for o in range(n_grid) for t in range(n_states)]
     packed = lax.ppermute(packed, ("grid", "states"), pairs)
     def flip_y(s):
@@ -226,19 +229,14 @@
         gathered = jnp.concatenate([gathered, partner], axis=0)
     block_owner = jnp.stack(origins(lax.axis_index("states"), exchanges))
     owner_block = jnp.argmax(block_owner[None, :] == atom_owner[:, None], axis=1)
-    gathered = gathered.reshape(n_states * slot_pairs, proj_count, line_span + 128)
+    gathered = gathered.reshape(n_states * slot_pairs, proj_count, block_rows + 1, line_depth)
     atom_slot = owner_block * PAIR_CAP + owner_rank
     atom_pack = jnp.take(gathered, atom_slot, axis=0)
-    proj_rows = atom_pack[:, :, :line_span].reshape(home_count * proj_count, line_span)
-    atom_gain = atom_pack[:, :, line_span].astype(jnp.float32)
     pick = (
         local_rows.reshape(-1)[:, None] == jnp.arange(tile_lines, dtype=jnp.int32)[None, :]
     ).astype(jnp.bfloat16)
     place = pick.T
-    proj_in = proj_rows.reshape(home_count * proj_count, breadth, line_depth)
-    gain_in = jnp.broadcast_to(
-        atom_gain.reshape(home_count * proj_count, 1, 1), (home_count * proj_count, 1, line_depth)
-    )
+    proj_in = atom_pack.reshape(home_count * proj_count, block_rows + 1, line_depth)
     skew = wrap_rows[0]
     shifts = jnp.stack(
         [
@@ -255,7 +253,7 @@
         low_rim = lax.ppermute(send_up, "grid", up)
         high_rim = lax.ppermute(send_down, "grid", down)
         return apply_op(
-            shifts, low_rim, field, high_rim, potential, pick, place, proj_in, gain_in, prev, scale
+            shifts, low_rim, field, high_rim, potential, pick, place, proj_in, prev, scale
         )
 
     field = states_in[0]

time: 91.8 us -> 98.5 us (1.073)
  local copies, waits for them, and re-layouts: 5.94 us -> 11.7 us
  waiting for transfers between devices: 34.2 us -> 32.7 us
  starting transfers between devices: 26.5 us -> 27.9 us
    ppermute x1, starting transfers between devices: 1.92 us -> 8.12 us  [shards(): packed = lax.ppermute(packed, ('grid', 'states'), pairs)]
    ppermute x4, waiting for transfers between devices: 21.9 us -> 17.8 us  [shards(): lax.ppermute(gathered, 'states', [(s, exchange(s)) for s in range(n_state...]
    ppermute x3, starting transfers between devices: 20.1 us -> 16.4 us  [step(): high_rim = lax.ppermute(send_down, 'grid', down)]
    ppermute x1, waiting for transfers between devices: 6.33 us -> 8.73 us  [shards(): packed = lax.ppermute(packed, ('grid', 'states'), pairs)]
    gather x1 -> x2, local copies, waits for them, and re-layouts: 0.63 us -> 2.43 us  [shards(): atom_pack = jnp.take(gathered, atom_slot, axis=0)]
    unnamed x19 -> x18, local copies, waits for them, and re-layouts: 3.21 us -> 4.86 us
    ppermute x3, starting transfers between devices: 2 us -> 0.48 us  [step(): low_rim = lax.ppermute(send_up, 'grid', up)]
  transfers between devices with their start and end apart: 11 -> 11, of which waited for: 7 -> 5; matrix products, arithmetic and copies ran while one was open for 10% -> 16% of each run, Pallas kernels for 0% -> 0%
where the time goes in v10:
time: 98.5 us; the launch traced here: 98.1 us
  waiting for transfers between devices  32.7 us (33%)
  starting transfers between devices  27.9 us (28%)
  Pallas kernels  16.9 us (17%)
  local copies, waits for them, and re-layouts  11.7 us (12%)
  other arithmetic  7.42 us (8%)
  between operations  1.52 us (2%)
    ppermute x4, waiting for transfers between devices, shards(): lax.ppermute(gathered, 'states', [(s, exchange(s)) for s in range(n_state...  17.8 us
    pallas_call x3, Pallas kernels, apply_op(): pl.pallas_call(make_kernel(scale, prev is not None, home_count, proj.shap...  16.9 us
    ppermute x3, starting transfers between devices, step(): high_rim = lax.ppermute(send_down, 'grid', down)  16.4 us
    ppermute x1, waiting for transfers between devices, shards(): packed = lax.ppermute(packed, ('grid', 'states'), pairs)  8.73 us
    ppermute x1, starting transfers between devices, shards(): packed = lax.ppermute(packed, ('grid', 'states'), pairs)  8.12 us
    ppermute x3, waiting for transfers between devices, step(): low_rim = lax.ppermute(send_up, 'grid', up)  6.17 us
    unnamed x18, local copies, waits for them, and re-layouts  4.86 us
    ppermute x4, starting transfers between devices, shards(): lax.ppermute(gathered, 'states', [(s, exchange(s)) for s in range(n_state...  2.87 us
  transfers between devices with their start and end apart: 11, of which 5 were waited for; matrix products, arithmetic and copies ran while one was open for 16% of the time, Pallas kernels for 0%

profile of v10, /device:TPU:6, one launch (start us, length us, event | category | flops | bytes accessed | tf_op | source)
XLA Modules:
  0.0 98.1 jit_solution(6611789977736962591)
XLA Ops:
  0.0 0.7 broadcast_in_dim.43
  0.7 0.9 pad_maximum_fusion.3
  1.7 8.1 %collective-permute-start.2 = (bf16[1,2,8,33,128]{4,2,3,1,0:T(8,128)(2,1)S(1)}, bf16[1,2,8,33,128]{4,2,3,1,0:T(8,128)(2,1)S(1)}, u32[]{:S(2)}, u32[]{:S(2)}) collective-permute-start(bf16[1,2,8,33,128]{4,2,3,1,0:T(8,128)(2,1)S(1)} %pad_maximum_fusion.3), channel_id=1, source_target_pairs={{0,0},{1,16},{2,32},{3,48},{4,64},{5,80},{6,96},{7,112},{8,128},{9... | collective-permute-start | bytes 405512 | tf_op jit(solution)/shard_map/ppermute | solution.py:203
  9.8 8.7 %collective-permute-done.2 = bf16[1,2,8,33,128]{4,2,3,1,0:T(8,128)(2,1)S(1)} collective-permute-done((bf16[1,2,8,33,128]{4,2,3,1,0:T(8,128)(2,1)S(1)}, bf16[1,2,8,33,128]{4,2,3,1,0:T(8,128)(2,1)S(1)}, u32[]{:S(2)}, u32[]{:S(2)}) %collective-permute-start.2) | collective-permute-done | bytes 135200 | tf_op jit(solution)/shard_map/ppermute | solution.py:203
  18.5 2.6 %collective-permute-start.3 = (bf16[2,8,33,128]{3,1,2,0:T(8,128)(2,1)S(1)}, bf16[2,8,33,128]{3,1,2,0:T(8,128)(2,1)S(1)}, u32[]{:S(2)}, u32[]{:S(2)}) collective-permute-start(bf16[2,8,33,128]{3,1,2,0:T(8,128)(2,1)S(1)} %bitcast.32), channel_id=1, source_target_pairs={{0,8},{1,9},{2,10},{3,11},{4,12},{5,13},{6,14},{7,15},{8,0},{9,1},... | collective-permute-start | bytes 405512 | tf_op jit(solution)/shard_map/ppermute | solution.py:226
  21.1 1.6 %slice_bitcast_fusion = (f32[6,32,128]{2,1,0:T(8,128)S(1)}, f32[6,32,128]{2,1,0:T(8,128)}) fusion(f32[1,16,32,128]{3,2,1,0:T(8,128)} %param.7), kind=kLoop, calls=%fused_computation.10 | loop fusion | bytes 393216 | tf_op jit(solution)/shard_map/slice | solution.py:260
  23.2 5.2 %collective-permute-start.1 = (f32[6,32,128]{2,1,0:T(8,128)S(1)}, f32[6,32,128]{2,1,0:T(8,128)S(1)}, u32[]{:S(2)}, u32[]{:S(2)}) collective-permute-start(f32[6,32,128]{2,1,0:T(8,128)S(1)} %get-tuple-element.23), channel_id=1, source_target_pairs={{16,0},{32,16},{48,32},{64,48},{80,64},{96,80},{112,96},{128,112},... | collective-permute-start | bytes 294920 | tf_op jit(solution)/shard_map/ppermute | solution.py:254
  28.5 0.9 convert_reduce_fusion
  30.9 1.4 %iota_reduce_fusion = (pred[10]{0:T(512)(128)(4,1)}, s32[10]{0:T(128)S(1)}) fusion(s32[16]{0:T(128)S(1)} %stack.79, s32[10]{0:T(128)} %param.11), kind=kLoop, calls=%fused_computation.19 | loop fusion | flops 1210 | bytes 154 | tf_op jit(solution)/shard_map/shards/reduce | solution.py:231
  32.3 4.2 %collective-permute-done.4 = bf16[4,8,33,128]{3,1,2,0:T(8,128)(2,1)S(1)} collective-permute-done((bf16[4,8,33,128]{3,1,2,0:T(8,128)(2,1)S(1)}, bf16[4,8,33,128]{3,1,2,0:T(8,128)(2,1)S(1)}, u32[]{:S(2)}, u32[]{:S(2)}) %collective-permute-start.4) | collective-permute-done | bytes 270368 | tf_op jit(solution)/shard_map/ppermute | solution.py:226
  37.3 13.6 %collective-permute-done.5 = bf16[8,8,33,128]{3,1,2,0:T(8,128)(2,1)S(1)} collective-permute-done((bf16[8,8,33,128]{3,1,2,0:T(8,128)(2,1)S(1)}, bf16[8,8,33,128]{3,1,2,0:T(8,128)(2,1)S(1)}, u32[]{:S(2)}, u32[]{:S(2)}) %collective-permute-start.5) | collective-permute-done | bytes 540704 | tf_op jit(solution)/shard_map/ppermute | solution.py:226
  52.6 0.9 fusion.1.pick_ref
  53.5 0.9 fusion.place_ref
  56.4 0.8 constant_dynamic-update-slice_fusion.1
  57.2 1.1 %constant_dynamic-update-slice_fusion = bf16[32,8,33,128]{3,1,2,0:T(8,128)(2,1)} fusion(bf16[32,8,33,128]{3,1,2,0:T(8,128)(2,1)} %constant_dynamic-update-slice_fusion.1, bf16[16,8,33,128]{3,1,2,0:T(8,128)(2,1)S(1)} %collective-permute-done.6), kind=kLoop, calls=%fused_computation.12 | loop fusion | bytes 2162688 | tf_op jit(solution)/shard_map/concatenate | solution.py:229
  58.3 2.3 %gather_fusion = bf16[10,8,33,128]{3,1,2,0:T(8,128)(2,1)S(1)} fusion(bf16[32,8,33,128]{3,1,2,0:T(8,128)(2,1)} %constant_dynamic-update-slice_fusion, s32[1024]{0:T(1024)S(1)} %pad_clamp_fusion), kind=kCustom, calls=%fused_computation | custom fusion | bytes 1351720 | tf_op jit(solution)/shard_map/jit(_take)/gather | solution.py:234
  60.7 1.1 %bitcast_select_fusion.proj_ref = bf16[80,33,128]{2,1,0:T(8,128)(2,1)} fusion(bf16[10,8,33,128]{3,2,1,0:T(8,128)(2,1)S(1)} %copy.9, pred[80]{0:T(512)(128)(4,1)S(1)} %broadcast_in_dim.40), kind=kLoop, calls=%fused_computation.2 | loop fusion | flops 337920 | bytes 1351760 | tf_op jit(solution)/shard_map/jit(_take)/select_n | solution.py:234
  62.5 5.6 %shard_map.73 = (f32[16,32,128]{2,1,0:T(8,128)}, f32[6,32,128]{2,1,0:T(8,128)}, f32[6,32,128]{2,1,0:T(8,128)}) custom-call(s32[4]{0:T(128)} %pad_add_fusion.shift_ref, f32[6,32,128]{2,1,0:T(8,128)} %copy-done, f32[16,32,128]{2,1,0:T(8,128)} %bitcast.36, f32[6,32,128]{2,1,0:T(8,128)} %copy-done.1, f32[16,32,128]{2,1,0:T(8,128)} %pot_ref.5, ...), custom_call_target="tpu_custom_call" | custom-call | tf_op jit(solution)/shard_map/pallas_call | solution.py:162
  68.1 5.6 %collective-permute-start.8 = (f32[6,32,128]{2,1,0:T(8,128)}, f32[6,32,128]{2,1,0:T(8,128)S(1)}, u32[]{:S(2)}, u32[]{:S(2)}) collective-permute-start(f32[6,32,128]{2,1,0:T(8,128)} %get-tuple-element.16), channel_id=1, source_target_pairs={{16,0},{32,16},{48,32},{64,48},{80,64},{96,80},{112,96},{128,112},... | collective-permute-start | bytes 294920 | tf_op jit(solution)/shard_map/ppermute | solution.py:254
  73.7 3.4 %collective-permute-done.7.lo_ref = f32[6,32,128]{2,1,0:T(8,128)S(1)} collective-permute-done((f32[6,32,128]{2,1,0:T(8,128)}, f32[6,32,128]{2,1,0:T(8,128)S(1)}, u32[]{:S(2)}, u32[]{:S(2)}) %collective-permute-start.7) | collective-permute-done | bytes 98336 | tf_op jit(solution)/shard_map/ppermute | solution.py:253
  77.7 5.6 %shard_map.74 = (f32[16,32,128]{2,1,0:T(8,128)}, f32[6,32,128]{2,1,0:T(8,128)}, f32[6,32,128]{2,1,0:T(8,128)}) custom-call(s32[4]{0:T(128)} %pad_add_fusion.shift_ref, f32[6,32,128]{2,1,0:T(8,128)} %copy-done.4, f32[16,32,128]{2,1,0:T(8,128)} %get-tuple-element.15.v_ref.rest_0_, f32[6,32,128]{2,1,0:T(8,128)} %copy-done.5, f32[16,32,128]{2,1,0:T(8,128)} %pot_ref.5, ...), custom_call_target="tpu_custom_call" | custom-call | tf_op jit(solution)/shard_map/pallas_call | solution.py:162
  83.4 5.6 %collective-permute-start.10 = (f32[6,32,128]{2,1,0:T(8,128)}, f32[6,32,128]{2,1,0:T(8,128)S(1)}, u32[]{:S(2)}, u32[]{:S(2)}) collective-permute-start(f32[6,32,128]{2,1,0:T(8,128)} %get-tuple-element.19), channel_id=1, source_target_pairs={{16,0},{32,16},{48,32},{64,48},{80,64},{96,80},{112,96},{128,112},... | collective-permute-start | bytes 294920 | tf_op jit(solution)/shard_map/ppermute | solution.py:254
  89.0 2.8 %collective-permute-done.9.lo_ref = f32[6,32,128]{2,1,0:T(8,128)S(1)} collective-permute-done((f32[6,32,128]{2,1,0:T(8,128)}, f32[6,32,128]{2,1,0:T(8,128)S(1)}, u32[]{:S(2)}, u32[]{:S(2)}) %collective-permute-start.9) | collective-permute-done | bytes 98336 | tf_op jit(solution)/shard_map/ppermute | solution.py:253
  92.5 5.6 %shard_map.75 = (f32[16,32,128]{2,1,0:T(8,128)}, f32[6,32,128]{2,1,0:T(8,128)}, f32[6,32,128]{2,1,0:T(8,128)}) custom-call(s32[4]{0:T(128)} %pad_add_fusion.shift_ref, f32[6,32,128]{2,1,0:T(8,128)} %copy-done.2, f32[16,32,128]{2,1,0:T(8,128)} %get-tuple-element.18.v_ref, f32[6,32,128]{2,1,0:T(8,128)} %copy-done.3, f32[16,32,128]{2,1,0:T(8,128)} %pot_ref.5, ...), custom_call_target="tpu_custom_call" | custom-call | tf_op jit(solution)/shard_map/pallas_call | solution.py:162
  (42 shorter events, 7.3 us)
Async XLA Ops:
  0.0 37.3 %copy-start.6 = (s32[10,32]{1,0:T(8,128)S(1)}, s32[10,32]{1,0:T(8,128)}, u32[]{:S(2)}) copy-start(s32[10,32]{1,0:T(8,128)} %param.12) | copy-start | bytes 3844
  1.7 16.9 %collective-permute-start.2 = (bf16[1,2,8,33,128]{4,2,3,1,0:T(8,128)(2,1)S(1)}, bf16[1,2,8,33,128]{4,2,3,1,0:T(8,128)(2,1)S(1)}, u32[]{:S(2)}, u32[]{:S(2)}) collective-permute-start(bf16[1,2,8,33,128]{4,2,3,1,0:T(8,128)(2,1)S(1)} %pad_maximum_fusion.3), channel_id=1, source_target_pairs={{0,0},{1,16},{2,32},{3,48},{4,64},{5,80},{6,96},{7,112},{8,128},{9... | collective-permute-start | bytes 405512 | tf_op jit(solution)/shard_map/ppermute | solution.py:203
  18.5 9.8 %collective-permute-start.3 = (bf16[2,8,33,128]{3,1,2,0:T(8,128)(2,1)S(1)}, bf16[2,8,33,128]{3,1,2,0:T(8,128)(2,1)S(1)}, u32[]{:S(2)}, u32[]{:S(2)}) collective-permute-start(bf16[2,8,33,128]{3,1,2,0:T(8,128)(2,1)S(1)} %bitcast.32), channel_id=1, source_target_pairs={{0,8},{1,9},{2,10},{3,11},{4,12},{5,13},{6,14},{7,15},{8,0},{9,1},... | collective-permute-start | bytes 405512 | tf_op jit(solution)/shard_map/ppermute | solution.py:226
  22.7 39.1 %collective-permute-start = (f32[6,32,128]{2,1,0:T(8,128)}, f32[6,32,128]{2,1,0:T(8,128)S(1)}, u32[]{:S(2)}, u32[]{:S(2)}) collective-permute-start(f32[6,32,128]{2,1,0:T(8,128)} %get-tuple-element.24), channel_id=1, source_target_pairs={{0,16},{16,32},{32,48},{48,64},{64,80},{80,96},{96,112},{112,128},... | collective-permute-start | bytes 294920 | tf_op jit(solution)/shard_map/ppermute | solution.py:253
  23.2 38.6 %collective-permute-start.1 = (f32[6,32,128]{2,1,0:T(8,128)S(1)}, f32[6,32,128]{2,1,0:T(8,128)S(1)}, u32[]{:S(2)}, u32[]{:S(2)}) collective-permute-start(f32[6,32,128]{2,1,0:T(8,128)S(1)} %get-tuple-element.23), channel_id=1, source_target_pairs={{16,0},{32,16},{48,32},{64,48},{80,64},{96,80},{112,96},{128,112},... | collective-permute-start | bytes 294920 | tf_op jit(solution)/shard_map/ppermute | solution.py:254
  28.4 8.2 %collective-permute-start.4 = (bf16[4,8,33,128]{3,1,2,0:T(8,128)(2,1)S(1)}, bf16[4,8,33,128]{3,1,2,0:T(8,128)(2,1)S(1)}, u32[]{:S(2)}, u32[]{:S(2)}) collective-permute-start(bf16[4,8,33,128]{3,1,2,0:T(8,128)(2,1)S(1)} %pad_maximum_fusion.2), channel_id=1, source_target_pairs={{0,2},{1,3},{2,0},{3,1},{4,6},{5,7},{6,4},{7,5},{8,10},{9,11},{10,... | collective-permute-start | bytes 811016 | tf_op jit(solution)/shard_map/ppermute | solution.py:226
  36.6 14.3 %collective-permute-start.5 = (bf16[8,8,33,128]{3,1,2,0:T(8,128)(2,1)S(1)}, bf16[8,8,33,128]{3,1,2,0:T(8,128)(2,1)S(1)}, u32[]{:S(2)}, u32[]{:S(2)}) collective-permute-start(bf16[8,8,33,128]{3,1,2,0:T(8,128)(2,1)S(1)} %pad_maximum_fusion.1), channel_id=1, source_target_pairs={{0,6},{1,7},{2,4},{3,5},{4,2},{5,3},{6,0},{7,1},{8,14},{9,15},{10,... | collective-permute-start | bytes 1622024 | tf_op jit(solution)/shard_map/ppermute | solution.py:226
  51.0 6.2 %collective-permute-start.6 = (bf16[16,8,33,128]{3,1,2,0:T(8,128)(2,1)S(1)}, bf16[16,8,33,128]{3,1,2,0:T(8,128)(2,1)S(1)}, u32[]{:S(2)}, u32[]{:S(2)}) collective-permute-start(bf16[16,8,33,128]{3,1,2,0:T(8,128)(2,1)S(1)} %pad_maximum_fusion), channel_id=1, source_target_pairs={{0,1},{1,0},{2,3},{3,2},{4,5},{5,4},{6,7},{7,6},{8,9},{9,8},{10,11... | collective-permute-start | bytes 3244040 | tf_op jit(solution)/shard_map/ppermute | solution.py:226
  61.8 0.6 copy-start
  61.8 0.7 copy-start.1
  68.1 9.0 %collective-permute-start.7 = (f32[6,32,128]{2,1,0:T(8,128)}, f32[6,32,128]{2,1,0:T(8,128)S(1)}, u32[]{:S(2)}, u32[]{:S(2)}) collective-permute-start(f32[6,32,128]{2,1,0:T(8,128)} %get-tuple-element.14), channel_id=1, source_target_pairs={{0,16},{16,32},{32,48},{48,64},{64,80},{80,96},{96,112},{112,128},... | collective-permute-start | bytes 294920 | tf_op jit(solution)/shard_map/ppermute | solution.py:253
  68.1 9.0 %collective-permute-start.8 = (f32[6,32,128]{2,1,0:T(8,128)}, f32[6,32,128]{2,1,0:T(8,128)S(1)}, u32[]{:S(2)}, u32[]{:S(2)}) collective-permute-start(f32[6,32,128]{2,1,0:T(8,128)} %get-tuple-element.16), channel_id=1, source_target_pairs={{16,0},{32,16},{48,32},{64,48},{80,64},{96,80},{112,96},{128,112},... | collective-permute-start | bytes 294920 | tf_op jit(solution)/shard_map/ppermute | solution.py:254
  77.1 0.6 copy-start.4
  77.1 0.7 copy-start.5
  83.4 8.4 %collective-permute-start.9 = (f32[6,32,128]{2,1,0:T(8,128)}, f32[6,32,128]{2,1,0:T(8,128)S(1)}, u32[]{:S(2)}, u32[]{:S(2)}) collective-permute-start(f32[6,32,128]{2,1,0:T(8,128)} %get-tuple-element.17), channel_id=1, source_target_pairs={{0,16},{16,32},{32,48},{48,64},{64,80},{80,96},{96,112},{112,128},... | collective-permute-start | bytes 294920 | tf_op jit(solution)/shard_map/ppermute | solution.py:253
  83.4 8.4 %collective-permute-start.10 = (f32[6,32,128]{2,1,0:T(8,128)}, f32[6,32,128]{2,1,0:T(8,128)S(1)}, u32[]{:S(2)}, u32[]{:S(2)}) collective-permute-start(f32[6,32,128]{2,1,0:T(8,128)} %get-tuple-element.19), channel_id=1, source_target_pairs={{16,0},{32,16},{48,32},{64,48},{80,64},{96,80},{112,96},{128,112},... | collective-permute-start | bytes 294920 | tf_op jit(solution)/shard_map/ppermute | solution.py:254
  91.8 0.6 copy-start.2
  91.8 0.7 copy-start.3

commit v11 on v9

--- a/solution.py
+++ b/solution.py
@@ -116,7 +116,7 @@
         def picked_ref_load(base):
             return rows_ref[pl.ds(base, block_rows), :].astype(jnp.float32)
 
-        lax.fori_loop(0, home_count, one_atom, 0)
+        lax.fori_loop(0, home_count, one_atom, 0, unroll=True)
         nonlocal_lines = jnp.dot(place_ref[...], rows_ref[...], preferred_element_type=jnp.float32)
         nonlocal_lines = nonlocal_lines.reshape(planes, breadth, depth)
 

time: 91.8 us -> 87.6 us (0.954)
  Pallas kernels: 16.7 us -> 12.5 us
    pallas_call x3, Pallas kernels: 16.7 us -> 12.5 us  [apply_op(): pl.pallas_call(make_kernel(scale, prev is not None, home_count, proj.shap...]
  transfers between devices with their start and end apart: 11 -> 11, of which waited for: 7 -> 7; matrix products, arithmetic and copies ran while one was open for 10% -> 11% of each run, Pallas kernels for 0% -> 0%
where the time goes in v11:
time: 87.6 us; the launch traced here: 87.2 us
  waiting for transfers between devices  34.2 us (39%)
  starting transfers between devices  26.5 us (30%)
  Pallas kernels  12.5 us (14%)
  other arithmetic  6.63 us (8%)
  local copies, waits for them, and re-layouts  5.94 us (7%)
  between operations  1.47 us (2%)
    ppermute x4, waiting for transfers between devices, shards(): lax.ppermute(gathered, 'states', [(s, exchange(s)) for s in range(n_state...  21.9 us
    ppermute x3, starting transfers between devices, step(): high_rim = lax.ppermute(send_down, 'grid', down)  20.1 us
    pallas_call x3, Pallas kernels, apply_op(): pl.pallas_call(make_kernel(scale, prev is not None, home_count, proj.shap...  12.5 us
    ppermute x1, waiting for transfers between devices, shards(): packed = lax.ppermute(packed, ('grid', 'states'), pairs)  6.33 us
    ppermute x3, waiting for transfers between devices, step(): low_rim = lax.ppermute(send_up, 'grid', up)  6.03 us
    unnamed x19, local copies, waits for them, and re-layouts  3.21 us
    ppermute x4, starting transfers between devices, shards(): lax.ppermute(gathered, 'states', [(s, exchange(s)) for s in range(n_state...  2.42 us
    ppermute x3, starting transfers between devices, step(): low_rim = lax.ppermute(send_up, 'grid', up)  2 us
  transfers between devices with their start and end apart: 11, of which 7 were waited for; matrix products, arithmetic and copies ran while one was open for 11% of the time, Pallas kernels for 0%

profile of v11, /device:TPU:6, one launch (start us, length us, event | category | flops | bytes accessed | tf_op | source)
XLA Modules:
  0.0 87.2 jit_solution(17261883075937281680)
XLA Ops:
  0.0 1.0 %slice_bitcast_fusion.1 = (f32[6,32,128]{2,1,0:T(8,128)S(1)}, f32[6,32,128]{2,1,0:T(8,128)S(1)}) fusion(f32[1,16,32,128]{3,2,1,0:T(8,128)} %param.9), kind=kLoop, calls=%fused_computation.13 | loop fusion | bytes 393216 | tf_op jit(solution)/shard_map/slice | solution.py:262
  1.0 2.0 %collective-permute-start = (f32[6,32,128]{2,1,0:T(8,128)S(1)}, f32[6,32,128]{2,1,0:T(8,128)S(1)}, u32[]{:S(2)}, u32[]{:S(2)}) collective-permute-start(f32[6,32,128]{2,1,0:T(8,128)S(1)} %get-tuple-element.36), channel_id=1, source_target_pairs={{0,16},{16,32},{32,48},{48,64},{64,80},{80,96},{96,112},{112,128},... | collective-permute-start | bytes 294920 | tf_op jit(solution)/shard_map/ppermute | solution.py:255
  3.0 6.7 %collective-permute-start.1 = (f32[6,32,128]{2,1,0:T(8,128)S(1)}, f32[6,32,128]{2,1,0:T(8,128)S(1)}, u32[]{:S(2)}, u32[]{:S(2)}) collective-permute-start(f32[6,32,128]{2,1,0:T(8,128)S(1)} %get-tuple-element.35), channel_id=1, source_target_pairs={{16,0},{32,16},{48,32},{64,48},{80,64},{96,80},{112,96},{128,112},... | collective-permute-start | bytes 294920 | tf_op jit(solution)/shard_map/ppermute | solution.py:256
  10.4 0.9 %fusion.3 = bf16[1,2,8,4224]{3,2,1,0:T(8,128)(2,1)S(1)} fusion(bf16[1,2,8,1]{3,2,1,0:T(8,128)(2,1)S(1)} %copy.11, bf16[1,2,8,4096]{3,2,1,0:T(8,128)(2,1)} %param.11), kind=kLoop, calls=%fused_computation.12 | loop fusion | flops 405504 | bytes 266272 | tf_op jit(solution)/shard_map/concatenate | solution.py:198
  11.3 1.9 %collective-permute-start.2 = (bf16[1,2,8,4224]{3,2,1,0:T(8,128)(2,1)S(1)}, bf16[1,2,8,4224]{3,2,1,0:T(8,128)(2,1)S(1)}, u32[]{:S(2)}, u32[]{:S(2)}) collective-permute-start(bf16[1,2,8,4224]{3,2,1,0:T(8,128)(2,1)S(1)} %fusion.3), channel_id=1, source_target_pairs={{0,0},{1,16},{2,32},{3,48},{4,64},{5,80},{6,96},{7,112},{8,128},{9... | collective-permute-start | bytes 405512 | tf_op jit(solution)/shard_map/ppermute | solution.py:200
  14.7 0.9 fusion.1.pick_ref
  15.5 0.8 fusion.place_ref
  17.0 0.9 %convert_reduce_fusion.1 = s32[10]{0:T(128)S(1)} fusion(s32[10]{0:T(128)} %param.13), kind=kLoop, calls=%fused_computation.21 | loop fusion | flops 490 | bytes 80 | tf_op jit(solution)/shard_map/reduce_sum | solution.py:192
  18.0 1.3 %iota_reduce_fusion = (pred[10]{0:T(512)(128)(4,1)}, s32[10]{0:T(128)S(1)}) fusion(s32[16]{0:T(128)S(1)} %stack.79, s32[10]{0:T(128)} %param.13), kind=kLoop, calls=%fused_computation.23 | loop fusion | flops 1210 | bytes 154 | tf_op jit(solution)/shard_map/shards/reduce | solution.py:228
  19.4 6.3 %collective-permute-done.2 = bf16[1,2,8,4224]{3,2,1,0:T(8,128)(2,1)S(1)} collective-permute-done((bf16[1,2,8,4224]{3,2,1,0:T(8,128)(2,1)S(1)}, bf16[1,2,8,4224]{3,2,1,0:T(8,128)(2,1)S(1)}, u32[]{:S(2)}, u32[]{:S(2)}) %collective-permute-start.2) | collective-permute-done | bytes 135200 | tf_op jit(solution)/shard_map/ppermute | solution.py:200
  25.7 1.6 %collective-permute-start.3 = (bf16[2,8,4224]{2,1,0:T(8,128)(2,1)S(1)}, bf16[2,8,4224]{2,1,0:T(8,128)(2,1)S(1)}, u32[]{:S(2)}, u32[]{:S(2)}) collective-permute-start(bf16[2,8,4224]{2,1,0:T(8,128)(2,1)S(1)} %bitcast.36), channel_id=1, source_target_pairs={{0,8},{1,9},{2,10},{3,11},{4,12},{5,13},{6,14},{7,15},{8,0},{9,1},... | collective-permute-start | bytes 405512 | tf_op jit(solution)/shard_map/ppermute | solution.py:223
  27.9 2.8 %collective-permute-done.3 = bf16[2,8,4224]{2,1,0:T(8,128)(2,1)S(1)} collective-permute-done((bf16[2,8,4224]{2,1,0:T(8,128)(2,1)S(1)}, bf16[2,8,4224]{2,1,0:T(8,128)(2,1)S(1)}, u32[]{:S(2)}, u32[]{:S(2)}) %collective-permute-start.3) | collective-permute-done | bytes 135200 | tf_op jit(solution)/shard_map/ppermute | solution.py:223
  31.4 5.9 %collective-permute-done.4 = bf16[4,8,4224]{2,1,0:T(8,128)(2,1)S(1)} collective-permute-done((bf16[4,8,4224]{2,1,0:T(8,128)(2,1)S(1)}, bf16[4,8,4224]{2,1,0:T(8,128)(2,1)S(1)}, u32[]{:S(2)}, u32[]{:S(2)}) %collective-permute-start.4) | collective-permute-done | bytes 270368 | tf_op jit(solution)/shard_map/ppermute | solution.py:223
  37.5 10.5 %collective-permute-done.5 = bf16[8,8,4224]{2,1,0:T(8,128)(2,1)S(1)} collective-permute-done((bf16[8,8,4224]{2,1,0:T(8,128)(2,1)S(1)}, bf16[8,8,4224]{2,1,0:T(8,128)(2,1)S(1)}, u32[]{:S(2)}, u32[]{:S(2)}) %collective-permute-start.5) | collective-permute-done | bytes 540704 | tf_op jit(solution)/shard_map/ppermute | solution.py:223
  48.4 2.6 %collective-permute-done.6 = bf16[16,8,4224]{2,1,0:T(8,128)(2,1)S(1)} collective-permute-done((bf16[16,8,4224]{2,1,0:T(8,128)(2,1)S(1)}, bf16[16,8,4224]{2,1,0:T(8,128)(2,1)S(1)}, u32[]{:S(2)}, u32[]{:S(2)}) %collective-permute-start.6) | collective-permute-done | bytes 1081376 | tf_op jit(solution)/shard_map/ppermute | solution.py:223
  51.9 1.0 %copy.12 = bf16[10,8,32,128]{3,2,1,0:T(8,128)(2,1)} copy(bf16[10,8,32,128]{3,1,2,0:T(8,128)(2,1)S(1)} %slice_bitcast_fusion) | data formatting | bytes 1310720
  53.1 0.8 broadcast_in_dim.36.gain_ref
  53.9 4.1 %shard_map.73 = (f32[16,32,128]{2,1,0:T(8,128)}, f32[6,32,128]{2,1,0:T(8,128)}, f32[6,32,128]{2,1,0:T(8,128)}) custom-call(s32[4]{0:T(128)} %pad_add_fusion.shift_ref, f32[6,32,128]{2,1,0:T(8,128)} %copy-done, f32[16,32,128]{2,1,0:T(8,128)} %bitcast.40, f32[6,32,128]{2,1,0:T(8,128)} %copy-done.1, f32[16,32,128]{2,1,0:T(8,128)} %pot_ref.5, ...), custom_call_target="tpu_custom_call" | custom-call | tf_op jit(solution)/shard_map/pallas_call | solution.py:161
  58.0 7.8 %collective-permute-start.8 = (f32[6,32,128]{2,1,0:T(8,128)}, f32[6,32,128]{2,1,0:T(8,128)S(1)}, u32[]{:S(2)}, u32[]{:S(2)}) collective-permute-start(f32[6,32,128]{2,1,0:T(8,128)} %get-tuple-element.28), channel_id=1, source_target_pairs={{16,0},{32,16},{48,32},{64,48},{80,64},{96,80},{112,96},{128,112},... | collective-permute-start | bytes 294920 | tf_op jit(solution)/shard_map/ppermute | solution.py:256
  65.8 3.2 %collective-permute-done.7.lo_ref = f32[6,32,128]{2,1,0:T(8,128)S(1)} collective-permute-done((f32[6,32,128]{2,1,0:T(8,128)}, f32[6,32,128]{2,1,0:T(8,128)S(1)}, u32[]{:S(2)}, u32[]{:S(2)}) %collective-permute-start.7) | collective-permute-done | bytes 98336 | tf_op jit(solution)/shard_map/ppermute | solution.py:255
  69.7 4.2 %shard_map.74 = (f32[16,32,128]{2,1,0:T(8,128)}, f32[6,32,128]{2,1,0:T(8,128)}, f32[6,32,128]{2,1,0:T(8,128)}) custom-call(s32[4]{0:T(128)} %pad_add_fusion.shift_ref, f32[6,32,128]{2,1,0:T(8,128)} %copy-done.4, f32[16,32,128]{2,1,0:T(8,128)} %get-tuple-element.27.v_ref.rest_0_, f32[6,32,128]{2,1,0:T(8,128)} %copy-done.5, f32[16,32,128]{2,1,0:T(8,128)} %pot_ref.5, ...), custom_call_target="tpu_custom_call" | custom-call | tf_op jit(solution)/shard_map/pallas_call | solution.py:161
  73.9 5.6 %collective-permute-start.10 = (f32[6,32,128]{2,1,0:T(8,128)}, f32[6,32,128]{2,1,0:T(8,128)S(1)}, u32[]{:S(2)}, u32[]{:S(2)}) collective-permute-start(f32[6,32,128]{2,1,0:T(8,128)} %get-tuple-element.31), channel_id=1, source_target_pairs={{16,0},{32,16},{48,32},{64,48},{80,64},{96,80},{112,96},{128,112},... | collective-permute-start | bytes 294920 | tf_op jit(solution)/shard_map/ppermute | solution.py:256
  79.6 2.8 %collective-permute-done.9.lo_ref = f32[6,32,128]{2,1,0:T(8,128)S(1)} collective-permute-done((f32[6,32,128]{2,1,0:T(8,128)}, f32[6,32,128]{2,1,0:T(8,128)S(1)}, u32[]{:S(2)}, u32[]{:S(2)}) %collective-permute-start.9) | collective-permute-done | bytes 98336 | tf_op jit(solution)/shard_map/ppermute | solution.py:255
  83.0 4.2 %shard_map.75 = (f32[16,32,128]{2,1,0:T(8,128)}, f32[6,32,128]{2,1,0:T(8,128)}, f32[6,32,128]{2,1,0:T(8,128)}) custom-call(s32[4]{0:T(128)} %pad_add_fusion.shift_ref, f32[6,32,128]{2,1,0:T(8,128)} %copy-done.2, f32[16,32,128]{2,1,0:T(8,128)} %get-tuple-element.30.v_ref, f32[6,32,128]{2,1,0:T(8,128)} %copy-done.3, f32[16,32,128]{2,1,0:T(8,128)} %pot_ref.5, ...), custom_call_target="tpu_custom_call" | custom-call | tf_op jit(solution)/shard_map/pallas_call | solution.py:161
  (42 shorter events, 5.9 us)
Async XLA Ops:
  1.0 52.1 %collective-permute-start = (f32[6,32,128]{2,1,0:T(8,128)S(1)}, f32[6,32,128]{2,1,0:T(8,128)S(1)}, u32[]{:S(2)}, u32[]{:S(2)}) collective-permute-start(f32[6,32,128]{2,1,0:T(8,128)S(1)} %get-tuple-element.36), channel_id=1, source_target_pairs={{0,16},{16,32},{32,48},{48,64},{64,80},{80,96},{96,112},{112,128},... | collective-permute-start | bytes 294920 | tf_op jit(solution)/shard_map/ppermute | solution.py:255
  3.0 50.2 %collective-permute-start.1 = (f32[6,32,128]{2,1,0:T(8,128)S(1)}, f32[6,32,128]{2,1,0:T(8,128)S(1)}, u32[]{:S(2)}, u32[]{:S(2)}) collective-permute-start(f32[6,32,128]{2,1,0:T(8,128)S(1)} %get-tuple-element.35), channel_id=1, source_target_pairs={{16,0},{32,16},{48,32},{64,48},{80,64},{96,80},{112,96},{128,112},... | collective-permute-start | bytes 294920 | tf_op jit(solution)/shard_map/ppermute | solution.py:256
  11.3 14.4 %collective-permute-start.2 = (bf16[1,2,8,4224]{3,2,1,0:T(8,128)(2,1)S(1)}, bf16[1,2,8,4224]{3,2,1,0:T(8,128)(2,1)S(1)}, u32[]{:S(2)}, u32[]{:S(2)}) collective-permute-start(bf16[1,2,8,4224]{3,2,1,0:T(8,128)(2,1)S(1)} %fusion.3), channel_id=1, source_target_pairs={{0,0},{1,16},{2,32},{3,48},{4,64},{5,80},{6,96},{7,112},{8,128},{9... | collective-permute-start | bytes 405512 | tf_op jit(solution)/shard_map/ppermute | solution.py:200
  25.7 5.0 %collective-permute-start.3 = (bf16[2,8,4224]{2,1,0:T(8,128)(2,1)S(1)}, bf16[2,8,4224]{2,1,0:T(8,128)(2,1)S(1)}, u32[]{:S(2)}, u32[]{:S(2)}) collective-permute-start(bf16[2,8,4224]{2,1,0:T(8,128)(2,1)S(1)} %bitcast.36), channel_id=1, source_target_pairs={{0,8},{1,9},{2,10},{3,11},{4,12},{5,13},{6,14},{7,15},{8,0},{9,1},... | collective-permute-start | bytes 405512 | tf_op jit(solution)/shard_map/ppermute | solution.py:223
  30.8 6.5 %collective-permute-start.4 = (bf16[4,8,4224]{2,1,0:T(8,128)(2,1)S(1)}, bf16[4,8,4224]{2,1,0:T(8,128)(2,1)S(1)}, u32[]{:S(2)}, u32[]{:S(2)}) collective-permute-start(bf16[4,8,4224]{2,1,0:T(8,128)(2,1)S(1)} %pad_maximum_fusion.2), channel_id=1, source_target_pairs={{0,2},{1,3},{2,0},{3,1},{4,6},{5,7},{6,4},{7,5},{8,10},{9,11},{10,... | collective-permute-start | bytes 811016 | tf_op jit(solution)/shard_map/ppermute | solution.py:223
  37.4 10.7 %collective-permute-start.5 = (bf16[8,8,4224]{2,1,0:T(8,128)(2,1)S(1)}, bf16[8,8,4224]{2,1,0:T(8,128)(2,1)S(1)}, u32[]{:S(2)}, u32[]{:S(2)}) collective-permute-start(bf16[8,8,4224]{2,1,0:T(8,128)(2,1)S(1)} %pad_maximum_fusion.1), channel_id=1, source_target_pairs={{0,6},{1,7},{2,4},{3,5},{4,2},{5,3},{6,0},{7,1},{8,14},{9,15},{10,... | collective-permute-start | bytes 1622024 | tf_op jit(solution)/shard_map/ppermute | solution.py:223
  48.2 2.8 %collective-permute-start.6 = (bf16[16,8,4224]{2,1,0:T(8,128)(2,1)S(1)}, bf16[16,8,4224]{2,1,0:T(8,128)(2,1)S(1)}, u32[]{:S(2)}, u32[]{:S(2)}) collective-permute-start(bf16[16,8,4224]{2,1,0:T(8,128)(2,1)S(1)} %pad_maximum_fusion), channel_id=1, source_target_pairs={{0,1},{1,0},{2,3},{3,2},{4,5},{5,4},{6,7},{7,6},{8,9},{9,8},{10,11... | collective-permute-start | bytes 3244040 | tf_op jit(solution)/shard_map/ppermute | solution.py:223
  53.1 0.8 copy-start
  53.1 0.8 copy-start.1
  58.0 11.1 %collective-permute-start.7 = (f32[6,32,128]{2,1,0:T(8,128)}, f32[6,32,128]{2,1,0:T(8,128)S(1)}, u32[]{:S(2)}, u32[]{:S(2)}) collective-permute-start(f32[6,32,128]{2,1,0:T(8,128)} %get-tuple-element.26), channel_id=1, source_target_pairs={{0,16},{16,32},{32,48},{48,64},{64,80},{80,96},{96,112},{112,128},... | collective-permute-start | bytes 294920 | tf_op jit(solution)/shard_map/ppermute | solution.py:255
  58.0 11.1 %collective-permute-start.8 = (f32[6,32,128]{2,1,0:T(8,128)}, f32[6,32,128]{2,1,0:T(8,128)S(1)}, u32[]{:S(2)}, u32[]{:S(2)}) collective-permute-start(f32[6,32,128]{2,1,0:T(8,128)} %get-tuple-element.28), channel_id=1, source_target_pairs={{16,0},{32,16},{48,32},{64,48},{80,64},{96,80},{112,96},{128,112},... | collective-permute-start | bytes 294920 | tf_op jit(solution)/shard_map/ppermute | solution.py:256
  69.1 0.6 copy-start.4
  69.1 0.7 copy-start.5
  73.9 8.4 %collective-permute-start.9 = (f32[6,32,128]{2,1,0:T(8,128)}, f32[6,32,128]{2,1,0:T(8,128)S(1)}, u32[]{:S(2)}, u32[]{:S(2)}) collective-permute-start(f32[6,32,128]{2,1,0:T(8,128)} %get-tuple-element.29), channel_id=1, source_target_pairs={{0,16},{16,32},{32,48},{48,64},{64,80},{80,96},{96,112},{112,128},... | collective-permute-start | bytes 294920 | tf_op jit(solution)/shard_map/ppermute | solution.py:255
  73.9 8.4 %collective-permute-start.10 = (f32[6,32,128]{2,1,0:T(8,128)}, f32[6,32,128]{2,1,0:T(8,128)S(1)}, u32[]{:S(2)}, u32[]{:S(2)}) collective-permute-start(f32[6,32,128]{2,1,0:T(8,128)} %get-tuple-element.31), channel_id=1, source_target_pairs={{16,0},{32,16},{48,32},{64,48},{80,64},{96,80},{112,96},{128,112},... | collective-permute-start | bytes 294920 | tf_op jit(solution)/shard_map/ppermute | solution.py:256
  82.4 0.6 copy-start.2
  82.4 0.7 copy-start.3

commit v12 on v11

--- a/solution.py
+++ b/solution.py
@@ -128,13 +128,14 @@
             zs = (jnp.where(lane < depth - k, pltpu.roll(v, depth - k, 2), 0.0)
                   + jnp.where(lane >= k, pltpu.roll(v, k, 2), 0.0))
             summed = summed + sw[k] * xs + sw[k] * ys + sw[k] * zs
-        padded = pad_ref[...]
-        slope = fw[1] * (pltpu.roll(padded, breadth - 1, 1) - pltpu.roll(padded, 1, 1))
+        x_slope = fw[1] * (pad_ref[RADIUS + 1:RADIUS + 1 + planes] - pad_ref[RADIUS - 1:RADIUS - 1 + planes])
         for k in range(2, RADIUS + 1):
-            slope = slope + fw[k] * (pltpu.roll(padded, breadth - k, 1) - pltpu.roll(padded, k, 1))
-        cross = fw[1] * (slope[RADIUS + 1:RADIUS + 1 + planes] - slope[RADIUS - 1:RADIUS - 1 + planes])
+            x_slope = x_slope + fw[k] * (
+                pad_ref[RADIUS + k:RADIUS + k + planes] - pad_ref[RADIUS - k:RADIUS - k + planes]
+            )
+        cross = fw[1] * (pltpu.roll(x_slope, breadth - 1, 1) - pltpu.roll(x_slope, 1, 1))
         for k in range(2, RADIUS + 1):
-            cross = cross + fw[k] * (slope[RADIUS + k:RADIUS + k + planes] - slope[RADIUS - k:RADIUS - k + planes])
+            cross = cross + fw[k] * (pltpu.roll(x_slope, breadth - k, 1) - pltpu.roll(x_slope, k, 1))
         lap = summed + 0.7 * cross
         hv = -0.5 * lap + pot_ref[...] * v + nonlocal_lines
         kv = (hv - 12.0 * v) / 8.0

time: 87.6 us -> 87.2 us (level)
  no operation moved by 1% of the time
where the time goes in v12:
time: 87.2 us; the launch traced here: 86.9 us
  waiting for transfers between devices  34.2 us (39%)
  starting transfers between devices  26.5 us (30%)
  Pallas kernels  12.2 us (14%)
  other arithmetic  6.63 us (8%)
  local copies, waits for them, and re-layouts  5.94 us (7%)
  between operations  1.47 us (2%)
    ppermute x4, waiting for transfers between devices, shards(): lax.ppermute(gathered, 'states', [(s, exchange(s)) for s in range(n_state...  21.9 us
    ppermute x3, starting transfers between devices, step(): high_rim = lax.ppermute(send_down, 'grid', down)  20.1 us
    pallas_call x3, Pallas kernels, apply_op(): pl.pallas_call(make_kernel(scale, prev is not None, home_count, proj.shap...  12.2 us
    ppermute x1, waiting for transfers between devices, shards(): packed = lax.ppermute(packed, ('grid', 'states'), pairs)  6.33 us
    ppermute x3, waiting for transfers between devices, step(): low_rim = lax.ppermute(send_up, 'grid', up)  6.03 us
    unnamed x19, local copies, waits for them, and re-layouts  3.21 us
    ppermute x4, starting transfers between devices, shards(): lax.ppermute(gathered, 'states', [(s, exchange(s)) for s in range(n_state...  2.42 us
    ppermute x3, starting transfers between devices, step(): low_rim = lax.ppermute(send_up, 'grid', up)  2 us
  transfers between devices with their start and end apart: 11, of which 7 were waited for; matrix products, arithmetic and copies ran while one was open for 11% of the time, Pallas kernels for 0%

profile of v12, /device:TPU:6, one launch (start us, length us, event | category | flops | bytes accessed | tf_op | source)
XLA Modules:
  0.0 86.9 jit_solution(17541543302782218103)
XLA Ops:
  0.0 1.0 %slice_bitcast_fusion.1 = (f32[6,32,128]{2,1,0:T(8,128)S(1)}, f32[6,32,128]{2,1,0:T(8,128)S(1)}) fusion(f32[1,16,32,128]{3,2,1,0:T(8,128)} %param.9), kind=kLoop, calls=%fused_computation.13 | loop fusion | bytes 393216 | tf_op jit(solution)/shard_map/slice | solution.py:263
  1.0 2.0 %collective-permute-start = (f32[6,32,128]{2,1,0:T(8,128)S(1)}, f32[6,32,128]{2,1,0:T(8,128)S(1)}, u32[]{:S(2)}, u32[]{:S(2)}) collective-permute-start(f32[6,32,128]{2,1,0:T(8,128)S(1)} %get-tuple-element.36), channel_id=1, source_target_pairs={{0,16},{16,32},{32,48},{48,64},{64,80},{80,96},{96,112},{112,128},... | collective-permute-start | bytes 294920 | tf_op jit(solution)/shard_map/ppermute | solution.py:256
  3.0 6.7 %collective-permute-start.1 = (f32[6,32,128]{2,1,0:T(8,128)S(1)}, f32[6,32,128]{2,1,0:T(8,128)S(1)}, u32[]{:S(2)}, u32[]{:S(2)}) collective-permute-start(f32[6,32,128]{2,1,0:T(8,128)S(1)} %get-tuple-element.35), channel_id=1, source_target_pairs={{16,0},{32,16},{48,32},{64,48},{80,64},{96,80},{112,96},{128,112},... | collective-permute-start | bytes 294920 | tf_op jit(solution)/shard_map/ppermute | solution.py:257
  10.4 0.9 %fusion.3 = bf16[1,2,8,4224]{3,2,1,0:T(8,128)(2,1)S(1)} fusion(bf16[1,2,8,1]{3,2,1,0:T(8,128)(2,1)S(1)} %copy.11, bf16[1,2,8,4096]{3,2,1,0:T(8,128)(2,1)} %param.11), kind=kLoop, calls=%fused_computation.12 | loop fusion | flops 405504 | bytes 266272 | tf_op jit(solution)/shard_map/concatenate | solution.py:199
  11.3 1.9 %collective-permute-start.2 = (bf16[1,2,8,4224]{3,2,1,0:T(8,128)(2,1)S(1)}, bf16[1,2,8,4224]{3,2,1,0:T(8,128)(2,1)S(1)}, u32[]{:S(2)}, u32[]{:S(2)}) collective-permute-start(bf16[1,2,8,4224]{3,2,1,0:T(8,128)(2,1)S(1)} %fusion.3), channel_id=1, source_target_pairs={{0,0},{1,16},{2,32},{3,48},{4,64},{5,80},{6,96},{7,112},{8,128},{9... | collective-permute-start | bytes 405512 | tf_op jit(solution)/shard_map/ppermute | solution.py:201
  14.7 0.9 fusion.1.pick_ref
  15.5 0.8 fusion.place_ref
  17.0 0.9 %convert_reduce_fusion.1 = s32[10]{0:T(128)S(1)} fusion(s32[10]{0:T(128)} %param.13), kind=kLoop, calls=%fused_computation.21 | loop fusion | flops 490 | bytes 80 | tf_op jit(solution)/shard_map/reduce_sum | solution.py:193
  18.0 1.3 %iota_reduce_fusion = (pred[10]{0:T(512)(128)(4,1)}, s32[10]{0:T(128)S(1)}) fusion(s32[16]{0:T(128)S(1)} %stack.79, s32[10]{0:T(128)} %param.13), kind=kLoop, calls=%fused_computation.23 | loop fusion | flops 1210 | bytes 154 | tf_op jit(solution)/shard_map/shards/reduce | solution.py:229
  19.4 6.3 %collective-permute-done.2 = bf16[1,2,8,4224]{3,2,1,0:T(8,128)(2,1)S(1)} collective-permute-done((bf16[1,2,8,4224]{3,2,1,0:T(8,128)(2,1)S(1)}, bf16[1,2,8,4224]{3,2,1,0:T(8,128)(2,1)S(1)}, u32[]{:S(2)}, u32[]{:S(2)}) %collective-permute-start.2) | collective-permute-done | bytes 135200 | tf_op jit(solution)/shard_map/ppermute | solution.py:201
  25.7 1.6 %collective-permute-start.3 = (bf16[2,8,4224]{2,1,0:T(8,128)(2,1)S(1)}, bf16[2,8,4224]{2,1,0:T(8,128)(2,1)S(1)}, u32[]{:S(2)}, u32[]{:S(2)}) collective-permute-start(bf16[2,8,4224]{2,1,0:T(8,128)(2,1)S(1)} %bitcast.36), channel_id=1, source_target_pairs={{0,8},{1,9},{2,10},{3,11},{4,12},{5,13},{6,14},{7,15},{8,0},{9,1},... | collective-permute-start | bytes 405512 | tf_op jit(solution)/shard_map/ppermute | solution.py:224
  27.9 2.8 %collective-permute-done.3 = bf16[2,8,4224]{2,1,0:T(8,128)(2,1)S(1)} collective-permute-done((bf16[2,8,4224]{2,1,0:T(8,128)(2,1)S(1)}, bf16[2,8,4224]{2,1,0:T(8,128)(2,1)S(1)}, u32[]{:S(2)}, u32[]{:S(2)}) %collective-permute-start.3) | collective-permute-done | bytes 135200 | tf_op jit(solution)/shard_map/ppermute | solution.py:224
  31.4 5.9 %collective-permute-done.4 = bf16[4,8,4224]{2,1,0:T(8,128)(2,1)S(1)} collective-permute-done((bf16[4,8,4224]{2,1,0:T(8,128)(2,1)S(1)}, bf16[4,8,4224]{2,1,0:T(8,128)(2,1)S(1)}, u32[]{:S(2)}, u32[]{:S(2)}) %collective-permute-start.4) | collective-permute-done | bytes 270368 | tf_op jit(solution)/shard_map/ppermute | solution.py:224
  37.5 10.5 %collective-permute-done.5 = bf16[8,8,4224]{2,1,0:T(8,128)(2,1)S(1)} collective-permute-done((bf16[8,8,4224]{2,1,0:T(8,128)(2,1)S(1)}, bf16[8,8,4224]{2,1,0:T(8,128)(2,1)S(1)}, u32[]{:S(2)}, u32[]{:S(2)}) %collective-permute-start.5) | collective-permute-done | bytes 540704 | tf_op jit(solution)/shard_map/ppermute | solution.py:224
  48.4 2.6 %collective-permute-done.6 = bf16[16,8,4224]{2,1,0:T(8,128)(2,1)S(1)} collective-permute-done((bf16[16,8,4224]{2,1,0:T(8,128)(2,1)S(1)}, bf16[16,8,4224]{2,1,0:T(8,128)(2,1)S(1)}, u32[]{:S(2)}, u32[]{:S(2)}) %collective-permute-start.6) | collective-permute-done | bytes 1081376 | tf_op jit(solution)/shard_map/ppermute | solution.py:224
  52.0 1.0 %copy.12 = bf16[10,8,32,128]{3,2,1,0:T(8,128)(2,1)} copy(bf16[10,8,32,128]{3,1,2,0:T(8,128)(2,1)S(1)} %slice_bitcast_fusion) | data formatting | bytes 1310720
  53.1 0.8 broadcast_in_dim.36.gain_ref
  53.9 4.0 %shard_map.73 = (f32[16,32,128]{2,1,0:T(8,128)}, f32[6,32,128]{2,1,0:T(8,128)}, f32[6,32,128]{2,1,0:T(8,128)}) custom-call(s32[4]{0:T(128)} %pad_add_fusion.shift_ref, f32[6,32,128]{2,1,0:T(8,128)} %copy-done, f32[16,32,128]{2,1,0:T(8,128)} %bitcast.40, f32[6,32,128]{2,1,0:T(8,128)} %copy-done.1, f32[16,32,128]{2,1,0:T(8,128)} %pot_ref.5, ...), custom_call_target="tpu_custom_call" | custom-call | tf_op jit(solution)/shard_map/pallas_call | solution.py:162
  57.9 7.8 %collective-permute-start.8 = (f32[6,32,128]{2,1,0:T(8,128)}, f32[6,32,128]{2,1,0:T(8,128)S(1)}, u32[]{:S(2)}, u32[]{:S(2)}) collective-permute-start(f32[6,32,128]{2,1,0:T(8,128)} %get-tuple-element.28), channel_id=1, source_target_pairs={{16,0},{32,16},{48,32},{64,48},{80,64},{96,80},{112,96},{128,112},... | collective-permute-start | bytes 294920 | tf_op jit(solution)/shard_map/ppermute | solution.py:257
  65.7 3.2 %collective-permute-done.7.lo_ref = f32[6,32,128]{2,1,0:T(8,128)S(1)} collective-permute-done((f32[6,32,128]{2,1,0:T(8,128)}, f32[6,32,128]{2,1,0:T(8,128)S(1)}, u32[]{:S(2)}, u32[]{:S(2)}) %collective-permute-start.7) | collective-permute-done | bytes 98336 | tf_op jit(solution)/shard_map/ppermute | solution.py:256
  69.6 4.1 %shard_map.74 = (f32[16,32,128]{2,1,0:T(8,128)}, f32[6,32,128]{2,1,0:T(8,128)}, f32[6,32,128]{2,1,0:T(8,128)}) custom-call(s32[4]{0:T(128)} %pad_add_fusion.shift_ref, f32[6,32,128]{2,1,0:T(8,128)} %copy-done.4, f32[16,32,128]{2,1,0:T(8,128)} %get-tuple-element.27.v_ref.rest_0_, f32[6,32,128]{2,1,0:T(8,128)} %copy-done.5, f32[16,32,128]{2,1,0:T(8,128)} %pot_ref.5, ...), custom_call_target="tpu_custom_call" | custom-call | tf_op jit(solution)/shard_map/pallas_call | solution.py:162
  73.7 5.6 %collective-permute-start.10 = (f32[6,32,128]{2,1,0:T(8,128)}, f32[6,32,128]{2,1,0:T(8,128)S(1)}, u32[]{:S(2)}, u32[]{:S(2)}) collective-permute-start(f32[6,32,128]{2,1,0:T(8,128)} %get-tuple-element.31), channel_id=1, source_target_pairs={{16,0},{32,16},{48,32},{64,48},{80,64},{96,80},{112,96},{128,112},... | collective-permute-start | bytes 294920 | tf_op jit(solution)/shard_map/ppermute | solution.py:257
  79.3 2.8 %collective-permute-done.9.lo_ref = f32[6,32,128]{2,1,0:T(8,128)S(1)} collective-permute-done((f32[6,32,128]{2,1,0:T(8,128)}, f32[6,32,128]{2,1,0:T(8,128)S(1)}, u32[]{:S(2)}, u32[]{:S(2)}) %collective-permute-start.9) | collective-permute-done | bytes 98336 | tf_op jit(solution)/shard_map/ppermute | solution.py:256
  82.8 4.1 %shard_map.75 = (f32[16,32,128]{2,1,0:T(8,128)}, f32[6,32,128]{2,1,0:T(8,128)}, f32[6,32,128]{2,1,0:T(8,128)}) custom-call(s32[4]{0:T(128)} %pad_add_fusion.shift_ref, f32[6,32,128]{2,1,0:T(8,128)} %copy-done.2, f32[16,32,128]{2,1,0:T(8,128)} %get-tuple-element.30.v_ref, f32[6,32,128]{2,1,0:T(8,128)} %copy-done.3, f32[16,32,128]{2,1,0:T(8,128)} %pot_ref.5, ...), custom_call_target="tpu_custom_call" | custom-call | tf_op jit(solution)/shard_map/pallas_call | solution.py:162
  (42 shorter events, 5.9 us)
Async XLA Ops:
  1.0 52.1 %collective-permute-start = (f32[6,32,128]{2,1,0:T(8,128)S(1)}, f32[6,32,128]{2,1,0:T(8,128)S(1)}, u32[]{:S(2)}, u32[]{:S(2)}) collective-permute-start(f32[6,32,128]{2,1,0:T(8,128)S(1)} %get-tuple-element.36), channel_id=1, source_target_pairs={{0,16},{16,32},{32,48},{48,64},{64,80},{80,96},{96,112},{112,128},... | collective-permute-start | bytes 294920 | tf_op jit(solution)/shard_map/ppermute | solution.py:256
  3.0 50.2 %collective-permute-start.1 = (f32[6,32,128]{2,1,0:T(8,128)S(1)}, f32[6,32,128]{2,1,0:T(8,128)S(1)}, u32[]{:S(2)}, u32[]{:S(2)}) collective-permute-start(f32[6,32,128]{2,1,0:T(8,128)S(1)} %get-tuple-element.35), channel_id=1, source_target_pairs={{16,0},{32,16},{48,32},{64,48},{80,64},{96,80},{112,96},{128,112},... | collective-permute-start | bytes 294920 | tf_op jit(solution)/shard_map/ppermute | solution.py:257
  11.3 14.4 %collective-permute-start.2 = (bf16[1,2,8,4224]{3,2,1,0:T(8,128)(2,1)S(1)}, bf16[1,2,8,4224]{3,2,1,0:T(8,128)(2,1)S(1)}, u32[]{:S(2)}, u32[]{:S(2)}) collective-permute-start(bf16[1,2,8,4224]{3,2,1,0:T(8,128)(2,1)S(1)} %fusion.3), channel_id=1, source_target_pairs={{0,0},{1,16},{2,32},{3,48},{4,64},{5,80},{6,96},{7,112},{8,128},{9... | collective-permute-start | bytes 405512 | tf_op jit(solution)/shard_map/ppermute | solution.py:201
  25.7 5.0 %collective-permute-start.3 = (bf16[2,8,4224]{2,1,0:T(8,128)(2,1)S(1)}, bf16[2,8,4224]{2,1,0:T(8,128)(2,1)S(1)}, u32[]{:S(2)}, u32[]{:S(2)}) collective-permute-start(bf16[2,8,4224]{2,1,0:T(8,128)(2,1)S(1)} %bitcast.36), channel_id=1, source_target_pairs={{0,8},{1,9},{2,10},{3,11},{4,12},{5,13},{6,14},{7,15},{8,0},{9,1},... | collective-permute-start | bytes 405512 | tf_op jit(solution)/shard_map/ppermute | solution.py:224
  30.8 6.5 %collective-permute-start.4 = (bf16[4,8,4224]{2,1,0:T(8,128)(2,1)S(1)}, bf16[4,8,4224]{2,1,0:T(8,128)(2,1)S(1)}, u32[]{:S(2)}, u32[]{:S(2)}) collective-permute-start(bf16[4,8,4224]{2,1,0:T(8,128)(2,1)S(1)} %pad_maximum_fusion.2), channel_id=1, source_target_pairs={{0,2},{1,3},{2,0},{3,1},{4,6},{5,7},{6,4},{7,5},{8,10},{9,11},{10,... | collective-permute-start | bytes 811016 | tf_op jit(solution)/shard_map/ppermute | solution.py:224
  37.4 10.7 %collective-permute-start.5 = (bf16[8,8,4224]{2,1,0:T(8,128)(2,1)S(1)}, bf16[8,8,4224]{2,1,0:T(8,128)(2,1)S(1)}, u32[]{:S(2)}, u32[]{:S(2)}) collective-permute-start(bf16[8,8,4224]{2,1,0:T(8,128)(2,1)S(1)} %pad_maximum_fusion.1), channel_id=1, source_target_pairs={{0,6},{1,7},{2,4},{3,5},{4,2},{5,3},{6,0},{7,1},{8,14},{9,15},{10,... | collective-permute-start | bytes 1622024 | tf_op jit(solution)/shard_map/ppermute | solution.py:224
  48.2 2.8 %collective-permute-start.6 = (bf16[16,8,4224]{2,1,0:T(8,128)(2,1)S(1)}, bf16[16,8,4224]{2,1,0:T(8,128)(2,1)S(1)}, u32[]{:S(2)}, u32[]{:S(2)}) collective-permute-start(bf16[16,8,4224]{2,1,0:T(8,128)(2,1)S(1)} %pad_maximum_fusion), channel_id=1, source_target_pairs={{0,1},{1,0},{2,3},{3,2},{4,5},{5,4},{6,7},{7,6},{8,9},{9,8},{10,11... | collective-permute-start | bytes 3244040 | tf_op jit(solution)/shard_map/ppermute | solution.py:224
  53.1 0.8 copy-start
  53.1 0.8 copy-start.1
  57.9 11.0 %collective-permute-start.7 = (f32[6,32,128]{2,1,0:T(8,128)}, f32[6,32,128]{2,1,0:T(8,128)S(1)}, u32[]{:S(2)}, u32[]{:S(2)}) collective-permute-start(f32[6,32,128]{2,1,0:T(8,128)} %get-tuple-element.26), channel_id=1, source_target_pairs={{0,16},{16,32},{32,48},{48,64},{64,80},{80,96},{96,112},{112,128},... | collective-permute-start | bytes 294920 | tf_op jit(solution)/shard_map/ppermute | solution.py:256
  57.9 11.1 %collective-permute-start.8 = (f32[6,32,128]{2,1,0:T(8,128)}, f32[6,32,128]{2,1,0:T(8,128)S(1)}, u32[]{:S(2)}, u32[]{:S(2)}) collective-permute-start(f32[6,32,128]{2,1,0:T(8,128)} %get-tuple-element.28), channel_id=1, source_target_pairs={{16,0},{32,16},{48,32},{64,48},{80,64},{96,80},{112,96},{128,112},... | collective-permute-start | bytes 294920 | tf_op jit(solution)/shard_map/ppermute | solution.py:257
  68.9 0.6 copy-start.4
  68.9 0.7 copy-start.5
  73.7 8.4 %collective-permute-start.9 = (f32[6,32,128]{2,1,0:T(8,128)}, f32[6,32,128]{2,1,0:T(8,128)S(1)}, u32[]{:S(2)}, u32[]{:S(2)}) collective-permute-start(f32[6,32,128]{2,1,0:T(8,128)} %get-tuple-element.29), channel_id=1, source_target_pairs={{0,16},{16,32},{32,48},{48,64},{64,80},{80,96},{96,112},{112,128},... | collective-permute-start | bytes 294920 | tf_op jit(solution)/shard_map/ppermute | solution.py:256
  73.7 8.4 %collective-permute-start.10 = (f32[6,32,128]{2,1,0:T(8,128)}, f32[6,32,128]{2,1,0:T(8,128)S(1)}, u32[]{:S(2)}, u32[]{:S(2)}) collective-permute-start(f32[6,32,128]{2,1,0:T(8,128)} %get-tuple-element.31), channel_id=1, source_target_pairs={{16,0},{32,16},{48,32},{64,48},{80,64},{96,80},{112,96},{128,112},... | collective-permute-start | bytes 294920 | tf_op jit(solution)/shard_map/ppermute | solution.py:257
  82.1 0.6 copy-start.2
  82.1 0.7 copy-start.3

commit v13 on v11

--- a/solution.py
+++ b/solution.py
@@ -80,11 +80,48 @@
     return summed + MIXED_WEIGHT * cross_term
 
 
-def make_kernel(scale, with_prev, home_count, proj_count, block_rows):
+def make_kernel(scale, with_prev, home_count, proj_count, block_rows, with_nonlocal=True):
     sw = second_table(RADIUS)
     fw = first_table(RADIUS)
 
-    def kernel(shift_ref, lo_ref, v_ref, hi_ref, pot_ref, pick_ref, place_ref, proj_ref, gain_ref, *rest):
+    def nonlocal_of(v, pick_ref, place_ref, proj_ref, gain_ref, rows_ref):
+        planes, breadth, depth = v.shape
+        lines = v.reshape(planes * breadth, depth).astype(jnp.bfloat16)
+        picked = jnp.dot(pick_ref[...], lines, preferred_element_type=jnp.float32)
+        rows_ref[...] = picked.astype(jnp.bfloat16)
+
+        def one_atom(a, carry):
+            base = pl.multiple_of(a * block_rows, block_rows)
+            here = rows_ref[pl.ds(base, block_rows), :].astype(jnp.float32)
+            acc = jnp.zeros((block_rows, depth), jnp.float32)
+            for j in range(proj_count):
+                proj = proj_ref[a * proj_count + j].astype(jnp.float32)
+                coef = jnp.sum(jnp.sum(proj * here, axis=0, keepdims=True), axis=1, keepdims=True)
+                gain = gain_ref[a * proj_count + j]
+                scaled = (coef * gain).astype(jnp.bfloat16).astype(jnp.float32)
+                acc = acc + proj * scaled
+            rows_ref[pl.ds(base, block_rows), :] = acc.astype(jnp.bfloat16)
+            return carry
+
+        lax.fori_loop(0, home_count, one_atom, 0, unroll=True)
+        placed = jnp.dot(place_ref[...], rows_ref[...], preferred_element_type=jnp.float32)
+        return placed.reshape(planes, breadth, depth)
+
+    if not with_nonlocal and with_prev is None:
+        def nonlocal_kernel(v_ref, base_ref, pick_ref, place_ref, proj_ref, gain_ref, out_ref, up_ref, down_ref, rows_ref):
+            planes = v_ref.shape[0]
+            nonlocal_lines = nonlocal_of(v_ref[...], pick_ref, place_ref, proj_ref, gain_ref, rows_ref)
+            result = base_ref[...] + nonlocal_lines / 8.0
+            out_ref[...] = result
+            up_ref[...] = result[planes - RADIUS:]
+            down_ref[...] = result[:RADIUS]
+
+        return nonlocal_kernel
+
+    def kernel(shift_ref, lo_ref, v_ref, hi_ref, pot_ref, *rest):
+        if with_nonlocal:
+            pick_ref, place_ref, proj_ref, gain_ref = rest[:4]
+            rest = rest[4:]
         if with_prev:
             prev_ref, out_ref, up_ref, down_ref, pad_ref, rows_ref = rest
         else:
@@ -95,30 +132,10 @@
         pad_ref[RADIUS:RADIUS + planes] = v
         pad_ref[RADIUS + planes:] = pltpu.roll(hi_ref[...], shift_ref[1], 1)
 
-        lines = v.reshape(planes * breadth, depth).astype(jnp.bfloat16)
-        picked = jnp.dot(pick_ref[...], lines, preferred_element_type=jnp.float32)
-
-        def one_atom(a, carry):
-            base = pl.multiple_of(a * block_rows, block_rows)
-            here = picked_ref_load(base)
-            acc = jnp.zeros((block_rows, depth), jnp.float32)
-            for j in range(proj_count):
-                proj = proj_ref[a * proj_count + j].astype(jnp.float32)
-                coef = jnp.sum(jnp.sum(proj * here, axis=0, keepdims=True), axis=1, keepdims=True)
-                gain = gain_ref[a * proj_count + j]
-                scaled = (coef * gain).astype(jnp.bfloat16).astype(jnp.float32)
-                acc = acc + proj * scaled
-            rows_ref[pl.ds(base, block_rows), :] = acc.astype(jnp.bfloat16)
-            return carry
-
-        rows_ref[...] = picked.astype(jnp.bfloat16)
-
-        def picked_ref_load(base):
-            return rows_ref[pl.ds(base, block_rows), :].astype(jnp.float32)
-
-        lax.fori_loop(0, home_count, one_atom, 0, unroll=True)
-        nonlocal_lines = jnp.dot(place_ref[...], rows_ref[...], preferred_element_type=jnp.float32)
-        nonlocal_lines = nonlocal_lines.reshape(planes, breadth, depth)
+        if with_nonlocal:
+            nonlocal_lines = nonlocal_of(v, pick_ref, place_ref, proj_ref, gain_ref, rows_ref)
+        else:
+            nonlocal_lines = 0.0
 
         lane = lax.broadcasted_iota(jnp.int32, v.shape, 2)
         summed = (3.0 * sw[0]) * v
@@ -147,6 +164,38 @@
         down_ref[...] = result[:RADIUS]
 
     return kernel
+
+
+def nonlocal_add(v, base, pick, place, proj, gain):
+    planes, breadth, depth = v.shape
+    picked_rows = pick.shape[0]
+    home_count = proj.shape[0] // 8
+    block_rows = picked_rows // home_count
+    vspec = pl.BlockSpec(memory_space=pltpu.VMEM)
+    rim_shape = jax.ShapeDtypeStruct((RADIUS, breadth, depth), jnp.float32)
+    return pl.pallas_call(
+        make_kernel(1.0, None, home_count, proj.shape[0] // home_count, block_rows, False),
+        out_shape=(jax.ShapeDtypeStruct(v.shape, jnp.float32), rim_shape, rim_shape),
+        in_specs=[vspec] * 6,
+        out_specs=(vspec, vspec, vspec),
+        scratch_shapes=[pltpu.VMEM((picked_rows, depth), jnp.bfloat16)],
+    )(v, base, pick, place, proj, gain)
+
+
+def apply_local(shifts, lo, v, hi, pot):
+    planes, breadth, depth = v.shape
+    vspec = pl.BlockSpec(memory_space=pltpu.VMEM)
+    rim_shape = jax.ShapeDtypeStruct((RADIUS, breadth, depth), jnp.float32)
+    return pl.pallas_call(
+        make_kernel(1.0, False, 0, 0, 0, False),
+        out_shape=(jax.ShapeDtypeStruct(v.shape, jnp.float32), rim_shape, rim_shape),
+        in_specs=[pl.BlockSpec(memory_space=pltpu.SMEM)] + [vspec] * 4,
+        out_specs=(vspec, vspec, vspec),
+        scratch_shapes=[
+            pltpu.VMEM((planes + 2 * RADIUS, breadth, depth), jnp.float32),
+            pltpu.VMEM((8, depth), jnp.bfloat16),
+        ],
+    )(shifts, lo, v, hi, pot)
 
 
 def apply_op(shifts, lo, v, hi, pot, pick, place, proj, gain, prev=None, scale=1.0):
@@ -259,7 +308,10 @@
         )
 
     field = states_in[0]
-    first_term = step(field, field[tile_width - RADIUS :], field[:RADIUS])
+    low_rim = lax.ppermute(field[tile_width - RADIUS :], "grid", up)
+    high_rim = lax.ppermute(field[:RADIUS], "grid", down)
+    local_part = apply_local(shifts, low_rim, field, high_rim, potential)[0]
+    first_term = nonlocal_add(field, local_part, pick, place, proj_in, gain_in)
     second_term = step(*first_term, field, 2.0)
     filtered = step(*second_term, first_term[0], 2.0)
     return filtered[0][None]

time: 87.6 us -> 92.3 us (1.054)
  starting transfers between devices: 26.5 us -> 29.6 us
  Pallas kernels: 12.5 us -> 14.8 us
  waiting for transfers between devices: 34.2 us -> 32.8 us
    ppermute x3 -> x2, starting transfers between devices: 20.1 us -> 9.86 us  [step(): high_rim = lax.ppermute(send_down, 'grid', down)]
    pallas_call x0 -> x2, Pallas kernels: none -> 6.4 us  [the longest x1 3.27 us: apply_local(): pl.pallas_call(make_kernel(1.0, False, 0, 0, 0, False), out_shape=(jax.Sh...]
    ppermute x1, waiting for transfers between devices: 6.33 us -> 0.01 us  [shards(): packed = lax.ppermute(packed, ('grid', 'states'), pairs)]
    ppermute x1, starting transfers between devices: 1.92 us -> 8.12 us  [shards(): packed = lax.ppermute(packed, ('grid', 'states'), pairs)]
    ppermute x0 -> x2, starting transfers between devices: none -> 5.72 us  [the longest x1 4.74 us: shards(): high_rim = lax.ppermute(field[:RADIUS], 'grid', down)]
    pallas_call x3 -> x2, Pallas kernels: 12.5 us -> 8.41 us  [apply_op(): pl.pallas_call(make_kernel(scale, prev is not None, home_count, proj.shap...]
    ppermute x3 -> x2, waiting for transfers between devices: 6.03 us -> 8.93 us  [step(): low_rim = lax.ppermute(send_up, 'grid', up)]
    ppermute x3 -> x2, waiting for transfers between devices: 0.01 us -> 2.53 us  [step(): high_rim = lax.ppermute(send_down, 'grid', down)]
  transfers between devices with their start and end apart: 11 -> 11, of which waited for: 7 -> 6; matrix products, arithmetic and copies ran while one was open for 11% -> 7% of each run, Pallas kernels for 0% -> 4%
where the time goes in v13:
time: 92.3 us; the launch traced here: 91.9 us
  waiting for transfers between devices  32.8 us (36%)
  starting transfers between devices  29.6 us (32%)
  Pallas kernels  14.8 us (16%)
  other arithmetic  6.72 us (7%)
  local copies, waits for them, and re-layouts  6.59 us (7%)
  between operations  1.45 us (2%)
    ppermute x4, waiting for transfers between devices, shards(): lax.ppermute(gathered, 'states', [(s, exchange(s)) for s in range(n_state...  21.3 us
    ppermute x2, starting transfers between devices, step(): high_rim = lax.ppermute(send_down, 'grid', down)  9.86 us
    ppermute x2, waiting for transfers between devices, step(): low_rim = lax.ppermute(send_up, 'grid', up)  8.93 us
    pallas_call x2, Pallas kernels, apply_op(): pl.pallas_call(make_kernel(scale, prev is not None, home_count, proj.shap...  8.41 us
    ppermute x1, starting transfers between devices, shards(): packed = lax.ppermute(packed, ('grid', 'states'), pairs)  8.12 us
    ppermute x1, starting transfers between devices, shards(): high_rim = lax.ppermute(field[:RADIUS], 'grid', down)  4.74 us
    ppermute x4, starting transfers between devices, shards(): lax.ppermute(gathered, 'states', [(s, exchange(s)) for s in range(n_state...  4.69 us
    unnamed x19, local copies, waits for them, and re-layouts  3.84 us
  transfers between devices with their start and end apart: 11, of which 6 were waited for; matrix products, arithmetic and copies ran while one was open for 7% of the time, Pallas kernels for 4%

profile of v13, /device:TPU:6, one launch (start us, length us, event | category | flops | bytes accessed | tf_op | source)
XLA Modules:
  0.0 91.9 jit_solution(17874573972318657306)
XLA Ops:
  0.8 0.9 fusion.3
  1.7 8.1 %collective-permute-start.2 = (bf16[1,2,8,4224]{3,2,1,0:T(8,128)(2,1)S(1)}, bf16[1,2,8,4224]{3,2,1,0:T(8,128)(2,1)S(1)}, u32[]{:S(2)}, u32[]{:S(2)}) collective-permute-start(bf16[1,2,8,4224]{3,2,1,0:T(8,128)(2,1)S(1)} %fusion.3), channel_id=1, source_target_pairs={{0,0},{1,16},{2,32},{3,48},{4,64},{5,80},{6,96},{7,112},{8,128},{9... | collective-permute-start | bytes 405512 | tf_op jit(solution)/shard_map/ppermute | solution.py:249
  9.8 1.0 %slice_bitcast_fusion.1 = (f32[6,32,128]{2,1,0:T(8,128)S(1)}, f32[6,32,128]{2,1,0:T(8,128)S(1)}) fusion(f32[1,16,32,128]{3,2,1,0:T(8,128)} %param.9), kind=kLoop, calls=%fused_computation.13 | loop fusion | bytes 393216 | tf_op jit(solution)/shard_map/slice | solution.py:312
  10.8 1.0 %collective-permute-start = (f32[6,32,128]{2,1,0:T(8,128)S(1)}, f32[6,32,128]{2,1,0:T(8,128)S(1)}, u32[]{:S(2)}, u32[]{:S(2)}) collective-permute-start(f32[6,32,128]{2,1,0:T(8,128)S(1)} %get-tuple-element.38), channel_id=1, source_target_pairs={{0,16},{16,32},{32,48},{48,64},{64,80},{80,96},{96,112},{112,128},... | collective-permute-start | bytes 294920 | tf_op jit(solution)/shard_map/ppermute | solution.py:311
  11.7 4.7 %collective-permute-start.1 = (f32[6,32,128]{2,1,0:T(8,128)S(1)}, f32[6,32,128]{2,1,0:T(8,128)S(1)}, u32[]{:S(2)}, u32[]{:S(2)}) collective-permute-start(f32[6,32,128]{2,1,0:T(8,128)S(1)} %get-tuple-element.37), channel_id=1, source_target_pairs={{16,0},{32,16},{48,32},{64,48},{80,64},{96,80},{112,96},{128,112},... | collective-permute-start | bytes 294920 | tf_op jit(solution)/shard_map/ppermute | solution.py:312
  17.3 0.9 fusion.place_ref.rest_1_
  19.0 0.9 convert_reduce_fusion.1
  20.0 1.4 %iota_reduce_fusion = (pred[10]{0:T(512)(128)(4,1)}, s32[10]{0:T(128)S(1)}) fusion(s32[16]{0:T(128)S(1)} %stack.79, s32[10]{0:T(128)} %param.13), kind=kLoop, calls=%fused_computation.23 | loop fusion | flops 1210 | bytes 154 | tf_op jit(solution)/shard_map/shards/reduce | solution.py:277
  21.3 2.7 %collective-permute-start.3 = (bf16[2,8,4224]{2,1,0:T(8,128)(2,1)S(1)}, bf16[2,8,4224]{2,1,0:T(8,128)(2,1)S(1)}, u32[]{:S(2)}, u32[]{:S(2)}) collective-permute-start(bf16[2,8,4224]{2,1,0:T(8,128)(2,1)S(1)} %bitcast.39), channel_id=1, source_target_pairs={{0,8},{1,9},{2,10},{3,11},{4,12},{5,13},{6,14},{7,15},{8,0},{9,1},... | collective-permute-start | bytes 405512 | tf_op jit(solution)/shard_map/ppermute | solution.py:272
  26.7 3.3 %shard_map.73 = (f32[16,32,128]{2,1,0:T(8,128)}, f32[6,32,128]{2,1,0:T(8,128)}, f32[6,32,128]{2,1,0:T(8,128)}) custom-call(s32[4]{0:T(128)} %pad_add_fusion.shift_ref, f32[6,32,128]{2,1,0:T(8,128)} %copy-done, f32[16,32,128]{2,1,0:T(8,128)} %bitcast.36, f32[6,32,128]{2,1,0:T(8,128)} %copy-done.1, f32[16,32,128]{2,1,0:T(8,128)} %pot_ref.5), custom_call_target="tpu_custom_call" | custom-call | tf_op jit(solution)/shard_map/pallas_call | solution.py:189
  30.0 1.8 %collective-permute-start.4 = (bf16[4,8,4224]{2,1,0:T(8,128)(2,1)S(1)}, bf16[4,8,4224]{2,1,0:T(8,128)(2,1)S(1)}, u32[]{:S(2)}, u32[]{:S(2)}) collective-permute-start(bf16[4,8,4224]{2,1,0:T(8,128)(2,1)S(1)} %pad_maximum_fusion.2), channel_id=1, source_target_pairs={{0,2},{1,3},{2,0},{3,1},{4,6},{5,7},{6,4},{7,5},{8,10},{9,11},{10,... | collective-permute-start | bytes 811016 | tf_op jit(solution)/shard_map/ppermute | solution.py:272
  31.8 5.5 %collective-permute-done.4 = bf16[4,8,4224]{2,1,0:T(8,128)(2,1)S(1)} collective-permute-done((bf16[4,8,4224]{2,1,0:T(8,128)(2,1)S(1)}, bf16[4,8,4224]{2,1,0:T(8,128)(2,1)S(1)}, u32[]{:S(2)}, u32[]{:S(2)}) %collective-permute-start.4) | collective-permute-done | bytes 270368 | tf_op jit(solution)/shard_map/ppermute | solution.py:272
  37.5 13.3 %collective-permute-done.5 = bf16[8,8,4224]{2,1,0:T(8,128)(2,1)S(1)} collective-permute-done((bf16[8,8,4224]{2,1,0:T(8,128)(2,1)S(1)}, bf16[8,8,4224]{2,1,0:T(8,128)(2,1)S(1)}, u32[]{:S(2)}, u32[]{:S(2)}) %collective-permute-start.5) | collective-permute-done | bytes 540704 | tf_op jit(solution)/shard_map/ppermute | solution.py:272
  51.1 2.6 %collective-permute-done.6 = bf16[16,8,4224]{2,1,0:T(8,128)(2,1)S(1)} collective-permute-done((bf16[16,8,4224]{2,1,0:T(8,128)(2,1)S(1)}, bf16[16,8,4224]{2,1,0:T(8,128)(2,1)S(1)}, u32[]{:S(2)}, u32[]{:S(2)}) %collective-permute-start.6) | collective-permute-done | bytes 1081376 | tf_op jit(solution)/shard_map/ppermute | solution.py:272
  54.8 1.0 %copy.12 = bf16[10,8,32,128]{3,2,1,0:T(8,128)(2,1)} copy(bf16[10,8,32,128]{3,1,2,0:T(8,128)(2,1)S(1)} %slice_bitcast_fusion) | data formatting | bytes 1310720
  56.6 3.1 %shard_map.74 = (f32[16,32,128]{2,1,0:T(8,128)}, f32[6,32,128]{2,1,0:T(8,128)}, f32[6,32,128]{2,1,0:T(8,128)}) custom-call(f32[16,32,128]{2,1,0:T(8,128)} %bitcast.37, f32[16,32,128]{2,1,0:T(8,128)} %get-tuple-element.26.base_ref, bf16[320,512]{1,0:T(8,128)(2,1)} %fusion.1.pick_ref.rest_0_, bf16[512,320]{1,0:T(8,128)(2,1)} %fusion.place_ref.rest_1_, ...), custom_call_target="tpu_custom_call" | custom-call | tf_op jit(solution)/shard_map/pallas_call | solution.py:176
  59.7 1.2 %collective-permute-start.7 = (f32[6,32,128]{2,1,0:T(8,128)}, f32[6,32,128]{2,1,0:T(8,128)S(1)}, u32[]{:S(2)}, u32[]{:S(2)}) collective-permute-start(f32[6,32,128]{2,1,0:T(8,128)} %get-tuple-element.28), channel_id=1, source_target_pairs={{0,16},{16,32},{32,48},{48,64},{64,80},{80,96},{96,112},{112,128},... | collective-permute-start | bytes 294920 | tf_op jit(solution)/shard_map/ppermute | solution.py:304
  60.9 4.5 %collective-permute-start.8 = (f32[6,32,128]{2,1,0:T(8,128)}, f32[6,32,128]{2,1,0:T(8,128)S(1)}, u32[]{:S(2)}, u32[]{:S(2)}) collective-permute-start(f32[6,32,128]{2,1,0:T(8,128)} %get-tuple-element.30), channel_id=1, source_target_pairs={{16,0},{32,16},{48,32},{64,48},{80,64},{96,80},{112,96},{128,112},... | collective-permute-start | bytes 294920 | tf_op jit(solution)/shard_map/ppermute | solution.py:305
  65.4 3.0 %collective-permute-done.7.lo_ref = f32[6,32,128]{2,1,0:T(8,128)S(1)} collective-permute-done((f32[6,32,128]{2,1,0:T(8,128)}, f32[6,32,128]{2,1,0:T(8,128)S(1)}, u32[]{:S(2)}, u32[]{:S(2)}) %collective-permute-start.7) | collective-permute-done | bytes 98336 | tf_op jit(solution)/shard_map/ppermute | solution.py:304
  69.1 4.2 %shard_map.75 = (f32[16,32,128]{2,1,0:T(8,128)}, f32[6,32,128]{2,1,0:T(8,128)}, f32[6,32,128]{2,1,0:T(8,128)}) custom-call(s32[4]{0:T(128)} %pad_add_fusion.shift_ref, f32[6,32,128]{2,1,0:T(8,128)} %copy-done.4, f32[16,32,128]{2,1,0:T(8,128)} %get-tuple-element.29.v_ref.rest_4_, f32[6,32,128]{2,1,0:T(8,128)} %copy-done.5, f32[16,32,128]{2,1,0:T(8,128)} %pot_ref.5, ...), custom_call_target="tpu_custom_call" | custom-call | tf_op jit(solution)/shard_map/pallas_call | solution.py:210
  73.3 5.4 %collective-permute-start.10 = (f32[6,32,128]{2,1,0:T(8,128)}, f32[6,32,128]{2,1,0:T(8,128)S(1)}, u32[]{:S(2)}, u32[]{:S(2)}) collective-permute-start(f32[6,32,128]{2,1,0:T(8,128)} %get-tuple-element.33), channel_id=1, source_target_pairs={{16,0},{32,16},{48,32},{64,48},{80,64},{96,80},{112,96},{128,112},... | collective-permute-start | bytes 294920 | tf_op jit(solution)/shard_map/ppermute | solution.py:305
  78.7 2.5 %collective-permute-done.10.hi_ref = f32[6,32,128]{2,1,0:T(8,128)S(1)} collective-permute-done((f32[6,32,128]{2,1,0:T(8,128)}, f32[6,32,128]{2,1,0:T(8,128)S(1)}, u32[]{:S(2)}, u32[]{:S(2)}) %collective-permute-start.10) | collective-permute-done | bytes 98336 | tf_op jit(solution)/shard_map/ppermute | solution.py:305
  81.2 5.9 %collective-permute-done.9.lo_ref = f32[6,32,128]{2,1,0:T(8,128)S(1)} collective-permute-done((f32[6,32,128]{2,1,0:T(8,128)}, f32[6,32,128]{2,1,0:T(8,128)S(1)}, u32[]{:S(2)}, u32[]{:S(2)}) %collective-permute-start.9) | collective-permute-done | bytes 98336 | tf_op jit(solution)/shard_map/ppermute | solution.py:304
  87.7 4.2 %shard_map.76 = (f32[16,32,128]{2,1,0:T(8,128)}, f32[6,32,128]{2,1,0:T(8,128)}, f32[6,32,128]{2,1,0:T(8,128)}) custom-call(s32[4]{0:T(128)} %pad_add_fusion.shift_ref, f32[6,32,128]{2,1,0:T(8,128)} %copy-done.3, f32[16,32,128]{2,1,0:T(8,128)} %get-tuple-element.32.v_ref, f32[6,32,128]{2,1,0:T(8,128)} %copy-done.2, f32[16,32,128]{2,1,0:T(8,128)} %pot_ref.5, ...), custom_call_target="tpu_custom_call" | custom-call | tf_op jit(solution)/shard_map/pallas_call | solution.py:210
  (43 shorter events, 7.5 us)
Async XLA Ops:
  1.7 19.7 %collective-permute-start.2 = (bf16[1,2,8,4224]{3,2,1,0:T(8,128)(2,1)S(1)}, bf16[1,2,8,4224]{3,2,1,0:T(8,128)(2,1)S(1)}, u32[]{:S(2)}, u32[]{:S(2)}) collective-permute-start(bf16[1,2,8,4224]{3,2,1,0:T(8,128)(2,1)S(1)} %fusion.3), channel_id=1, source_target_pairs={{0,0},{1,16},{2,32},{3,48},{4,64},{5,80},{6,96},{7,112},{8,128},{9... | collective-permute-start | bytes 405512 | tf_op jit(solution)/shard_map/ppermute | solution.py:249
  10.8 15.3 %collective-permute-start = (f32[6,32,128]{2,1,0:T(8,128)S(1)}, f32[6,32,128]{2,1,0:T(8,128)S(1)}, u32[]{:S(2)}, u32[]{:S(2)}) collective-permute-start(f32[6,32,128]{2,1,0:T(8,128)S(1)} %get-tuple-element.38), channel_id=1, source_target_pairs={{0,16},{16,32},{32,48},{48,64},{64,80},{80,96},{96,112},{112,128},... | collective-permute-start | bytes 294920 | tf_op jit(solution)/shard_map/ppermute | solution.py:311
  11.7 14.3 %collective-permute-start.1 = (f32[6,32,128]{2,1,0:T(8,128)S(1)}, f32[6,32,128]{2,1,0:T(8,128)S(1)}, u32[]{:S(2)}, u32[]{:S(2)}) collective-permute-start(f32[6,32,128]{2,1,0:T(8,128)S(1)} %get-tuple-element.37), channel_id=1, source_target_pairs={{16,0},{32,16},{48,32},{64,48},{80,64},{96,80},{112,96},{128,112},... | collective-permute-start | bytes 294920 | tf_op jit(solution)/shard_map/ppermute | solution.py:312
  21.3 8.6 %collective-permute-start.3 = (bf16[2,8,4224]{2,1,0:T(8,128)(2,1)S(1)}, bf16[2,8,4224]{2,1,0:T(8,128)(2,1)S(1)}, u32[]{:S(2)}, u32[]{:S(2)}) collective-permute-start(bf16[2,8,4224]{2,1,0:T(8,128)(2,1)S(1)} %bitcast.39), channel_id=1, source_target_pairs={{0,8},{1,9},{2,10},{3,11},{4,12},{5,13},{6,14},{7,15},{8,0},{9,1},... | collective-permute-start | bytes 405512 | tf_op jit(solution)/shard_map/ppermute | solution.py:272
  26.0 0.6 copy-start
  26.0 0.7 copy-start.1
  30.0 7.3 %collective-permute-start.4 = (bf16[4,8,4224]{2,1,0:T(8,128)(2,1)S(1)}, bf16[4,8,4224]{2,1,0:T(8,128)(2,1)S(1)}, u32[]{:S(2)}, u32[]{:S(2)}) collective-permute-start(bf16[4,8,4224]{2,1,0:T(8,128)(2,1)S(1)} %pad_maximum_fusion.2), channel_id=1, source_target_pairs={{0,2},{1,3},{2,0},{3,1},{4,6},{5,7},{6,4},{7,5},{8,10},{9,11},{10,... | collective-permute-start | bytes 811016 | tf_op jit(solution)/shard_map/ppermute | solution.py:272
  37.4 13.4 %collective-permute-start.5 = (bf16[8,8,4224]{2,1,0:T(8,128)(2,1)S(1)}, bf16[8,8,4224]{2,1,0:T(8,128)(2,1)S(1)}, u32[]{:S(2)}, u32[]{:S(2)}) collective-permute-start(bf16[8,8,4224]{2,1,0:T(8,128)(2,1)S(1)} %pad_maximum_fusion.1), channel_id=1, source_target_pairs={{0,6},{1,7},{2,4},{3,5},{4,2},{5,3},{6,0},{7,1},{8,14},{9,15},{10,... | collective-permute-start | bytes 1622024 | tf_op jit(solution)/shard_map/ppermute | solution.py:272
  50.9 2.8 %collective-permute-start.6 = (bf16[16,8,4224]{2,1,0:T(8,128)(2,1)S(1)}, bf16[16,8,4224]{2,1,0:T(8,128)(2,1)S(1)}, u32[]{:S(2)}, u32[]{:S(2)}) collective-permute-start(bf16[16,8,4224]{2,1,0:T(8,128)(2,1)S(1)} %pad_maximum_fusion), channel_id=1, source_target_pairs={{0,1},{1,0},{2,3},{3,2},{4,5},{5,4},{6,7},{7,6},{8,9},{9,8},{10,11... | collective-permute-start | bytes 3244040 | tf_op jit(solution)/shard_map/ppermute | solution.py:272
  59.7 8.7 %collective-permute-start.7 = (f32[6,32,128]{2,1,0:T(8,128)}, f32[6,32,128]{2,1,0:T(8,128)S(1)}, u32[]{:S(2)}, u32[]{:S(2)}) collective-permute-start(f32[6,32,128]{2,1,0:T(8,128)} %get-tuple-element.28), channel_id=1, source_target_pairs={{0,16},{16,32},{32,48},{48,64},{64,80},{80,96},{96,112},{112,128},... | collective-permute-start | bytes 294920 | tf_op jit(solution)/shard_map/ppermute | solution.py:304
  60.9 7.5 %collective-permute-start.8 = (f32[6,32,128]{2,1,0:T(8,128)}, f32[6,32,128]{2,1,0:T(8,128)S(1)}, u32[]{:S(2)}, u32[]{:S(2)}) collective-permute-start(f32[6,32,128]{2,1,0:T(8,128)} %get-tuple-element.30), channel_id=1, source_target_pairs={{16,0},{32,16},{48,32},{64,48},{80,64},{96,80},{112,96},{128,112},... | collective-permute-start | bytes 294920 | tf_op jit(solution)/shard_map/ppermute | solution.py:305
  68.4 0.6 copy-start.4
  68.4 0.7 copy-start.5
  73.3 7.9 %collective-permute-start.10 = (f32[6,32,128]{2,1,0:T(8,128)}, f32[6,32,128]{2,1,0:T(8,128)S(1)}, u32[]{:S(2)}, u32[]{:S(2)}) collective-permute-start(f32[6,32,128]{2,1,0:T(8,128)} %get-tuple-element.33), channel_id=1, source_target_pairs={{16,0},{32,16},{48,32},{64,48},{80,64},{96,80},{112,96},{128,112},... | collective-permute-start | bytes 294920 | tf_op jit(solution)/shard_map/ppermute | solution.py:305
  78.7 8.4 %collective-permute-start.9 = (f32[6,32,128]{2,1,0:T(8,128)}, f32[6,32,128]{2,1,0:T(8,128)S(1)}, u32[]{:S(2)}, u32[]{:S(2)}) collective-permute-start(f32[6,32,128]{2,1,0:T(8,128)} %get-tuple-element.31), channel_id=1, source_target_pairs={{0,16},{16,32},{32,48},{48,64},{64,80},{80,96},{96,112},{112,128},... | collective-permute-start | bytes 294920 | tf_op jit(solution)/shard_map/ppermute | solution.py:304
  81.2 5.9 %copy-start.2 = (f32[6,32,128]{2,1,0:T(8,128)}, f32[6,32,128]{2,1,0:T(8,128)S(1)}, u32[]{:S(2)}) copy-start(f32[6,32,128]{2,1,0:T(8,128)S(1)} %collective-permute-done.10.hi_ref) | copy-start | bytes 294916
  87.1 0.6 copy-start.3

commit v14 on v11

--- a/solution.py
+++ b/solution.py
@@ -156,7 +156,8 @@
     block_rows = picked_rows // home_count
     args = [shifts, lo, v, hi, pot, pick, place, proj, gain] + ([prev] if prev is not None else [])
     vspec = pl.BlockSpec(memory_space=pltpu.VMEM)
-    in_specs = [pl.BlockSpec(memory_space=pltpu.SMEM)] + [vspec] * (len(args) - 1)
+    sspec = pl.BlockSpec(memory_space=pltpu.SMEM)
+    in_specs = [sspec] + [vspec] * 7 + [sspec] + [vspec] * (len(args) - 9)
     rim_shape = jax.ShapeDtypeStruct((RADIUS, breadth, depth), jnp.float32)
     return pl.pallas_call(
         make_kernel(scale, prev is not None, home_count, proj.shape[0] // home_count, block_rows),
@@ -236,9 +237,7 @@
     ).astype(jnp.bfloat16)
     place = pick.T
     proj_in = proj_rows.reshape(home_count * proj_count, breadth, line_depth)
-    gain_in = jnp.broadcast_to(
-        atom_gain.reshape(home_count * proj_count, 1, 1), (home_count * proj_count, 1, line_depth)
-    )
+    gain_in = atom_gain.reshape(home_count * proj_count)
     skew = wrap_rows[0]
     shifts = jnp.stack(
         [

time: 87.6 us -> 87.9 us (level)
  transfers between devices with their start and end apart: 11 -> 11, of which waited for: 7 -> 7; matrix products, arithmetic and copies ran while one was open for 11% -> 12% of each run, Pallas kernels for 0% -> 0%
where the time goes in v14:
time: 87.9 us; the launch traced here: 87.6 us
  waiting for transfers between devices  34.1 us (39%)
  starting transfers between devices  26.5 us (30%)
  Pallas kernels  12.5 us (14%)
  other arithmetic  6.72 us (8%)
  local copies, waits for them, and re-layouts  6.34 us (7%)
  between operations  1.45 us (2%)
    ppermute x4, waiting for transfers between devices, shards(): lax.ppermute(gathered, 'states', [(s, exchange(s)) for s in range(n_state...  21.8 us
    ppermute x3, starting transfers between devices, step(): high_rim = lax.ppermute(send_down, 'grid', down)  20.1 us
    pallas_call x3, Pallas kernels, apply_op(): pl.pallas_call(make_kernel(scale, prev is not None, home_count, proj.shap...  12.5 us
    ppermute x1, waiting for transfers between devices, shards(): packed = lax.ppermute(packed, ('grid', 'states'), pairs)  6.33 us
    ppermute x3, waiting for transfers between devices, step(): low_rim = lax.ppermute(send_up, 'grid', up)  6.03 us
    unnamed x19, local copies, waits for them, and re-layouts  3.86 us
    ppermute x4, starting transfers between devices, shards(): lax.ppermute(gathered, 'states', [(s, exchange(s)) for s in range(n_state...  2.42 us
    ppermute x3, starting transfers between devices, step(): low_rim = lax.ppermute(send_up, 'grid', up)  2 us
  transfers between devices with their start and end apart: 11, of which 7 were waited for; matrix products, arithmetic and copies ran while one was open for 12% of the time, Pallas kernels for 0%

profile of v14, /device:TPU:6, one launch (start us, length us, event | category | flops | bytes accessed | tf_op | source)
XLA Modules:
  0.0 87.6 jit_solution(18311220064037948262)
XLA Ops:
  0.0 1.0 %slice_bitcast_fusion.1 = (f32[6,32,128]{2,1,0:T(8,128)S(1)}, f32[6,32,128]{2,1,0:T(8,128)S(1)}) fusion(f32[1,16,32,128]{3,2,1,0:T(8,128)} %param.9), kind=kLoop, calls=%fused_computation.13 | loop fusion | bytes 393216 | tf_op jit(solution)/shard_map/slice | solution.py:261
  1.0 2.0 %collective-permute-start = (f32[6,32,128]{2,1,0:T(8,128)S(1)}, f32[6,32,128]{2,1,0:T(8,128)S(1)}, u32[]{:S(2)}, u32[]{:S(2)}) collective-permute-start(f32[6,32,128]{2,1,0:T(8,128)S(1)} %get-tuple-element.36), channel_id=1, source_target_pairs={{0,16},{16,32},{32,48},{48,64},{64,80},{80,96},{96,112},{112,128},... | collective-permute-start | bytes 294920 | tf_op jit(solution)/shard_map/ppermute | solution.py:254
  3.0 6.7 %collective-permute-start.1 = (f32[6,32,128]{2,1,0:T(8,128)S(1)}, f32[6,32,128]{2,1,0:T(8,128)S(1)}, u32[]{:S(2)}, u32[]{:S(2)}) collective-permute-start(f32[6,32,128]{2,1,0:T(8,128)S(1)} %get-tuple-element.35), channel_id=1, source_target_pairs={{16,0},{32,16},{48,32},{64,48},{80,64},{96,80},{112,96},{128,112},... | collective-permute-start | bytes 294920 | tf_op jit(solution)/shard_map/ppermute | solution.py:255
  9.6 0.8 copy.11
  10.4 0.9 %fusion.3 = bf16[1,2,8,4224]{3,2,1,0:T(8,128)(2,1)S(1)} fusion(bf16[1,2,8,1]{3,2,1,0:T(8,128)(2,1)S(1)} %copy.11, bf16[1,2,8,4096]{3,2,1,0:T(8,128)(2,1)} %param.11), kind=kLoop, calls=%fused_computation.12 | loop fusion | flops 405504 | bytes 266272 | tf_op jit(solution)/shard_map/concatenate | solution.py:199
  11.3 1.9 %collective-permute-start.2 = (bf16[1,2,8,4224]{3,2,1,0:T(8,128)(2,1)S(1)}, bf16[1,2,8,4224]{3,2,1,0:T(8,128)(2,1)S(1)}, u32[]{:S(2)}, u32[]{:S(2)}) collective-permute-start(bf16[1,2,8,4224]{3,2,1,0:T(8,128)(2,1)S(1)} %fusion.3), channel_id=1, source_target_pairs={{0,0},{1,16},{2,32},{3,48},{4,64},{5,80},{6,96},{7,112},{8,128},{9... | collective-permute-start | bytes 405512 | tf_op jit(solution)/shard_map/ppermute | solution.py:201
  14.7 0.9 fusion.1.pick_ref
  15.5 0.8 fusion.place_ref
  17.0 0.9 %convert_reduce_fusion.1 = s32[10]{0:T(128)S(1)} fusion(s32[10]{0:T(128)} %param.13), kind=kLoop, calls=%fused_computation.21 | loop fusion | flops 490 | bytes 80 | tf_op jit(solution)/shard_map/reduce_sum | solution.py:193
  18.0 1.3 %iota_reduce_fusion = (pred[10]{0:T(512)(128)(4,1)}, s32[10]{0:T(128)S(1)}) fusion(s32[16]{0:T(128)S(1)} %stack.79, s32[10]{0:T(128)} %param.13), kind=kLoop, calls=%fused_computation.23 | loop fusion | flops 1210 | bytes 154 | tf_op jit(solution)/shard_map/shards/reduce | solution.py:229
  19.4 6.3 %collective-permute-done.2 = bf16[1,2,8,4224]{3,2,1,0:T(8,128)(2,1)S(1)} collective-permute-done((bf16[1,2,8,4224]{3,2,1,0:T(8,128)(2,1)S(1)}, bf16[1,2,8,4224]{3,2,1,0:T(8,128)(2,1)S(1)}, u32[]{:S(2)}, u32[]{:S(2)}) %collective-permute-start.2) | collective-permute-done | bytes 135200 | tf_op jit(solution)/shard_map/ppermute | solution.py:201
  25.7 1.6 %collective-permute-start.3 = (bf16[2,8,4224]{2,1,0:T(8,128)(2,1)S(1)}, bf16[2,8,4224]{2,1,0:T(8,128)(2,1)S(1)}, u32[]{:S(2)}, u32[]{:S(2)}) collective-permute-start(bf16[2,8,4224]{2,1,0:T(8,128)(2,1)S(1)} %bitcast.36), channel_id=1, source_target_pairs={{0,8},{1,9},{2,10},{3,11},{4,12},{5,13},{6,14},{7,15},{8,0},{9,1},... | collective-permute-start | bytes 405512 | tf_op jit(solution)/shard_map/ppermute | solution.py:224
  28.0 2.8 %collective-permute-done.3 = bf16[2,8,4224]{2,1,0:T(8,128)(2,1)S(1)} collective-permute-done((bf16[2,8,4224]{2,1,0:T(8,128)(2,1)S(1)}, bf16[2,8,4224]{2,1,0:T(8,128)(2,1)S(1)}, u32[]{:S(2)}, u32[]{:S(2)}) %collective-permute-start.3) | collective-permute-done | bytes 135200 | tf_op jit(solution)/shard_map/ppermute | solution.py:224
  31.4 5.9 %collective-permute-done.4 = bf16[4,8,4224]{2,1,0:T(8,128)(2,1)S(1)} collective-permute-done((bf16[4,8,4224]{2,1,0:T(8,128)(2,1)S(1)}, bf16[4,8,4224]{2,1,0:T(8,128)(2,1)S(1)}, u32[]{:S(2)}, u32[]{:S(2)}) %collective-permute-start.4) | collective-permute-done | bytes 270368 | tf_op jit(solution)/shard_map/ppermute | solution.py:224
  37.5 10.5 %collective-permute-done.5 = bf16[8,8,4224]{2,1,0:T(8,128)(2,1)S(1)} collective-permute-done((bf16[8,8,4224]{2,1,0:T(8,128)(2,1)S(1)}, bf16[8,8,4224]{2,1,0:T(8,128)(2,1)S(1)}, u32[]{:S(2)}, u32[]{:S(2)}) %collective-permute-start.5) | collective-permute-done | bytes 540704 | tf_op jit(solution)/shard_map/ppermute | solution.py:224
  48.4 2.6 %collective-permute-done.6 = bf16[16,8,4224]{2,1,0:T(8,128)(2,1)S(1)} collective-permute-done((bf16[16,8,4224]{2,1,0:T(8,128)(2,1)S(1)}, bf16[16,8,4224]{2,1,0:T(8,128)(2,1)S(1)}, u32[]{:S(2)}, u32[]{:S(2)}) %collective-permute-start.6) | collective-permute-done | bytes 1081376 | tf_op jit(solution)/shard_map/ppermute | solution.py:224
  51.9 1.0 %copy.12 = bf16[10,8,32,128]{3,2,1,0:T(8,128)(2,1)} copy(bf16[10,8,32,128]{3,1,2,0:T(8,128)(2,1)S(1)} %slice_bitcast_fusion) | data formatting | bytes 1310720
  54.3 4.1 %shard_map.73 = (f32[16,32,128]{2,1,0:T(8,128)}, f32[6,32,128]{2,1,0:T(8,128)}, f32[6,32,128]{2,1,0:T(8,128)}) custom-call(s32[4]{0:T(128)} %pad_add_fusion.shift_ref, f32[6,32,128]{2,1,0:T(8,128)} %copy-done.4, f32[16,32,128]{2,1,0:T(8,128)} %bitcast.40, f32[6,32,128]{2,1,0:T(8,128)} %copy-done.5, f32[16,32,128]{2,1,0:T(8,128)} %pot_ref.5, ...), custom_call_target="tpu_custom_call" | custom-call | tf_op jit(solution)/shard_map/pallas_call | solution.py:162
  58.4 7.8 %collective-permute-start.8 = (f32[6,32,128]{2,1,0:T(8,128)}, f32[6,32,128]{2,1,0:T(8,128)S(1)}, u32[]{:S(2)}, u32[]{:S(2)}) collective-permute-start(f32[6,32,128]{2,1,0:T(8,128)} %get-tuple-element.28), channel_id=1, source_target_pairs={{16,0},{32,16},{48,32},{64,48},{80,64},{96,80},{112,96},{128,112},... | collective-permute-start | bytes 294920 | tf_op jit(solution)/shard_map/ppermute | solution.py:255
  66.2 3.2 %collective-permute-done.7.lo_ref = f32[6,32,128]{2,1,0:T(8,128)S(1)} collective-permute-done((f32[6,32,128]{2,1,0:T(8,128)}, f32[6,32,128]{2,1,0:T(8,128)S(1)}, u32[]{:S(2)}, u32[]{:S(2)}) %collective-permute-start.7) | collective-permute-done | bytes 98336 | tf_op jit(solution)/shard_map/ppermute | solution.py:254
  70.1 4.2 %shard_map.74 = (f32[16,32,128]{2,1,0:T(8,128)}, f32[6,32,128]{2,1,0:T(8,128)}, f32[6,32,128]{2,1,0:T(8,128)}) custom-call(s32[4]{0:T(128)} %pad_add_fusion.shift_ref, f32[6,32,128]{2,1,0:T(8,128)} %copy-done.2, f32[16,32,128]{2,1,0:T(8,128)} %get-tuple-element.27.v_ref.rest_0_, f32[6,32,128]{2,1,0:T(8,128)} %copy-done.3, f32[16,32,128]{2,1,0:T(8,128)} %pot_ref.5, ...), custom_call_target="tpu_custom_call" | custom-call | tf_op jit(solution)/shard_map/pallas_call | solution.py:162
  74.3 5.6 %collective-permute-start.10 = (f32[6,32,128]{2,1,0:T(8,128)}, f32[6,32,128]{2,1,0:T(8,128)S(1)}, u32[]{:S(2)}, u32[]{:S(2)}) collective-permute-start(f32[6,32,128]{2,1,0:T(8,128)} %get-tuple-element.31), channel_id=1, source_target_pairs={{16,0},{32,16},{48,32},{64,48},{80,64},{96,80},{112,96},{128,112},... | collective-permute-start | bytes 294920 | tf_op jit(solution)/shard_map/ppermute | solution.py:255
  79.9 2.8 %collective-permute-done.9.lo_ref = f32[6,32,128]{2,1,0:T(8,128)S(1)} collective-permute-done((f32[6,32,128]{2,1,0:T(8,128)}, f32[6,32,128]{2,1,0:T(8,128)S(1)}, u32[]{:S(2)}, u32[]{:S(2)}) %collective-permute-start.9) | collective-permute-done | bytes 98336 | tf_op jit(solution)/shard_map/ppermute | solution.py:254
  83.4 4.2 %shard_map.75 = (f32[16,32,128]{2,1,0:T(8,128)}, f32[6,32,128]{2,1,0:T(8,128)}, f32[6,32,128]{2,1,0:T(8,128)}) custom-call(s32[4]{0:T(128)} %pad_add_fusion.shift_ref, f32[6,32,128]{2,1,0:T(8,128)} %copy-done, f32[16,32,128]{2,1,0:T(8,128)} %get-tuple-element.30.v_ref, f32[6,32,128]{2,1,0:T(8,128)} %copy-done.1, f32[16,32,128]{2,1,0:T(8,128)} %pot_ref.5, ...), custom_call_target="tpu_custom_call" | custom-call | tf_op jit(solution)/shard_map/pallas_call | solution.py:162
  (41 shorter events, 6.4 us)
Async XLA Ops:
  1.0 52.6 %collective-permute-start = (f32[6,32,128]{2,1,0:T(8,128)S(1)}, f32[6,32,128]{2,1,0:T(8,128)S(1)}, u32[]{:S(2)}, u32[]{:S(2)}) collective-permute-start(f32[6,32,128]{2,1,0:T(8,128)S(1)} %get-tuple-element.36), channel_id=1, source_target_pairs={{0,16},{16,32},{32,48},{48,64},{64,80},{80,96},{96,112},{112,128},... | collective-permute-start | bytes 294920 | tf_op jit(solution)/shard_map/ppermute | solution.py:254
  3.0 50.7 %collective-permute-start.1 = (f32[6,32,128]{2,1,0:T(8,128)S(1)}, f32[6,32,128]{2,1,0:T(8,128)S(1)}, u32[]{:S(2)}, u32[]{:S(2)}) collective-permute-start(f32[6,32,128]{2,1,0:T(8,128)S(1)} %get-tuple-element.35), channel_id=1, source_target_pairs={{16,0},{32,16},{48,32},{64,48},{80,64},{96,80},{112,96},{128,112},... | collective-permute-start | bytes 294920 | tf_op jit(solution)/shard_map/ppermute | solution.py:255
  11.3 14.4 %collective-permute-start.2 = (bf16[1,2,8,4224]{3,2,1,0:T(8,128)(2,1)S(1)}, bf16[1,2,8,4224]{3,2,1,0:T(8,128)(2,1)S(1)}, u32[]{:S(2)}, u32[]{:S(2)}) collective-permute-start(bf16[1,2,8,4224]{3,2,1,0:T(8,128)(2,1)S(1)} %fusion.3), channel_id=1, source_target_pairs={{0,0},{1,16},{2,32},{3,48},{4,64},{5,80},{6,96},{7,112},{8,128},{9... | collective-permute-start | bytes 405512 | tf_op jit(solution)/shard_map/ppermute | solution.py:201
  25.7 5.0 %collective-permute-start.3 = (bf16[2,8,4224]{2,1,0:T(8,128)(2,1)S(1)}, bf16[2,8,4224]{2,1,0:T(8,128)(2,1)S(1)}, u32[]{:S(2)}, u32[]{:S(2)}) collective-permute-start(bf16[2,8,4224]{2,1,0:T(8,128)(2,1)S(1)} %bitcast.36), channel_id=1, source_target_pairs={{0,8},{1,9},{2,10},{3,11},{4,12},{5,13},{6,14},{7,15},{8,0},{9,1},... | collective-permute-start | bytes 405512 | tf_op jit(solution)/shard_map/ppermute | solution.py:224
  30.8 6.5 %collective-permute-start.4 = (bf16[4,8,4224]{2,1,0:T(8,128)(2,1)S(1)}, bf16[4,8,4224]{2,1,0:T(8,128)(2,1)S(1)}, u32[]{:S(2)}, u32[]{:S(2)}) collective-permute-start(bf16[4,8,4224]{2,1,0:T(8,128)(2,1)S(1)} %pad_maximum_fusion.2), channel_id=1, source_target_pairs={{0,2},{1,3},{2,0},{3,1},{4,6},{5,7},{6,4},{7,5},{8,10},{9,11},{10,... | collective-permute-start | bytes 811016 | tf_op jit(solution)/shard_map/ppermute | solution.py:224
  37.4 10.7 %collective-permute-start.5 = (bf16[8,8,4224]{2,1,0:T(8,128)(2,1)S(1)}, bf16[8,8,4224]{2,1,0:T(8,128)(2,1)S(1)}, u32[]{:S(2)}, u32[]{:S(2)}) collective-permute-start(bf16[8,8,4224]{2,1,0:T(8,128)(2,1)S(1)} %pad_maximum_fusion.1), channel_id=1, source_target_pairs={{0,6},{1,7},{2,4},{3,5},{4,2},{5,3},{6,0},{7,1},{8,14},{9,15},{10,... | collective-permute-start | bytes 1622024 | tf_op jit(solution)/shard_map/ppermute | solution.py:224
  48.2 2.8 %collective-permute-start.6 = (bf16[16,8,4224]{2,1,0:T(8,128)(2,1)S(1)}, bf16[16,8,4224]{2,1,0:T(8,128)(2,1)S(1)}, u32[]{:S(2)}, u32[]{:S(2)}) collective-permute-start(bf16[16,8,4224]{2,1,0:T(8,128)(2,1)S(1)} %pad_maximum_fusion), channel_id=1, source_target_pairs={{0,1},{1,0},{2,3},{3,2},{4,5},{5,4},{6,7},{7,6},{8,9},{9,8},{10,11... | collective-permute-start | bytes 3244040 | tf_op jit(solution)/shard_map/ppermute | solution.py:224
  53.6 0.6 copy-start.4
  53.6 0.7 copy-start.5
  58.4 11.1 %collective-permute-start.7 = (f32[6,32,128]{2,1,0:T(8,128)}, f32[6,32,128]{2,1,0:T(8,128)S(1)}, u32[]{:S(2)}, u32[]{:S(2)}) collective-permute-start(f32[6,32,128]{2,1,0:T(8,128)} %get-tuple-element.26), channel_id=1, source_target_pairs={{0,16},{16,32},{32,48},{48,64},{64,80},{80,96},{96,112},{112,128},... | collective-permute-start | bytes 294920 | tf_op jit(solution)/shard_map/ppermute | solution.py:254
  58.4 11.1 %collective-permute-start.8 = (f32[6,32,128]{2,1,0:T(8,128)}, f32[6,32,128]{2,1,0:T(8,128)S(1)}, u32[]{:S(2)}, u32[]{:S(2)}) collective-permute-start(f32[6,32,128]{2,1,0:T(8,128)} %get-tuple-element.28), channel_id=1, source_target_pairs={{16,0},{32,16},{48,32},{64,48},{80,64},{96,80},{112,96},{128,112},... | collective-permute-start | bytes 294920 | tf_op jit(solution)/shard_map/ppermute | solution.py:255
  69.4 0.6 copy-start.2
  69.5 0.7 copy-start.3
  74.3 8.4 %collective-permute-start.9 = (f32[6,32,128]{2,1,0:T(8,128)}, f32[6,32,128]{2,1,0:T(8,128)S(1)}, u32[]{:S(2)}, u32[]{:S(2)}) collective-permute-start(f32[6,32,128]{2,1,0:T(8,128)} %get-tuple-element.29), channel_id=1, source_target_pairs={{0,16},{16,32},{32,48},{48,64},{64,80},{80,96},{96,112},{112,128},... | collective-permute-start | bytes 294920 | tf_op jit(solution)/shard_map/ppermute | solution.py:254
  74.3 8.4 %collective-permute-start.10 = (f32[6,32,128]{2,1,0:T(8,128)}, f32[6,32,128]{2,1,0:T(8,128)S(1)}, u32[]{:S(2)}, u32[]{:S(2)}) collective-permute-start(f32[6,32,128]{2,1,0:T(8,128)} %get-tuple-element.31), channel_id=1, source_target_pairs={{16,0},{32,16},{48,32},{64,48},{80,64},{96,80},{112,96},{128,112},... | collective-permute-start | bytes 294920 | tf_op jit(solution)/shard_map/ppermute | solution.py:255
  82.7 0.6 copy-start
  82.7 0.7 copy-start.1

commit v15 on v11

--- a/solution.py
+++ b/solution.py
@@ -91,9 +91,15 @@
             out_ref, up_ref, down_ref, pad_ref, rows_ref = rest
         planes, breadth, depth = v_ref.shape
         v = v_ref[...]
-        pad_ref[0:RADIUS] = pltpu.roll(lo_ref[...], shift_ref[0], 1)
+        even = shift_ref[2].astype(jnp.float32)
+        odd = 1.0 - even
+        first_swap = lo_ref[...]
+        second_swap = hi_ref[...]
+        low_rim = even * second_swap + odd * first_swap
+        high_rim = even * first_swap + odd * second_swap
+        pad_ref[0:RADIUS] = pltpu.roll(low_rim, shift_ref[0], 1)
         pad_ref[RADIUS:RADIUS + planes] = v
-        pad_ref[RADIUS + planes:] = pltpu.roll(hi_ref[...], shift_ref[1], 1)
+        pad_ref[RADIUS + planes:] = pltpu.roll(high_rim, shift_ref[1], 1)
 
         lines = v.reshape(planes * breadth, depth).astype(jnp.bfloat16)
         picked = jnp.dot(pick_ref[...], lines, preferred_element_type=jnp.float32)
@@ -143,8 +149,10 @@
         else:
             result = kv
         out_ref[...] = result
-        up_ref[...] = result[planes - RADIUS:]
-        down_ref[...] = result[:RADIUS]
+        top = result[planes - RADIUS:]
+        bottom = result[:RADIUS]
+        up_ref[...] = even * top + odd * bottom
+        down_ref[...] = even * bottom + odd * top
 
     return kernel
 
@@ -244,22 +252,29 @@
         [
             jnp.where(tile_index == 0, (breadth - skew) % breadth, 0),
             jnp.where(tile_index == n_grid - 1, skew, 0),
-            jnp.zeros((), jnp.int32),
+            (tile_index % 2 == 0).astype(jnp.int32),
             jnp.zeros((), jnp.int32),
         ]
     ).astype(jnp.int32)
     up = [(i, (i + 1) % n_grid) for i in range(n_grid)]
     down = [(j, i) for i, j in up]
 
-    def step(field, send_up, send_down, prev=None, scale=1.0):
-        low_rim = lax.ppermute(send_up, "grid", up)
-        high_rim = lax.ppermute(send_down, "grid", down)
+    first_pairs = [(g, g ^ 1) for g in range(n_grid)]
+    second_pairs = [(g, (g + 1) % n_grid if g % 2 else (g - 1) % n_grid) for g in range(n_grid)]
+
+    def step(field, send_first, send_second, prev=None, scale=1.0):
+        low_rim = lax.ppermute(send_first, "grid", first_pairs)
+        high_rim = lax.ppermute(send_second, "grid", second_pairs)
         return apply_op(
             shifts, low_rim, field, high_rim, potential, pick, place, proj_in, gain_in, prev, scale
         )
 
     field = states_in[0]
-    first_term = step(field, field[tile_width - RADIUS :], field[:RADIUS])
+    is_even = tile_index % 2 == 0
+    top, bottom = field[tile_width - RADIUS :], field[:RADIUS]
+    first_term = step(
+        field, jnp.where(is_even, top, bottom), jnp.where(is_even, bottom, top)
+    )
     second_term = step(*first_term, field, 2.0)
     filtered = step(*second_term, first_term[0], 2.0)
     return filtered[0][None]

time: 87.6 us -> 90.7 us (1.035)
  the two profiles are of different devices: /device:TPU:6 before, /device:TPU:22 now
where the time goes in v15:
time: 90.7 us; the launch traced here: 90.3 us
  waiting for transfers between devices  51.5 us (57%)
  Pallas kernels  12.6 us (14%)
  starting transfers between devices  12.1 us (13%)
  other arithmetic  7.67 us (8%)
  local copies, waits for them, and re-layouts  4.93 us (5%)
  between operations  1.49 us (2%)
    ppermute x4, waiting for transfers between devices, shards(): lax.ppermute(gathered, 'states', [(s, exchange(s)) for s in range(n_state...  29.4 us
    pallas_call x3, Pallas kernels, apply_op(): pl.pallas_call(make_kernel(scale, prev is not None, home_count, proj.shap...  12.6 us
    ppermute x3, waiting for transfers between devices, step(): low_rim = lax.ppermute(send_first, 'grid', first_pairs)  9.41 us
    ppermute x3, waiting for transfers between devices, step(): high_rim = lax.ppermute(send_second, 'grid', second_pairs)  7.4 us
    ppermute x1, waiting for transfers between devices, shards(): packed = lax.ppermute(packed, ('grid', 'states'), pairs)  5.26 us
    ppermute x3, starting transfers between devices, step(): high_rim = lax.ppermute(send_second, 'grid', second_pairs)  5.17 us
    ppermute x1, starting transfers between devices, shards(): packed = lax.ppermute(packed, ('grid', 'states'), pairs)  3.39 us
    unnamed x19, local copies, waits for them, and re-layouts  3.15 us
  transfers between devices with their start and end apart: 11, of which 9 were waited for; matrix products, arithmetic and copies ran while one was open for 11% of the time, Pallas kernels for 0%

profile of v15, /device:TPU:22, one launch (start us, length us, event | category | flops | bytes accessed | tf_op | source)
XLA Modules:
  0.0 90.3 jit_solution(9542811214263403920)
XLA Ops:
  0.0 1.0 %select_bitcast_fusion = (f32[6,32,128]{2,1,0:T(8,128)S(1)}, f32[6,32,128]{2,1,0:T(8,128)S(1)}) fusion(f32[1,16,32,128]{3,2,1,0:T(8,128)} %param.9, pred[]{:T(512)S(6)} %eq.68), kind=kLoop, calls=%fused_computation.13 | loop fusion | flops 49152 | bytes 393217 | tf_op jit(solution)/shard_map/jit(_where)/select_n | solution.py:276
  1.0 2.0 %collective-permute-start = (f32[6,32,128]{2,1,0:T(8,128)S(1)}, f32[6,32,128]{2,1,0:T(8,128)S(1)}, u32[]{:S(2)}, u32[]{:S(2)}) collective-permute-start(f32[6,32,128]{2,1,0:T(8,128)S(1)} %get-tuple-element.36), channel_id=1, source_target_pairs={{0,16},{16,0},{32,48},{48,32},{64,80},{80,64},{96,112},{112,96},{1... | collective-permute-start | bytes 294920 | tf_op jit(solution)/shard_map/ppermute | solution.py:266
  3.0 4.7 %collective-permute-start.1 = (f32[6,32,128]{2,1,0:T(8,128)S(1)}, f32[6,32,128]{2,1,0:T(8,128)S(1)}, u32[]{:S(2)}, u32[]{:S(2)}) collective-permute-start(f32[6,32,128]{2,1,0:T(8,128)S(1)} %get-tuple-element.35), channel_id=1, source_target_pairs={{0,240},{16,32},{32,16},{48,64},{64,48},{80,96},{96,80},{112,128},... | collective-permute-start | bytes 294920 | tf_op jit(solution)/shard_map/ppermute | solution.py:267
  8.4 0.9 %fusion.3 = bf16[1,2,8,4224]{3,2,1,0:T(8,128)(2,1)S(1)} fusion(bf16[1,2,8,1]{3,2,1,0:T(8,128)(2,1)S(1)} %copy.11, bf16[1,2,8,4096]{3,2,1,0:T(8,128)(2,1)} %param.11), kind=kLoop, calls=%fused_computation.12 | loop fusion | flops 405504 | bytes 266272 | tf_op jit(solution)/shard_map/concatenate | solution.py:206
  9.4 3.4 %collective-permute-start.2 = (bf16[1,2,8,4224]{3,2,1,0:T(8,128)(2,1)S(1)}, bf16[1,2,8,4224]{3,2,1,0:T(8,128)(2,1)S(1)}, u32[]{:S(2)}, u32[]{:S(2)}) collective-permute-start(bf16[1,2,8,4224]{3,2,1,0:T(8,128)(2,1)S(1)} %fusion.3), channel_id=1, source_target_pairs={{0,0},{1,16},{2,32},{3,48},{4,64},{5,80},{6,96},{7,112},{8,128},{9... | collective-permute-start | bytes 405512 | tf_op jit(solution)/shard_map/ppermute | solution.py:208
  14.2 0.9 fusion.1.pick_ref
  15.1 0.8 fusion.place_ref
  16.5 0.9 %convert_reduce_fusion.1 = s32[10]{0:T(128)S(1)} fusion(s32[10]{0:T(128)} %param.13), kind=kLoop, calls=%fused_computation.21 | loop fusion | flops 490 | bytes 80 | tf_op jit(solution)/shard_map/reduce_sum | solution.py:200
  17.6 1.4 %iota_reduce_fusion = (pred[10]{0:T(512)(128)(4,1)}, s32[10]{0:T(128)S(1)}) fusion(s32[16]{0:T(128)S(1)} %stack.87, s32[10]{0:T(128)} %param.13), kind=kLoop, calls=%fused_computation.23 | loop fusion | flops 1210 | bytes 154 | tf_op jit(solution)/shard_map/shards/reduce | solution.py:236
  19.0 5.3 %collective-permute-done.2 = bf16[1,2,8,4224]{3,2,1,0:T(8,128)(2,1)S(1)} collective-permute-done((bf16[1,2,8,4224]{3,2,1,0:T(8,128)(2,1)S(1)}, bf16[1,2,8,4224]{3,2,1,0:T(8,128)(2,1)S(1)}, u32[]{:S(2)}, u32[]{:S(2)}) %collective-permute-start.2) | collective-permute-done | bytes 135200 | tf_op jit(solution)/shard_map/ppermute | solution.py:208
  24.3 1.3 %collective-permute-start.3 = (bf16[2,8,4224]{2,1,0:T(8,128)(2,1)S(1)}, bf16[2,8,4224]{2,1,0:T(8,128)(2,1)S(1)}, u32[]{:S(2)}, u32[]{:S(2)}) collective-permute-start(bf16[2,8,4224]{2,1,0:T(8,128)(2,1)S(1)} %bitcast.37), channel_id=1, source_target_pairs={{0,8},{1,9},{2,10},{3,11},{4,12},{5,13},{6,14},{7,15},{8,0},{9,1},... | collective-permute-start | bytes 405512 | tf_op jit(solution)/shard_map/ppermute | solution.py:231
  26.1 4.3 %collective-permute-done.3 = bf16[2,8,4224]{2,1,0:T(8,128)(2,1)S(1)} collective-permute-done((bf16[2,8,4224]{2,1,0:T(8,128)(2,1)S(1)}, bf16[2,8,4224]{2,1,0:T(8,128)(2,1)S(1)}, u32[]{:S(2)}, u32[]{:S(2)}) %collective-permute-start.3) | collective-permute-done | bytes 135200 | tf_op jit(solution)/shard_map/ppermute | solution.py:231
  30.6 8.2 %collective-permute-done.4 = bf16[4,8,4224]{2,1,0:T(8,128)(2,1)S(1)} collective-permute-done((bf16[4,8,4224]{2,1,0:T(8,128)(2,1)S(1)}, bf16[4,8,4224]{2,1,0:T(8,128)(2,1)S(1)}, u32[]{:S(2)}, u32[]{:S(2)}) %collective-permute-start.4) | collective-permute-done | bytes 270368 | tf_op jit(solution)/shard_map/ppermute | solution.py:231
  39.0 14.3 %collective-permute-done.5 = bf16[8,8,4224]{2,1,0:T(8,128)(2,1)S(1)} collective-permute-done((bf16[8,8,4224]{2,1,0:T(8,128)(2,1)S(1)}, bf16[8,8,4224]{2,1,0:T(8,128)(2,1)S(1)}, u32[]{:S(2)}, u32[]{:S(2)}) %collective-permute-start.5) | collective-permute-done | bytes 540704 | tf_op jit(solution)/shard_map/ppermute | solution.py:231
  53.6 2.6 %collective-permute-done.6 = bf16[16,8,4224]{2,1,0:T(8,128)(2,1)S(1)} collective-permute-done((bf16[16,8,4224]{2,1,0:T(8,128)(2,1)S(1)}, bf16[16,8,4224]{2,1,0:T(8,128)(2,1)S(1)}, u32[]{:S(2)}, u32[]{:S(2)}) %collective-permute-start.6) | collective-permute-done | bytes 1081376 | tf_op jit(solution)/shard_map/ppermute | solution.py:231
  57.2 1.0 %copy.12 = bf16[10,8,32,128]{3,2,1,0:T(8,128)(2,1)} copy(bf16[10,8,32,128]{3,1,2,0:T(8,128)(2,1)S(1)} %slice_bitcast_fusion) | data formatting | bytes 1310720
  58.4 0.8 broadcast_in_dim.36.gain_ref
  59.2 4.2 %shard_map.73 = (f32[16,32,128]{2,1,0:T(8,128)}, f32[6,32,128]{2,1,0:T(8,128)}, f32[6,32,128]{2,1,0:T(8,128)}) custom-call(s32[4]{0:T(128)} %pad_add_fusion.shift_ref, f32[6,32,128]{2,1,0:T(8,128)} %copy-done, f32[16,32,128]{2,1,0:T(8,128)} %bitcast.41, f32[6,32,128]{2,1,0:T(8,128)} %copy-done.1, f32[16,32,128]{2,1,0:T(8,128)} %pot_ref.5, ...), custom_call_target="tpu_custom_call" | custom-call | tf_op jit(solution)/shard_map/pallas_call | solution.py:169
  63.4 4.9 %collective-permute-done.7.lo_ref = f32[6,32,128]{2,1,0:T(8,128)S(1)} collective-permute-done((f32[6,32,128]{2,1,0:T(8,128)}, f32[6,32,128]{2,1,0:T(8,128)S(1)}, u32[]{:S(2)}, u32[]{:S(2)}) %collective-permute-start.7) | collective-permute-done | bytes 98336 | tf_op jit(solution)/shard_map/ppermute | solution.py:266
  68.4 3.7 %collective-permute-done.8.hi_ref = f32[6,32,128]{2,1,0:T(8,128)S(1)} collective-permute-done((f32[6,32,128]{2,1,0:T(8,128)}, f32[6,32,128]{2,1,0:T(8,128)S(1)}, u32[]{:S(2)}, u32[]{:S(2)}) %collective-permute-start.8) | collective-permute-done | bytes 98336 | tf_op jit(solution)/shard_map/ppermute | solution.py:267
  72.7 4.2 %shard_map.74 = (f32[16,32,128]{2,1,0:T(8,128)}, f32[6,32,128]{2,1,0:T(8,128)}, f32[6,32,128]{2,1,0:T(8,128)}) custom-call(s32[4]{0:T(128)} %pad_add_fusion.shift_ref, f32[6,32,128]{2,1,0:T(8,128)} %copy-done.4, f32[16,32,128]{2,1,0:T(8,128)} %get-tuple-element.27.v_ref.rest_0_, f32[6,32,128]{2,1,0:T(8,128)} %copy-done.5, f32[16,32,128]{2,1,0:T(8,128)} %pot_ref.5, ...), custom_call_target="tpu_custom_call" | custom-call | tf_op jit(solution)/shard_map/pallas_call | solution.py:169
  77.3 4.5 %collective-permute-done.9.lo_ref = f32[6,32,128]{2,1,0:T(8,128)S(1)} collective-permute-done((f32[6,32,128]{2,1,0:T(8,128)}, f32[6,32,128]{2,1,0:T(8,128)S(1)}, u32[]{:S(2)}, u32[]{:S(2)}) %collective-permute-start.9) | collective-permute-done | bytes 98336 | tf_op jit(solution)/shard_map/ppermute | solution.py:266
  81.8 3.7 %collective-permute-done.10.hi_ref = f32[6,32,128]{2,1,0:T(8,128)S(1)} collective-permute-done((f32[6,32,128]{2,1,0:T(8,128)}, f32[6,32,128]{2,1,0:T(8,128)S(1)}, u32[]{:S(2)}, u32[]{:S(2)}) %collective-permute-start.10) | collective-permute-done | bytes 98336 | tf_op jit(solution)/shard_map/ppermute | solution.py:267
  86.1 4.2 %shard_map.75 = (f32[16,32,128]{2,1,0:T(8,128)}, f32[6,32,128]{2,1,0:T(8,128)}, f32[6,32,128]{2,1,0:T(8,128)}) custom-call(s32[4]{0:T(128)} %pad_add_fusion.shift_ref, f32[6,32,128]{2,1,0:T(8,128)} %copy-done.2, f32[16,32,128]{2,1,0:T(8,128)} %get-tuple-element.30.v_ref, f32[6,32,128]{2,1,0:T(8,128)} %copy-done.3, f32[16,32,128]{2,1,0:T(8,128)} %pot_ref.5, ...), custom_call_target="tpu_custom_call" | custom-call | tf_op jit(solution)/shard_map/pallas_call | solution.py:169
  (41 shorter events, 5.7 us)
Async XLA Ops:
  1.0 57.4 %collective-permute-start = (f32[6,32,128]{2,1,0:T(8,128)S(1)}, f32[6,32,128]{2,1,0:T(8,128)S(1)}, u32[]{:S(2)}, u32[]{:S(2)}) collective-permute-start(f32[6,32,128]{2,1,0:T(8,128)S(1)} %get-tuple-element.36), channel_id=1, source_target_pairs={{0,16},{16,0},{32,48},{48,32},{64,80},{80,64},{96,112},{112,96},{1... | collective-permute-start | bytes 294920 | tf_op jit(solution)/shard_map/ppermute | solution.py:266
  3.0 55.4 %collective-permute-start.1 = (f32[6,32,128]{2,1,0:T(8,128)S(1)}, f32[6,32,128]{2,1,0:T(8,128)S(1)}, u32[]{:S(2)}, u32[]{:S(2)}) collective-permute-start(f32[6,32,128]{2,1,0:T(8,128)S(1)} %get-tuple-element.35), channel_id=1, source_target_pairs={{0,240},{16,32},{32,16},{48,64},{64,48},{80,96},{96,80},{112,128},... | collective-permute-start | bytes 294920 | tf_op jit(solution)/shard_map/ppermute | solution.py:267
  9.4 14.9 %collective-permute-start.2 = (bf16[1,2,8,4224]{3,2,1,0:T(8,128)(2,1)S(1)}, bf16[1,2,8,4224]{3,2,1,0:T(8,128)(2,1)S(1)}, u32[]{:S(2)}, u32[]{:S(2)}) collective-permute-start(bf16[1,2,8,4224]{3,2,1,0:T(8,128)(2,1)S(1)} %fusion.3), channel_id=1, source_target_pairs={{0,0},{1,16},{2,32},{3,48},{4,64},{5,80},{6,96},{7,112},{8,128},{9... | collective-permute-start | bytes 405512 | tf_op jit(solution)/shard_map/ppermute | solution.py:208
  24.3 6.2 %collective-permute-start.3 = (bf16[2,8,4224]{2,1,0:T(8,128)(2,1)S(1)}, bf16[2,8,4224]{2,1,0:T(8,128)(2,1)S(1)}, u32[]{:S(2)}, u32[]{:S(2)}) collective-permute-start(bf16[2,8,4224]{2,1,0:T(8,128)(2,1)S(1)} %bitcast.37), channel_id=1, source_target_pairs={{0,8},{1,9},{2,10},{3,11},{4,12},{5,13},{6,14},{7,15},{8,0},{9,1},... | collective-permute-start | bytes 405512 | tf_op jit(solution)/shard_map/ppermute | solution.py:231
  30.5 8.3 %collective-permute-start.4 = (bf16[4,8,4224]{2,1,0:T(8,128)(2,1)S(1)}, bf16[4,8,4224]{2,1,0:T(8,128)(2,1)S(1)}, u32[]{:S(2)}, u32[]{:S(2)}) collective-permute-start(bf16[4,8,4224]{2,1,0:T(8,128)(2,1)S(1)} %pad_maximum_fusion.2), channel_id=1, source_target_pairs={{0,2},{1,3},{2,0},{3,1},{4,6},{5,7},{6,4},{7,5},{8,10},{9,11},{10,... | collective-permute-start | bytes 811016 | tf_op jit(solution)/shard_map/ppermute | solution.py:231
  38.9 14.4 %collective-permute-start.5 = (bf16[8,8,4224]{2,1,0:T(8,128)(2,1)S(1)}, bf16[8,8,4224]{2,1,0:T(8,128)(2,1)S(1)}, u32[]{:S(2)}, u32[]{:S(2)}) collective-permute-start(bf16[8,8,4224]{2,1,0:T(8,128)(2,1)S(1)} %pad_maximum_fusion.1), channel_id=1, source_target_pairs={{0,6},{1,7},{2,4},{3,5},{4,2},{5,3},{6,0},{7,1},{8,14},{9,15},{10,... | collective-permute-start | bytes 1622024 | tf_op jit(solution)/shard_map/ppermute | solution.py:231
  53.5 2.8 %collective-permute-start.6 = (bf16[16,8,4224]{2,1,0:T(8,128)(2,1)S(1)}, bf16[16,8,4224]{2,1,0:T(8,128)(2,1)S(1)}, u32[]{:S(2)}, u32[]{:S(2)}) collective-permute-start(bf16[16,8,4224]{2,1,0:T(8,128)(2,1)S(1)} %pad_maximum_fusion), channel_id=1, source_target_pairs={{0,1},{1,0},{2,3},{3,2},{4,5},{5,4},{6,7},{7,6},{8,9},{9,8},{10,11... | collective-permute-start | bytes 3244040 | tf_op jit(solution)/shard_map/ppermute | solution.py:231
  58.4 0.8 copy-start
  58.4 0.8 copy-start.1
  63.3 5.0 %collective-permute-start.7 = (f32[6,32,128]{2,1,0:T(8,128)}, f32[6,32,128]{2,1,0:T(8,128)S(1)}, u32[]{:S(2)}, u32[]{:S(2)}) collective-permute-start(f32[6,32,128]{2,1,0:T(8,128)} %get-tuple-element.26), channel_id=1, source_target_pairs={{0,16},{16,0},{32,48},{48,32},{64,80},{80,64},{96,112},{112,96},{1... | collective-permute-start | bytes 294920 | tf_op jit(solution)/shard_map/ppermute | solution.py:266
  63.3 8.7 %collective-permute-start.8 = (f32[6,32,128]{2,1,0:T(8,128)}, f32[6,32,128]{2,1,0:T(8,128)S(1)}, u32[]{:S(2)}, u32[]{:S(2)}) collective-permute-start(f32[6,32,128]{2,1,0:T(8,128)} %get-tuple-element.28), channel_id=1, source_target_pairs={{0,240},{16,32},{32,16},{48,64},{64,48},{80,96},{96,80},{112,128},... | collective-permute-start | bytes 294920 | tf_op jit(solution)/shard_map/ppermute | solution.py:267
  68.4 3.7 %copy-start.4 = (f32[6,32,128]{2,1,0:T(8,128)}, f32[6,32,128]{2,1,0:T(8,128)S(1)}, u32[]{:S(2)}) copy-start(f32[6,32,128]{2,1,0:T(8,128)S(1)} %collective-permute-done.7.lo_ref) | copy-start | bytes 294916
  72.1 0.6 copy-start.5
  76.9 4.8 %collective-permute-start.9 = (f32[6,32,128]{2,1,0:T(8,128)}, f32[6,32,128]{2,1,0:T(8,128)S(1)}, u32[]{:S(2)}, u32[]{:S(2)}) collective-permute-start(f32[6,32,128]{2,1,0:T(8,128)} %get-tuple-element.29), channel_id=1, source_target_pairs={{0,16},{16,0},{32,48},{48,32},{64,80},{80,64},{96,112},{112,96},{1... | collective-permute-start | bytes 294920 | tf_op jit(solution)/shard_map/ppermute | solution.py:266
  76.9 8.5 %collective-permute-start.10 = (f32[6,32,128]{2,1,0:T(8,128)}, f32[6,32,128]{2,1,0:T(8,128)S(1)}, u32[]{:S(2)}, u32[]{:S(2)}) collective-permute-start(f32[6,32,128]{2,1,0:T(8,128)} %get-tuple-element.31), channel_id=1, source_target_pairs={{0,240},{16,32},{32,16},{48,64},{64,48},{80,96},{96,80},{112,128},... | collective-permute-start | bytes 294920 | tf_op jit(solution)/shard_map/ppermute | solution.py:267
  81.8 3.7 %copy-start.2 = (f32[6,32,128]{2,1,0:T(8,128)}, f32[6,32,128]{2,1,0:T(8,128)S(1)}, u32[]{:S(2)}) copy-start(f32[6,32,128]{2,1,0:T(8,128)S(1)} %collective-permute-done.9.lo_ref) | copy-start | bytes 294916
  85.5 0.6 copy-start.3

commit v16 on v12

--- a/solution.py
+++ b/solution.py
@@ -157,7 +157,8 @@
     block_rows = picked_rows // home_count
     args = [shifts, lo, v, hi, pot, pick, place, proj, gain] + ([prev] if prev is not None else [])
     vspec = pl.BlockSpec(memory_space=pltpu.VMEM)
-    in_specs = [pl.BlockSpec(memory_space=pltpu.SMEM)] + [vspec] * (len(args) - 1)
+    sspec = pl.BlockSpec(memory_space=pltpu.SMEM)
+    in_specs = [sspec] + [vspec] * 7 + [sspec] + [vspec] * (len(args) - 9)
     rim_shape = jax.ShapeDtypeStruct((RADIUS, breadth, depth), jnp.float32)
     return pl.pallas_call(
         make_kernel(scale, prev is not None, home_count, proj.shape[0] // home_count, block_rows),
@@ -237,9 +238,7 @@
     ).astype(jnp.bfloat16)
     place = pick.T
     proj_in = proj_rows.reshape(home_count * proj_count, breadth, line_depth)
-    gain_in = jnp.broadcast_to(
-        atom_gain.reshape(home_count * proj_count, 1, 1), (home_count * proj_count, 1, line_depth)
-    )
+    gain_in = atom_gain.reshape(home_count * proj_count)
     skew = wrap_rows[0]
     shifts = jnp.stack(
         [

time: 87.2 us -> 87.6 us (level)
  transfers between devices with their start and end apart: 11 -> 11, of which waited for: 7 -> 7; matrix products, arithmetic and copies ran while one was open for 11% -> 12% of each run, Pallas kernels for 0% -> 0%
where the time goes in v16:
time: 87.6 us; the launch traced here: 87.3 us
  waiting for transfers between devices  34.1 us (39%)
  starting transfers between devices  26.5 us (30%)
  Pallas kernels  12.1 us (14%)
  other arithmetic  6.72 us (8%)
  local copies, waits for them, and re-layouts  6.34 us (7%)
  between operations  1.45 us (2%)
    ppermute x4, waiting for transfers between devices, shards(): lax.ppermute(gathered, 'states', [(s, exchange(s)) for s in range(n_state...  21.8 us
    ppermute x3, starting transfers between devices, step(): high_rim = lax.ppermute(send_down, 'grid', down)  20.1 us
    pallas_call x3, Pallas kernels, apply_op(): pl.pallas_call(make_kernel(scale, prev is not None, home_count, proj.shap...  12.1 us
    ppermute x1, waiting for transfers between devices, shards(): packed = lax.ppermute(packed, ('grid', 'states'), pairs)  6.33 us
    ppermute x3, waiting for transfers between devices, step(): low_rim = lax.ppermute(send_up, 'grid', up)  6.03 us
    unnamed x19, local copies, waits for them, and re-layouts  3.86 us
    ppermute x4, starting transfers between devices, shards(): lax.ppermute(gathered, 'states', [(s, exchange(s)) for s in range(n_state...  2.42 us
    ppermute x3, starting transfers between devices, step(): low_rim = lax.ppermute(send_up, 'grid', up)  2 us
  transfers between devices with their start and end apart: 11, of which 7 were waited for; matrix products, arithmetic and copies ran while one was open for 12% of the time, Pallas kernels for 0%

profile of v16, /device:TPU:6, one launch (start us, length us, event | category | flops | bytes accessed | tf_op | source)
XLA Modules:
  0.0 87.3 jit_solution(1130575213108243431)
XLA Ops:
  0.0 1.0 %slice_bitcast_fusion.1 = (f32[6,32,128]{2,1,0:T(8,128)S(1)}, f32[6,32,128]{2,1,0:T(8,128)S(1)}) fusion(f32[1,16,32,128]{3,2,1,0:T(8,128)} %param.9), kind=kLoop, calls=%fused_computation.13 | loop fusion | bytes 393216 | tf_op jit(solution)/shard_map/slice | solution.py:262
  1.0 2.0 %collective-permute-start = (f32[6,32,128]{2,1,0:T(8,128)S(1)}, f32[6,32,128]{2,1,0:T(8,128)S(1)}, u32[]{:S(2)}, u32[]{:S(2)}) collective-permute-start(f32[6,32,128]{2,1,0:T(8,128)S(1)} %get-tuple-element.36), channel_id=1, source_target_pairs={{0,16},{16,32},{32,48},{48,64},{64,80},{80,96},{96,112},{112,128},... | collective-permute-start | bytes 294920 | tf_op jit(solution)/shard_map/ppermute | solution.py:255
  3.0 6.7 %collective-permute-start.1 = (f32[6,32,128]{2,1,0:T(8,128)S(1)}, f32[6,32,128]{2,1,0:T(8,128)S(1)}, u32[]{:S(2)}, u32[]{:S(2)}) collective-permute-start(f32[6,32,128]{2,1,0:T(8,128)S(1)} %get-tuple-element.35), channel_id=1, source_target_pairs={{16,0},{32,16},{48,32},{64,48},{80,64},{96,80},{112,96},{128,112},... | collective-permute-start | bytes 294920 | tf_op jit(solution)/shard_map/ppermute | solution.py:256
  9.6 0.8 copy.11
  10.4 0.9 %fusion.3 = bf16[1,2,8,4224]{3,2,1,0:T(8,128)(2,1)S(1)} fusion(bf16[1,2,8,1]{3,2,1,0:T(8,128)(2,1)S(1)} %copy.11, bf16[1,2,8,4096]{3,2,1,0:T(8,128)(2,1)} %param.11), kind=kLoop, calls=%fused_computation.12 | loop fusion | flops 405504 | bytes 266272 | tf_op jit(solution)/shard_map/concatenate | solution.py:200
  11.3 1.9 %collective-permute-start.2 = (bf16[1,2,8,4224]{3,2,1,0:T(8,128)(2,1)S(1)}, bf16[1,2,8,4224]{3,2,1,0:T(8,128)(2,1)S(1)}, u32[]{:S(2)}, u32[]{:S(2)}) collective-permute-start(bf16[1,2,8,4224]{3,2,1,0:T(8,128)(2,1)S(1)} %fusion.3), channel_id=1, source_target_pairs={{0,0},{1,16},{2,32},{3,48},{4,64},{5,80},{6,96},{7,112},{8,128},{9... | collective-permute-start | bytes 405512 | tf_op jit(solution)/shard_map/ppermute | solution.py:202
  14.7 0.9 fusion.1.pick_ref
  15.5 0.8 fusion.place_ref
  17.0 0.9 %convert_reduce_fusion.1 = s32[10]{0:T(128)S(1)} fusion(s32[10]{0:T(128)} %param.13), kind=kLoop, calls=%fused_computation.21 | loop fusion | flops 490 | bytes 80 | tf_op jit(solution)/shard_map/reduce_sum | solution.py:194
  18.0 1.3 %iota_reduce_fusion = (pred[10]{0:T(512)(128)(4,1)}, s32[10]{0:T(128)S(1)}) fusion(s32[16]{0:T(128)S(1)} %stack.79, s32[10]{0:T(128)} %param.13), kind=kLoop, calls=%fused_computation.23 | loop fusion | flops 1210 | bytes 154 | tf_op jit(solution)/shard_map/shards/reduce | solution.py:230
  19.4 6.3 %collective-permute-done.2 = bf16[1,2,8,4224]{3,2,1,0:T(8,128)(2,1)S(1)} collective-permute-done((bf16[1,2,8,4224]{3,2,1,0:T(8,128)(2,1)S(1)}, bf16[1,2,8,4224]{3,2,1,0:T(8,128)(2,1)S(1)}, u32[]{:S(2)}, u32[]{:S(2)}) %collective-permute-start.2) | collective-permute-done | bytes 135200 | tf_op jit(solution)/shard_map/ppermute | solution.py:202
  25.7 1.6 %collective-permute-start.3 = (bf16[2,8,4224]{2,1,0:T(8,128)(2,1)S(1)}, bf16[2,8,4224]{2,1,0:T(8,128)(2,1)S(1)}, u32[]{:S(2)}, u32[]{:S(2)}) collective-permute-start(bf16[2,8,4224]{2,1,0:T(8,128)(2,1)S(1)} %bitcast.36), channel_id=1, source_target_pairs={{0,8},{1,9},{2,10},{3,11},{4,12},{5,13},{6,14},{7,15},{8,0},{9,1},... | collective-permute-start | bytes 405512 | tf_op jit(solution)/shard_map/ppermute | solution.py:225
  28.0 2.8 %collective-permute-done.3 = bf16[2,8,4224]{2,1,0:T(8,128)(2,1)S(1)} collective-permute-done((bf16[2,8,4224]{2,1,0:T(8,128)(2,1)S(1)}, bf16[2,8,4224]{2,1,0:T(8,128)(2,1)S(1)}, u32[]{:S(2)}, u32[]{:S(2)}) %collective-permute-start.3) | collective-permute-done | bytes 135200 | tf_op jit(solution)/shard_map/ppermute | solution.py:225
  31.4 5.9 %collective-permute-done.4 = bf16[4,8,4224]{2,1,0:T(8,128)(2,1)S(1)} collective-permute-done((bf16[4,8,4224]{2,1,0:T(8,128)(2,1)S(1)}, bf16[4,8,4224]{2,1,0:T(8,128)(2,1)S(1)}, u32[]{:S(2)}, u32[]{:S(2)}) %collective-permute-start.4) | collective-permute-done | bytes 270368 | tf_op jit(solution)/shard_map/ppermute | solution.py:225
  37.5 10.5 %collective-permute-done.5 = bf16[8,8,4224]{2,1,0:T(8,128)(2,1)S(1)} collective-permute-done((bf16[8,8,4224]{2,1,0:T(8,128)(2,1)S(1)}, bf16[8,8,4224]{2,1,0:T(8,128)(2,1)S(1)}, u32[]{:S(2)}, u32[]{:S(2)}) %collective-permute-start.5) | collective-permute-done | bytes 540704 | tf_op jit(solution)/shard_map/ppermute | solution.py:225
  48.4 2.6 %collective-permute-done.6 = bf16[16,8,4224]{2,1,0:T(8,128)(2,1)S(1)} collective-permute-done((bf16[16,8,4224]{2,1,0:T(8,128)(2,1)S(1)}, bf16[16,8,4224]{2,1,0:T(8,128)(2,1)S(1)}, u32[]{:S(2)}, u32[]{:S(2)}) %collective-permute-start.6) | collective-permute-done | bytes 1081376 | tf_op jit(solution)/shard_map/ppermute | solution.py:225
  51.9 1.0 %copy.12 = bf16[10,8,32,128]{3,2,1,0:T(8,128)(2,1)} copy(bf16[10,8,32,128]{3,1,2,0:T(8,128)(2,1)S(1)} %slice_bitcast_fusion) | data formatting | bytes 1310720
  54.3 4.0 %shard_map.73 = (f32[16,32,128]{2,1,0:T(8,128)}, f32[6,32,128]{2,1,0:T(8,128)}, f32[6,32,128]{2,1,0:T(8,128)}) custom-call(s32[4]{0:T(128)} %pad_add_fusion.shift_ref, f32[6,32,128]{2,1,0:T(8,128)} %copy-done.4, f32[16,32,128]{2,1,0:T(8,128)} %bitcast.40, f32[6,32,128]{2,1,0:T(8,128)} %copy-done.5, f32[16,32,128]{2,1,0:T(8,128)} %pot_ref.5, ...), custom_call_target="tpu_custom_call" | custom-call | tf_op jit(solution)/shard_map/pallas_call | solution.py:163
  58.3 7.8 %collective-permute-start.8 = (f32[6,32,128]{2,1,0:T(8,128)}, f32[6,32,128]{2,1,0:T(8,128)S(1)}, u32[]{:S(2)}, u32[]{:S(2)}) collective-permute-start(f32[6,32,128]{2,1,0:T(8,128)} %get-tuple-element.28), channel_id=1, source_target_pairs={{16,0},{32,16},{48,32},{64,48},{80,64},{96,80},{112,96},{128,112},... | collective-permute-start | bytes 294920 | tf_op jit(solution)/shard_map/ppermute | solution.py:256
  66.1 3.2 %collective-permute-done.7.lo_ref = f32[6,32,128]{2,1,0:T(8,128)S(1)} collective-permute-done((f32[6,32,128]{2,1,0:T(8,128)}, f32[6,32,128]{2,1,0:T(8,128)S(1)}, u32[]{:S(2)}, u32[]{:S(2)}) %collective-permute-start.7) | collective-permute-done | bytes 98336 | tf_op jit(solution)/shard_map/ppermute | solution.py:255
  70.0 4.1 %shard_map.74 = (f32[16,32,128]{2,1,0:T(8,128)}, f32[6,32,128]{2,1,0:T(8,128)}, f32[6,32,128]{2,1,0:T(8,128)}) custom-call(s32[4]{0:T(128)} %pad_add_fusion.shift_ref, f32[6,32,128]{2,1,0:T(8,128)} %copy-done.2, f32[16,32,128]{2,1,0:T(8,128)} %get-tuple-element.27.v_ref.rest_0_, f32[6,32,128]{2,1,0:T(8,128)} %copy-done.3, f32[16,32,128]{2,1,0:T(8,128)} %pot_ref.5, ...), custom_call_target="tpu_custom_call" | custom-call | tf_op jit(solution)/shard_map/pallas_call | solution.py:163
  74.1 5.6 %collective-permute-start.10 = (f32[6,32,128]{2,1,0:T(8,128)}, f32[6,32,128]{2,1,0:T(8,128)S(1)}, u32[]{:S(2)}, u32[]{:S(2)}) collective-permute-start(f32[6,32,128]{2,1,0:T(8,128)} %get-tuple-element.31), channel_id=1, source_target_pairs={{16,0},{32,16},{48,32},{64,48},{80,64},{96,80},{112,96},{128,112},... | collective-permute-start | bytes 294920 | tf_op jit(solution)/shard_map/ppermute | solution.py:256
  79.7 2.8 %collective-permute-done.9.lo_ref = f32[6,32,128]{2,1,0:T(8,128)S(1)} collective-permute-done((f32[6,32,128]{2,1,0:T(8,128)}, f32[6,32,128]{2,1,0:T(8,128)S(1)}, u32[]{:S(2)}, u32[]{:S(2)}) %collective-permute-start.9) | collective-permute-done | bytes 98336 | tf_op jit(solution)/shard_map/ppermute | solution.py:255
  83.2 4.1 %shard_map.75 = (f32[16,32,128]{2,1,0:T(8,128)}, f32[6,32,128]{2,1,0:T(8,128)}, f32[6,32,128]{2,1,0:T(8,128)}) custom-call(s32[4]{0:T(128)} %pad_add_fusion.shift_ref, f32[6,32,128]{2,1,0:T(8,128)} %copy-done, f32[16,32,128]{2,1,0:T(8,128)} %get-tuple-element.30.v_ref, f32[6,32,128]{2,1,0:T(8,128)} %copy-done.1, f32[16,32,128]{2,1,0:T(8,128)} %pot_ref.5, ...), custom_call_target="tpu_custom_call" | custom-call | tf_op jit(solution)/shard_map/pallas_call | solution.py:163
  (41 shorter events, 6.4 us)
Async XLA Ops:
  1.0 52.6 %collective-permute-start = (f32[6,32,128]{2,1,0:T(8,128)S(1)}, f32[6,32,128]{2,1,0:T(8,128)S(1)}, u32[]{:S(2)}, u32[]{:S(2)}) collective-permute-start(f32[6,32,128]{2,1,0:T(8,128)S(1)} %get-tuple-element.36), channel_id=1, source_target_pairs={{0,16},{16,32},{32,48},{48,64},{64,80},{80,96},{96,112},{112,128},... | collective-permute-start | bytes 294920 | tf_op jit(solution)/shard_map/ppermute | solution.py:255
  3.0 50.7 %collective-permute-start.1 = (f32[6,32,128]{2,1,0:T(8,128)S(1)}, f32[6,32,128]{2,1,0:T(8,128)S(1)}, u32[]{:S(2)}, u32[]{:S(2)}) collective-permute-start(f32[6,32,128]{2,1,0:T(8,128)S(1)} %get-tuple-element.35), channel_id=1, source_target_pairs={{16,0},{32,16},{48,32},{64,48},{80,64},{96,80},{112,96},{128,112},... | collective-permute-start | bytes 294920 | tf_op jit(solution)/shard_map/ppermute | solution.py:256
  11.3 14.4 %collective-permute-start.2 = (bf16[1,2,8,4224]{3,2,1,0:T(8,128)(2,1)S(1)}, bf16[1,2,8,4224]{3,2,1,0:T(8,128)(2,1)S(1)}, u32[]{:S(2)}, u32[]{:S(2)}) collective-permute-start(bf16[1,2,8,4224]{3,2,1,0:T(8,128)(2,1)S(1)} %fusion.3), channel_id=1, source_target_pairs={{0,0},{1,16},{2,32},{3,48},{4,64},{5,80},{6,96},{7,112},{8,128},{9... | collective-permute-start | bytes 405512 | tf_op jit(solution)/shard_map/ppermute | solution.py:202
  25.7 5.0 %collective-permute-start.3 = (bf16[2,8,4224]{2,1,0:T(8,128)(2,1)S(1)}, bf16[2,8,4224]{2,1,0:T(8,128)(2,1)S(1)}, u32[]{:S(2)}, u32[]{:S(2)}) collective-permute-start(bf16[2,8,4224]{2,1,0:T(8,128)(2,1)S(1)} %bitcast.36), channel_id=1, source_target_pairs={{0,8},{1,9},{2,10},{3,11},{4,12},{5,13},{6,14},{7,15},{8,0},{9,1},... | collective-permute-start | bytes 405512 | tf_op jit(solution)/shard_map/ppermute | solution.py:225
  30.8 6.5 %collective-permute-start.4 = (bf16[4,8,4224]{2,1,0:T(8,128)(2,1)S(1)}, bf16[4,8,4224]{2,1,0:T(8,128)(2,1)S(1)}, u32[]{:S(2)}, u32[]{:S(2)}) collective-permute-start(bf16[4,8,4224]{2,1,0:T(8,128)(2,1)S(1)} %pad_maximum_fusion.2), channel_id=1, source_target_pairs={{0,2},{1,3},{2,0},{3,1},{4,6},{5,7},{6,4},{7,5},{8,10},{9,11},{10,... | collective-permute-start | bytes 811016 | tf_op jit(solution)/shard_map/ppermute | solution.py:225
  37.4 10.7 %collective-permute-start.5 = (bf16[8,8,4224]{2,1,0:T(8,128)(2,1)S(1)}, bf16[8,8,4224]{2,1,0:T(8,128)(2,1)S(1)}, u32[]{:S(2)}, u32[]{:S(2)}) collective-permute-start(bf16[8,8,4224]{2,1,0:T(8,128)(2,1)S(1)} %pad_maximum_fusion.1), channel_id=1, source_target_pairs={{0,6},{1,7},{2,4},{3,5},{4,2},{5,3},{6,0},{7,1},{8,14},{9,15},{10,... | collective-permute-start | bytes 1622024 | tf_op jit(solution)/shard_map/ppermute | solution.py:225
  48.2 2.8 %collective-permute-start.6 = (bf16[16,8,4224]{2,1,0:T(8,128)(2,1)S(1)}, bf16[16,8,4224]{2,1,0:T(8,128)(2,1)S(1)}, u32[]{:S(2)}, u32[]{:S(2)}) collective-permute-start(bf16[16,8,4224]{2,1,0:T(8,128)(2,1)S(1)} %pad_maximum_fusion), channel_id=1, source_target_pairs={{0,1},{1,0},{2,3},{3,2},{4,5},{5,4},{6,7},{7,6},{8,9},{9,8},{10,11... | collective-permute-start | bytes 3244040 | tf_op jit(solution)/shard_map/ppermute | solution.py:225
  53.6 0.6 copy-start.4
  53.6 0.7 copy-start.5
  58.3 11.0 %collective-permute-start.7 = (f32[6,32,128]{2,1,0:T(8,128)}, f32[6,32,128]{2,1,0:T(8,128)S(1)}, u32[]{:S(2)}, u32[]{:S(2)}) collective-permute-start(f32[6,32,128]{2,1,0:T(8,128)} %get-tuple-element.26), channel_id=1, source_target_pairs={{0,16},{16,32},{32,48},{48,64},{64,80},{80,96},{96,112},{112,128},... | collective-permute-start | bytes 294920 | tf_op jit(solution)/shard_map/ppermute | solution.py:255
  58.3 11.1 %collective-permute-start.8 = (f32[6,32,128]{2,1,0:T(8,128)}, f32[6,32,128]{2,1,0:T(8,128)S(1)}, u32[]{:S(2)}, u32[]{:S(2)}) collective-permute-start(f32[6,32,128]{2,1,0:T(8,128)} %get-tuple-element.28), channel_id=1, source_target_pairs={{16,0},{32,16},{48,32},{64,48},{80,64},{96,80},{112,96},{128,112},... | collective-permute-start | bytes 294920 | tf_op jit(solution)/shard_map/ppermute | solution.py:256
  69.3 0.6 copy-start.2
  69.3 0.7 copy-start.3
  74.1 8.4 %collective-permute-start.9 = (f32[6,32,128]{2,1,0:T(8,128)}, f32[6,32,128]{2,1,0:T(8,128)S(1)}, u32[]{:S(2)}, u32[]{:S(2)}) collective-permute-start(f32[6,32,128]{2,1,0:T(8,128)} %get-tuple-element.29), channel_id=1, source_target_pairs={{0,16},{16,32},{32,48},{48,64},{64,80},{80,96},{96,112},{112,128},... | collective-permute-start | bytes 294920 | tf_op jit(solution)/shard_map/ppermute | solution.py:255
  74.1 8.4 %collective-permute-start.10 = (f32[6,32,128]{2,1,0:T(8,128)}, f32[6,32,128]{2,1,0:T(8,128)S(1)}, u32[]{:S(2)}, u32[]{:S(2)}) collective-permute-start(f32[6,32,128]{2,1,0:T(8,128)} %get-tuple-element.31), channel_id=1, source_target_pairs={{16,0},{32,16},{48,32},{64,48},{80,64},{96,80},{112,96},{128,112},... | collective-permute-start | bytes 294920 | tf_op jit(solution)/shard_map/ppermute | solution.py:256
  82.5 0.6 copy-start
  82.5 0.7 copy-start.1

commit v17 on v11

--- a/solution.py
+++ b/solution.py
@@ -252,8 +252,8 @@
     down = [(j, i) for i, j in up]
 
     def step(field, send_up, send_down, prev=None, scale=1.0):
+        high_rim = lax.ppermute(send_down, "grid", down)
         low_rim = lax.ppermute(send_up, "grid", up)
-        high_rim = lax.ppermute(send_down, "grid", down)
         return apply_op(
             shifts, low_rim, field, high_rim, potential, pick, place, proj_in, gain_in, prev, scale
         )

time: 87.6 us -> 87.6 us (level)
  no operation moved by 1% of the time
where the time goes in v17:
time: 87.6 us; the launch traced here: 87.2 us
  waiting for transfers between devices  34.2 us (39%)
  starting transfers between devices  26.5 us (30%)
  Pallas kernels  12.5 us (14%)
  other arithmetic  6.63 us (8%)
  local copies, waits for them, and re-layouts  5.94 us (7%)
  between operations  1.47 us (2%)
    ppermute x4, waiting for transfers between devices, shards(): lax.ppermute(gathered, 'states', [(s, exchange(s)) for s in range(n_state...  21.9 us
    ppermute x3, starting transfers between devices, step(): high_rim = lax.ppermute(send_down, 'grid', down)  20.1 us
    pallas_call x3, Pallas kernels, apply_op(): pl.pallas_call(make_kernel(scale, prev is not None, home_count, proj.shap...  12.5 us
    ppermute x1, waiting for transfers between devices, shards(): packed = lax.ppermute(packed, ('grid', 'states'), pairs)  6.33 us
    ppermute x3, waiting for transfers between devices, step(): low_rim = lax.ppermute(send_up, 'grid', up)  6.03 us
    unnamed x19, local copies, waits for them, and re-layouts  3.21 us
    ppermute x4, starting transfers between devices, shards(): lax.ppermute(gathered, 'states', [(s, exchange(s)) for s in range(n_state...  2.42 us
    ppermute x3, starting transfers between devices, step(): low_rim = lax.ppermute(send_up, 'grid', up)  2 us
  transfers between devices with their start and end apart: 11, of which 7 were waited for; matrix products, arithmetic and copies ran while one was open for 11% of the time, Pallas kernels for 0%

profile of v17, /device:TPU:6, one launch (start us, length us, event | category | flops | bytes accessed | tf_op | source)
XLA Modules:
  0.0 87.2 jit_solution(17261883075937281680)
XLA Ops:
  0.0 1.0 %slice_bitcast_fusion.1 = (f32[6,32,128]{2,1,0:T(8,128)S(1)}, f32[6,32,128]{2,1,0:T(8,128)S(1)}) fusion(f32[1,16,32,128]{3,2,1,0:T(8,128)} %param.9), kind=kLoop, calls=%fused_computation.13 | loop fusion | bytes 393216 | tf_op jit(solution)/shard_map/slice | solution.py:262
  1.0 2.0 %collective-permute-start = (f32[6,32,128]{2,1,0:T(8,128)S(1)}, f32[6,32,128]{2,1,0:T(8,128)S(1)}, u32[]{:S(2)}, u32[]{:S(2)}) collective-permute-start(f32[6,32,128]{2,1,0:T(8,128)S(1)} %get-tuple-element.36), channel_id=1, source_target_pairs={{0,16},{16,32},{32,48},{48,64},{64,80},{80,96},{96,112},{112,128},... | collective-permute-start | bytes 294920 | tf_op jit(solution)/shard_map/ppermute | solution.py:256
  3.0 6.7 %collective-permute-start.1 = (f32[6,32,128]{2,1,0:T(8,128)S(1)}, f32[6,32,128]{2,1,0:T(8,128)S(1)}, u32[]{:S(2)}, u32[]{:S(2)}) collective-permute-start(f32[6,32,128]{2,1,0:T(8,128)S(1)} %get-tuple-element.35), channel_id=1, source_target_pairs={{16,0},{32,16},{48,32},{64,48},{80,64},{96,80},{112,96},{128,112},... | collective-permute-start | bytes 294920 | tf_op jit(solution)/shard_map/ppermute | solution.py:255
  10.4 0.9 %fusion.3 = bf16[1,2,8,4224]{3,2,1,0:T(8,128)(2,1)S(1)} fusion(bf16[1,2,8,1]{3,2,1,0:T(8,128)(2,1)S(1)} %copy.11, bf16[1,2,8,4096]{3,2,1,0:T(8,128)(2,1)} %param.11), kind=kLoop, calls=%fused_computation.12 | loop fusion | flops 405504 | bytes 266272 | tf_op jit(solution)/shard_map/concatenate | solution.py:198
  11.3 1.9 %collective-permute-start.2 = (bf16[1,2,8,4224]{3,2,1,0:T(8,128)(2,1)S(1)}, bf16[1,2,8,4224]{3,2,1,0:T(8,128)(2,1)S(1)}, u32[]{:S(2)}, u32[]{:S(2)}) collective-permute-start(bf16[1,2,8,4224]{3,2,1,0:T(8,128)(2,1)S(1)} %fusion.3), channel_id=1, source_target_pairs={{0,0},{1,16},{2,32},{3,48},{4,64},{5,80},{6,96},{7,112},{8,128},{9... | collective-permute-start | bytes 405512 | tf_op jit(solution)/shard_map/ppermute | solution.py:200
  14.7 0.9 fusion.1.pick_ref
  15.5 0.8 fusion.place_ref
  17.0 0.9 %convert_reduce_fusion.1 = s32[10]{0:T(128)S(1)} fusion(s32[10]{0:T(128)} %param.13), kind=kLoop, calls=%fused_computation.21 | loop fusion | flops 490 | bytes 80 | tf_op jit(solution)/shard_map/reduce_sum | solution.py:192
  18.0 1.3 %iota_reduce_fusion = (pred[10]{0:T(512)(128)(4,1)}, s32[10]{0:T(128)S(1)}) fusion(s32[16]{0:T(128)S(1)} %stack.79, s32[10]{0:T(128)} %param.13), kind=kLoop, calls=%fused_computation.23 | loop fusion | flops 1210 | bytes 154 | tf_op jit(solution)/shard_map/shards/reduce | solution.py:228
  19.4 6.3 %collective-permute-done.2 = bf16[1,2,8,4224]{3,2,1,0:T(8,128)(2,1)S(1)} collective-permute-done((bf16[1,2,8,4224]{3,2,1,0:T(8,128)(2,1)S(1)}, bf16[1,2,8,4224]{3,2,1,0:T(8,128)(2,1)S(1)}, u32[]{:S(2)}, u32[]{:S(2)}) %collective-permute-start.2) | collective-permute-done | bytes 135200 | tf_op jit(solution)/shard_map/ppermute | solution.py:200
  25.7 1.6 %collective-permute-start.3 = (bf16[2,8,4224]{2,1,0:T(8,128)(2,1)S(1)}, bf16[2,8,4224]{2,1,0:T(8,128)(2,1)S(1)}, u32[]{:S(2)}, u32[]{:S(2)}) collective-permute-start(bf16[2,8,4224]{2,1,0:T(8,128)(2,1)S(1)} %bitcast.36), channel_id=1, source_target_pairs={{0,8},{1,9},{2,10},{3,11},{4,12},{5,13},{6,14},{7,15},{8,0},{9,1},... | collective-permute-start | bytes 405512 | tf_op jit(solution)/shard_map/ppermute | solution.py:223
  27.9 2.8 %collective-permute-done.3 = bf16[2,8,4224]{2,1,0:T(8,128)(2,1)S(1)} collective-permute-done((bf16[2,8,4224]{2,1,0:T(8,128)(2,1)S(1)}, bf16[2,8,4224]{2,1,0:T(8,128)(2,1)S(1)}, u32[]{:S(2)}, u32[]{:S(2)}) %collective-permute-start.3) | collective-permute-done | bytes 135200 | tf_op jit(solution)/shard_map/ppermute | solution.py:223
  31.4 5.9 %collective-permute-done.4 = bf16[4,8,4224]{2,1,0:T(8,128)(2,1)S(1)} collective-permute-done((bf16[4,8,4224]{2,1,0:T(8,128)(2,1)S(1)}, bf16[4,8,4224]{2,1,0:T(8,128)(2,1)S(1)}, u32[]{:S(2)}, u32[]{:S(2)}) %collective-permute-start.4) | collective-permute-done | bytes 270368 | tf_op jit(solution)/shard_map/ppermute | solution.py:223
  37.5 10.5 %collective-permute-done.5 = bf16[8,8,4224]{2,1,0:T(8,128)(2,1)S(1)} collective-permute-done((bf16[8,8,4224]{2,1,0:T(8,128)(2,1)S(1)}, bf16[8,8,4224]{2,1,0:T(8,128)(2,1)S(1)}, u32[]{:S(2)}, u32[]{:S(2)}) %collective-permute-start.5) | collective-permute-done | bytes 540704 | tf_op jit(solution)/shard_map/ppermute | solution.py:223
  48.4 2.6 %collective-permute-done.6 = bf16[16,8,4224]{2,1,0:T(8,128)(2,1)S(1)} collective-permute-done((bf16[16,8,4224]{2,1,0:T(8,128)(2,1)S(1)}, bf16[16,8,4224]{2,1,0:T(8,128)(2,1)S(1)}, u32[]{:S(2)}, u32[]{:S(2)}) %collective-permute-start.6) | collective-permute-done | bytes 1081376 | tf_op jit(solution)/shard_map/ppermute | solution.py:223
  51.9 1.0 %copy.12 = bf16[10,8,32,128]{3,2,1,0:T(8,128)(2,1)} copy(bf16[10,8,32,128]{3,1,2,0:T(8,128)(2,1)S(1)} %slice_bitcast_fusion) | data formatting | bytes 1310720
  53.1 0.8 broadcast_in_dim.36.gain_ref
  53.9 4.1 %shard_map.73 = (f32[16,32,128]{2,1,0:T(8,128)}, f32[6,32,128]{2,1,0:T(8,128)}, f32[6,32,128]{2,1,0:T(8,128)}) custom-call(s32[4]{0:T(128)} %pad_add_fusion.shift_ref, f32[6,32,128]{2,1,0:T(8,128)} %copy-done, f32[16,32,128]{2,1,0:T(8,128)} %bitcast.40, f32[6,32,128]{2,1,0:T(8,128)} %copy-done.1, f32[16,32,128]{2,1,0:T(8,128)} %pot_ref.5, ...), custom_call_target="tpu_custom_call" | custom-call | tf_op jit(solution)/shard_map/pallas_call | solution.py:161
  58.0 7.8 %collective-permute-start.8 = (f32[6,32,128]{2,1,0:T(8,128)}, f32[6,32,128]{2,1,0:T(8,128)S(1)}, u32[]{:S(2)}, u32[]{:S(2)}) collective-permute-start(f32[6,32,128]{2,1,0:T(8,128)} %get-tuple-element.28), channel_id=1, source_target_pairs={{16,0},{32,16},{48,32},{64,48},{80,64},{96,80},{112,96},{128,112},... | collective-permute-start | bytes 294920 | tf_op jit(solution)/shard_map/ppermute | solution.py:255
  65.8 3.2 %collective-permute-done.7.lo_ref = f32[6,32,128]{2,1,0:T(8,128)S(1)} collective-permute-done((f32[6,32,128]{2,1,0:T(8,128)}, f32[6,32,128]{2,1,0:T(8,128)S(1)}, u32[]{:S(2)}, u32[]{:S(2)}) %collective-permute-start.7) | collective-permute-done | bytes 98336 | tf_op jit(solution)/shard_map/ppermute | solution.py:256
  69.7 4.2 %shard_map.74 = (f32[16,32,128]{2,1,0:T(8,128)}, f32[6,32,128]{2,1,0:T(8,128)}, f32[6,32,128]{2,1,0:T(8,128)}) custom-call(s32[4]{0:T(128)} %pad_add_fusion.shift_ref, f32[6,32,128]{2,1,0:T(8,128)} %copy-done.4, f32[16,32,128]{2,1,0:T(8,128)} %get-tuple-element.27.v_ref.rest_0_, f32[6,32,128]{2,1,0:T(8,128)} %copy-done.5, f32[16,32,128]{2,1,0:T(8,128)} %pot_ref.5, ...), custom_call_target="tpu_custom_call" | custom-call | tf_op jit(solution)/shard_map/pallas_call | solution.py:161
  73.9 5.6 %collective-permute-start.10 = (f32[6,32,128]{2,1,0:T(8,128)}, f32[6,32,128]{2,1,0:T(8,128)S(1)}, u32[]{:S(2)}, u32[]{:S(2)}) collective-permute-start(f32[6,32,128]{2,1,0:T(8,128)} %get-tuple-element.31), channel_id=1, source_target_pairs={{16,0},{32,16},{48,32},{64,48},{80,64},{96,80},{112,96},{128,112},... | collective-permute-start | bytes 294920 | tf_op jit(solution)/shard_map/ppermute | solution.py:255
  79.6 2.8 %collective-permute-done.9.lo_ref = f32[6,32,128]{2,1,0:T(8,128)S(1)} collective-permute-done((f32[6,32,128]{2,1,0:T(8,128)}, f32[6,32,128]{2,1,0:T(8,128)S(1)}, u32[]{:S(2)}, u32[]{:S(2)}) %collective-permute-start.9) | collective-permute-done | bytes 98336 | tf_op jit(solution)/shard_map/ppermute | solution.py:256
  83.0 4.2 %shard_map.75 = (f32[16,32,128]{2,1,0:T(8,128)}, f32[6,32,128]{2,1,0:T(8,128)}, f32[6,32,128]{2,1,0:T(8,128)}) custom-call(s32[4]{0:T(128)} %pad_add_fusion.shift_ref, f32[6,32,128]{2,1,0:T(8,128)} %copy-done.2, f32[16,32,128]{2,1,0:T(8,128)} %get-tuple-element.30.v_ref, f32[6,32,128]{2,1,0:T(8,128)} %copy-done.3, f32[16,32,128]{2,1,0:T(8,128)} %pot_ref.5, ...), custom_call_target="tpu_custom_call" | custom-call | tf_op jit(solution)/shard_map/pallas_call | solution.py:161
  (42 shorter events, 5.9 us)
Async XLA Ops:
  1.0 52.1 %collective-permute-start = (f32[6,32,128]{2,1,0:T(8,128)S(1)}, f32[6,32,128]{2,1,0:T(8,128)S(1)}, u32[]{:S(2)}, u32[]{:S(2)}) collective-permute-start(f32[6,32,128]{2,1,0:T(8,128)S(1)} %get-tuple-element.36), channel_id=1, source_target_pairs={{0,16},{16,32},{32,48},{48,64},{64,80},{80,96},{96,112},{112,128},... | collective-permute-start | bytes 294920 | tf_op jit(solution)/shard_map/ppermute | solution.py:256
  3.0 50.2 %collective-permute-start.1 = (f32[6,32,128]{2,1,0:T(8,128)S(1)}, f32[6,32,128]{2,1,0:T(8,128)S(1)}, u32[]{:S(2)}, u32[]{:S(2)}) collective-permute-start(f32[6,32,128]{2,1,0:T(8,128)S(1)} %get-tuple-element.35), channel_id=1, source_target_pairs={{16,0},{32,16},{48,32},{64,48},{80,64},{96,80},{112,96},{128,112},... | collective-permute-start | bytes 294920 | tf_op jit(solution)/shard_map/ppermute | solution.py:255
  11.3 14.4 %collective-permute-start.2 = (bf16[1,2,8,4224]{3,2,1,0:T(8,128)(2,1)S(1)}, bf16[1,2,8,4224]{3,2,1,0:T(8,128)(2,1)S(1)}, u32[]{:S(2)}, u32[]{:S(2)}) collective-permute-start(bf16[1,2,8,4224]{3,2,1,0:T(8,128)(2,1)S(1)} %fusion.3), channel_id=1, source_target_pairs={{0,0},{1,16},{2,32},{3,48},{4,64},{5,80},{6,96},{7,112},{8,128},{9... | collective-permute-start | bytes 405512 | tf_op jit(solution)/shard_map/ppermute | solution.py:200
  25.7 5.0 %collective-permute-start.3 = (bf16[2,8,4224]{2,1,0:T(8,128)(2,1)S(1)}, bf16[2,8,4224]{2,1,0:T(8,128)(2,1)S(1)}, u32[]{:S(2)}, u32[]{:S(2)}) collective-permute-start(bf16[2,8,4224]{2,1,0:T(8,128)(2,1)S(1)} %bitcast.36), channel_id=1, source_target_pairs={{0,8},{1,9},{2,10},{3,11},{4,12},{5,13},{6,14},{7,15},{8,0},{9,1},... | collective-permute-start | bytes 405512 | tf_op jit(solution)/shard_map/ppermute | solution.py:223
  30.8 6.5 %collective-permute-start.4 = (bf16[4,8,4224]{2,1,0:T(8,128)(2,1)S(1)}, bf16[4,8,4224]{2,1,0:T(8,128)(2,1)S(1)}, u32[]{:S(2)}, u32[]{:S(2)}) collective-permute-start(bf16[4,8,4224]{2,1,0:T(8,128)(2,1)S(1)} %pad_maximum_fusion.2), channel_id=1, source_target_pairs={{0,2},{1,3},{2,0},{3,1},{4,6},{5,7},{6,4},{7,5},{8,10},{9,11},{10,... | collective-permute-start | bytes 811016 | tf_op jit(solution)/shard_map/ppermute | solution.py:223
  37.4 10.7 %collective-permute-start.5 = (bf16[8,8,4224]{2,1,0:T(8,128)(2,1)S(1)}, bf16[8,8,4224]{2,1,0:T(8,128)(2,1)S(1)}, u32[]{:S(2)}, u32[]{:S(2)}) collective-permute-start(bf16[8,8,4224]{2,1,0:T(8,128)(2,1)S(1)} %pad_maximum_fusion.1), channel_id=1, source_target_pairs={{0,6},{1,7},{2,4},{3,5},{4,2},{5,3},{6,0},{7,1},{8,14},{9,15},{10,... | collective-permute-start | bytes 1622024 | tf_op jit(solution)/shard_map/ppermute | solution.py:223
  48.2 2.8 %collective-permute-start.6 = (bf16[16,8,4224]{2,1,0:T(8,128)(2,1)S(1)}, bf16[16,8,4224]{2,1,0:T(8,128)(2,1)S(1)}, u32[]{:S(2)}, u32[]{:S(2)}) collective-permute-start(bf16[16,8,4224]{2,1,0:T(8,128)(2,1)S(1)} %pad_maximum_fusion), channel_id=1, source_target_pairs={{0,1},{1,0},{2,3},{3,2},{4,5},{5,4},{6,7},{7,6},{8,9},{9,8},{10,11... | collective-permute-start | bytes 3244040 | tf_op jit(solution)/shard_map/ppermute | solution.py:223
  53.1 0.8 copy-start
  53.1 0.8 copy-start.1
  58.0 11.1 %collective-permute-start.7 = (f32[6,32,128]{2,1,0:T(8,128)}, f32[6,32,128]{2,1,0:T(8,128)S(1)}, u32[]{:S(2)}, u32[]{:S(2)}) collective-permute-start(f32[6,32,128]{2,1,0:T(8,128)} %get-tuple-element.26), channel_id=1, source_target_pairs={{0,16},{16,32},{32,48},{48,64},{64,80},{80,96},{96,112},{112,128},... | collective-permute-start | bytes 294920 | tf_op jit(solution)/shard_map/ppermute | solution.py:256
  58.0 11.1 %collective-permute-start.8 = (f32[6,32,128]{2,1,0:T(8,128)}, f32[6,32,128]{2,1,0:T(8,128)S(1)}, u32[]{:S(2)}, u32[]{:S(2)}) collective-permute-start(f32[6,32,128]{2,1,0:T(8,128)} %get-tuple-element.28), channel_id=1, source_target_pairs={{16,0},{32,16},{48,32},{64,48},{80,64},{96,80},{112,96},{128,112},... | collective-permute-start | bytes 294920 | tf_op jit(solution)/shard_map/ppermute | solution.py:255
  69.1 0.6 copy-start.4
  69.1 0.7 copy-start.5
  73.9 8.4 %collective-permute-start.9 = (f32[6,32,128]{2,1,0:T(8,128)}, f32[6,32,128]{2,1,0:T(8,128)S(1)}, u32[]{:S(2)}, u32[]{:S(2)}) collective-permute-start(f32[6,32,128]{2,1,0:T(8,128)} %get-tuple-element.29), channel_id=1, source_target_pairs={{0,16},{16,32},{32,48},{48,64},{64,80},{80,96},{96,112},{112,128},... | collective-permute-start | bytes 294920 | tf_op jit(solution)/shard_map/ppermute | solution.py:256
  73.9 8.4 %collective-permute-start.10 = (f32[6,32,128]{2,1,0:T(8,128)}, f32[6,32,128]{2,1,0:T(8,128)S(1)}, u32[]{:S(2)}, u32[]{:S(2)}) collective-permute-start(f32[6,32,128]{2,1,0:T(8,128)} %get-tuple-element.31), channel_id=1, source_target_pairs={{16,0},{32,16},{48,32},{64,48},{80,64},{96,80},{112,96},{128,112},... | collective-permute-start | bytes 294920 | tf_op jit(solution)/shard_map/ppermute | solution.py:255
  82.4 0.6 copy-start.2
  82.4 0.7 copy-start.3
